TPU v7x, 32 devices: a whole 2x2x4 slice. The times are simulated.
32 devices in a mesh: group: 2 (over x), tm: 16 (over z, y, core).
Axes of the slice: x: 2, y: 2, z: 4, core: 2. Of those that a mesh axis runs over, the one named last changes fastest.
Arguments:
- queries: bfloat16 [8192, 1536], P(('group', 'tm')), parts along dimension 0, may hold values from -7 to 7, as said below
- keys: bfloat16 [8192, 1536], P(('group', 'tm')), parts along dimension 0, may hold values from -6 to 6, as said below
- values: bfloat16 [8192, 1536], P(('group', 'tm')), parts along dimension 0, may hold values from -6 to 6
- grad_out: bfloat16 [8192, 1536], P(('group', 'tm')), parts along dimension 0, may hold values from -96 to 96
- block_list: int32 [128, 30], P(('group', 'tm')), parts along dimension 0, may hold values 0 or 1
Outputs:
- grad_queries: bfloat16 [8192, 1536], P(('group', 'tm')), parts along dimension 0
- grad_keys: bfloat16 [8192, 1536], P(('group', 'tm')), parts along dimension 0
- grad_values: bfloat16 [8192, 1536], P(('group', 'tm')), parts along dimension 0
There are 2 independent parts, one for each index of `group`. A program takes and returns all parts, laid end to end along the dimension named above; each array names one. Nothing has to cross between parts.
Inputs may be any that keep to these rules, and one draw needn't show every extreme that they name: `queries`: entries of order one. `keys`: entries of order one. `block_list`: columns follow the candidate order of the steps.
All inputs are finite; a program needn't handle non-finite values. No bound on the sum of `block_list` on one device may be relied on, other than what follows from the above.
Results may differ from a plain program's by a relative error of at most 0.0073.
Values may be sent and summed in bfloat16 or wider, within the bound.
No kernel may reach another device: no remote copies, remote signals or barrier semaphores. Data moves between devices by JAX's collectives and lax.ppermute only.
A program may use at most 128 MiB of HBM per device.

v0:
```python
import jax
import jax.numpy as jnp
import numpy as np
from jax import lax
from jax.sharding import PartitionSpec as P

HEADS = 12
HDIM = 128
BLOCK = 64
REACH = 2
FRAMES = 2
BANDS = 2


def from_behind(value, axis, steps):
    count = lax.axis_size(axis)
    first, last = (max(0, -steps), min(count, count - steps))
    return lax.ppermute(value, axis, [(source, source + steps) for source in range(first, last)])


def settle(tensor):
    return lax.optimization_barrier(tensor.astype(jnp.bfloat16)).astype(jnp.float32)


def pair_tables(slots):
    blocks_group = FRAMES * BANDS
    query_block = np.arange(blocks_group)[:, None]
    key_block = np.arange(slots * blocks_group)[None, :]
    slot_of = key_block // blocks_group
    frame_key = key_block // BANDS % FRAMES
    band_key = key_block % BANDS
    frame_query = query_block // BANDS
    band_query = query_block % BANDS
    cand = (slot_of * FRAMES + frame_key) * 3 + band_key - band_query + 1
    own_block = (slot_of == REACH) & (frame_key == frame_query) & (band_key == band_query)
    cand = cand + 0 * query_block
    slot_full = slot_of + 0 * query_block
    return (cand, own_block, slot_full)


def listed_mask(block_rows, group_index, groups):
    slots = 2 * REACH + 1
    cand, own_block, slot_full = pair_tables(slots)
    chosen = (block_rows > 0)[np.arange(FRAMES * BANDS)[:, None], cand]
    group_pos = group_index + jnp.asarray(slot_full, jnp.int32) - REACH
    group_ok = (group_pos >= 0) & (group_pos < groups)
    allowed = chosen & group_ok | jnp.asarray(own_block)
    return allowed[:, None, :, None]


def group_grads(query_rows, grad_rows, key_window, value_window, block_rows, group_index, groups):
    scaling = HDIM ** (-0.5)
    allowed = listed_mask(block_rows, group_index, groups)
    slots = key_window.shape[0]
    tok_dev = query_rows.shape[0]
    width = query_rows.shape[1]
    key_flat = key_window.reshape(slots * tok_dev, width)
    value_flat = value_window.reshape(slots * tok_dev, width)
    query_list, key_list, value_list, log_list, delta_list = ([], [], [], [], [])
    for head_index in range(HEADS):
        cols = slice(head_index * HDIM, (head_index + 1) * HDIM)
        query_head = query_rows[:, cols]
        grad_head = grad_rows[:, cols]
        key_head = key_flat[:, cols]
        value_head = value_flat[:, cols]
        scores = (
            jnp.einsum("qd,kd->qk", query_head, key_head, preferred_element_type=jnp.float32)
            * scaling
        )
        shaped = jnp.where(
            allowed, scores.reshape(FRAMES * BANDS, BLOCK, slots * FRAMES * BANDS, BLOCK), -jnp.inf
        )
        row_max = jnp.max(shaped, axis=(2, 3), keepdims=True)
        log_total = row_max + jnp.log(
            jnp.sum(jnp.exp(shaped - row_max), axis=(2, 3), keepdims=True)
        )
        weights = jnp.exp(shaped - log_total).reshape(scores.shape)
        weights_low = weights.astype(jnp.bfloat16)
        attended = jnp.einsum(
            "qk,kd->qd", weights_low, value_head, preferred_element_type=jnp.float32
        )
        deltas = jnp.sum(grad_head.astype(jnp.float32) * attended, axis=-1, keepdims=True)
        grad_probs = jnp.einsum(
            "qd,kd->qk", grad_head, value_head, preferred_element_type=jnp.float32
        )
        grad_scores = (weights * (grad_probs - deltas)).astype(jnp.bfloat16)
        query_list.append(
            jnp.einsum("qk,kd->qd", grad_scores, key_head, preferred_element_type=jnp.float32)
            * scaling
        )
        log_list.append(log_total.reshape(tok_dev))
        delta_list.append(deltas.reshape(tok_dev))
        key_grad = (
            jnp.einsum("qk,qd->kd", grad_scores, query_head, preferred_element_type=jnp.float32)
            * scaling
        )
        value_grad = jnp.einsum(
            "qk,qd->kd", weights_low, grad_head, preferred_element_type=jnp.float32
        )
        key_list.append(key_grad.reshape(slots, tok_dev, HDIM))
        value_list.append(value_grad.reshape(slots, tok_dev, HDIM))
    key_all = jnp.concatenate(key_list, axis=-1)
    value_all = jnp.concatenate(value_list, axis=-1)
    return (
        jnp.concatenate(query_list, axis=-1),
        key_all,
        value_all,
        jnp.stack(log_list),
        jnp.stack(delta_list),
    )


def local(queries, keys, values, grad_out, block_list):
    groups = lax.axis_size("tm")
    here_index = lax.axis_index("tm")
    key_parts = []
    value_parts = []
    for offset in range(-REACH, REACH + 1):
        if offset == 0:
            key_parts.append(keys)
            value_parts.append(values)
        else:
            near_keys, near_values = from_behind((keys, values), "tm", -offset)
            key_parts.append(near_keys)
            value_parts.append(near_values)
    key_window = jnp.stack(key_parts)
    value_window = jnp.stack(value_parts)
    key_total = jnp.zeros(keys.shape, jnp.float32)
    value_total = jnp.zeros(values.shape, jnp.float32)
    query_grad, key_grad, value_grad, log_totals, deltas = group_grads(
        queries, grad_out, key_window, value_window, block_list, here_index, groups
    )
    for offset in range(-REACH, REACH + 1):
        slot_index = offset + REACH
        if offset == 0:
            key_total = key_total + settle(key_grad[slot_index])
            value_total = value_total + settle(value_grad[slot_index])
        else:
            back_keys, back_values = from_behind(
                (
                    key_grad[slot_index].astype(jnp.bfloat16),
                    value_grad[slot_index].astype(jnp.bfloat16),
                ),
                "tm",
                offset,
            )
            key_total = key_total + back_keys.astype(jnp.float32)
            value_total = value_total + back_values.astype(jnp.float32)
    return (
        query_grad.astype(jnp.bfloat16),
        key_total.astype(jnp.bfloat16),
        value_total.astype(jnp.bfloat16),
    )


def solution(mesh):
    placed = (
        P(("group", "tm"), None),
        P(("group", "tm"), None),
        P(("group", "tm"), None),
        P(("group", "tm"), None),
        P(("group", "tm"), None),
    )
    return jax.shard_map(
        local,
        mesh=mesh,
        in_specs=placed,
        out_specs=(P(("group", "tm"), None), P(("group", "tm"), None), P(("group", "tm"), None)),
        check_vma=False,
    )
```

profile of v0, /device:TPU:8, one launch (start us, length us, event | category | flops | bytes accessed | tf_op | source)
XLA Modules:
  0.0 256.1 jit_solution(282285221689418240)
XLA Ops:
  0.6 3.6 %collective-permute-start = (bf16[256,1536]{1,0:T(8,128)(2,1)}, bf16[256,1536]{1,0:T(8,128)(2,1)}, u32[]{:S(2)}, u32[]{:S(2)}) collective-permute-start(bf16[256,1536]{1,0:T(8,128)(2,1)} %param.12), channel_id=1, source_target_pairs={{0,2},{1,3},{2,4},{3,5},{4,6},{5,7},{6,8},{7,9},{8,10},{9,11},{10,... | collective-permute-start | bytes 2359304 | tf_op jit(solution)/shard_map/ppermute | solution.py:18
  4.2 1.9 collective-permute-start.1
  6.1 4.5 %collective-permute-start.2 = (bf16[256,1536]{1,0:T(8,128)(2,1)}, bf16[256,1536]{1,0:T(8,128)(2,1)}, u32[]{:S(2)}, u32[]{:S(2)}) collective-permute-start(bf16[256,1536]{1,0:T(8,128)(2,1)} %param.12), channel_id=1, source_target_pairs={{1,0},{2,1},{3,2},{4,3},{5,4},{6,5},{7,6},{8,7},{9,8},{10,9},{11,1... | collective-permute-start | bytes 2359304 | tf_op jit(solution)/shard_map/ppermute | solution.py:18
  10.7 2.4 collective-permute-start.3
  13.1 3.4 %collective-permute-start.4 = (bf16[256,1536]{1,0:T(8,128)(2,1)}, bf16[256,1536]{1,0:T(8,128)(2,1)S(1)}, u32[]{:S(2)}, u32[]{:S(2)}) collective-permute-start(bf16[256,1536]{1,0:T(8,128)(2,1)} %param.13), channel_id=1, source_target_pairs={{0,2},{1,3},{2,4},{3,5},{4,6},{5,7},{6,8},{7,9},{8,10},{9,11},{10,... | collective-permute-start | bytes 2359304 | tf_op jit(solution)/shard_map/ppermute | solution.py:18
  16.6 0.7 broadcast_compare_fusion
  17.2 2.1 gather_fusion
  19.5 0.7 fusion.196
  20.7 1.1 broadcast_in_dim.106
  21.8 0.9 fusion.221
  22.7 1.6 copy.44
  24.2 1.6 copy.45
  25.8 1.6 copy.46
  27.3 1.6 copy.47
  28.9 1.6 copy.48
  30.5 1.6 copy.49
  32.0 1.6 copy.50
  33.6 1.6 copy.51
  35.1 1.6 copy.52
  36.7 1.6 copy.53
  38.3 1.6 copy.54
  39.9 0.7 copy.55
  40.6 7.1 %collective-permute-done = bf16[256,1536]{1,0:T(8,128)(2,1)} collective-permute-done((bf16[256,1536]{1,0:T(8,128)(2,1)}, bf16[256,1536]{1,0:T(8,128)(2,1)}, u32[]{:S(2)}, u32[]{:S(2)}) %collective-permute-start) | collective-permute-done | bytes 786464 | tf_op jit(solution)/shard_map/ppermute | solution.py:18
  47.7 1.9 collective-permute-start.5
  49.6 1.2 bitcast_dynamic-update-slice_fusion.9
  50.8 4.5 %collective-permute-start.6 = (bf16[256,1536]{1,0:T(8,128)(2,1)S(1)}, bf16[256,1536]{1,0:T(8,128)(2,1)S(1)}, u32[]{:S(2)}, u32[]{:S(2)}) collective-permute-start(bf16[256,1536]{1,0:T(8,128)(2,1)S(1)} %copy-done.3), channel_id=1, source_target_pairs={{1,0},{2,1},{3,2},{4,3},{5,4},{6,5},{7,6},{8,7},{9,8},{10,9},{11,1... | collective-permute-start | bytes 2359304 | tf_op jit(solution)/shard_map/ppermute | solution.py:18
  55.4 1.2 bitcast_dynamic-update-slice_fusion.8
  56.7 21.8 %collective-permute-start.7 = (bf16[256,1536]{1,0:T(8,128)(2,1)S(1)}, bf16[256,1536]{1,0:T(8,128)(2,1)S(1)}, u32[]{:S(2)}, u32[]{:S(2)}) collective-permute-start(bf16[256,1536]{1,0:T(8,128)(2,1)S(1)} %copy-done.3), channel_id=1, source_target_pairs={{2,0},{3,1},{4,2},{5,3},{6,4},{7,5},{8,6},{9,7},{10,8},{11,9},{12,... | collective-permute-start | bytes 2359304 | tf_op jit(solution)/shard_map/ppermute | solution.py:18
  78.5 1.2 bitcast_dynamic-update-slice_fusion.6
  79.7 4.5 %collective-permute-done.3 = bf16[256,1536]{1,0:T(8,128)(2,1)S(1)} collective-permute-done((bf16[256,1536]{1,0:T(8,128)(2,1)}, bf16[256,1536]{1,0:T(8,128)(2,1)S(1)}, u32[]{:S(2)}, u32[]{:S(2)}) %collective-permute-start.3) | collective-permute-done | bytes 786464 | tf_op jit(solution)/shard_map/ppermute | solution.py:18
  90.0 17.3 %collective-permute-done.7 = bf16[256,1536]{1,0:T(8,128)(2,1)S(1)} collective-permute-done((bf16[256,1536]{1,0:T(8,128)(2,1)S(1)}, bf16[256,1536]{1,0:T(8,128)(2,1)S(1)}, u32[]{:S(2)}, u32[]{:S(2)}) %collective-permute-start.7) | collective-permute-done | bytes 786464 | tf_op jit(solution)/shard_map/ppermute | solution.py:18
  108.1 0.9 fusion.73
  109.8 0.6 copy-done.14
  111.5 1.0 fusion.75
  112.9 0.6 copy-done.13
  114.6 1.0 fusion.77
  116.0 0.6 copy-done.12
  117.6 1.0 fusion.79
  119.0 0.6 copy-done.11
  120.7 1.0 fusion.81
  122.3 0.6 copy-done.10
  124.0 1.0 fusion.83
  127.1 1.0 fusion.85
  139.6 1.8 slice_bitcast_fusion.9
  146.4 4.3 %collective-permute-start.15 = (bf16[256,1536]{0,1:T(8,128)(2,1)S(1)}, bf16[256,1536]{0,1:T(8,128)(2,1)}, u32[]{:S(2)}, u32[]{:S(2)}) collective-permute-start(bf16[256,1536]{0,1:T(8,128)(2,1)S(1)} %get-tuple-element.13), channel_id=1, source_target_pairs={{0,2},{1,3},{2,4},{3,5},{4,6},{5,7},{6,8},{7,9},{8,10},{9,11},{10,... | collective-permute-start | bytes 2359304 | tf_op jit(solution)/shard_map/ppermute | solution.py:18
  150.8 1.9 collective-permute-start.14
  152.7 4.5 %collective-permute-start.13 = (bf16[256,1536]{0,1:T(8,128)(2,1)S(1)}, bf16[256,1536]{0,1:T(8,128)(2,1)}, u32[]{:S(2)}, u32[]{:S(2)}) collective-permute-start(bf16[256,1536]{0,1:T(8,128)(2,1)S(1)} %get-tuple-element.12), channel_id=1, source_target_pairs={{1,0},{2,1},{3,2},{4,3},{5,4},{6,5},{7,6},{8,7},{9,8},{10,9},{11,1... | collective-permute-start | bytes 2359304 | tf_op jit(solution)/shard_map/ppermute | solution.py:18
  157.2 0.9 fusion.87
  158.2 1.9 collective-permute-start.12
  160.1 1.0 fusion.89
  161.1 3.9 %collective-permute-start.11 = (bf16[256,1536]{1,0:T(8,128)(2,1)}, bf16[256,1536]{1,0:T(8,128)(2,1)S(1)}, u32[]{:S(2)}, u32[]{:S(2)}) collective-permute-start(bf16[256,1536]{1,0:T(8,128)(2,1)} %get-tuple-element.18), channel_id=1, source_target_pairs={{0,2},{1,3},{2,4},{3,5},{4,6},{5,7},{6,8},{7,9},{8,10},{9,11},{10,... | collective-permute-start | bytes 2359304 | tf_op jit(solution)/shard_map/ppermute | solution.py:18
  165.0 1.0 fusion.91
  165.9 0.9 fusion.93
  166.9 27.1 %collective-permute-done.15 = bf16[256,1536]{0,1:T(8,128)(2,1)} collective-permute-done((bf16[256,1536]{0,1:T(8,128)(2,1)S(1)}, bf16[256,1536]{0,1:T(8,128)(2,1)}, u32[]{:S(2)}, u32[]{:S(2)}) %collective-permute-start.15) | collective-permute-done | bytes 786464 | tf_op jit(solution)/shard_map/ppermute | solution.py:18
  194.0 1.9 collective-permute-start.10
  195.9 4.5 %collective-permute-start.9 = (bf16[256,1536]{1,0:T(8,128)(2,1)}, bf16[256,1536]{1,0:T(8,128)(2,1)}, u32[]{:S(2)}, u32[]{:S(2)}) collective-permute-start(bf16[256,1536]{1,0:T(8,128)(2,1)} %get-tuple-element.17), channel_id=1, source_target_pairs={{1,0},{2,1},{3,2},{4,3},{5,4},{6,5},{7,6},{8,7},{9,8},{10,9},{11,1... | collective-permute-start | bytes 2359304 | tf_op jit(solution)/shard_map/ppermute | solution.py:18
  200.5 17.7 %collective-permute-start.8 = (bf16[256,1536]{1,0:T(8,128)(2,1)}, bf16[256,1536]{1,0:T(8,128)(2,1)}, u32[]{:S(2)}, u32[]{:S(2)}) collective-permute-start(bf16[256,1536]{1,0:T(8,128)(2,1)} %get-tuple-element.14), channel_id=1, source_target_pairs={{2,0},{3,1},{4,2},{5,3},{6,4},{7,5},{8,6},{9,7},{10,8},{11,9},{12,... | collective-permute-start | bytes 2359304 | tf_op jit(solution)/shard_map/ppermute | solution.py:18
  218.2 0.9 fusion.95
  219.1 2.3 copy.42
  221.4 10.2 %collective-permute-done.12 = bf16[256,1536]{0,1:T(8,128)(2,1)} collective-permute-done((bf16[256,1536]{0,1:T(8,128)(2,1)S(1)}, bf16[256,1536]{0,1:T(8,128)(2,1)}, u32[]{:S(2)}, u32[]{:S(2)}) %collective-permute-start.12) | collective-permute-done | bytes 786464 | tf_op jit(solution)/shard_map/ppermute | solution.py:18
  231.6 2.3 add_convert_fusion
  234.0 1.2 copy.43
  235.1 17.9 %collective-permute-done.8 = bf16[256,1536]{1,0:T(8,128)(2,1)} collective-permute-done((bf16[256,1536]{1,0:T(8,128)(2,1)}, bf16[256,1536]{1,0:T(8,128)(2,1)}, u32[]{:S(2)}, u32[]{:S(2)}) %collective-permute-start.8) | collective-permute-done | bytes 786464 | tf_op jit(solution)/shard_map/ppermute | solution.py:18
  253.1 3.0 %add_convert_fusion.1 = bf16[256,1536]{1,0:T(8,128)(2,1)} fusion(bf16[256,1536]{1,0:T(8,128)(2,1)S(1)} %collective-permute-done.11, bf16[256,1536]{1,0:T(8,128)(2,1)} %collective-permute-done.10, bf16[256,1536]{1,0:T(8,128)(2,1)S(1)} %get-tuple-element.16, bf16[256,1536]{1,0:T(8,128)(2,1)} %collective-permute-done.9, bf16[256,1536]{1,0:T(8,128)(2,1)} %collective-permute-done.8), kind=kLoop, calls=%fused_computation.98 | loop fusion | flops 3932160 | bytes 4718592 | tf_op jit(solution)/shard_map/convert_element_type | solution.py:151
  (156 shorter events, 33.4 us)
Async XLA Ops:
  0.6 21.1 %copy-start = (bf16[256,1536]{1,0:T(8,128)(2,1)S(1)}, bf16[256,1536]{1,0:T(8,128)(2,1)}, u32[]{:S(2)}) copy-start(bf16[256,1536]{1,0:T(8,128)(2,1)} %param.14) | copy-start | bytes 2359300
  0.6 47.1 %collective-permute-start = (bf16[256,1536]{1,0:T(8,128)(2,1)}, bf16[256,1536]{1,0:T(8,128)(2,1)}, u32[]{:S(2)}, u32[]{:S(2)}) collective-permute-start(bf16[256,1536]{1,0:T(8,128)(2,1)} %param.12), channel_id=1, source_target_pairs={{0,2},{1,3},{2,4},{3,5},{4,6},{5,7},{6,8},{7,9},{8,10},{9,11},{10,... | collective-permute-start | bytes 2359304 | tf_op jit(solution)/shard_map/ppermute | solution.py:18
  4.2 46.6 %collective-permute-start.1 = (bf16[256,1536]{1,0:T(8,128)(2,1)}, bf16[256,1536]{1,0:T(8,128)(2,1)}, u32[]{:S(2)}, u32[]{:S(2)}) collective-permute-start(bf16[256,1536]{1,0:T(8,128)(2,1)} %param.12), channel_id=1, source_target_pairs={{0,1},{1,2},{2,3},{3,4},{4,5},{5,6},{6,7},{7,8},{8,9},{9,10},{10,1... | collective-permute-start | bytes 2359304 | tf_op jit(solution)/shard_map/ppermute | solution.py:18
  6.1 50.5 %collective-permute-start.2 = (bf16[256,1536]{1,0:T(8,128)(2,1)}, bf16[256,1536]{1,0:T(8,128)(2,1)}, u32[]{:S(2)}, u32[]{:S(2)}) collective-permute-start(bf16[256,1536]{1,0:T(8,128)(2,1)} %param.12), channel_id=1, source_target_pairs={{1,0},{2,1},{3,2},{4,3},{5,4},{6,5},{7,6},{8,7},{9,8},{10,9},{11,1... | collective-permute-start | bytes 2359304 | tf_op jit(solution)/shard_map/ppermute | solution.py:18
  10.7 73.6 %collective-permute-start.3 = (bf16[256,1536]{1,0:T(8,128)(2,1)}, bf16[256,1536]{1,0:T(8,128)(2,1)S(1)}, u32[]{:S(2)}, u32[]{:S(2)}) collective-permute-start(bf16[256,1536]{1,0:T(8,128)(2,1)} %param.12), channel_id=1, source_target_pairs={{2,0},{3,1},{4,2},{5,3},{6,4},{7,5},{8,6},{9,7},{10,8},{11,9},{12,... | collective-permute-start | bytes 2359304 | tf_op jit(solution)/shard_map/ppermute | solution.py:18
  13.1 75.6 %collective-permute-start.4 = (bf16[256,1536]{1,0:T(8,128)(2,1)}, bf16[256,1536]{1,0:T(8,128)(2,1)S(1)}, u32[]{:S(2)}, u32[]{:S(2)}) collective-permute-start(bf16[256,1536]{1,0:T(8,128)(2,1)} %param.13), channel_id=1, source_target_pairs={{0,2},{1,3},{2,4},{3,5},{4,6},{5,7},{6,8},{7,9},{8,10},{9,11},{10,... | collective-permute-start | bytes 2359304 | tf_op jit(solution)/shard_map/ppermute | solution.py:18
  21.8 26.0 %copy-start.3 = (bf16[256,1536]{1,0:T(8,128)(2,1)S(1)}, bf16[256,1536]{1,0:T(8,128)(2,1)}, u32[]{:S(2)}) copy-start(bf16[256,1536]{1,0:T(8,128)(2,1)} %param.13) | copy-start | bytes 2359300
  40.6 16.0 %copy-start.2 = (bf16[256,1536]{1,0:T(8,128)(2,1)S(1)}, bf16[256,1536]{1,0:T(8,128)(2,1)}, u32[]{:S(2)}) copy-start(bf16[256,1536]{1,0:T(8,128)(2,1)} %param.12) | copy-start | bytes 2359300
  47.7 41.0 %collective-permute-start.5 = (bf16[256,1536]{1,0:T(8,128)(2,1)S(1)}, bf16[256,1536]{1,0:T(8,128)(2,1)S(1)}, u32[]{:S(2)}, u32[]{:S(2)}) collective-permute-start(bf16[256,1536]{1,0:T(8,128)(2,1)S(1)} %copy-done.3), channel_id=1, source_target_pairs={{0,1},{1,2},{2,3},{3,4},{4,5},{5,6},{6,7},{7,8},{8,9},{9,10},{10,1... | collective-permute-start | bytes 2359304 | tf_op jit(solution)/shard_map/ppermute | solution.py:18
  50.8 38.5 %collective-permute-start.6 = (bf16[256,1536]{1,0:T(8,128)(2,1)S(1)}, bf16[256,1536]{1,0:T(8,128)(2,1)S(1)}, u32[]{:S(2)}, u32[]{:S(2)}) collective-permute-start(bf16[256,1536]{1,0:T(8,128)(2,1)S(1)} %copy-done.3), channel_id=1, source_target_pairs={{1,0},{2,1},{3,2},{4,3},{5,4},{6,5},{7,6},{8,7},{9,8},{10,9},{11,1... | collective-permute-start | bytes 2359304 | tf_op jit(solution)/shard_map/ppermute | solution.py:18
  56.7 27.6 %copy-start.1 = (bf16[256,1536]{1,0:T(8,128)(2,1)S(1)}, bf16[256,1536]{1,0:T(8,128)(2,1)}, u32[]{:S(2)}) copy-start(bf16[256,1536]{1,0:T(8,128)(2,1)} %param.11) | copy-start | bytes 2359300
  56.7 50.6 %collective-permute-start.7 = (bf16[256,1536]{1,0:T(8,128)(2,1)S(1)}, bf16[256,1536]{1,0:T(8,128)(2,1)S(1)}, u32[]{:S(2)}, u32[]{:S(2)}) collective-permute-start(bf16[256,1536]{1,0:T(8,128)(2,1)S(1)} %copy-done.3), channel_id=1, source_target_pairs={{2,0},{3,1},{4,2},{5,3},{6,4},{7,5},{8,6},{9,7},{10,8},{11,9},{12,... | collective-permute-start | bytes 2359304 | tf_op jit(solution)/shard_map/ppermute | solution.py:18
  89.8 17.6 %copy-start.15 = (bf16[256,128]{0,1:T(8,128)(2,1)S(1)}, bf16[256,128]{0,1:T(8,128)(2,1)}, u32[]{:S(2)}) copy-start(bf16[256,128]{0,1:T(8,128)(2,1)} %copy.44) | copy-start | bytes 196612
  109.6 0.8 copy-start.14
  112.7 0.8 copy-start.13
  115.8 0.8 copy-start.12
  118.8 0.8 copy-start.11
  122.1 0.8 copy-start.10
  125.2 0.8 copy-start.9
  128.3 0.8 copy-start.8
  130.0 0.8 copy-start.7
  131.8 0.8 copy-start.6
  133.6 0.8 copy-start.5
  135.4 0.8 copy-start.4
  146.4 47.6 %collective-permute-start.15 = (bf16[256,1536]{0,1:T(8,128)(2,1)S(1)}, bf16[256,1536]{0,1:T(8,128)(2,1)}, u32[]{:S(2)}, u32[]{:S(2)}) collective-permute-start(bf16[256,1536]{0,1:T(8,128)(2,1)S(1)} %get-tuple-element.13), channel_id=1, source_target_pairs={{0,2},{1,3},{2,4},{3,5},{4,6},{5,7},{6,8},{7,9},{8,10},{9,11},{10,... | collective-permute-start | bytes 2359304 | tf_op jit(solution)/shard_map/ppermute | solution.py:18
  150.8 45.2 %collective-permute-start.14 = (bf16[256,1536]{0,1:T(8,128)(2,1)S(1)}, bf16[256,1536]{0,1:T(8,128)(2,1)}, u32[]{:S(2)}, u32[]{:S(2)}) collective-permute-start(bf16[256,1536]{0,1:T(8,128)(2,1)S(1)} %get-tuple-element.10), channel_id=1, source_target_pairs={{0,1},{1,2},{2,3},{3,4},{4,5},{5,6},{6,7},{7,8},{8,9},{9,10},{10,1... | collective-permute-start | bytes 2359304 | tf_op jit(solution)/shard_map/ppermute | solution.py:18
  152.7 47.8 %collective-permute-start.13 = (bf16[256,1536]{0,1:T(8,128)(2,1)S(1)}, bf16[256,1536]{0,1:T(8,128)(2,1)}, u32[]{:S(2)}, u32[]{:S(2)}) collective-permute-start(bf16[256,1536]{0,1:T(8,128)(2,1)S(1)} %get-tuple-element.12), channel_id=1, source_target_pairs={{1,0},{2,1},{3,2},{4,3},{5,4},{6,5},{7,6},{8,7},{9,8},{10,9},{11,1... | collective-permute-start | bytes 2359304 | tf_op jit(solution)/shard_map/ppermute | solution.py:18
  158.2 73.4 %collective-permute-start.12 = (bf16[256,1536]{0,1:T(8,128)(2,1)S(1)}, bf16[256,1536]{0,1:T(8,128)(2,1)}, u32[]{:S(2)}, u32[]{:S(2)}) collective-permute-start(bf16[256,1536]{0,1:T(8,128)(2,1)S(1)} %get-tuple-element.9), channel_id=1, source_target_pairs={{2,0},{3,1},{4,2},{5,3},{6,4},{7,5},{8,6},{9,7},{10,8},{11,9},{12,... | collective-permute-start | bytes 2359304 | tf_op jit(solution)/shard_map/ppermute | solution.py:18
  161.1 74.1 %collective-permute-start.11 = (bf16[256,1536]{1,0:T(8,128)(2,1)}, bf16[256,1536]{1,0:T(8,128)(2,1)S(1)}, u32[]{:S(2)}, u32[]{:S(2)}) collective-permute-start(bf16[256,1536]{1,0:T(8,128)(2,1)} %get-tuple-element.18), channel_id=1, source_target_pairs={{0,2},{1,3},{2,4},{3,5},{4,6},{5,7},{6,8},{7,9},{8,10},{9,11},{10,... | collective-permute-start | bytes 2359304 | tf_op jit(solution)/shard_map/ppermute | solution.py:18
  194.0 41.1 %collective-permute-start.10 = (bf16[256,1536]{1,0:T(8,128)(2,1)}, bf16[256,1536]{1,0:T(8,128)(2,1)}, u32[]{:S(2)}, u32[]{:S(2)}) collective-permute-start(bf16[256,1536]{1,0:T(8,128)(2,1)} %get-tuple-element.15), channel_id=1, source_target_pairs={{0,1},{1,2},{2,3},{3,4},{4,5},{5,6},{6,7},{7,8},{8,9},{9,10},{10,1... | collective-permute-start | bytes 2359304 | tf_op jit(solution)/shard_map/ppermute | solution.py:18
  195.9 39.2 %collective-permute-start.9 = (bf16[256,1536]{1,0:T(8,128)(2,1)}, bf16[256,1536]{1,0:T(8,128)(2,1)}, u32[]{:S(2)}, u32[]{:S(2)}) collective-permute-start(bf16[256,1536]{1,0:T(8,128)(2,1)} %get-tuple-element.17), channel_id=1, source_target_pairs={{1,0},{2,1},{3,2},{4,3},{5,4},{6,5},{7,6},{8,7},{9,8},{10,9},{11,1... | collective-permute-start | bytes 2359304 | tf_op jit(solution)/shard_map/ppermute | solution.py:18
  200.5 52.6 %collective-permute-start.8 = (bf16[256,1536]{1,0:T(8,128)(2,1)}, bf16[256,1536]{1,0:T(8,128)(2,1)}, u32[]{:S(2)}, u32[]{:S(2)}) collective-permute-start(bf16[256,1536]{1,0:T(8,128)(2,1)} %get-tuple-element.14), channel_id=1, source_target_pairs={{2,0},{3,1},{4,2},{5,3},{6,4},{7,5},{8,6},{9,7},{10,8},{11,9},{12,... | collective-permute-start | bytes 2359304 | tf_op jit(solution)/shard_map/ppermute | solution.py:18
where the time goes:
time: 258 us; the launch traced here: 256 us
  starting transfers between devices  84.9 us (33%)
  waiting for transfers between devices  84.4 us (33%)
  local copies, waits for them, and re-layouts  40 us (16%)
  matrix products  33.1 us (13%)
  other arithmetic  12.2 us (5%)
    ppermute x16, starting transfers between devices, from_behind(): lax.ppermute(value, axis, [(source, source + steps) for source in range(f...  84.9 us
    ppermute x16, waiting for transfers between devices, from_behind(): lax.ppermute(value, axis, [(source, source + steps) for source in range(f...  84.4 us
    unnamed x66, local copies, waits for them, and re-layouts  34 us
    dot_general x12, matrix products, group_grads(): jnp.einsum('qk,kd->qd', grad_scores, key_head, preferred_element_type=jnp...  11.4 us
  transfers between devices with their start and end apart: 16, of which 6 were waited for; matrix products, arithmetic and copies ran while one was open for 17% of the time, Pallas kernels for 0%

commit v1 on v0

v1 whole, which is shorter than its diff:
```python
import jax
import jax.numpy as jnp
import numpy as np
from jax import lax
from jax.sharding import PartitionSpec as P

HEADS = 12
HDIM = 128
BLOCK = 64
REACH = 2
FRAMES = 2
BANDS = 2
NEG = -1e30


def from_behind(value, axis, steps):
    count = lax.axis_size(axis)
    first, last = (max(0, -steps), min(count, count - steps))
    return lax.ppermute(value, axis, [(source, source + steps) for source in range(first, last)])


def pick_table(offset):
    blocks = FRAMES * BANDS
    slot = REACH - offset
    table = np.zeros((blocks, 30, blocks), np.float32)
    own = np.zeros((blocks, blocks), bool)
    for qb in range(blocks):
        for kb in range(blocks):
            cand = (slot * FRAMES + kb // BANDS) * 3 + kb % BANDS - qb % BANDS + 1
            table[qb, cand, kb] = 1.0
            own[qb, kb] = offset == 0 and qb == kb
    return table, own


def pair_mask(block_rows, offset, valid):
    table, own = pick_table(offset)
    chosen = jnp.einsum("qc,qck->qk", block_rows.astype(jnp.float32), jnp.asarray(table)) > 0
    return (chosen & valid) | jnp.asarray(own)


def expand(mask4):
    return mask4[None, :, None, :, None]


def blocked(x):
    return x.reshape(HEADS, FRAMES * BANDS, BLOCK, FRAMES * BANDS, BLOCK)


def local(queries, keys, values, grad_out, block_list):
    groups = lax.axis_size("tm")
    here = lax.axis_index("tm")
    scaling = HDIM ** (-0.5)
    tok = queries.shape[0]
    key_h = keys.reshape(tok, HEADS, HDIM)
    value_h = values.reshape(tok, HEADS, HDIM)
    offsets = list(range(-REACH, REACH + 1))

    arrived = {}
    for offset in offsets:
        if offset == 0:
            arrived[offset] = (queries, grad_out, block_list)
        else:
            arrived[offset] = from_behind((queries, grad_out, block_list), "tm", -offset)

    parts = {}
    stats_back = {}
    for offset in offsets:
        q_rows, g_rows, b_rows = arrived[offset]
        source = here + offset
        valid = (source >= 0) & (source < groups)
        mask = expand(pair_mask(b_rows, offset, valid))
        q_h = q_rows.reshape(tok, HEADS, HDIM)
        g_h = g_rows.reshape(tok, HEADS, HDIM)
        scores = blocked(
            jnp.einsum("qhd,khd->hqk", q_h, key_h, preferred_element_type=jnp.float32) * scaling
        )
        grad_probs = blocked(
            jnp.einsum("qhd,khd->hqk", g_h, value_h, preferred_element_type=jnp.float32)
        )
        masked = jnp.where(mask, scores, NEG)
        row_max = jnp.max(masked, axis=(3, 4))
        expd = jnp.where(mask, jnp.exp(masked - row_max[:, :, :, None, None]), 0.0)
        row_sum = jnp.sum(expd, axis=(3, 4))
        row_dot = jnp.sum(expd * grad_probs, axis=(3, 4))
        stats = jnp.stack([row_max, row_sum, row_dot]).reshape(3, HEADS, tok)
        parts[offset] = (q_h, g_h, mask, scores, grad_probs)
        stats_back[offset] = stats if offset == 0 else from_behind(stats, "tm", offset)

    all_stats = jnp.stack([stats_back[offset] for offset in offsets])
    maxes, sums, dots = all_stats[:, 0], all_stats[:, 1], all_stats[:, 2]
    top = jnp.max(maxes, axis=0)
    scale = jnp.exp(maxes - top[None])
    total = jnp.sum(sums * scale, axis=0)
    log_total = top + jnp.log(total)
    deltas = jnp.sum(dots * scale, axis=0) / total
    final = jnp.stack([log_total, deltas])

    key_grad = jnp.zeros((tok, HEADS, HDIM), jnp.float32)
    value_grad = jnp.zeros((tok, HEADS, HDIM), jnp.float32)
    query_grad = None
    for offset in offsets:
        q_h, g_h, mask, scores, grad_probs = parts[offset]
        got = final if offset == 0 else from_behind(final, "tm", -offset)
        lse = got[0].reshape(HEADS, FRAMES * BANDS, BLOCK)[:, :, :, None, None]
        dlt = got[1].reshape(HEADS, FRAMES * BANDS, BLOCK)[:, :, :, None, None]
        weights = jnp.where(mask, jnp.exp(scores - lse), 0.0)
        weights_low = weights.astype(jnp.bfloat16).reshape(HEADS, tok, tok)
        grad_scores = (weights * (grad_probs - dlt)).astype(jnp.bfloat16).reshape(HEADS, tok, tok)
        key_grad = key_grad + jnp.einsum(
            "hqk,qhd->khd", grad_scores, q_h, preferred_element_type=jnp.float32
        ) * scaling
        value_grad = value_grad + jnp.einsum(
            "hqk,qhd->khd", weights_low, g_h, preferred_element_type=jnp.float32
        )
        q_part = jnp.einsum(
            "hqk,khd->qhd", grad_scores, key_h, preferred_element_type=jnp.float32
        ) * scaling
        if offset == 0:
            own_part = q_part
        else:
            sent = from_behind(q_part.astype(jnp.bfloat16), "tm", offset).astype(jnp.float32)
            query_grad = sent if query_grad is None else query_grad + sent
    query_grad = query_grad + own_part
    return (
        query_grad.reshape(tok, HEADS * HDIM).astype(jnp.bfloat16),
        key_grad.reshape(tok, HEADS * HDIM).astype(jnp.bfloat16),
        value_grad.reshape(tok, HEADS * HDIM).astype(jnp.bfloat16),
    )


def solution(mesh):
    placed = (
        P(("group", "tm"), None),
        P(("group", "tm"), None),
        P(("group", "tm"), None),
        P(("group", "tm"), None),
        P(("group", "tm"), None),
    )
    return jax.shard_map(
        local,
        mesh=mesh,
        in_specs=placed,
        out_specs=(P(("group", "tm"), None), P(("group", "tm"), None), P(("group", "tm"), None)),
        check_vma=False,
    )
```

time: 258 us -> 255 us (0.988)
  local copies, waits for them, and re-layouts: 40 us -> 18.4 us
  waiting for transfers between devices: 84.4 us -> 96.4 us
  matrix products: 33.1 us -> 45 us
  other arithmetic: 12.2 us -> 8.89 us
    unnamed x66 -> x52, local copies, waits for them, and re-layouts: 34 us -> 11.5 us
    ppermute x16 -> x24, waiting for transfers between devices: 84.4 us -> 96.4 us  [from_behind(): lax.ppermute(value, axis, [(source, source + steps) for source in range(f...]
    dot_general x72 -> x30, matrix products: 33.1 us -> 45 us  [the longest x5 16.1 us: local(): jnp.einsum('qhd,khd->hqk', g_h, value_h, preferred_element_type=jnp.float32)]
    broadcast_in_dim x2 -> x10, local copies, waits for them, and re-layouts: 1.48 us -> 5.04 us  [the longest x8 3.1 us: local(): masked = jnp.where(mask, scores, NEG)]
    reduce_sum x12 -> x1, other arithmetic: 3.31 us -> 0.03 us  [local(): total = jnp.sum(sums * scale, axis=0)]
    ppermute x16 -> x24, starting transfers between devices: 84.9 us -> 83.1 us  [from_behind(): lax.ppermute(value, axis, [(source, source + steps) for source in range(f...]
    convert_element_type x14 -> x10, other arithmetic: 7.47 us -> 8.08 us  [the longest x5 7.38 us: local(): (weights * (grad_probs - dlt)).astype(jnp.bfloat16).reshape(HEADS, tok, tok)]
  transfers between devices with their start and end apart: 16 -> 24, of which waited for: 6 -> 6; matrix products, arithmetic and copies ran while one was open for 17% -> 21% of each run, Pallas kernels for 0% -> 0%
where the time goes in v1:
time: 255 us; the launch traced here: 253 us
  waiting for transfers between devices  96.4 us (38%)
  starting transfers between devices  83.1 us (33%)
  matrix products  45 us (18%)
  local copies, waits for them, and re-layouts  18.4 us (7%)
  other arithmetic  8.89 us (3%)
    ppermute x24, waiting for transfers between devices, from_behind(): lax.ppermute(value, axis, [(source, source + steps) for source in range(f...  96.4 us
    ppermute x24, starting transfers between devices, from_behind(): lax.ppermute(value, axis, [(source, source + steps) for source in range(f...  83.1 us
    dot_general x5, matrix products, local(): jnp.einsum('qhd,khd->hqk', g_h, value_h, preferred_element_type=jnp.float32)  16.1 us
    unnamed x52, local copies, waits for them, and re-layouts  11.5 us
    dot_general x5, matrix products, local(): jnp.einsum('hqk,khd->qhd', grad_scores, key_h, preferred_element_type=jnp...  8.87 us
    dot_general x5, matrix products, local(): jnp.einsum('hqk,qhd->khd', weights_low, g_h, preferred_element_type=jnp.f...  8.56 us
    convert_element_type x5, other arithmetic, local(): (weights * (grad_probs - dlt)).astype(jnp.bfloat16).reshape(HEADS, tok, tok)  7.38 us
    dot_general x5, matrix products, local(): jnp.einsum('hqk,qhd->khd', grad_scores, q_h, preferred_element_type=jnp.f...  6.53 us
  transfers between devices with their start and end apart: 24, of which 6 were waited for; matrix products, arithmetic and copies ran while one was open for 21% of the time, Pallas kernels for 0%

profile of v1, /device:TPU:8, one launch (start us, length us, event | category | flops | bytes accessed | tf_op | source)
XLA Modules:
  0.0 253.3 jit_solution(17060211831972539674)
XLA Ops:
  0.6 2.1 collective-permute-start.4
  2.7 3.4 %collective-permute-start = (s32[4,30]{1,0:T(4,128)}, s32[4,30]{1,0:T(4,128)S(1)}, u32[]{:S(2)}, u32[]{:S(2)}) collective-permute-start(s32[4,30]{1,0:T(4,128)} %param.19), channel_id=1, source_target_pairs={{0,2},{1,3},{2,4},{3,5},{4,6},{5,7},{6,8},{7,9},{8,10},{9,11},{10,... | collective-permute-start | bytes 1448 | tf_op jit(solution)/shard_map/ppermute | solution.py:19
  6.1 3.3 %collective-permute-start.12 = (s32[4,30]{1,0:T(4,128)}, s32[4,30]{1,0:T(4,128)S(1)}, u32[]{:S(2)}, u32[]{:S(2)}) collective-permute-start(s32[4,30]{1,0:T(4,128)} %param.19), channel_id=1, source_target_pairs={{2,0},{3,1},{4,2},{5,3},{6,4},{7,5},{8,6},{9,7},{10,8},{11,9},{12,... | collective-permute-start | bytes 1448 | tf_op jit(solution)/shard_map/ppermute | solution.py:19
  9.5 3.1 %collective-permute-start.8 = (s32[4,30]{1,0:T(4,128)}, s32[4,30]{1,0:T(4,128)S(1)}, u32[]{:S(2)}, u32[]{:S(2)}) collective-permute-start(s32[4,30]{1,0:T(4,128)} %param.19), channel_id=1, source_target_pairs={{1,0},{2,1},{3,2},{4,3},{5,4},{6,5},{7,6},{8,7},{9,8},{10,9},{11,1... | collective-permute-start | bytes 1448 | tf_op jit(solution)/shard_map/ppermute | solution.py:19
  12.6 1.4 copy.73
  14.0 1.9 collective-permute-start.14
  16.6 0.9 fusion.71
  18.6 1.4 copy.69
  20.3 1.4 copy.74
  22.5 1.7 copy-done
  24.1 2.9 %fusion.7 = (f32[12,256]{1,0:T(8,128)S(1)}, f32[12,256]{1,0:T(8,128)S(1)}, f32[12,256,256]{1,2,0:T(8,128)}) fusion(f32[12,256,256]{1,2,0:T(8,128)S(1)} %get-tuple-element.38, f32[12,256]{1,0:T(8,128)S(1)} %get-tuple-element.37, pred[256,256]{0,1:T(8,128)(4,1)S(1)} %broadcast_in_dim.118, bf16[256,12,128]{0,2,1:T(8,128)(2,1)S(1)} %bitcast.221, ...), kind=kOutput, calls=%fused_computation.32 | convolution fusion | flops 206825472 | bytes 7966720 | tf_op jit(solution)/shard_map/qhd,khd->hqk/dot_general | solution.py:78
  27.0 1.9 collective-permute-start.10
  29.1 2.4 collective-permute-start.6
  31.6 3.9 %collective-permute-start.2 = (bf16[256,1536]{0,1:T(8,128)(2,1)S(1)}, bf16[256,1536]{0,1:T(8,128)(2,1)}, u32[]{:S(2)}, u32[]{:S(2)}) collective-permute-start(bf16[256,1536]{0,1:T(8,128)(2,1)S(1)} %copy.73), channel_id=1, source_target_pairs={{0,2},{1,3},{2,4},{3,5},{4,6},{5,7},{6,8},{7,9},{8,10},{9,11},{10,... | collective-permute-start | bytes 2359304 | tf_op jit(solution)/shard_map/ppermute | solution.py:19
  36.0 2.8 %collective-permute-start.13 = (bf16[256,1536]{0,1:T(8,128)(2,1)S(1)}, bf16[256,1536]{0,1:T(8,128)(2,1)S(1)}, u32[]{:S(2)}, u32[]{:S(2)}) collective-permute-start(bf16[256,1536]{0,1:T(8,128)(2,1)S(1)} %copy.69), channel_id=1, source_target_pairs={{2,0},{3,1},{4,2},{5,3},{6,4},{7,5},{8,6},{9,7},{10,8},{11,9},{12,... | collective-permute-start | bytes 2359304 | tf_op jit(solution)/shard_map/ppermute | solution.py:19
  39.9 0.8 broadcast_in_dim.109
  40.7 1.1 broadcast_in_dim.110
  42.6 1.1 broadcast_in_dim.115
  43.8 42.0 %collective-permute-done.13 = bf16[256,1536]{0,1:T(8,128)(2,1)S(1)} collective-permute-done((bf16[256,1536]{0,1:T(8,128)(2,1)S(1)}, bf16[256,1536]{0,1:T(8,128)(2,1)S(1)}, u32[]{:S(2)}, u32[]{:S(2)}) %collective-permute-start.13) | collective-permute-done | bytes 786464 | tf_op jit(solution)/shard_map/ppermute | solution.py:19
  85.8 1.9 collective-permute-start.9
  88.4 2.4 collective-permute-start.5
  90.9 4.1 %fusion.9 = (f32[12,256]{1,0:T(8,128)S(1)}, f32[12,256]{1,0:T(8,128)S(1)}, f32[12,256,256]{1,2,0:T(8,128)}) fusion(f32[12,256,256]{1,2,0:T(8,128)S(1)} %get-tuple-element.44, f32[12,256]{1,0:T(8,128)S(1)} %get-tuple-element.43, pred[256,256]{0,1:T(8,128)(4,1)S(1)} %broadcast_in_dim.124, bf16[256,12,128]{0,2,1:T(8,128)(2,1)} %bitcast.43, ...), kind=kOutput, calls=%fused_computation.34 | convolution fusion | flops 206825472 | bytes 7966720 | tf_op jit(solution)/shard_map/qhd,khd->hqk/dot_general | solution.py:78
  94.9 2.3 collective-permute-done.9
  97.2 18.2 %collective-permute-start.1 = (bf16[256,1536]{0,1:T(8,128)(2,1)S(1)}, bf16[256,1536]{0,1:T(8,128)(2,1)S(1)}, u32[]{:S(2)}, u32[]{:S(2)}) collective-permute-start(bf16[256,1536]{0,1:T(8,128)(2,1)S(1)} %copy.69), channel_id=1, source_target_pairs={{0,2},{1,3},{2,4},{3,5},{4,6},{5,7},{6,8},{7,9},{8,10},{9,11},{10,... | collective-permute-start | bytes 2359304 | tf_op jit(solution)/shard_map/ppermute | solution.py:19
  116.2 1.9 collective-permute-start.15
  118.2 4.1 %fusion.8 = (f32[12,256]{1,0:T(8,128)S(1)}, f32[12,256]{1,0:T(8,128)S(1)}, f32[12,256,256]{1,2,0:T(8,128)}) fusion(f32[12,256,256]{1,2,0:T(8,128)S(1)} %get-tuple-element.41, f32[12,256]{1,0:T(8,128)S(1)} %get-tuple-element.40, pred[256,256]{0,1:T(8,128)(4,1)S(1)} %broadcast_in_dim.121, bf16[256,12,128]{0,2,1:T(8,128)(2,1)} %bitcast.34, ...), kind=kOutput, calls=%fused_computation.33 | convolution fusion | flops 206825472 | bytes 7966720 | tf_op jit(solution)/shard_map/qhd,khd->hqk/dot_general | solution.py:78
  122.3 11.0 %collective-permute-done.1 = bf16[256,1536]{0,1:T(8,128)(2,1)S(1)} collective-permute-done((bf16[256,1536]{0,1:T(8,128)(2,1)S(1)}, bf16[256,1536]{0,1:T(8,128)(2,1)S(1)}, u32[]{:S(2)}, u32[]{:S(2)}) %collective-permute-start.1) | collective-permute-done | bytes 786464 | tf_op jit(solution)/shard_map/ppermute | solution.py:19
  133.3 2.1 collective-permute-start.11
  136.1 2.5 fusion.5
  138.6 1.9 collective-permute-start.3
  141.3 2.6 %fusion.6 = (f32[12,256]{1,0:T(8,128)S(1)}, f32[12,256]{1,0:T(8,128)S(1)}, f32[12,256,256]{1,2,0:T(8,128)S(1)}) fusion(f32[12,256,256]{1,2,0:T(8,128)S(1)} %get-tuple-element.35, f32[12,256]{1,0:T(8,128)S(1)} %get-tuple-element.34, pred[256,256]{0,1:T(8,128)(4,1)S(1)} %broadcast_in_dim.115, bf16[256,12,128]{0,2,1:T(8,128)(2,1)} %bitcast.17, ...), kind=kOutput, calls=%fused_computation.31 | convolution fusion | flops 206825472 | bytes 7966720 | tf_op jit(solution)/shard_map/qhd,khd->hqk/dot_general | solution.py:78
  143.9 4.5 %collective-permute-start.7 = (f32[3,12,256]{2,1,0:T(8,128)S(1)}, f32[3,12,256]{2,1,0:T(8,128)S(1)}, u32[]{:S(2)}, u32[]{:S(2)}) collective-permute-start(f32[3,12,256]{2,1,0:T(8,128)S(1)} %pad_maximum_fusion.1), channel_id=1, source_target_pairs={{1,0},{2,1},{3,2},{4,3},{5,4},{6,5},{7,6},{8,7},{9,8},{10,9},{11,1... | collective-permute-start | bytes 110600 | tf_op jit(solution)/shard_map/ppermute | solution.py:19
  148.5 1.7 collective-permute-done.7
  151.1 1.9 collective-permute-start.22
  153.1 4.7 %collective-permute-start.20 = (f32[2,12,256]{2,1,0:T(8,128)S(1)}, f32[2,12,256]{2,1,0:T(8,128)S(1)}, u32[]{:S(2)}, u32[]{:S(2)}) collective-permute-start(f32[2,12,256]{2,1,0:T(8,128)S(1)} %pad_maximum_fusion.4), channel_id=1, source_target_pairs={{1,0},{2,1},{3,2},{4,3},{5,4},{6,5},{7,6},{8,7},{9,8},{10,9},{11,1... | collective-permute-start | bytes 73736 | tf_op jit(solution)/shard_map/ppermute | solution.py:19
  157.8 2.0 collective-permute-start.18
  159.8 3.5 %collective-permute-start.16 = (f32[2,12,256]{2,1,0:T(8,128)S(1)}, f32[2,12,256]{2,1,0:T(8,128)S(1)}, u32[]{:S(2)}, u32[]{:S(2)}) collective-permute-start(f32[2,12,256]{2,1,0:T(8,128)S(1)} %pad_maximum_fusion.4), channel_id=1, source_target_pairs={{0,2},{1,3},{2,4},{3,5},{4,6},{5,7},{6,8},{7,9},{8,10},{9,11},{10,... | collective-permute-start | bytes 73736 | tf_op jit(solution)/shard_map/ppermute | solution.py:19
  163.4 0.9 multiply_convert_fusion
  164.3 1.8 fusion.76
  166.0 1.9 fusion.14
  168.0 1.9 fusion.18
  169.9 0.9 multiply_convert_fusion.4
  170.8 1.7 fusion.74
  172.5 1.5 fusion.43
  174.0 1.9 fusion.16
  176.0 0.9 multiply_convert_fusion.3
  176.9 1.7 fusion.75
  178.6 1.6 fusion.44
  180.1 2.1 add_convert_fusion
  182.2 1.2 copy.132
  183.4 3.8 %multiply_convert_fusion.2 = bf16[12,256,256]{1,2,0:T(8,128)(2,1)S(1)} fusion(f32[12,256,256]{1,2,0:T(8,128)} %get-tuple-element.42, f32[12,256,256]{1,2,0:T(8,128)} %copy-done.4, f32[12,256]{1,0:T(8,128)S(1)} %get-tuple-element.26, f32[12,256]{1,0:T(8,128)S(1)} %get-tuple-element.25, pred[256,256]{0,1:T(8,128)(4,1)S(1)} %broadcast_in_dim.121), kind=kLoop, calls=%fused_computation.4 | loop fusion | flops 4718592 | bytes 7954432 | tf_op jit(solution)/shard_map/convert_element_type | solution.py:108
  187.2 1.5 fusion.45
  189.4 0.9 multiply_convert_fusion.1
  190.3 1.5 fusion.46
  191.8 4.5 %collective-permute-start.23 = (bf16[256,12,128]{2,0,1:T(8,128)(2,1)}, bf16[256,12,128]{2,0,1:T(8,128)(2,1)}, u32[]{:S(2)}, u32[]{:S(2)}) collective-permute-start(bf16[256,12,128]{2,0,1:T(8,128)(2,1)} %fusion.46), channel_id=1, source_target_pairs={{0,2},{1,3},{2,4},{3,5},{4,6},{5,7},{6,8},{7,9},{8,10},{9,11},{10,... | collective-permute-start | bytes 2359304 | tf_op jit(solution)/shard_map/ppermute | solution.py:19
  196.3 3.1 %collective-permute-start.21 = (bf16[256,12,128]{2,0,1:T(8,128)(2,1)}, bf16[256,12,128]{2,0,1:T(8,128)(2,1)}, u32[]{:S(2)}, u32[]{:S(2)}) collective-permute-start(bf16[256,12,128]{2,0,1:T(8,128)(2,1)} %fusion.45), channel_id=1, source_target_pairs={{0,1},{1,2},{2,3},{3,4},{4,5},{5,6},{6,7},{7,8},{8,9},{9,10},{10,1... | collective-permute-start | bytes 2359304 | tf_op jit(solution)/shard_map/ppermute | solution.py:19
  199.4 3.4 %collective-permute-start.19 = (bf16[256,12,128]{2,0,1:T(8,128)(2,1)}, bf16[256,12,128]{2,0,1:T(8,128)(2,1)}, u32[]{:S(2)}, u32[]{:S(2)}) collective-permute-start(bf16[256,12,128]{2,0,1:T(8,128)(2,1)} %fusion.44), channel_id=1, source_target_pairs={{1,0},{2,1},{3,2},{4,3},{5,4},{6,5},{7,6},{8,7},{9,8},{10,9},{11,1... | collective-permute-start | bytes 2359304 | tf_op jit(solution)/shard_map/ppermute | solution.py:19
  202.8 2.1 collective-permute-start.17
  206.4 1.2 copy.124
  207.5 2.3 copy.131
  209.8 29.6 %collective-permute-done.23 = bf16[256,12,128]{2,0,1:T(8,128)(2,1)} collective-permute-done((bf16[256,12,128]{2,0,1:T(8,128)(2,1)}, bf16[256,12,128]{2,0,1:T(8,128)(2,1)}, u32[]{:S(2)}, u32[]{:S(2)}) %collective-permute-start.23) | collective-permute-done | bytes 786464 | tf_op jit(solution)/shard_map/ppermute | solution.py:19
  239.4 9.8 %collective-permute-done.17 = bf16[256,12,128]{2,0,1:T(8,128)(2,1)} collective-permute-done((bf16[256,12,128]{2,0,1:T(8,128)(2,1)}, bf16[256,12,128]{2,0,1:T(8,128)(2,1)}, u32[]{:S(2)}, u32[]{:S(2)}) %collective-permute-start.17) | collective-permute-done | bytes 786464 | tf_op jit(solution)/shard_map/ppermute | solution.py:19
  249.2 2.7 %fusion.20 = bf16[256,12,128]{2,0,1:T(8,128)(2,1)S(1)} fusion(bf16[256,12,128]{2,0,1:T(8,128)(2,1)} %collective-permute-done.23, bf16[256,12,128]{2,0,1:T(8,128)(2,1)} %collective-permute-done.21, bf16[256,12,128]{2,0,1:T(8,128)(2,1)} %collective-permute-done.19, bf16[256,12,128]{2,0,1:T(8,128)(2,1)} %collective-permute-done.17, ...), kind=kOutput, calls=%fused_computation.42 | convolution fusion | flops 205258752 | bytes 6291456 | tf_op jit(solution)/shard_map/hqk,khd->qhd/dot_general | solution.py:115
  252.2 1.2 copy.130
  (112 shorter events, 11.5 us)
Async XLA Ops:
  0.6 19.4 %copy-start.14 = (bf16[256,1536]{1,0:T(8,128)(2,1)S(1)}, bf16[256,1536]{1,0:T(8,128)(2,1)}, u32[]{:S(2)}) copy-start(bf16[256,1536]{1,0:T(8,128)(2,1)} %param.16) | copy-start | bytes 2359300
  0.6 26.4 %collective-permute-start.4 = (s32[4,30]{1,0:T(4,128)}, s32[4,30]{1,0:T(4,128)S(1)}, u32[]{:S(2)}, u32[]{:S(2)}) collective-permute-start(s32[4,30]{1,0:T(4,128)} %param.19), channel_id=1, source_target_pairs={{0,1},{1,2},{2,3},{3,4},{4,5},{5,6},{6,7},{7,8},{8,9},{9,10},{10,1... | collective-permute-start | bytes 1448 | tf_op jit(solution)/shard_map/ppermute | solution.py:19
  2.7 26.4 %collective-permute-start = (s32[4,30]{1,0:T(4,128)}, s32[4,30]{1,0:T(4,128)S(1)}, u32[]{:S(2)}, u32[]{:S(2)}) collective-permute-start(s32[4,30]{1,0:T(4,128)} %param.19), channel_id=1, source_target_pairs={{0,2},{1,3},{2,4},{3,5},{4,6},{5,7},{6,8},{7,9},{8,10},{9,11},{10,... | collective-permute-start | bytes 1448 | tf_op jit(solution)/shard_map/ppermute | solution.py:19
  6.1 25.5 %collective-permute-start.12 = (s32[4,30]{1,0:T(4,128)}, s32[4,30]{1,0:T(4,128)S(1)}, u32[]{:S(2)}, u32[]{:S(2)}) collective-permute-start(s32[4,30]{1,0:T(4,128)} %param.19), channel_id=1, source_target_pairs={{2,0},{3,1},{4,2},{5,3},{6,4},{7,5},{8,6},{9,7},{10,8},{11,9},{12,... | collective-permute-start | bytes 1448 | tf_op jit(solution)/shard_map/ppermute | solution.py:19
  9.5 26.5 %collective-permute-start.8 = (s32[4,30]{1,0:T(4,128)}, s32[4,30]{1,0:T(4,128)S(1)}, u32[]{:S(2)}, u32[]{:S(2)}) collective-permute-start(s32[4,30]{1,0:T(4,128)} %param.19), channel_id=1, source_target_pairs={{1,0},{2,1},{3,2},{4,3},{5,4},{6,5},{7,6},{8,7},{9,8},{10,9},{11,1... | collective-permute-start | bytes 1448 | tf_op jit(solution)/shard_map/ppermute | solution.py:19
  14.0 74.5 %collective-permute-start.14 = (bf16[256,1536]{0,1:T(8,128)(2,1)S(1)}, bf16[256,1536]{0,1:T(8,128)(2,1)}, u32[]{:S(2)}, u32[]{:S(2)}) collective-permute-start(bf16[256,1536]{0,1:T(8,128)(2,1)S(1)} %copy.73), channel_id=1, source_target_pairs={{2,0},{3,1},{4,2},{5,3},{6,4},{7,5},{8,6},{9,7},{10,8},{11,9},{12,... | collective-permute-start | bytes 2359304 | tf_op jit(solution)/shard_map/ppermute | solution.py:19
  21.7 5.3 %copy-start.15 = (bf16[256,1536]{0,1:T(8,128)(2,1)}, bf16[256,1536]{0,1:T(8,128)(2,1)S(1)}, u32[]{:S(2)}) copy-start(bf16[256,1536]{0,1:T(8,128)(2,1)S(1)} %copy.74) | copy-start | bytes 2359300
  22.5 1.7 copy-start
  24.1 4.8 %copy-start.20 = (bf16[4,30,4]{2,1,0:T(8,128)(2,1)S(1)}, bf16[4,30,4]{2,1,0:T(8,128)(2,1)}, u32[]{:S(2)}) copy-start(bf16[4,30,4]{2,1,0:T(8,128)(2,1)} %constant.139) | copy-start | bytes 2884
  24.1 7.4 %copy-start.19 = (bf16[4,30,4]{2,1,0:T(8,128)(2,1)S(1)}, bf16[4,30,4]{2,1,0:T(8,128)(2,1)}, u32[]{:S(2)}) copy-start(bf16[4,30,4]{2,1,0:T(8,128)(2,1)} %constant.138) | copy-start | bytes 2884
  24.1 11.4 %copy-start.18 = (bf16[4,30,4]{2,1,0:T(8,128)(2,1)S(1)}, bf16[4,30,4]{2,1,0:T(8,128)(2,1)}, u32[]{:S(2)}) copy-start(bf16[4,30,4]{2,1,0:T(8,128)(2,1)} %constant.142) | copy-start | bytes 2884
  24.1 14.7 %copy-start.17 = (bf16[4,30,4]{2,1,0:T(8,128)(2,1)S(1)}, bf16[4,30,4]{2,1,0:T(8,128)(2,1)}, u32[]{:S(2)}) copy-start(bf16[4,30,4]{2,1,0:T(8,128)(2,1)} %constant.141) | copy-start | bytes 2884
  27.0 89.2 %collective-permute-start.10 = (bf16[256,1536]{0,1:T(8,128)(2,1)S(1)}, bf16[256,1536]{0,1:T(8,128)(2,1)}, u32[]{:S(2)}, u32[]{:S(2)}) collective-permute-start(bf16[256,1536]{0,1:T(8,128)(2,1)S(1)} %copy.73), channel_id=1, source_target_pairs={{1,0},{2,1},{3,2},{4,3},{5,4},{6,5},{7,6},{8,7},{9,8},{10,9},{11,1... | collective-permute-start | bytes 2359304 | tf_op jit(solution)/shard_map/ppermute | solution.py:19
  29.1 112.2 %collective-permute-start.6 = (bf16[256,1536]{0,1:T(8,128)(2,1)S(1)}, bf16[256,1536]{0,1:T(8,128)(2,1)}, u32[]{:S(2)}, u32[]{:S(2)}) collective-permute-start(bf16[256,1536]{0,1:T(8,128)(2,1)S(1)} %copy.73), channel_id=1, source_target_pairs={{0,1},{1,2},{2,3},{3,4},{4,5},{5,6},{6,7},{7,8},{8,9},{9,10},{10,1... | collective-permute-start | bytes 2359304 | tf_op jit(solution)/shard_map/ppermute | solution.py:19
  31.6 104.5 %collective-permute-start.2 = (bf16[256,1536]{0,1:T(8,128)(2,1)S(1)}, bf16[256,1536]{0,1:T(8,128)(2,1)}, u32[]{:S(2)}, u32[]{:S(2)}) collective-permute-start(bf16[256,1536]{0,1:T(8,128)(2,1)S(1)} %copy.73), channel_id=1, source_target_pairs={{0,2},{1,3},{2,4},{3,5},{4,6},{5,7},{6,8},{7,9},{8,10},{9,11},{10,... | collective-permute-start | bytes 2359304 | tf_op jit(solution)/shard_map/ppermute | solution.py:19
  36.0 49.8 %collective-permute-start.13 = (bf16[256,1536]{0,1:T(8,128)(2,1)S(1)}, bf16[256,1536]{0,1:T(8,128)(2,1)S(1)}, u32[]{:S(2)}, u32[]{:S(2)}) collective-permute-start(bf16[256,1536]{0,1:T(8,128)(2,1)S(1)} %copy.69), channel_id=1, source_target_pairs={{2,0},{3,1},{4,2},{5,3},{6,4},{7,5},{8,6},{9,7},{10,8},{11,9},{12,... | collective-permute-start | bytes 2359304 | tf_op jit(solution)/shard_map/ppermute | solution.py:19
  43.8 47.1 %copy-start.16 = (bf16[256,1536]{0,1:T(8,128)(2,1)S(1)}, bf16[256,1536]{0,1:T(8,128)(2,1)}, u32[]{:S(2)}) copy-start(bf16[256,1536]{0,1:T(8,128)(2,1)} %copy-done.15) | copy-start | bytes 2359300
  85.8 9.2 %copy-start.8 = (bf16[256,1536]{0,1:T(8,128)(2,1)}, bf16[256,1536]{0,1:T(8,128)(2,1)S(1)}, u32[]{:S(2)}) copy-start(bf16[256,1536]{0,1:T(8,128)(2,1)S(1)} %collective-permute-done.13) | copy-start | bytes 2359300
  85.8 11.4 %collective-permute-start.9 = (bf16[256,1536]{0,1:T(8,128)(2,1)S(1)}, bf16[256,1536]{0,1:T(8,128)(2,1)S(1)}, u32[]{:S(2)}, u32[]{:S(2)}) collective-permute-start(bf16[256,1536]{0,1:T(8,128)(2,1)S(1)} %copy.69), channel_id=1, source_target_pairs={{1,0},{2,1},{3,2},{4,3},{5,4},{6,5},{7,6},{8,7},{9,8},{10,9},{11,1... | collective-permute-start | bytes 2359304 | tf_op jit(solution)/shard_map/ppermute | solution.py:19
  88.4 91.7 %copy-start.2 = (f32[12,256,256]{1,2,0:T(8,128)}, f32[12,256,256]{1,2,0:T(8,128)S(1)}, u32[]{:S(2)}) copy-start(f32[12,256,256]{1,2,0:T(8,128)S(1)} %get-tuple-element.44) | copy-start | bytes 9437188
  88.4 52.1 %collective-permute-start.5 = (bf16[256,1536]{0,1:T(8,128)(2,1)S(1)}, bf16[256,1536]{0,1:T(8,128)(2,1)S(1)}, u32[]{:S(2)}, u32[]{:S(2)}) collective-permute-start(bf16[256,1536]{0,1:T(8,128)(2,1)S(1)} %copy.69), channel_id=1, source_target_pairs={{0,1},{1,2},{2,3},{3,4},{4,5},{5,6},{6,7},{7,8},{8,9},{9,10},{10,1... | collective-permute-start | bytes 2359304 | tf_op jit(solution)/shard_map/ppermute | solution.py:19
  97.2 25.1 %copy-start.12 = (bf16[256,1536]{0,1:T(8,128)(2,1)}, bf16[256,1536]{0,1:T(8,128)(2,1)S(1)}, u32[]{:S(2)}) copy-start(bf16[256,1536]{0,1:T(8,128)(2,1)S(1)} %collective-permute-done.9) | copy-start | bytes 2359300
  97.2 36.1 %collective-permute-start.1 = (bf16[256,1536]{0,1:T(8,128)(2,1)S(1)}, bf16[256,1536]{0,1:T(8,128)(2,1)S(1)}, u32[]{:S(2)}, u32[]{:S(2)}) collective-permute-start(bf16[256,1536]{0,1:T(8,128)(2,1)S(1)} %copy.69), channel_id=1, source_target_pairs={{0,2},{1,3},{2,4},{3,5},{4,6},{5,7},{6,8},{7,9},{8,10},{9,11},{10,... | collective-permute-start | bytes 2359304 | tf_op jit(solution)/shard_map/ppermute | solution.py:19
  116.2 49.8 %copy-start.4 = (f32[12,256,256]{1,2,0:T(8,128)}, f32[12,256,256]{1,2,0:T(8,128)S(1)}, u32[]{:S(2)}) copy-start(f32[12,256,256]{1,2,0:T(8,128)S(1)} %get-tuple-element.41) | copy-start | bytes 9437188
  116.2 34.0 %collective-permute-start.15 = (f32[3,12,256]{2,1,0:T(8,128)S(1)}, f32[3,12,256]{2,1,0:T(8,128)S(1)}, u32[]{:S(2)}, u32[]{:S(2)}) collective-permute-start(f32[3,12,256]{2,1,0:T(8,128)S(1)} %pad_maximum_fusion.3), channel_id=1, source_target_pairs={{0,2},{1,3},{2,4},{3,5},{4,6},{5,7},{6,8},{7,9},{8,10},{9,11},{10,... | collective-permute-start | bytes 110600 | tf_op jit(solution)/shard_map/ppermute | solution.py:19
  133.3 16.9 %collective-permute-start.11 = (f32[3,12,256]{2,1,0:T(8,128)S(1)}, f32[3,12,256]{2,1,0:T(8,128)S(1)}, u32[]{:S(2)}, u32[]{:S(2)}) collective-permute-start(f32[3,12,256]{2,1,0:T(8,128)S(1)} %pad_maximum_fusion.2), channel_id=1, source_target_pairs={{0,1},{1,2},{2,3},{3,4},{4,5},{5,6},{6,7},{7,8},{8,9},{9,10},{10,1... | collective-permute-start | bytes 110600 | tf_op jit(solution)/shard_map/ppermute | solution.py:19
  138.6 9.9 %collective-permute-start.3 = (f32[3,12,256]{2,1,0:T(8,128)S(1)}, f32[3,12,256]{2,1,0:T(8,128)S(1)}, u32[]{:S(2)}, u32[]{:S(2)}) collective-permute-start(f32[3,12,256]{2,1,0:T(8,128)S(1)} %pad_maximum_fusion), channel_id=1, source_target_pairs={{2,0},{3,1},{4,2},{5,3},{6,4},{7,5},{8,6},{9,7},{10,8},{11,9},{12,... | collective-permute-start | bytes 110600 | tf_op jit(solution)/shard_map/ppermute | solution.py:19
  141.3 9.1 %copy-start.1 = (f32[12,256,256]{1,2,0:T(8,128)S(1)}, f32[12,256,256]{1,2,0:T(8,128)}, u32[]{:S(2)}) copy-start(f32[12,256,256]{1,2,0:T(8,128)} %copy-done) | copy-start | bytes 9437188
  143.9 6.3 %collective-permute-start.7 = (f32[3,12,256]{2,1,0:T(8,128)S(1)}, f32[3,12,256]{2,1,0:T(8,128)S(1)}, u32[]{:S(2)}, u32[]{:S(2)}) collective-permute-start(f32[3,12,256]{2,1,0:T(8,128)S(1)} %pad_maximum_fusion.1), channel_id=1, source_target_pairs={{1,0},{2,1},{3,2},{4,3},{5,4},{6,5},{7,6},{8,7},{9,8},{10,9},{11,1... | collective-permute-start | bytes 110600 | tf_op jit(solution)/shard_map/ppermute | solution.py:19
  150.2 13.2 %copy-start.10 = (f32[12,256,256]{1,2,0:T(8,128)S(1)}, f32[12,256,256]{1,2,0:T(8,128)}, u32[]{:S(2)}) copy-start(f32[12,256,256]{1,2,0:T(8,128)} %get-tuple-element.39) | copy-start | bytes 9437188
  151.1 29.0 %collective-permute-start.22 = (f32[2,12,256]{2,1,0:T(8,128)S(1)}, f32[2,12,256]{2,1,0:T(8,128)S(1)}, u32[]{:S(2)}, u32[]{:S(2)}) collective-permute-start(f32[2,12,256]{2,1,0:T(8,128)S(1)} %pad_maximum_fusion.4), channel_id=1, source_target_pairs={{2,0},{3,1},{4,2},{5,3},{6,4},{7,5},{8,6},{9,7},{10,8},{11,9},{12,... | collective-permute-start | bytes 73736 | tf_op jit(solution)/shard_map/ppermute | solution.py:19
  153.1 12.9 %collective-permute-start.20 = (f32[2,12,256]{2,1,0:T(8,128)S(1)}, f32[2,12,256]{2,1,0:T(8,128)S(1)}, u32[]{:S(2)}, u32[]{:S(2)}) collective-permute-start(f32[2,12,256]{2,1,0:T(8,128)S(1)} %pad_maximum_fusion.4), channel_id=1, source_target_pairs={{1,0},{2,1},{3,2},{4,3},{5,4},{6,5},{7,6},{8,7},{9,8},{10,9},{11,1... | collective-permute-start | bytes 73736 | tf_op jit(solution)/shard_map/ppermute | solution.py:19
  157.8 16.3 %collective-permute-start.18 = (f32[2,12,256]{2,1,0:T(8,128)S(1)}, f32[2,12,256]{2,1,0:T(8,128)S(1)}, u32[]{:S(2)}, u32[]{:S(2)}) collective-permute-start(f32[2,12,256]{2,1,0:T(8,128)S(1)} %pad_maximum_fusion.4), channel_id=1, source_target_pairs={{0,1},{1,2},{2,3},{3,4},{4,5},{5,6},{6,7},{7,8},{8,9},{9,10},{10,1... | collective-permute-start | bytes 73736 | tf_op jit(solution)/shard_map/ppermute | solution.py:19
  159.8 8.1 %collective-permute-start.16 = (f32[2,12,256]{2,1,0:T(8,128)S(1)}, f32[2,12,256]{2,1,0:T(8,128)S(1)}, u32[]{:S(2)}, u32[]{:S(2)}) collective-permute-start(f32[2,12,256]{2,1,0:T(8,128)S(1)} %pad_maximum_fusion.4), channel_id=1, source_target_pairs={{0,2},{1,3},{2,4},{3,5},{4,6},{5,7},{6,8},{7,9},{8,10},{9,11},{10,... | collective-permute-start | bytes 73736 | tf_op jit(solution)/shard_map/ppermute | solution.py:19
  183.4 5.4 %copy-start.11 = (f32[12,256,256]{1,2,0:T(8,128)S(1)}, f32[12,256,256]{1,2,0:T(8,128)}, u32[]{:S(2)}) copy-start(f32[12,256,256]{1,2,0:T(8,128)} %get-tuple-element.45) | copy-start | bytes 9437188
  187.2 2.2 copy-start.3
  189.3 15.6 %copy-start.13 = (bf16[256,1536]{0,1:T(8,128)(2,1)S(1)}, bf16[256,1536]{0,1:T(8,128)(2,1)}, u32[]{:S(2)}) copy-start(bf16[256,1536]{0,1:T(8,128)(2,1)} %copy-done.12) | copy-start | bytes 2359300
  190.2 15.3 %copy-start.5 = (f32[12,256,128]{2,1,0:T(8,128)S(1)}, f32[12,256,128]{2,1,0:T(8,128)}, u32[]{:S(2)}) copy-start(f32[12,256,128]{2,1,0:T(8,128)} %fusion.76) | copy-start | bytes 4718596
  190.3 15.3 %copy-start.6 = (f32[12,256,128]{2,1,0:T(8,128)S(1)}, f32[12,256,128]{2,1,0:T(8,128)}, u32[]{:S(2)}) copy-start(f32[12,256,128]{2,1,0:T(8,128)} %fusion.74) | copy-start | bytes 4718596
  190.3 15.3 %copy-start.7 = (f32[12,256,128]{2,1,0:T(8,128)S(1)}, f32[12,256,128]{2,1,0:T(8,128)}, u32[]{:S(2)}) copy-start(f32[12,256,128]{2,1,0:T(8,128)} %fusion.75) | copy-start | bytes 4718596
  190.3 15.3 %copy-start.9 = (bf16[256,1536]{0,1:T(8,128)(2,1)S(1)}, bf16[256,1536]{0,1:T(8,128)(2,1)}, u32[]{:S(2)}) copy-start(bf16[256,1536]{0,1:T(8,128)(2,1)} %copy-done.8) | copy-start | bytes 2359300
  191.8 47.6 %collective-permute-start.23 = (bf16[256,12,128]{2,0,1:T(8,128)(2,1)}, bf16[256,12,128]{2,0,1:T(8,128)(2,1)}, u32[]{:S(2)}, u32[]{:S(2)}) collective-permute-start(bf16[256,12,128]{2,0,1:T(8,128)(2,1)} %fusion.46), channel_id=1, source_target_pairs={{0,2},{1,3},{2,4},{3,5},{4,6},{5,7},{6,8},{7,9},{8,10},{9,11},{10,... | collective-permute-start | bytes 2359304 | tf_op jit(solution)/shard_map/ppermute | solution.py:19
  196.3 43.1 %collective-permute-start.21 = (bf16[256,12,128]{2,0,1:T(8,128)(2,1)}, bf16[256,12,128]{2,0,1:T(8,128)(2,1)}, u32[]{:S(2)}, u32[]{:S(2)}) collective-permute-start(bf16[256,12,128]{2,0,1:T(8,128)(2,1)} %fusion.45), channel_id=1, source_target_pairs={{0,1},{1,2},{2,3},{3,4},{4,5},{5,6},{6,7},{7,8},{8,9},{9,10},{10,1... | collective-permute-start | bytes 2359304 | tf_op jit(solution)/shard_map/ppermute | solution.py:19
  199.4 40.0 %collective-permute-start.19 = (bf16[256,12,128]{2,0,1:T(8,128)(2,1)}, bf16[256,12,128]{2,0,1:T(8,128)(2,1)}, u32[]{:S(2)}, u32[]{:S(2)}) collective-permute-start(bf16[256,12,128]{2,0,1:T(8,128)(2,1)} %fusion.44), channel_id=1, source_target_pairs={{1,0},{2,1},{3,2},{4,3},{5,4},{6,5},{7,6},{8,7},{9,8},{10,9},{11,1... | collective-permute-start | bytes 2359304 | tf_op jit(solution)/shard_map/ppermute | solution.py:19
  202.8 46.4 %collective-permute-start.17 = (bf16[256,12,128]{2,0,1:T(8,128)(2,1)}, bf16[256,12,128]{2,0,1:T(8,128)(2,1)}, u32[]{:S(2)}, u32[]{:S(2)}) collective-permute-start(bf16[256,12,128]{2,0,1:T(8,128)(2,1)} %fusion.43), channel_id=1, source_target_pairs={{2,0},{3,1},{4,2},{5,3},{6,4},{7,5},{8,6},{9,7},{10,8},{11,9},{12,... | collective-permute-start | bytes 2359304 | tf_op jit(solution)/shard_map/ppermute | solution.py:19

commit v2 on v1

v2 whole, which is shorter than its diff:
```python
import jax
import jax.numpy as jnp
import numpy as np
from jax import lax
from jax.sharding import PartitionSpec as P

HEADS = 12
HDIM = 128
BLOCK = 64
REACH = 2
FRAMES = 2
BANDS = 2
NEG = -1e30
LIST_ROWS = 16


def from_behind(value, axis, steps):
    count = lax.axis_size(axis)
    first, last = (max(0, -steps), min(count, count - steps))
    return lax.ppermute(value, axis, [(source, source + steps) for source in range(first, last)])


def swap_cores(value):
    count = lax.axis_size("tm")
    return lax.ppermute(value, "tm", [(source, source ^ 1) for source in range(count)])


def swap_chips(value):
    count = lax.axis_size("tm")
    pairs = []
    for source in range(count):
        target = source - 1 if source % 2 == 0 else source + 1
        if 0 <= target < count:
            pairs.append((source, target))
    return lax.ppermute(value, "tm", pairs)


def pick_table(offset):
    blocks = FRAMES * BANDS
    slot = REACH - offset
    table = np.zeros((blocks, 30, blocks), np.float32)
    own = np.zeros((blocks, blocks), bool)
    for qb in range(blocks):
        for kb in range(blocks):
            cand = (slot * FRAMES + kb // BANDS) * 3 + kb % BANDS - qb % BANDS + 1
            table[qb, cand, kb] = 1.0
            own[qb, kb] = offset == 0 and qb == kb
    return table, own


def pair_mask(list_rows, table, own, valid):
    chosen = jnp.einsum("qc,qck->qk", list_rows, table) > 0
    return (chosen & valid) | own


def blocked(x):
    return x.reshape(HEADS, FRAMES * BANDS, BLOCK, FRAMES * BANDS, BLOCK)


def local(queries, keys, values, grad_out, block_list):
    groups = lax.axis_size("tm")
    here = lax.axis_index("tm")
    even = here % 2 == 0
    scaling = HDIM ** (-0.5)
    tok, width = queries.shape
    blocks = FRAMES * BANDS
    cands = block_list.shape[1]
    key_h = keys.reshape(tok, HEADS, HDIM)
    value_h = values.reshape(tok, HEADS, HDIM)

    flags = (block_list > 0).astype(jnp.bfloat16).reshape(1, blocks * cands)
    flags = jnp.pad(flags, ((0, LIST_ROWS - 1), (0, width - blocks * cands)))
    pack = jnp.concatenate([queries, grad_out, flags], axis=0)

    from_below = from_behind(pack, "tm", 2)
    from_above = from_behind(pack, "tm", -2)
    relay = jnp.where(even, from_above, from_below)
    partner, relayed = swap_cores((pack, relay))

    up = jnp.where(even, 1, -1)
    slots = {
        "own": (pack, 0),
        "below": (from_below, -2),
        "above": (from_above, 2),
        "partner": (partner, up),
        "relayed": (relayed, -up),
    }
    static_tables = {offset: pick_table(offset) for offset in (-2, -1, 0, 1, 2)}

    def tables_for(offset):
        if isinstance(offset, int):
            table, own = static_tables[offset]
            return jnp.asarray(table), jnp.asarray(own)
        t_up, o_up = static_tables[1]
        t_dn, o_dn = static_tables[-1]
        return (
            jnp.where(offset > 0, jnp.asarray(t_up), jnp.asarray(t_dn)),
            jnp.where(offset > 0, jnp.asarray(o_up), jnp.asarray(o_dn)),
        )

    parts = {}
    stats_out = {}
    for name, (data, offset) in slots.items():
        q_h = data[:tok].reshape(tok, HEADS, HDIM)
        g_h = data[tok : 2 * tok].reshape(tok, HEADS, HDIM)
        list_rows = data[2 * tok, : blocks * cands].astype(jnp.float32).reshape(blocks, cands)
        source = here + offset
        valid = (source >= 0) & (source < groups)
        table, own = tables_for(offset)
        mask = pair_mask(list_rows, table, own, valid)[None, :, None, :, None]
        scores = blocked(
            jnp.einsum("qhd,khd->hqk", q_h, key_h, preferred_element_type=jnp.float32) * scaling
        )
        grad_probs = blocked(
            jnp.einsum("qhd,khd->hqk", g_h, value_h, preferred_element_type=jnp.float32)
        )
        masked = jnp.where(mask, scores, NEG)
        row_max = jnp.max(masked, axis=(3, 4))
        expd = jnp.where(mask, jnp.exp(masked - row_max[:, :, :, None, None]), 0.0)
        row_sum = jnp.sum(expd, axis=(3, 4))
        row_dot = jnp.sum(expd * grad_probs, axis=(3, 4))
        parts[name] = (q_h, g_h, mask, scores, grad_probs)
        stats_out[name] = jnp.stack([row_max, row_sum, row_dot]).reshape(3, HEADS, tok)

    stats_in = {
        "own": (stats_out["own"], 0),
        "below": (from_behind(stats_out["above"], "tm", 2), -2),
        "above": (from_behind(stats_out["below"], "tm", -2), 2),
        "partner": (swap_cores(stats_out["partner"]), up),
        "relayed": (swap_chips(stats_out["relayed"]), -up),
    }
    maxes, sums, dots = [], [], []
    for name, (stats, offset) in stats_in.items():
        source = here + offset
        valid = (source >= 0) & (source < groups)
        maxes.append(jnp.where(valid, stats[0], NEG))
        sums.append(jnp.where(valid, stats[1], 0.0))
        dots.append(jnp.where(valid, stats[2], 0.0))
    maxes, sums, dots = jnp.stack(maxes), jnp.stack(sums), jnp.stack(dots)
    top = jnp.max(maxes, axis=0)
    scale = jnp.exp(maxes - top[None])
    total = jnp.sum(sums * scale, axis=0)
    log_total = top + jnp.log(total)
    deltas = jnp.sum(dots * scale, axis=0) / total
    final = jnp.stack([log_total, deltas])

    finals = {
        "own": final,
        "below": from_behind(final, "tm", 2),
        "above": from_behind(final, "tm", -2),
        "partner": swap_cores(final),
        "relayed": swap_chips(final),
    }

    key_grad = jnp.zeros((tok, HEADS, HDIM), jnp.float32)
    value_grad = jnp.zeros((tok, HEADS, HDIM), jnp.float32)
    q_parts = {}
    for name in slots:
        q_h, g_h, mask, scores, grad_probs = parts[name]
        got = finals[name]
        lse = got[0].reshape(HEADS, blocks, BLOCK)[:, :, :, None, None]
        dlt = got[1].reshape(HEADS, blocks, BLOCK)[:, :, :, None, None]
        weights = jnp.where(mask, jnp.exp(scores - lse), 0.0)
        weights_low = weights.astype(jnp.bfloat16).reshape(HEADS, tok, tok)
        grad_scores = (weights * (grad_probs - dlt)).astype(jnp.bfloat16).reshape(HEADS, tok, tok)
        key_grad = key_grad + jnp.einsum(
            "hqk,qhd->khd", grad_scores, q_h, preferred_element_type=jnp.float32
        ) * scaling
        value_grad = value_grad + jnp.einsum(
            "hqk,qhd->khd", weights_low, g_h, preferred_element_type=jnp.float32
        )
        q_parts[name] = jnp.einsum(
            "hqk,khd->qhd", grad_scores, key_h, preferred_element_type=jnp.float32
        ) * scaling

    from_partner, relay_part = swap_cores((q_parts["partner"], q_parts["relayed"]))
    zero = jnp.zeros_like(relay_part)
    send_up = q_parts["above"] + jnp.where(even, relay_part, zero)
    send_down = q_parts["below"] + jnp.where(even, zero, relay_part)
    got_below = from_behind(send_up.astype(jnp.bfloat16), "tm", 2).astype(jnp.float32)
    got_above = from_behind(send_down.astype(jnp.bfloat16), "tm", -2).astype(jnp.float32)
    query_grad = q_parts["own"] + from_partner + got_below + got_above
    return (
        query_grad.reshape(tok, width).astype(jnp.bfloat16),
        key_grad.reshape(tok, width).astype(jnp.bfloat16),
        value_grad.reshape(tok, width).astype(jnp.bfloat16),
    )


def solution(mesh):
    placed = (
        P(("group", "tm"), None),
        P(("group", "tm"), None),
        P(("group", "tm"), None),
        P(("group", "tm"), None),
        P(("group", "tm"), None),
    )
    return jax.shard_map(
        local,
        mesh=mesh,
        in_specs=placed,
        out_specs=(P(("group", "tm"), None), P(("group", "tm"), None), P(("group", "tm"), None)),
        check_vma=False,
    )
```

time: 255 us -> 219 us (0.86)
  starting transfers between devices: 83.1 us -> 33.1 us
  local copies, waits for them, and re-layouts: 18.4 us -> 40.2 us
  waiting for transfers between devices: 96.4 us -> 84.7 us
  other arithmetic: 8.89 us -> 19.1 us
  matrix products: 45 us -> 39.1 us
    ppermute x24 -> x8, starting transfers between devices: 83.1 us -> 27.6 us  [from_behind(): lax.ppermute(value, axis, [(source, source + steps) for source in range(f...]
    unnamed x52 -> x115, local copies, waits for them, and re-layouts: 11.5 us -> 26.9 us
    ppermute x24 -> x8, waiting for transfers between devices: 96.4 us -> 81.1 us  [from_behind(): lax.ppermute(value, axis, [(source, source + steps) for source in range(f...]
    slice x0 -> x8, local copies, waits for them, and re-layouts: none -> 10.5 us  [the longest x3 5.36 us: local(): g_h = data[tok:2 * tok].reshape(tok, HEADS, HDIM)]
    ppermute x0 -> x8, starting transfers between devices: none -> 5.5 us  [the longest x2 3.95 us: swap_chips(): return lax.ppermute(value, 'tm', pairs)]
    dot_general x5, matrix products: 8.56 us -> 4.86 us  [local(): jnp.einsum('hqk,qhd->khd', weights_low, g_h, preferred_element_type=jnp.f...]
    ppermute x0 -> x8, waiting for transfers between devices: none -> 3.61 us  [the longest x2 3.6 us: swap_chips(): return lax.ppermute(value, 'tm', pairs)]
    unnamed x1 -> x5, other arithmetic: 0.01 us -> 3.23 us
  transfers between devices with their start and end apart: 24 -> 16, of which waited for: 6 -> 5; matrix products, arithmetic and copies ran while one was open for 21% -> 32% of each run, Pallas kernels for 0% -> 0%
where the time goes in v2:
time: 219 us; the launch traced here: 218 us
  waiting for transfers between devices  84.7 us (39%)
  local copies, waits for them, and re-layouts  40.2 us (18%)
  matrix products  39.1 us (18%)
  starting transfers between devices  33.1 us (15%)
  other arithmetic  19.1 us (9%)
    ppermute x8, waiting for transfers between devices, from_behind(): lax.ppermute(value, axis, [(source, source + steps) for source in range(f...  81.1 us
    ppermute x8, starting transfers between devices, from_behind(): lax.ppermute(value, axis, [(source, source + steps) for source in range(f...  27.6 us
    unnamed x115, local copies, waits for them, and re-layouts  26.9 us
    dot_general x5, matrix products, local(): jnp.einsum('qhd,khd->hqk', g_h, value_h, preferred_element_type=jnp.float32)  13 us
    dot_general x5, matrix products, local(): jnp.einsum('hqk,khd->qhd', grad_scores, key_h, preferred_element_type=jnp...  9.37 us
    dot_general x5, matrix products, local(): jnp.einsum('hqk,qhd->khd', grad_scores, q_h, preferred_element_type=jnp.f...  6.94 us
    convert_element_type x5, other arithmetic, local(): (weights * (grad_probs - dlt)).astype(jnp.bfloat16).reshape(HEADS, tok, tok)  5.62 us
    slice x3, local copies, waits for them, and re-layouts, local(): g_h = data[tok:2 * tok].reshape(tok, HEADS, HDIM)  5.36 us
  transfers between devices with their start and end apart: 16, of which 5 were waited for; matrix products, arithmetic and copies ran while one was open for 32% of the time, Pallas kernels for 0%

profile of v2, /device:TPU:8, one launch (start us, length us, event | category | flops | bytes accessed | tf_op | source)
XLA Modules:
  0.0 217.6 jit_solution(16194457064753336424)
XLA Ops:
  0.7 0.8 fusion.79
  1.5 2.6 %fusion.11 = bf16[528,1536]{1,0:T(8,128)(2,1)} fusion(bf16[1,120]{1,0:T(2,128)(2,1)S(1)} %reshape.365, bf16[256,1536]{1,0:T(8,128)(2,1)} %param.18, bf16[256,1536]{1,0:T(8,128)(2,1)} %param.15), kind=kLoop, calls=%fused_computation.37 | loop fusion | flops 6488064 | bytes 3195120 | tf_op jit(solution)/shard_map/concatenate | solution.py:73
  4.2 3.4 %collective-permute-start.2 = (bf16[528,1536]{1,0:T(8,128)(2,1)}, bf16[528,1536]{1,0:T(8,128)(2,1)}, u32[]{:S(2)}, u32[]{:S(2)}) collective-permute-start(bf16[528,1536]{1,0:T(8,128)(2,1)} %fusion.11), channel_id=1, source_target_pairs={{0,2},{1,3},{2,4},{3,5},{4,6},{5,7},{6,8},{7,9},{8,10},{9,11},{10,... | collective-permute-start | bytes 4866056 | tf_op jit(solution)/shard_map/ppermute | solution.py:20
  7.6 3.3 %collective-permute-start = (bf16[528,1536]{1,0:T(8,128)(2,1)}, bf16[528,1536]{1,0:T(8,128)(2,1)}, u32[]{:S(2)}, u32[]{:S(2)}) collective-permute-start(bf16[528,1536]{1,0:T(8,128)(2,1)} %fusion.11), channel_id=1, source_target_pairs={{2,0},{3,1},{4,2},{5,3},{6,4},{7,5},{8,6},{9,7},{10,8},{11,9},{12,... | collective-permute-start | bytes 4866056 | tf_op jit(solution)/shard_map/ppermute | solution.py:20
  12.2 1.4 copy.174
  13.6 1.4 copy.181
  15.7 1.7 copy-done
  17.4 2.9 %fusion.10 = (f32[12,256]{1,0:T(8,128)S(1)}, f32[12,256]{1,0:T(8,128)S(1)}, f32[12,256,256]{1,2,0:T(8,128)}) fusion(f32[12,256,256]{1,2,0:T(8,128)S(1)} %get-tuple-element.60, f32[12,256]{1,0:T(8,128)S(1)} %get-tuple-element.59, pred[256,256]{0,1:T(8,128)(4,1)S(1)} %broadcast_in_dim.137, bf16[256,12,128]{0,2,1:T(8,128)(2,1)S(1)} %bitcast.238, ...), kind=kOutput, calls=%fused_computation.36 | convolution fusion | flops 206825472 | bytes 7966720 | tf_op jit(solution)/shard_map/qhd,khd->hqk/dot_general | solution.py:115
  21.5 2.4 %fusion.83 = (bf16[256,1536]{1,0:T(8,128)(2,1)}, bf16[256,1536]{1,0:T(8,128)(2,1)S(1)}) fusion(bf16[528,1536]{1,0:T(8,128)(2,1)} %collective-permute-done.4), kind=kLoop, calls=%fused_computation.175 | loop fusion | bytes 3145728 | tf_op jit(solution)/shard_map/slice | solution.py:104
  23.9 1.4 copy.288
  26.7 1.2 copy.289
  27.8 50.2 %collective-permute-done.2 = bf16[528,1536]{1,0:T(8,128)(2,1)} collective-permute-done((bf16[528,1536]{1,0:T(8,128)(2,1)}, bf16[528,1536]{1,0:T(8,128)(2,1)}, u32[]{:S(2)}, u32[]{:S(2)}) %collective-permute-start.2) | collective-permute-done | bytes 1622048 | tf_op jit(solution)/shard_map/ppermute | solution.py:20
  79.5 2.4 %fusion.81 = (bf16[256,1536]{1,0:T(8,128)(2,1)S(1)}, bf16[256,1536]{1,0:T(8,128)(2,1)}) fusion(bf16[528,1536]{1,0:T(8,128)(2,1)} %collective-permute-done.2), kind=kLoop, calls=%fused_computation.173 | loop fusion | bytes 3145728 | tf_op jit(solution)/shard_map/slice | solution.py:105
  81.8 1.2 copy.287
  83.0 1.4 copy.286
  84.5 2.9 %fusion.82 = (bf16[256,1536]{1,0:T(8,128)(2,1)}, bf16[256,1536]{1,0:T(8,128)(2,1)}) fusion(bf16[528,1536]{1,0:T(8,128)(2,1)} %collective-permute-done), kind=kLoop, calls=%fused_computation.174 | loop fusion | bytes 3145728 | tf_op jit(solution)/shard_map/slice | solution.py:105
  87.4 2.3 %copy.285 = bf16[256,1536]{0,1:T(8,128)(2,1)} copy(bf16[256,1536]{1,0:T(8,128)(2,1)} %get-tuple-element.33) | data formatting | bytes 1572864
  91.1 2.3 %copy.284 = bf16[256,1536]{0,1:T(8,128)(2,1)} copy(bf16[256,1536]{1,0:T(8,128)(2,1)} %get-tuple-element.34) | data formatting | bytes 1572864
  93.4 1.6 broadcast_select_fusion
  96.3 2.9 %fusion.8 = (f32[12,256]{1,0:T(8,128)S(1)}, f32[12,256]{1,0:T(8,128)S(1)}, f32[12,256,256]{1,2,0:T(8,128)}) fusion(f32[12,256,256]{1,2,0:T(8,128)S(1)} %get-tuple-element.69, f32[12,256]{1,0:T(8,128)S(1)} %get-tuple-element.68, pred[256,256]{0,1:T(8,128)(4,1)S(1)} %broadcast_in_dim.150, bf16[256,12,128]{0,2,1:T(8,128)(2,1)S(1)} %bitcast.240, ...), kind=kOutput, calls=%fused_computation.34 | convolution fusion | flops 206825472 | bytes 7966720 | tf_op jit(solution)/shard_map/qhd,khd->hqk/dot_general | solution.py:115
  100.6 3.0 %fusion.6 = (f32[12,256]{1,0:T(8,128)S(1)}, f32[12,256]{1,0:T(8,128)S(1)}, f32[12,256,256]{1,2,0:T(8,128)}) fusion(f32[12,256,256]{1,2,0:T(8,128)S(1)} %get-tuple-element.63, f32[12,256]{1,0:T(8,128)S(1)} %get-tuple-element.62, pred[256,256]{0,1:T(8,128)(4,1)S(1)} %broadcast_in_dim.142, bf16[256,12,128]{0,2,1:T(8,128)(2,1)S(1)} %bitcast.244, ...), kind=kOutput, calls=%fused_computation.32 | convolution fusion | flops 206825472 | bytes 7966720 | tf_op jit(solution)/shard_map/qhd,khd->hqk/dot_general | solution.py:115
  103.6 4.7 %collective-permute-start.1 = (f32[3,12,256]{2,1,0:T(8,128)S(1)}, f32[3,12,256]{2,1,0:T(8,128)S(1)}, u32[]{:S(2)}, u32[]{:S(2)}) collective-permute-start(f32[3,12,256]{2,1,0:T(8,128)S(1)} %pad_maximum_fusion), channel_id=1, source_target_pairs={{0,2},{1,3},{2,4},{3,5},{4,6},{5,7},{6,8},{7,9},{8,10},{9,11},{10,... | collective-permute-start | bytes 110600 | tf_op jit(solution)/shard_map/ppermute | solution.py:20
  109.1 2.9 %fusion.7 = (f32[12,256]{1,0:T(8,128)S(1)}, f32[12,256]{1,0:T(8,128)S(1)}, f32[12,256,256]{1,2,0:T(8,128)}) fusion(f32[12,256,256]{1,2,0:T(8,128)S(1)} %get-tuple-element.66, f32[12,256]{1,0:T(8,128)S(1)} %get-tuple-element.65, pred[256,256]{0,1:T(8,128)(4,1)S(1)} %broadcast_in_dim.147, bf16[256,12,128]{0,2,1:T(8,128)(2,1)S(1)} %bitcast.242, ...), kind=kOutput, calls=%fused_computation.33 | convolution fusion | flops 206825472 | bytes 7966720 | tf_op jit(solution)/shard_map/qhd,khd->hqk/dot_general | solution.py:115
  112.0 2.4 %collective-permute-start.3 = (f32[3,12,256]{2,1,0:T(8,128)S(1)}, f32[3,12,256]{2,1,0:T(8,128)S(1)}, u32[]{:S(2)}, u32[]{:S(2)}) collective-permute-start(f32[3,12,256]{2,1,0:T(8,128)S(1)} %pad_maximum_fusion.1), channel_id=1, source_target_pairs={{2,0},{3,1},{4,2},{5,3},{6,4},{7,5},{8,6},{9,7},{10,8},{11,9},{12,... | collective-permute-start | bytes 110600 | tf_op jit(solution)/shard_map/ppermute | solution.py:20
  115.0 3.0 %collective-permute-done.3 = f32[3,12,256]{2,1,0:T(8,128)S(1)} collective-permute-done((f32[3,12,256]{2,1,0:T(8,128)S(1)}, f32[3,12,256]{2,1,0:T(8,128)S(1)}, u32[]{:S(2)}, u32[]{:S(2)}) %collective-permute-start.3) | collective-permute-done | bytes 36896 | tf_op jit(solution)/shard_map/ppermute | solution.py:20
  118.6 1.2 copy-done.34
  119.9 1.2 copy.291
  121.9 0.9 fusion.51
  125.0 1.3 fusion.9
  126.3 1.9 collective-permute-start.7
  129.0 3.6 %collective-permute-done.7 = f32[3,12,256]{2,1,0:T(8,128)S(1)} collective-permute-done((f32[3,12,256]{2,1,0:T(8,128)S(1)}, f32[3,12,256]{2,1,0:T(8,128)S(1)}, u32[]{:S(2)}, u32[]{:S(2)}) %collective-permute-start.7) | collective-permute-done | bytes 36896 | tf_op jit(solution)/shard_map/ppermute | solution.py:35
  133.5 0.9 fusion.60
  134.4 3.0 %collective-permute-start.14 = (f32[2,12,256]{2,1,0:T(8,128)S(1)}, f32[2,12,256]{2,1,0:T(8,128)S(1)}, u32[]{:S(2)}, u32[]{:S(2)}) collective-permute-start(f32[2,12,256]{2,1,0:T(8,128)S(1)} %pad_maximum_fusion.4), channel_id=1, source_target_pairs={{0,2},{1,3},{2,4},{3,5},{4,6},{5,7},{6,8},{7,9},{8,10},{9,11},{10,... | collective-permute-start | bytes 73736 | tf_op jit(solution)/shard_map/ppermute | solution.py:20
  137.4 2.0 collective-permute-start.11
  139.4 3.7 %collective-permute-start.10 = (f32[2,12,256]{2,1,0:T(8,128)S(1)}, f32[2,12,256]{2,1,0:T(8,128)S(1)}, u32[]{:S(2)}, u32[]{:S(2)}) collective-permute-start(f32[2,12,256]{2,1,0:T(8,128)S(1)} %pad_maximum_fusion.4), channel_id=1, source_target_pairs={{2,0},{3,1},{4,2},{5,3},{6,4},{7,5},{8,6},{9,7},{10,8},{11,9},{12,... | collective-permute-start | bytes 73736 | tf_op jit(solution)/shard_map/ppermute | solution.py:20
  143.1 1.0 collective-permute-start.8
  144.1 0.8 fusion.20
  144.9 0.9 multiply_convert_fusion.4
  145.8 1.8 fusion.86
  147.6 1.6 fusion.90
  149.2 0.8 fusion.12
  150.0 1.0 copy-done.3
  151.2 0.8 fusion.16
  152.6 0.8 fusion.18
  154.0 0.9 multiply_convert_fusion.3
  154.9 1.6 multiply_bitcast_fusion.1
  156.5 0.9 multiply_convert_fusion.1
  157.4 1.5 multiply_bitcast_fusion
  159.9 2.0 multiply_convert_fusion
  161.9 1.8 fusion.89
  164.4 0.9 multiply_convert_fusion.2
  165.3 1.8 fusion.22
  167.1 1.8 fusion.88
  168.9 2.3 %copy.230 = bf16[256,1536]{1,0:T(8,128)(2,1)} copy(bf16[256,1536]{0,1:T(8,128)(2,1)} %bitcast.249) | data formatting | bytes 1572864
  171.2 3.4 %fusion.25 = bf16[256,12,128]{0,2,1:T(8,128)(2,1)} fusion(f32[256,12,128]{0,2,1:T(8,128)} %collective-permute-done.12, bf16[256,12,128]{0,2,1:T(8,128)(2,1)S(1)} %bitcast.225, bf16[12,256,256]{1,2,0:T(8,128)(2,1)} %copy-done.9, pred[]{:T(512)S(6)} %eq.5), kind=kOutput, calls=%fused_computation.57 | convolution fusion | flops 202899456 | bytes 4718593 | tf_op jit(solution)/shard_map/hqk,khd->qhd/dot_general | solution.py:172
  174.6 3.1 %collective-permute-start.13 = (bf16[256,12,128]{0,2,1:T(8,128)(2,1)}, bf16[256,12,128]{0,2,1:T(8,128)(2,1)}, u32[]{:S(2)}, u32[]{:S(2)}) collective-permute-start(bf16[256,12,128]{0,2,1:T(8,128)(2,1)} %fusion.25), channel_id=1, source_target_pairs={{0,2},{1,3},{2,4},{3,5},{4,6},{5,7},{6,8},{7,9},{8,10},{9,11},{10,... | collective-permute-start | bytes 2359304 | tf_op jit(solution)/shard_map/ppermute | solution.py:20
  177.7 1.3 fusion.24
  179.0 4.0 %collective-permute-start.15 = (bf16[256,12,128]{0,2,1:T(8,128)(2,1)}, bf16[256,12,128]{0,2,1:T(8,128)(2,1)}, u32[]{:S(2)}, u32[]{:S(2)}) collective-permute-start(bf16[256,12,128]{0,2,1:T(8,128)(2,1)} %fusion.24), channel_id=1, source_target_pairs={{2,0},{3,1},{4,2},{5,3},{6,4},{7,5},{8,6},{9,7},{10,8},{11,9},{12,... | collective-permute-start | bytes 2359304 | tf_op jit(solution)/shard_map/ppermute | solution.py:20
  183.7 0.9 fusion.23
  184.6 1.2 copy.229
  185.8 25.6 %collective-permute-done.13 = bf16[256,12,128]{0,2,1:T(8,128)(2,1)} collective-permute-done((bf16[256,12,128]{0,2,1:T(8,128)(2,1)}, bf16[256,12,128]{0,2,1:T(8,128)(2,1)}, u32[]{:S(2)}, u32[]{:S(2)}) %collective-permute-start.13) | collective-permute-done | bytes 786464 | tf_op jit(solution)/shard_map/ppermute | solution.py:20
  211.3 2.3 %collective-permute-done.15 = bf16[256,12,128]{0,2,1:T(8,128)(2,1)} collective-permute-done((bf16[256,12,128]{0,2,1:T(8,128)(2,1)}, bf16[256,12,128]{0,2,1:T(8,128)(2,1)}, u32[]{:S(2)}, u32[]{:S(2)}) %collective-permute-start.15) | collective-permute-done | bytes 786464 | tf_op jit(solution)/shard_map/ppermute | solution.py:20
  213.6 2.8 %fusion.28 = bf16[256,12,128]{0,2,1:T(8,128)(2,1)S(1)} fusion(f32[256,12,128]{0,2,1:T(8,128)} %collective-permute-done.9, bf16[256,12,128]{0,2,1:T(8,128)(2,1)} %collective-permute-done.15, bf16[256,12,128]{0,2,1:T(8,128)(2,1)} %collective-permute-done.13, f32[12,256,128]{1,2,0:T(8,128)} %fusion.90), kind=kLoop, calls=%fused_computation.61 | loop fusion | flops 2752512 | bytes 5505024 | tf_op jit(solution)/shard_map/convert_element_type | solution.py:184
  216.5 1.2 copy.228
  (174 shorter events, 20.4 us)
Async XLA Ops:
  0.6 10.6 %copy-start.20 = (bf16[256,1536]{1,0:T(8,128)(2,1)S(1)}, bf16[256,1536]{1,0:T(8,128)(2,1)}, u32[]{:S(2)}) copy-start(bf16[256,1536]{1,0:T(8,128)(2,1)} %param.18) | copy-start | bytes 2359300
  0.6 10.3 %copy-start.19 = (bf16[256,1536]{1,0:T(8,128)(2,1)S(1)}, bf16[256,1536]{1,0:T(8,128)(2,1)}, u32[]{:S(2)}) copy-start(bf16[256,1536]{1,0:T(8,128)(2,1)} %param.15) | copy-start | bytes 2359300
  1.5 10.0 %copy-start.49 = (bf16[4,30,4]{2,1,0:T(8,128)(2,1)S(1)}, bf16[4,30,4]{2,1,0:T(8,128)(2,1)}, u32[]{:S(2)}) copy-start(bf16[4,30,4]{2,1,0:T(8,128)(2,1)} %constant.219) | copy-start | bytes 2884
  1.5 10.2 %copy-start.46 = (pred[4,4]{0,1:T(4,128)(4,1)S(1)}, pred[4,4]{0,1:T(4,128)(4,1)}, u32[]{:S(2)}) copy-start(pred[4,4]{0,1:T(4,128)(4,1)} %constant.54.clone) | copy-start | bytes 52
  4.2 17.3 %collective-permute-start.4 = (bf16[528,1536]{1,0:T(8,128)(2,1)}, bf16[528,1536]{1,0:T(8,128)(2,1)}, u32[]{:S(2)}, u32[]{:S(2)}) collective-permute-start(bf16[528,1536]{1,0:T(8,128)(2,1)} %fusion.11), channel_id=1, source_target_pairs={{0,1},{1,0},{2,3},{3,2},{4,5},{5,4},{6,7},{7,6},{8,9},{9,8},{10,11... | collective-permute-start | bytes 4866056 | tf_op jit(solution)/shard_map/ppermute | solution.py:25
  4.2 73.9 %collective-permute-start.2 = (bf16[528,1536]{1,0:T(8,128)(2,1)}, bf16[528,1536]{1,0:T(8,128)(2,1)}, u32[]{:S(2)}, u32[]{:S(2)}) collective-permute-start(bf16[528,1536]{1,0:T(8,128)(2,1)} %fusion.11), channel_id=1, source_target_pairs={{0,2},{1,3},{2,4},{3,5},{4,6},{5,7},{6,8},{7,9},{8,10},{9,11},{10,... | collective-permute-start | bytes 4866056 | tf_op jit(solution)/shard_map/ppermute | solution.py:20
  7.6 76.9 %collective-permute-start = (bf16[528,1536]{1,0:T(8,128)(2,1)}, bf16[528,1536]{1,0:T(8,128)(2,1)}, u32[]{:S(2)}, u32[]{:S(2)}) collective-permute-start(bf16[528,1536]{1,0:T(8,128)(2,1)} %fusion.11), channel_id=1, source_target_pairs={{2,0},{3,1},{4,2},{5,3},{6,4},{7,5},{8,6},{9,7},{10,8},{11,9},{12,... | collective-permute-start | bytes 4866056 | tf_op jit(solution)/shard_map/ppermute | solution.py:20
  11.5 4.2 %copy-start.25 = (bf16[256,1536]{0,1:T(8,128)(2,1)}, bf16[256,1536]{0,1:T(8,128)(2,1)S(1)}, u32[]{:S(2)}) copy-start(bf16[256,1536]{0,1:T(8,128)(2,1)S(1)} %copy.202) | copy-start | bytes 2359300
  15.0 5.3 %copy-start.35 = (bf16[256,1536]{0,1:T(8,128)(2,1)}, bf16[256,1536]{0,1:T(8,128)(2,1)S(1)}, u32[]{:S(2)}) copy-start(bf16[256,1536]{0,1:T(8,128)(2,1)S(1)} %copy.181) | copy-start | bytes 2359300
  15.7 1.7 copy-start
  20.3 5.8 %copy-start.41 = (bf16[4,30,4]{2,1,0:T(8,128)(2,1)S(1)}, bf16[4,30,4]{2,1,0:T(8,128)(2,1)}, u32[]{:S(2)}) copy-start(bf16[4,30,4]{2,1,0:T(8,128)(2,1)} %constant.223) | copy-start | bytes 2884
  20.3 5.8 %copy-start.42 = (bf16[4,30,4]{2,1,0:T(8,128)(2,1)S(1)}, bf16[4,30,4]{2,1,0:T(8,128)(2,1)}, u32[]{:S(2)}) copy-start(bf16[4,30,4]{2,1,0:T(8,128)(2,1)} %constant.222) | copy-start | bytes 2884
  21.5 57.4 %copy-start.48 = (bf16[4,30,4]{2,1,0:T(8,128)(2,1)S(1)}, bf16[4,30,4]{2,1,0:T(8,128)(2,1)}, u32[]{:S(2)}) copy-start(bf16[4,30,4]{2,1,0:T(8,128)(2,1)} %constant.221) | copy-start | bytes 2884
  25.3 69.8 %copy-start.10 = (bf16[256,1536]{0,1:T(8,128)(2,1)}, bf16[256,1536]{0,1:T(8,128)(2,1)S(1)}, u32[]{:S(2)}) copy-start(bf16[256,1536]{0,1:T(8,128)(2,1)S(1)} %copy.288) | copy-start | bytes 2359300
  83.0 7.4 %copy-start.47 = (bf16[4,30,4]{2,1,0:T(8,128)(2,1)S(1)}, bf16[4,30,4]{2,1,0:T(8,128)(2,1)}, u32[]{:S(2)}) copy-start(bf16[4,30,4]{2,1,0:T(8,128)(2,1)} %constant.220) | copy-start | bytes 2884
  84.5 23.9 %copy-start.12 = (bf16[256,1536]{0,1:T(8,128)(2,1)}, bf16[256,1536]{0,1:T(8,128)(2,1)S(1)}, u32[]{:S(2)}) copy-start(bf16[256,1536]{0,1:T(8,128)(2,1)S(1)} %copy.286) | copy-start | bytes 2359300
  95.0 1.4 copy-start.36
  95.0 23.6 %collective-permute-start.6 = (bf16[528,1536]{1,0:T(8,128)(2,1)S(1)}, bf16[528,1536]{1,0:T(8,128)(2,1)S(1)}, u32[]{:S(2)}, u32[]{:S(2)}) collective-permute-start(bf16[528,1536]{1,0:T(8,128)(2,1)S(1)} %broadcast_select_fusion), channel_id=1, source_target_pairs={{0,1},{1,0},{2,3},{3,2},{4,5},{5,4},{6,7},{7,6},{8,9},{9,8},{10,11... | collective-permute-start | bytes 4866056 | tf_op jit(solution)/shard_map/ppermute | solution.py:25
  95.8 3.5 %copy-start.4 = (f32[12,256,256]{1,2,0:T(8,128)}, f32[12,256,256]{1,2,0:T(8,128)S(1)}, u32[]{:S(2)}) copy-start(f32[12,256,256]{1,2,0:T(8,128)S(1)} %get-tuple-element.69) | copy-start | bytes 9437188
  96.3 3.5 %copy-start.14 = (bf16[256,1536]{0,1:T(8,128)(2,1)S(1)}, bf16[256,1536]{0,1:T(8,128)(2,1)}, u32[]{:S(2)}) copy-start(bf16[256,1536]{0,1:T(8,128)(2,1)} %copy.284) | copy-start | bytes 2359300
  99.3 1.4 copy-start.31
  99.9 28.4 %collective-permute-start.5 = (f32[3,12,256]{2,1,0:T(8,128)}, f32[3,12,256]{2,1,0:T(8,128)}, u32[]{:S(2)}, u32[]{:S(2)}) collective-permute-start(f32[3,12,256]{2,1,0:T(8,128)} %pad_maximum_fusion.2), channel_id=1, source_target_pairs={{0,1},{1,0},{2,3},{3,2},{4,5},{5,4},{6,7},{7,6},{8,9},{9,8},{10,11... | collective-permute-start | bytes 110600 | tf_op jit(solution)/shard_map/ppermute | solution.py:25
  100.6 3.0 %copy-start.2 = (f32[12,256,256]{1,2,0:T(8,128)}, f32[12,256,256]{1,2,0:T(8,128)S(1)}, u32[]{:S(2)}) copy-start(f32[12,256,256]{1,2,0:T(8,128)S(1)} %get-tuple-element.63) | copy-start | bytes 9437188
  103.6 5.5 %copy-start.29 = (bf16[256,1536]{0,1:T(8,128)(2,1)S(1)}, bf16[256,1536]{0,1:T(8,128)(2,1)}, u32[]{:S(2)}) copy-start(bf16[256,1536]{0,1:T(8,128)(2,1)} %copy.287) | copy-start | bytes 2359300
  103.6 10.7 %collective-permute-start.1 = (f32[3,12,256]{2,1,0:T(8,128)S(1)}, f32[3,12,256]{2,1,0:T(8,128)S(1)}, u32[]{:S(2)}, u32[]{:S(2)}) collective-permute-start(f32[3,12,256]{2,1,0:T(8,128)S(1)} %pad_maximum_fusion), channel_id=1, source_target_pairs={{0,2},{1,3},{2,4},{3,5},{4,6},{5,7},{6,8},{7,9},{8,10},{9,11},{10,... | collective-permute-start | bytes 110600 | tf_op jit(solution)/shard_map/ppermute | solution.py:20
  109.1 2.9 %copy-start.6 = (f32[12,256,256]{1,2,0:T(8,128)}, f32[12,256,256]{1,2,0:T(8,128)S(1)}, u32[]{:S(2)}) copy-start(f32[12,256,256]{1,2,0:T(8,128)S(1)} %get-tuple-element.66) | copy-start | bytes 9437188
  112.0 6.0 %collective-permute-start.3 = (f32[3,12,256]{2,1,0:T(8,128)S(1)}, f32[3,12,256]{2,1,0:T(8,128)S(1)}, u32[]{:S(2)}, u32[]{:S(2)}) collective-permute-start(f32[3,12,256]{2,1,0:T(8,128)S(1)} %pad_maximum_fusion.1), channel_id=1, source_target_pairs={{2,0},{3,1},{4,2},{5,3},{6,4},{7,5},{8,6},{9,7},{10,8},{11,9},{12,... | collective-permute-start | bytes 110600 | tf_op jit(solution)/shard_map/ppermute | solution.py:20
  114.4 18.3 %copy-start.38 = (f32[3,12,256]{2,1,0:T(8,128)}, f32[3,12,256]{2,1,0:T(8,128)S(1)}, u32[]{:S(2)}) copy-start(f32[3,12,256]{2,1,0:T(8,128)S(1)} %collective-permute-done.1) | copy-start | bytes 110596
  118.0 4.9 %copy-start.39 = (f32[3,12,256]{2,1,0:T(8,128)}, f32[3,12,256]{2,1,0:T(8,128)S(1)}, u32[]{:S(2)}) copy-start(f32[3,12,256]{2,1,0:T(8,128)S(1)} %collective-permute-done.3) | copy-start | bytes 110596
  118.6 1.2 copy-start.34
  123.6 1.4 copy-start.37
  125.0 3.3 %copy-start.43 = (f32[5,12,256]{2,1,0:T(8,128)S(1)}, f32[5,12,256]{2,1,0:T(8,128)}, u32[]{:S(2)}) copy-start(f32[5,12,256]{2,1,0:T(8,128)} %get-tuple-element.43) | copy-start | bytes 184324
  125.0 3.3 %copy-start.45 = (f32[5,12,256]{2,1,0:T(8,128)S(1)}, f32[5,12,256]{2,1,0:T(8,128)}, u32[]{:S(2)}) copy-start(f32[5,12,256]{2,1,0:T(8,128)} %get-tuple-element.44) | copy-start | bytes 184324
  125.0 7.7 %copy-start.40 = (f32[3,12,256]{2,1,0:T(8,128)S(1)}, f32[3,12,256]{2,1,0:T(8,128)}, u32[]{:S(2)}) copy-start(f32[3,12,256]{2,1,0:T(8,128)} %copy-done.39) | copy-start | bytes 110596
  125.0 7.7 %copy-start.44 = (f32[5,12,256]{2,1,0:T(8,128)S(1)}, f32[5,12,256]{2,1,0:T(8,128)}, u32[]{:S(2)}) copy-start(f32[5,12,256]{2,1,0:T(8,128)} %get-tuple-element.45) | copy-start | bytes 184324
  125.0 19.1 %copy-start.1 = (f32[12,256,256]{1,2,0:T(8,128)S(1)}, f32[12,256,256]{1,2,0:T(8,128)}, u32[]{:S(2)}) copy-start(f32[12,256,256]{1,2,0:T(8,128)} %copy-done) | copy-start | bytes 9437188
  125.0 19.1 %copy-start.26 = (bf16[256,1536]{0,1:T(8,128)(2,1)S(1)}, bf16[256,1536]{0,1:T(8,128)(2,1)}, u32[]{:S(2)}) copy-start(bf16[256,1536]{0,1:T(8,128)(2,1)} %copy-done.25) | copy-start | bytes 2359300
  126.3 6.3 %collective-permute-start.7 = (f32[3,12,256]{2,1,0:T(8,128)S(1)}, f32[3,12,256]{2,1,0:T(8,128)S(1)}, u32[]{:S(2)}, u32[]{:S(2)}) collective-permute-start(f32[3,12,256]{2,1,0:T(8,128)S(1)} %pad_maximum_fusion.3), channel_id=1, source_target_pairs={{1,2},{2,1},{3,4},{4,3},{5,6},{6,5},{7,8},{8,7},{9,10},{10,9},{11,... | collective-permute-start | bytes 110600 | tf_op jit(solution)/shard_map/ppermute | solution.py:35
  133.4 11.4 %copy-start.21 = (f32[12,256,256]{1,2,0:T(8,128)S(1)}, f32[12,256,256]{1,2,0:T(8,128)}, u32[]{:S(2)}) copy-start(f32[12,256,256]{1,2,0:T(8,128)} %get-tuple-element.61) | copy-start | bytes 9437188
  134.4 14.7 %collective-permute-start.14 = (f32[2,12,256]{2,1,0:T(8,128)S(1)}, f32[2,12,256]{2,1,0:T(8,128)S(1)}, u32[]{:S(2)}, u32[]{:S(2)}) collective-permute-start(f32[2,12,256]{2,1,0:T(8,128)S(1)} %pad_maximum_fusion.4), channel_id=1, source_target_pairs={{0,2},{1,3},{2,4},{3,5},{4,6},{5,7},{6,8},{7,9},{8,10},{9,11},{10,... | collective-permute-start | bytes 73736 | tf_op jit(solution)/shard_map/ppermute | solution.py:20
  137.4 19.1 %collective-permute-start.11 = (f32[2,12,256]{2,1,0:T(8,128)S(1)}, f32[2,12,256]{2,1,0:T(8,128)S(1)}, u32[]{:S(2)}, u32[]{:S(2)}) collective-permute-start(f32[2,12,256]{2,1,0:T(8,128)S(1)} %pad_maximum_fusion.4), channel_id=1, source_target_pairs={{1,2},{2,1},{3,4},{4,3},{5,6},{6,5},{7,8},{8,7},{9,10},{10,9},{11,... | collective-permute-start | bytes 73736 | tf_op jit(solution)/shard_map/ppermute | solution.py:35
  139.4 10.6 %collective-permute-start.10 = (f32[2,12,256]{2,1,0:T(8,128)S(1)}, f32[2,12,256]{2,1,0:T(8,128)S(1)}, u32[]{:S(2)}, u32[]{:S(2)}) collective-permute-start(f32[2,12,256]{2,1,0:T(8,128)S(1)} %pad_maximum_fusion.4), channel_id=1, source_target_pairs={{2,0},{3,1},{4,2},{5,3},{6,4},{7,5},{8,6},{9,7},{10,8},{11,9},{12,... | collective-permute-start | bytes 73736 | tf_op jit(solution)/shard_map/ppermute | solution.py:20
  143.1 8.9 %collective-permute-start.8 = (f32[2,12,256]{2,1,0:T(8,128)S(1)}, f32[2,12,256]{2,1,0:T(8,128)S(1)}, u32[]{:S(2)}, u32[]{:S(2)}) collective-permute-start(f32[2,12,256]{2,1,0:T(8,128)S(1)} %pad_maximum_fusion.4), channel_id=1, source_target_pairs={{0,1},{1,0},{2,3},{3,2},{4,5},{5,4},{6,7},{7,6},{8,9},{9,8},{10,11... | collective-permute-start | bytes 73736 | tf_op jit(solution)/shard_map/ppermute | solution.py:25
  145.8 3.4 %copy-start.7 = (f32[12,256,256]{1,2,0:T(8,128)S(1)}, f32[12,256,256]{1,2,0:T(8,128)}, u32[]{:S(2)}) copy-start(f32[12,256,256]{1,2,0:T(8,128)} %copy-done.6) | copy-start | bytes 9437188
  145.8 3.4 %copy-start.30 = (bf16[256,1536]{0,1:T(8,128)(2,1)S(1)}, bf16[256,1536]{0,1:T(8,128)(2,1)}, u32[]{:S(2)}) copy-start(bf16[256,1536]{0,1:T(8,128)(2,1)} %copy.287) | copy-start | bytes 2359300
  149.1 1.9 copy-start.3
  149.1 2.1 copy-start.32
  150.0 2.5 %copy-start.5 = (f32[12,256,256]{1,2,0:T(8,128)S(1)}, f32[12,256,256]{1,2,0:T(8,128)}, u32[]{:S(2)}) copy-start(f32[12,256,256]{1,2,0:T(8,128)} %copy-done.4) | copy-start | bytes 9437188
  150.0 2.6 %copy-start.28 = (bf16[256,1536]{0,1:T(8,128)(2,1)S(1)}, bf16[256,1536]{0,1:T(8,128)(2,1)}, u32[]{:S(2)}) copy-start(bf16[256,1536]{0,1:T(8,128)(2,1)} %copy.289) | copy-start | bytes 2359300
  152.0 2.1 copy-start.23
  157.4 2.5 %copy-start.24 = (f32[12,256,256]{1,2,0:T(8,128)S(1)}, f32[12,256,256]{1,2,0:T(8,128)}, u32[]{:S(2)}) copy-start(f32[12,256,256]{1,2,0:T(8,128)} %get-tuple-element.67) | copy-start | bytes 9437188
  159.0 12.2 %collective-permute-start.12 = (f32[256,12,128]{0,2,1:T(8,128)}, f32[256,12,128]{0,2,1:T(8,128)}, u32[]{:S(2)}, u32[]{:S(2)}) collective-permute-start(f32[256,12,128]{0,2,1:T(8,128)} %multiply_bitcast_fusion), channel_id=1, source_target_pairs={{0,1},{1,0},{2,3},{3,2},{4,5},{5,4},{6,7},{7,6},{8,9},{9,8},{10,11... | collective-permute-start | bytes 4718600 | tf_op jit(solution)/shard_map/ppermute | solution.py:25
  159.0 26.8 %collective-permute-start.9 = (f32[256,12,128]{0,2,1:T(8,128)}, f32[256,12,128]{0,2,1:T(8,128)}, u32[]{:S(2)}, u32[]{:S(2)}) collective-permute-start(f32[256,12,128]{0,2,1:T(8,128)} %multiply_bitcast_fusion.1), channel_id=1, source_target_pairs={{0,1},{1,0},{2,3},{3,2},{4,5},{5,4},{6,7},{7,6},{8,9},{9,8},{10,11... | collective-permute-start | bytes 4718600 | tf_op jit(solution)/shard_map/ppermute | solution.py:25
  159.9 2.0 copy-start.11
  161.9 2.5 %copy-start.22 = (f32[12,256,256]{1,2,0:T(8,128)S(1)}, f32[12,256,256]{1,2,0:T(8,128)}, u32[]{:S(2)}) copy-start(f32[12,256,256]{1,2,0:T(8,128)} %get-tuple-element.64) | copy-start | bytes 9437188
  165.3 1.8 copy-start.9
  165.3 1.8 copy-start.15
  171.2 6.5 %copy-start.8 = (bf16[12,256,256]{1,2,0:T(8,128)(2,1)S(1)}, bf16[12,256,256]{1,2,0:T(8,128)(2,1)}, u32[]{:S(2)}) copy-start(bf16[12,256,256]{1,2,0:T(8,128)(2,1)} %multiply_convert_fusion) | copy-start | bytes 4718596
  174.6 8.5 %copy-start.13 = (bf16[256,1536]{0,1:T(8,128)(2,1)S(1)}, bf16[256,1536]{0,1:T(8,128)(2,1)}, u32[]{:S(2)}) copy-start(bf16[256,1536]{0,1:T(8,128)(2,1)} %copy-done.12) | copy-start | bytes 2359300
  174.6 36.8 %collective-permute-start.13 = (bf16[256,12,128]{0,2,1:T(8,128)(2,1)}, bf16[256,12,128]{0,2,1:T(8,128)(2,1)}, u32[]{:S(2)}, u32[]{:S(2)}) collective-permute-start(bf16[256,12,128]{0,2,1:T(8,128)(2,1)} %fusion.25), channel_id=1, source_target_pairs={{0,2},{1,3},{2,4},{3,5},{4,6},{5,7},{6,8},{7,9},{8,10},{9,11},{10,... | collective-permute-start | bytes 2359304 | tf_op jit(solution)/shard_map/ppermute | solution.py:20
  177.7 6.0 %copy-start.18 = (f32[12,128,256]{2,1,0:T(8,128)S(1)}, f32[12,128,256]{2,1,0:T(8,128)}, u32[]{:S(2)}) copy-start(f32[12,128,256]{2,1,0:T(8,128)} %fusion.88) | copy-start | bytes 4718596
  179.0 4.7 %copy-start.16 = (f32[12,256,128]{1,2,0:T(8,128)S(1)}, f32[12,256,128]{1,2,0:T(8,128)}, u32[]{:S(2)}) copy-start(f32[12,256,128]{1,2,0:T(8,128)} %fusion.86) | copy-start | bytes 4718596
  179.0 4.7 %copy-start.17 = (f32[12,128,256]{2,1,0:T(8,128)S(1)}, f32[12,128,256]{2,1,0:T(8,128)}, u32[]{:S(2)}) copy-start(f32[12,128,256]{2,1,0:T(8,128)} %fusion.89) | copy-start | bytes 4718596
  179.0 34.6 %collective-permute-start.15 = (bf16[256,12,128]{0,2,1:T(8,128)(2,1)}, bf16[256,12,128]{0,2,1:T(8,128)(2,1)}, u32[]{:S(2)}, u32[]{:S(2)}) collective-permute-start(bf16[256,12,128]{0,2,1:T(8,128)(2,1)} %fusion.24), channel_id=1, source_target_pairs={{2,0},{3,1},{4,2},{5,3},{6,4},{7,5},{8,6},{9,7},{10,8},{11,9},{12,... | collective-permute-start | bytes 2359304 | tf_op jit(solution)/shard_map/ppermute | solution.py:20
  (2 other events, 2.3 us)

commit v3 on v2

v3 whole, which is shorter than its diff:
```python
import jax
import jax.numpy as jnp
import numpy as np
from jax import lax
from jax.sharding import PartitionSpec as P

HEADS = 12
HDIM = 128
BLOCK = 64
REACH = 2
FRAMES = 2
BANDS = 2
NEG = -1e30
LIST_ROWS = 16


def permute(value, rule):
    count = lax.axis_size("tm")
    pairs = []
    for source in range(count):
        target = rule(source)
        if 0 <= target < count:
            pairs.append((source, target))
    return lax.ppermute(value, "tm", pairs)


def swap_cores(value):
    return permute(value, lambda s: s ^ 1)


def down_even(value):
    return permute(value, lambda s: s - 2 if s % 2 == 0 else s + 2)


def up_even(value):
    return permute(value, lambda s: s + 2 if s % 2 == 0 else s - 2)


def pick_table(offset):
    blocks = FRAMES * BANDS
    slot = REACH - offset
    table = np.zeros((blocks, 30, blocks), np.float32)
    own = np.zeros((blocks, blocks), bool)
    if abs(offset) <= REACH:
        for qb in range(blocks):
            for kb in range(blocks):
                cand = (slot * FRAMES + kb // BANDS) * 3 + kb % BANDS - qb % BANDS + 1
                table[qb, cand, kb] = 1.0
                own[qb, kb] = offset == 0 and qb == kb
    return table, own


def parity_tables(even, even_offsets, odd_offsets):
    tables, owns = [], []
    for off_e, off_o in zip(even_offsets, odd_offsets):
        t_e, o_e = pick_table(off_e)
        t_o, o_o = pick_table(off_o)
        tables.append(jnp.where(even, jnp.asarray(t_e), jnp.asarray(t_o)))
        owns.append(jnp.where(even, jnp.asarray(o_e), jnp.asarray(o_o)))
    return jnp.concatenate(tables, axis=2), jnp.concatenate(owns, axis=1)


def local(queries, keys, values, grad_out, block_list):
    groups = lax.axis_size("tm")
    here = lax.axis_index("tm")
    even = here % 2 == 0
    up = jnp.where(even, 1, -1)
    scaling = HDIM ** (-0.5)
    tok, width = queries.shape
    blocks = FRAMES * BANDS
    cands = block_list.shape[1]

    flags = (block_list > 0).astype(jnp.bfloat16).reshape(1, blocks * cands)
    flags = jnp.pad(flags, ((0, LIST_ROWS - 1), (0, width - blocks * cands)))
    pack = jnp.concatenate([queries, grad_out, flags], axis=0)

    far_data = down_even(pack)
    near_data = up_even(pack)
    partner_keys, partner_values = swap_cores((keys, values))

    key_own = keys.reshape(tok, HEADS, HDIM)
    value_own = values.reshape(tok, HEADS, HDIM)
    key_both = jnp.concatenate([keys, partner_keys], axis=0).reshape(2 * tok, HEADS, HDIM)
    value_both = jnp.concatenate([values, partner_values], axis=0).reshape(2 * tok, HEADS, HDIM)

    slots = {
        "far": (far_data, 2 * up, "both", (2, 1), (-2, -1)),
        "near": (near_data, -2 * up, "own", (-2,), (2,)),
        "own": (pack, 0, "own_both", (0, -1), (0, 1)),
    }

    parts = {}
    stats_out = {}
    for name in ("own", "far", "near"):
        data, q_off, key_set, offs_e, offs_o = slots[name]
        if key_set == "own":
            key_h, value_h = key_own, value_own
        else:
            key_h, value_h = key_both, value_both
        nkb = key_h.shape[0] // BLOCK
        q_h = data[:tok].reshape(tok, HEADS, HDIM)
        g_h = data[tok : 2 * tok].reshape(tok, HEADS, HDIM)
        list_rows = data[2 * tok, : blocks * cands].astype(jnp.float32).reshape(blocks, cands)
        source = here + q_off
        valid = (source >= 0) & (source < groups)
        table, own = parity_tables(even, offs_e, offs_o)
        chosen = jnp.einsum("qc,qck->qk", list_rows, table) > 0
        mask = ((chosen & valid) | own)[None, :, None, :, None]
        shape5 = (HEADS, blocks, BLOCK, nkb, BLOCK)
        scores = (
            jnp.einsum("qhd,khd->hqk", q_h, key_h, preferred_element_type=jnp.float32) * scaling
        ).reshape(shape5)
        grad_probs = jnp.einsum(
            "qhd,khd->hqk", g_h, value_h, preferred_element_type=jnp.float32
        ).reshape(shape5)
        masked = jnp.where(mask, scores, NEG)
        row_max = jnp.max(masked, axis=(3, 4))
        expd = jnp.where(mask, jnp.exp(masked - row_max[:, :, :, None, None]), 0.0)
        row_sum = jnp.sum(expd, axis=(3, 4))
        row_dot = jnp.sum(expd * grad_probs, axis=(3, 4))
        parts[name] = (q_h, g_h, key_h, mask, scores, grad_probs)
        stats_out[name] = jnp.stack([row_max, row_sum, row_dot]).reshape(3, HEADS, tok)

    stats_in = [
        (stats_out["own"], 0),
        (up_even(stats_out["far"]), -2 * up),
        (down_even(stats_out["near"]), 2 * up),
    ]
    maxes, sums, dots = [], [], []
    for stats, offset in stats_in:
        source = here + offset
        valid = (source >= 0) & (source < groups)
        maxes.append(jnp.where(valid, stats[0], NEG))
        sums.append(jnp.where(valid, stats[1], 0.0))
        dots.append(jnp.where(valid, stats[2], 0.0))
    maxes, sums, dots = jnp.stack(maxes), jnp.stack(sums), jnp.stack(dots)
    top = jnp.max(maxes, axis=0)
    scale = jnp.exp(maxes - top[None])
    total = jnp.sum(sums * scale, axis=0)
    log_total = top + jnp.log(total)
    deltas = jnp.sum(dots * scale, axis=0) / total
    final = jnp.stack([log_total, deltas])
    finals = {"own": final, "far": down_even(final), "near": up_even(final)}

    def backward(name, got):
        q_h, g_h, key_h, mask, scores, grad_probs = parts[name]
        lse = got[0].reshape(HEADS, blocks, BLOCK)[:, :, :, None, None]
        dlt = got[1].reshape(HEADS, blocks, BLOCK)[:, :, :, None, None]
        weights = jnp.where(mask, jnp.exp(scores - lse), 0.0)
        nk = key_h.shape[0]
        weights_low = weights.astype(jnp.bfloat16).reshape(HEADS, tok, nk)
        grad_scores = (weights * (grad_probs - dlt)).astype(jnp.bfloat16).reshape(HEADS, tok, nk)
        q_part = jnp.einsum(
            "hqk,khd->qhd", grad_scores, key_h, preferred_element_type=jnp.float32
        ) * scaling
        return q_h, g_h, weights_low, grad_scores, q_part

    far_b = backward("far", finals["far"])
    near_b = backward("near", finals["near"])
    far_send, near_send, far_b, near_b, own_final = lax.optimization_barrier(
        (far_b[4].astype(jnp.bfloat16), near_b[4].astype(jnp.bfloat16), far_b, near_b, final)
    )
    from_far = up_even(far_send)
    from_near = down_even(near_send)
    own_b = backward("own", own_final)

    def key_value(b):
        q_h, g_h, weights_low, grad_scores, _ = b
        kg = jnp.einsum("hqk,qhd->khd", grad_scores, q_h, preferred_element_type=jnp.float32)
        vg = jnp.einsum("hqk,qhd->khd", weights_low, g_h, preferred_element_type=jnp.float32)
        return kg * scaling, vg

    kg_far, vg_far = key_value(far_b)
    kg_own, vg_own = key_value(own_b)
    kg_near, vg_near = key_value(near_b)
    partner_kg = kg_far[tok:] + kg_own[tok:]
    partner_vg = vg_far[tok:] + vg_own[tok:]
    back_kg, back_vg = swap_cores((partner_kg, partner_vg))
    key_grad = kg_far[:tok] + kg_own[:tok] + kg_near + back_kg
    value_grad = vg_far[:tok] + vg_own[:tok] + vg_near + back_vg
    query_grad = (
        own_b[4] + from_far.astype(jnp.float32) + from_near.astype(jnp.float32)
    )
    return (
        query_grad.reshape(tok, width).astype(jnp.bfloat16),
        key_grad.reshape(tok, width).astype(jnp.bfloat16),
        value_grad.reshape(tok, width).astype(jnp.bfloat16),
    )


def solution(mesh):
    placed = (
        P(("group", "tm"), None),
        P(("group", "tm"), None),
        P(("group", "tm"), None),
        P(("group", "tm"), None),
        P(("group", "tm"), None),
    )
    return jax.shard_map(
        local,
        mesh=mesh,
        in_specs=placed,
        out_specs=(P(("group", "tm"), None), P(("group", "tm"), None), P(("group", "tm"), None)),
        check_vma=False,
    )
```

time: 219 us -> 194 us (0.89)
  waiting for transfers between devices: 84.7 us -> 73.8 us
  local copies, waits for them, and re-layouts: 40.2 us -> 30.5 us
  starting transfers between devices: 33.1 us -> 27.1 us
  other arithmetic: 19.1 us -> 22.6 us
  matrix products: 39.1 us -> 35.9 us
    ppermute x16 -> x12, waiting for transfers between devices: 84.7 us -> 73.8 us  [permute(): return lax.ppermute(value, 'tm', pairs)]
    unnamed x115 -> x73, local copies, waits for them, and re-layouts: 26.9 us -> 20.3 us
    ppermute x16 -> x12, starting transfers between devices: 33.1 us -> 27.1 us  [permute(): return lax.ppermute(value, 'tm', pairs)]
    convert_element_type x6 -> x3, other arithmetic: 8.43 us -> 12.3 us  [the longest x2 7.71 us: backward(): weights_low = weights.astype(jnp.bfloat16).reshape(HEADS, tok, nk)]
    add x0 -> x2, other arithmetic: none -> 3.48 us  [the longest x1 1.92 us: local(): partner_vg = vg_far[tok:] + vg_own[tok:]]
    concatenate x0 -> x2, other arithmetic: none -> 3.29 us  [the longest x1 1.81 us: local(): jnp.concatenate([keys, partner_keys], axis=0).reshape(2 * tok, HEADS, HDIM)]
    unnamed x5 -> x1, other arithmetic: 3.23 us -> 0.01 us
    slice x3 -> x1, local copies, waits for them, and re-layouts: 5.36 us -> 2.35 us  [local(): g_h = data[tok:2 * tok].reshape(tok, HEADS, HDIM)]
  transfers between devices with their start and end apart: 16 -> 12, of which waited for: 5 -> 3; matrix products, arithmetic and copies ran while one was open for 32% -> 29% of each run, Pallas kernels for 0% -> 0%
where the time goes in v3:
time: 194 us; the launch traced here: 191 us
  waiting for transfers between devices  73.8 us (38%)
  matrix products  35.9 us (19%)
  local copies, waits for them, and re-layouts  30.5 us (16%)
  starting transfers between devices  27.1 us (14%)
  other arithmetic  22.6 us (12%)
    ppermute x12, waiting for transfers between devices, permute(): return lax.ppermute(value, 'tm', pairs)  73.8 us
    ppermute x12, starting transfers between devices, permute(): return lax.ppermute(value, 'tm', pairs)  27.1 us
    unnamed x73, local copies, waits for them, and re-layouts  20.3 us
    dot_general x3, matrix products, local(): jnp.einsum('qhd,khd->hqk', g_h, value_h, preferred_element_type=jnp.float32)  11.3 us
    convert_element_type x2, other arithmetic, backward(): weights_low = weights.astype(jnp.bfloat16).reshape(HEADS, tok, nk)  7.71 us
    dot_general x3, matrix products, key_value(): jnp.einsum('hqk,qhd->khd', weights_low, g_h, preferred_element_type=jnp.f...  7.53 us
    dot_general x3, matrix products, key_value(): jnp.einsum('hqk,qhd->khd', grad_scores, q_h, preferred_element_type=jnp.f...  6.55 us
    dot_general x3, matrix products, backward(): jnp.einsum('hqk,khd->qhd', grad_scores, key_h, preferred_element_type=jnp...  5.65 us
  transfers between devices with their start and end apart: 12, of which 3 were waited for; matrix products, arithmetic and copies ran while one was open for 29% of the time, Pallas kernels for 0%

profile of v3, /device:TPU:8, one launch (start us, length us, event | category | flops | bytes accessed | tf_op | source)
XLA Modules:
  0.0 191.2 jit_solution(9465862886598770005)
XLA Ops:
  0.7 2.4 %copy.148 = bf16[256,1536]{0,1:T(8,128)(2,1)} copy(bf16[256,1536]{1,0:T(8,128)(2,1)} %param.27) | data formatting | bytes 1572864 | tf_op args[2]
  3.1 0.7 fusion.56
  3.9 2.7 %fusion.22 = bf16[528,1536]{1,0:T(8,128)(2,1)} fusion(bf16[1,120]{1,0:T(2,128)(2,1)S(1)} %reshape.236, bf16[256,1536]{1,0:T(8,128)(2,1)} %param.28, bf16[256,1536]{1,0:T(8,128)(2,1)} %param.25), kind=kLoop, calls=%fused_computation.38 | loop fusion | flops 6488064 | bytes 3195120 | tf_op jit(solution)/shard_map/concatenate | solution.py:75
  6.6 3.5 %collective-permute-start.4 = (bf16[528,1536]{1,0:T(8,128)(2,1)}, bf16[528,1536]{1,0:T(8,128)(2,1)}, u32[]{:S(2)}, u32[]{:S(2)}) collective-permute-start(bf16[528,1536]{1,0:T(8,128)(2,1)} %fusion.22), channel_id=1, source_target_pairs={{0,2},{2,4},{3,1},{4,6},{5,3},{6,8},{7,5},{8,10},{9,7},{10,12},{11... | collective-permute-start | bytes 4866056 | tf_op jit(solution)/shard_map/ppermute | solution.py:24
  10.2 3.3 %collective-permute-start.1 = (bf16[528,1536]{1,0:T(8,128)(2,1)}, bf16[528,1536]{1,0:T(8,128)(2,1)}, u32[]{:S(2)}, u32[]{:S(2)}) collective-permute-start(bf16[528,1536]{1,0:T(8,128)(2,1)} %fusion.22), channel_id=1, source_target_pairs={{1,3},{2,0},{3,5},{4,2},{5,7},{6,4},{7,9},{8,6},{9,11},{10,8},{11,... | collective-permute-start | bytes 4866056 | tf_op jit(solution)/shard_map/ppermute | solution.py:24
  13.5 0.3 copy.138
  14.0 0.3 copy.139
  14.3 1.2 copy.160
  15.5 0.1 fusion.34
  15.8 0.2 broadcast_in_dim.95
  16.0 0.5 broadcast_in_dim.96
  16.5 1.5 pad_maximum_fusion.1
  18.0 1.8 pad_maximum_fusion
  19.8 1.3 fusion.5
  21.1 4.5 %fusion.9 = (f32[12,256]{1,0:T(8,128)S(1)}, f32[12,256]{1,0:T(8,128)S(1)}, f32[12,512,256]{2,1,0:T(8,128)}) fusion(f32[12,512,256]{2,1,0:T(8,128)S(1)} %get-tuple-element.82, f32[12,256]{1,0:T(8,128)S(1)} %get-tuple-element.81, pred[256,512]{0,1:T(8,128)(4,1)S(1)} %broadcast_in_dim.96, bf16[512,12,128]{0,2,1:T(8,128)(2,1)S(1)} %bitcast.181, ...), kind=kOutput, calls=%fused_computation.19 | convolution fusion | flops 413657088 | bytes 15110144 | tf_op jit(solution)/shard_map/qhd,khd->hqk/dot_general | solution.py:113
  25.6 54.9 %collective-permute-done.4 = bf16[528,1536]{1,0:T(8,128)(2,1)} collective-permute-done((bf16[528,1536]{1,0:T(8,128)(2,1)}, bf16[528,1536]{1,0:T(8,128)(2,1)}, u32[]{:S(2)}, u32[]{:S(2)}) %collective-permute-start.4) | collective-permute-done | bytes 1622048 | tf_op jit(solution)/shard_map/ppermute | solution.py:24
  80.5 2.4 %fusion.57 = (bf16[256,1536]{1,0:T(8,128)(2,1)}, bf16[256,1536]{1,0:T(8,128)(2,1)S(1)}) fusion(bf16[528,1536]{1,0:T(8,128)(2,1)} %collective-permute-done.4), kind=kLoop, calls=%fused_computation.115 | loop fusion | bytes 3145728 | tf_op jit(solution)/shard_map/slice | solution.py:102
  82.8 2.3 %copy.212 = bf16[256,1536]{0,1:T(8,128)(2,1)} copy(bf16[256,1536]{1,0:T(8,128)(2,1)} %get-tuple-element.55) | data formatting | bytes 1572864
  85.1 0.7 slice_reduce_fusion
  85.9 0.1 fusion.42
  86.1 0.1 broadcast_in_dim.105
  86.3 0.2 broadcast_in_dim.106
  86.5 1.2 copy.211
  87.7 2.6 %fusion.58 = (bf16[256,1536]{1,0:T(8,128)(2,1)}, bf16[256,1536]{1,0:T(8,128)(2,1)}) fusion(bf16[528,1536]{1,0:T(8,128)(2,1)} %collective-permute-done.1), kind=kLoop, calls=%fused_computation.116 | loop fusion | bytes 3145728 | tf_op jit(solution)/shard_map/slice | solution.py:101
  90.3 1.4 copy.209
  91.7 0.7 slice_reduce_fusion.1
  92.5 0.1 fusion.38
  92.8 0.9 broadcast_in_dim.98
  93.7 1.4 broadcast_in_dim.99
  95.1 2.3 %copy.210 = bf16[256,1536]{0,1:T(8,128)(2,1)} copy(bf16[256,1536]{1,0:T(8,128)(2,1)} %get-tuple-element.58) | data formatting | bytes 1572864
  97.4 1.9 %select_reduce_fusion.1 = (f32[12,256]{1,0:T(8,128)S(1)}, f32[12,256,256]{1,2,0:T(8,128)S(1)}) fusion(pred[256,256]{0,1:T(8,128)(4,1)S(1)} %broadcast_in_dim.106, bf16[256,12,128]{0,2,1:T(8,128)(2,1)} %bitcast.170, bf16[256,12,128]{0,2,1:T(8,128)(2,1)S(1)} %bitcast.164), kind=kOutput, calls=%fused_computation.33 | convolution fusion | flops 203682816 | bytes 4796416 | tf_op jit(solution)/shard_map/qhd,khd->hqk/dot_general | solution.py:111
  99.3 2.5 %fusion.18 = (f32[12,256]{1,0:T(8,128)S(1)}, f32[12,256]{1,0:T(8,128)S(1)}, f32[12,256,256]{1,2,0:T(8,128)S(1)}) fusion(f32[12,256,256]{1,2,0:T(8,128)S(1)} %get-tuple-element.79, f32[12,256]{1,0:T(8,128)S(1)} %get-tuple-element.78, pred[256,256]{0,1:T(8,128)(4,1)S(1)} %broadcast_in_dim.106, bf16[256,12,128]{0,2,1:T(8,128)(2,1)S(1)} %bitcast.178, ...), kind=kOutput, calls=%fused_computation.35 | convolution fusion | flops 206825472 | bytes 7966720 | tf_op jit(solution)/shard_map/qhd,khd->hqk/dot_general | solution.py:113
  101.8 4.5 %collective-permute-start.5 = (f32[3,12,256]{2,1,0:T(8,128)S(1)}, f32[3,12,256]{2,1,0:T(8,128)S(1)}, u32[]{:S(2)}, u32[]{:S(2)}) collective-permute-start(f32[3,12,256]{2,1,0:T(8,128)S(1)} %pad_maximum_fusion.3), channel_id=1, source_target_pairs={{1,3},{2,0},{3,5},{4,2},{5,7},{6,4},{7,9},{8,6},{9,11},{10,8},{11,... | collective-permute-start | bytes 110600 | tf_op jit(solution)/shard_map/ppermute | solution.py:24
  106.3 1.3 select_reduce_fusion
  107.6 0.4 copy-done.21
  107.9 4.4 %fusion.8 = (f32[12,256]{1,0:T(8,128)S(1)}, f32[12,256]{1,0:T(8,128)S(1)}, f32[12,256,512]{1,2,0:T(8,128)}) fusion(f32[12,256,512]{1,2,0:T(8,128)S(1)} %get-tuple-element.76, f32[12,256]{1,0:T(8,128)S(1)} %get-tuple-element.75, pred[256,512]{0,1:T(8,128)(4,1)S(1)} %broadcast_in_dim.99, bf16[256,12,128]{0,2,1:T(8,128)(2,1)S(1)} %bitcast.174, ...), kind=kOutput, calls=%fused_computation.18 | convolution fusion | flops 413657088 | bytes 15110144 | tf_op jit(solution)/shard_map/qhd,khd->hqk/dot_general | solution.py:113
  112.3 2.0 %collective-permute-start.3 = (f32[3,12,256]{2,1,0:T(8,128)S(1)}, f32[3,12,256]{2,1,0:T(8,128)S(1)}, u32[]{:S(2)}, u32[]{:S(2)}) collective-permute-start(f32[3,12,256]{2,1,0:T(8,128)S(1)} %pad_maximum_fusion.2), channel_id=1, source_target_pairs={{0,2},{2,4},{3,1},{4,6},{5,3},{6,8},{7,5},{8,10},{9,7},{10,12},{11... | collective-permute-start | bytes 110600 | tf_op jit(solution)/shard_map/ppermute | solution.py:24
  114.4 4.8 %collective-permute-done.3 = f32[3,12,256]{2,1,0:T(8,128)S(1)} collective-permute-done((f32[3,12,256]{2,1,0:T(8,128)S(1)}, f32[3,12,256]{2,1,0:T(8,128)S(1)}, u32[]{:S(2)}, u32[]{:S(2)}) %collective-permute-start.3) | collective-permute-done | bytes 36896 | tf_op jit(solution)/shard_map/ppermute | solution.py:24
  119.3 1.9 %collective-permute-start.7 = (f32[2,12,256]{2,1,0:T(8,128)S(1)}, f32[2,12,256]{2,1,0:T(8,128)S(1)}, u32[]{:S(2)}, u32[]{:S(2)}) collective-permute-start(f32[2,12,256]{2,1,0:T(8,128)S(1)} %pad_maximum_fusion.4), channel_id=1, source_target_pairs={{0,2},{2,4},{3,1},{4,6},{5,3},{6,8},{7,5},{8,10},{9,7},{10,12},{11... | collective-permute-start | bytes 73736 | tf_op jit(solution)/shard_map/ppermute | solution.py:24
  121.2 4.8 %collective-permute-start.6 = (f32[2,12,256]{2,1,0:T(8,128)S(1)}, f32[2,12,256]{2,1,0:T(8,128)S(1)}, u32[]{:S(2)}, u32[]{:S(2)}) collective-permute-start(f32[2,12,256]{2,1,0:T(8,128)S(1)} %pad_maximum_fusion.4), channel_id=1, source_target_pairs={{1,3},{2,0},{3,5},{4,2},{5,7},{6,4},{7,9},{8,6},{9,11},{10,8},{11,... | collective-permute-start | bytes 73736 | tf_op jit(solution)/shard_map/ppermute | solution.py:24
  126.1 2.2 %fusion.17 = (bf16[12,256,256]{1,2,0:T(8,128)(2,1)}, bf16[12,256,256]{1,2,0:T(8,128)(2,1)S(1)}) fusion(f32[12,256,256]{1,2,0:T(8,128)S(1)} %get-tuple-element.79, f32[12,256]{1,0:T(8,128)S(1)} %get-tuple-element.69, pred[256,256]{0,1:T(8,128)(4,1)S(1)} %broadcast_in_dim.106, f32[12,256,256]{1,2,0:T(8,128)S(1)} %get-tuple-element.80, ...), kind=kLoop, calls=%fused_computation.34 | loop fusion | flops 5505024 | bytes 9527296 | tf_op jit(solution)/shard_map/convert_element_type | solution.py:151
  128.2 1.3 multiply_bitcast_fusion.2
  129.5 5.6 %fusion.6 = (bf16[12,256,512]{1,2,0:T(8,128)(2,1)}, bf16[12,256,512]{1,2,0:T(8,128)(2,1)S(1)}) fusion(f32[12,256,512]{1,2,0:T(8,128)S(1)} %get-tuple-element.76, f32[12,256]{1,0:T(8,128)S(1)} %get-tuple-element.71, pred[256,512]{0,1:T(8,128)(4,1)S(1)} %broadcast_in_dim.99, f32[12,256,512]{1,2,0:T(8,128)} %get-tuple-element.77, ...), kind=kLoop, calls=%fused_computation.16 | loop fusion | flops 11010048 | bytes 19030016 | tf_op jit(solution)/shard_map/convert_element_type | solution.py:151
  135.1 1.5 multiply_bitcast_fusion.3
  136.6 3.1 %fusion.19 = f32[512,12,128]{0,2,1:T(8,128)} fusion(bf16[256,12,128]{0,2,1:T(8,128)(2,1)S(1)} %bitcast.173, f32[12,512,256]{2,1,0:T(8,128)S(1)} %bitcast.159, f32[12,256]{1,0:T(8,128)S(1)} %get-tuple-element.67, pred[256,512]{0,1:T(8,128)(4,1)S(1)} %broadcast_in_dim.96), kind=kOutput, calls=%fused_computation.37 | convolution fusion | flops 408944640 | bytes 10366976 | tf_op jit(solution)/shard_map/hqk,qhd->khd/dot_general | solution.py:170
  139.7 3.2 %collective-permute-start.8 = (bf16[256,12,128]{0,2,1:T(8,128)(2,1)}, bf16[256,12,128]{0,2,1:T(8,128)(2,1)}, u32[]{:S(2)}, u32[]{:S(2)}) collective-permute-start(bf16[256,12,128]{0,2,1:T(8,128)(2,1)} %multiply_bitcast_fusion.3), channel_id=1, source_target_pairs={{0,2},{2,4},{3,1},{4,6},{5,3},{6,8},{7,5},{8,10},{9,7},{10,12},{11... | collective-permute-start | bytes 2359304 | tf_op jit(solution)/shard_map/ppermute | solution.py:24
  142.9 3.8 %collective-permute-start.9 = (bf16[256,12,128]{0,2,1:T(8,128)(2,1)}, bf16[256,12,128]{0,2,1:T(8,128)(2,1)}, u32[]{:S(2)}, u32[]{:S(2)}) collective-permute-start(bf16[256,12,128]{0,2,1:T(8,128)(2,1)} %multiply_bitcast_fusion.2), channel_id=1, source_target_pairs={{1,3},{2,0},{3,5},{4,2},{5,7},{6,4},{7,9},{8,6},{9,11},{10,8},{11,... | collective-permute-start | bytes 2359304 | tf_op jit(solution)/shard_map/ppermute | solution.py:24
  146.7 4.5 %fusion.2 = bf16[12,256,512]{1,2,0:T(8,128)(2,1)S(1)} fusion(f32[12,512,256]{2,1,0:T(8,128)} %get-tuple-element.83, f32[12,512,256]{2,1,0:T(8,128)S(1)} %bitcast.159, f32[12,256]{1,0:T(8,128)S(1)} %get-tuple-element.68, f32[12,256]{1,0:T(8,128)S(1)} %get-tuple-element.67, pred[256,512]{0,1:T(8,128)(4,1)S(1)} %broadcast_in_dim.96), kind=kLoop, calls=%fused_computation.4 | loop fusion | flops 9437184 | bytes 15884288 | tf_op jit(solution)/shard_map/convert_element_type | solution.py:152
  151.3 1.2 multiply_bitcast_fusion
  152.5 1.2 multiply_bitcast_fusion.1
  153.6 0.5 copy-done.5
  154.1 1.6 slice_add_fusion.2
  155.7 0.8 copy-done.6
  156.5 1.2 copy-done.1
  157.7 0.2 copy-done.16
  157.9 1.1 convolution_bitcast_fusion
  159.1 1.9 %slice_add_fusion = f32[256,12,128]{0,2,1:T(8,128)} fusion(f32[512,12,128]{0,2,1:T(8,128)S(1)} %copy-done.7, f32[512,12,128]{0,2,1:T(8,128)S(1)} %convolution_bitcast_fusion), kind=kLoop, calls=%fused_computation.39 | loop fusion | flops 393216 | bytes 4718592 | tf_op jit(solution)/shard_map/add | solution.py:177
  161.0 14.0 %collective-permute-done.8 = bf16[256,12,128]{0,2,1:T(8,128)(2,1)} collective-permute-done((bf16[256,12,128]{0,2,1:T(8,128)(2,1)}, bf16[256,12,128]{0,2,1:T(8,128)(2,1)}, u32[]{:S(2)}, u32[]{:S(2)}) %collective-permute-start.8) | collective-permute-done | bytes 786464 | tf_op jit(solution)/shard_map/ppermute | solution.py:24
  175.1 2.9 %fusion.30 = bf16[256,12,128]{0,2,1:T(8,128)(2,1)} fusion(bf16[256,12,128]{0,2,1:T(8,128)(2,1)} %collective-permute-done.9, bf16[256,12,128]{0,2,1:T(8,128)(2,1)} %collective-permute-done.8, bf16[512,12,128]{0,2,1:T(8,128)(2,1)S(1)} %bitcast.163, bf16[12,256,512]{1,2,0:T(8,128)(2,1)S(1)} %fusion.2), kind=kOutput, calls=%fused_computation.53 | convolution fusion | flops 405012480 | bytes 7077888 | tf_op jit(solution)/shard_map/hqk,khd->qhd/dot_general | solution.py:153
  178.0 2.3 %copy.175 = bf16[256,1536]{1,0:T(8,128)(2,1)} copy(bf16[256,1536]{0,1:T(8,128)(2,1)} %bitcast.176) | data formatting | bytes 1572864
  180.2 4.2 %fusion.28 = bf16[256,12,128]{0,2,1:T(8,128)(2,1)} fusion(f32[256,12,128]{0,2,1:T(8,128)} %collective-permute-done.10, f32[512,12,128]{0,2,1:T(8,128)} %copy-done.5, f32[512,12,128]{0,2,1:T(8,128)} %copy-done.6, bf16[256,12,128]{0,2,1:T(8,128)(2,1)} %bitcast.171, bf16[12,256,256]{1,2,0:T(8,128)(2,1)S(1)} %get-tuple-element.20), kind=kOutput, calls=%fused_computation.48 | convolution fusion | flops 203292672 | bytes 7864320 | tf_op jit(solution)/shard_map/hqk,qhd->khd/dot_general | solution.py:169
  184.5 2.3 %copy.176 = bf16[256,1536]{1,0:T(8,128)(2,1)} copy(bf16[256,1536]{0,1:T(8,128)(2,1)} %bitcast.179) | data formatting | bytes 1572864
  186.8 3.2 %fusion.25 = bf16[256,12,128]{0,2,1:T(8,128)(2,1)S(1)} fusion(f32[256,12,128]{0,2,1:T(8,128)} %collective-permute-done.11, f32[512,12,128]{0,2,1:T(8,128)} %fusion.19, f32[512,12,128]{0,2,1:T(8,128)} %copy-done.4, bf16[256,12,128]{0,2,1:T(8,128)(2,1)} %bitcast.177, bf16[12,256,256]{1,2,0:T(8,128)(2,1)S(1)} %copy-done.12), kind=kOutput, calls=%fused_computation.43 | convolution fusion | flops 202899456 | bytes 7864320 | tf_op jit(solution)/shard_map/hqk,qhd->khd/dot_general | solution.py:170
  190.0 1.2 copy.177
  (95 shorter events, 1.0 us)
Async XLA Ops:
  0.6 13.3 %copy-start.23 = (bf16[4,30,4]{1,2,0:T(4,128)(2,1)S(1)}, bf16[4,30,4]{1,2,0:T(4,128)(2,1)}, u32[]{:S(2)}) copy-start(bf16[4,30,4]{1,2,0:T(4,128)(2,1)} %constant.143) | copy-start | bytes 2884
  0.6 13.3 %copy-start.24 = (bf16[4,30,4]{1,2,0:T(4,128)(2,1)S(1)}, bf16[4,30,4]{1,2,0:T(4,128)(2,1)}, u32[]{:S(2)}) copy-start(bf16[4,30,4]{1,2,0:T(4,128)(2,1)} %constant.144) | copy-start | bytes 2884
  0.7 13.3 %copy-start.25 = (bf16[4,30,4]{1,2,0:T(4,128)(2,1)S(1)}, bf16[4,30,4]{1,2,0:T(4,128)(2,1)}, u32[]{:S(2)}) copy-start(bf16[4,30,4]{1,2,0:T(4,128)(2,1)} %constant.146) | copy-start | bytes 2884
  0.7 13.3 %copy-start.26 = (bf16[4,30,4]{1,2,0:T(4,128)(2,1)S(1)}, bf16[4,30,4]{1,2,0:T(4,128)(2,1)}, u32[]{:S(2)}) copy-start(bf16[4,30,4]{1,2,0:T(4,128)(2,1)} %constant.145) | copy-start | bytes 2884
  0.7 13.3 %copy-start.17 = (bf16[256,1536]{1,0:T(8,128)(2,1)S(1)}, bf16[256,1536]{1,0:T(8,128)(2,1)}, u32[]{:S(2)}) copy-start(bf16[256,1536]{1,0:T(8,128)(2,1)} %param.25) | copy-start | bytes 2359300
  0.7 12.8 %copy-start.22 = (bf16[256,1536]{1,0:T(8,128)(2,1)S(1)}, bf16[256,1536]{1,0:T(8,128)(2,1)}, u32[]{:S(2)}) copy-start(bf16[256,1536]{1,0:T(8,128)(2,1)} %param.26) | copy-start | bytes 2359300
  3.1 13.3 %collective-permute-start.2 = (bf16[256,1536]{0,1:T(8,128)(2,1)}, bf16[256,1536]{0,1:T(8,128)(2,1)}, u32[]{:S(2)}, u32[]{:S(2)}) collective-permute-start(bf16[256,1536]{0,1:T(8,128)(2,1)} %copy.148), channel_id=1, source_target_pairs={{0,1},{1,0},{2,3},{3,2},{4,5},{5,4},{6,7},{7,6},{8,9},{9,8},{10,11... | collective-permute-start | bytes 2359304 | tf_op jit(solution)/shard_map/ppermute | solution.py:24
  3.9 10.4 %copy-start.18 = (bf16[256,1536]{1,0:T(8,128)(2,1)S(1)}, bf16[256,1536]{1,0:T(8,128)(2,1)}, u32[]{:S(2)}) copy-start(bf16[256,1536]{1,0:T(8,128)(2,1)} %param.28) | copy-start | bytes 2359300
  6.6 8.9 %copy-start.28 = (bf16[4,30,4]{1,2,0:T(4,128)(2,1)S(1)}, bf16[4,30,4]{1,2,0:T(4,128)(2,1)}, u32[]{:S(2)}) copy-start(bf16[4,30,4]{1,2,0:T(4,128)(2,1)} %constant.147) | copy-start | bytes 2884
  6.6 9.1 %copy-start.27 = (pred[4,8]{0,1:T(8,128)(4,1)S(1)}, pred[4,8]{0,1:T(8,128)(4,1)}, u32[]{:S(2)}) copy-start(pred[4,8]{0,1:T(8,128)(4,1)} %constant.65) | copy-start | bytes 100
  6.6 73.8 %collective-permute-start.4 = (bf16[528,1536]{1,0:T(8,128)(2,1)}, bf16[528,1536]{1,0:T(8,128)(2,1)}, u32[]{:S(2)}, u32[]{:S(2)}) collective-permute-start(bf16[528,1536]{1,0:T(8,128)(2,1)} %fusion.22), channel_id=1, source_target_pairs={{0,2},{2,4},{3,1},{4,6},{5,3},{6,8},{7,5},{8,10},{9,7},{10,12},{11... | collective-permute-start | bytes 4866056 | tf_op jit(solution)/shard_map/ppermute | solution.py:24
  10.2 77.5 %collective-permute-start.1 = (bf16[528,1536]{1,0:T(8,128)(2,1)}, bf16[528,1536]{1,0:T(8,128)(2,1)}, u32[]{:S(2)}, u32[]{:S(2)}) collective-permute-start(bf16[528,1536]{1,0:T(8,128)(2,1)} %fusion.22), channel_id=1, source_target_pairs={{1,3},{2,0},{3,5},{4,2},{5,7},{6,4},{7,9},{8,6},{9,11},{10,8},{11,... | collective-permute-start | bytes 4866056 | tf_op jit(solution)/shard_map/ppermute | solution.py:24
  13.8 83.6 %copy-start.2 = (bf16[256,1536]{0,1:T(8,128)(2,1)}, bf16[256,1536]{0,1:T(8,128)(2,1)S(1)}, u32[]{:S(2)}) copy-start(bf16[256,1536]{0,1:T(8,128)(2,1)S(1)} %copy.138) | copy-start | bytes 2359300
  13.8 4.1 %collective-permute-start = (bf16[256,1536]{0,1:T(8,128)(2,1)S(1)}, bf16[256,1536]{0,1:T(8,128)(2,1)}, u32[]{:S(2)}, u32[]{:S(2)}) collective-permute-start(bf16[256,1536]{0,1:T(8,128)(2,1)S(1)} %copy.138), channel_id=1, source_target_pairs={{0,1},{1,0},{2,3},{3,2},{4,5},{5,4},{6,7},{7,6},{8,9},{9,8},{10,11... | collective-permute-start | bytes 2359304 | tf_op jit(solution)/shard_map/ppermute | solution.py:24
  14.3 5.5 %copy-start.8 = (bf16[256,1536]{0,1:T(8,128)(2,1)}, bf16[256,1536]{0,1:T(8,128)(2,1)S(1)}, u32[]{:S(2)}) copy-start(bf16[256,1536]{0,1:T(8,128)(2,1)S(1)} %copy.139) | copy-start | bytes 2359300
  17.9 3.1 %copy-start.20 = (bf16[512,1536]{0,1:T(8,128)(2,1)}, bf16[512,1536]{0,1:T(8,128)(2,1)S(1)}, u32[]{:S(2)}) copy-start(bf16[512,1536]{0,1:T(8,128)(2,1)S(1)} %pad_maximum_fusion.1) | copy-start | bytes 4718596
  19.8 1.3 copy-start.13
  21.1 4.5 %copy-start = (f32[12,512,256]{2,1,0:T(8,128)}, f32[12,512,256]{2,1,0:T(8,128)S(1)}, u32[]{:S(2)}) copy-start(f32[12,512,256]{2,1,0:T(8,128)S(1)} %get-tuple-element.82) | copy-start | bytes 18874372
  91.7 14.6 %copy-start.10 = (bf16[256,1536]{0,1:T(8,128)(2,1)}, bf16[256,1536]{0,1:T(8,128)(2,1)S(1)}, u32[]{:S(2)}) copy-start(bf16[256,1536]{0,1:T(8,128)(2,1)S(1)} %copy.209) | copy-start | bytes 2359300
  97.4 1.9 %copy-start.19 = (bf16[256,1536]{0,1:T(8,128)(2,1)S(1)}, bf16[256,1536]{0,1:T(8,128)(2,1)}, u32[]{:S(2)}) copy-start(bf16[256,1536]{0,1:T(8,128)(2,1)} %copy.212) | copy-start | bytes 2359300
  101.8 12.6 %collective-permute-start.5 = (f32[3,12,256]{2,1,0:T(8,128)S(1)}, f32[3,12,256]{2,1,0:T(8,128)S(1)}, u32[]{:S(2)}, u32[]{:S(2)}) collective-permute-start(f32[3,12,256]{2,1,0:T(8,128)S(1)} %pad_maximum_fusion.3), channel_id=1, source_target_pairs={{1,3},{2,0},{3,5},{4,2},{5,7},{6,4},{7,9},{8,6},{9,11},{10,8},{11,... | collective-permute-start | bytes 110600 | tf_op jit(solution)/shard_map/ppermute | solution.py:24
  106.3 1.3 copy-start.15
  106.3 1.6 copy-start.21
  112.3 6.9 %collective-permute-start.3 = (f32[3,12,256]{2,1,0:T(8,128)S(1)}, f32[3,12,256]{2,1,0:T(8,128)S(1)}, u32[]{:S(2)}, u32[]{:S(2)}) collective-permute-start(f32[3,12,256]{2,1,0:T(8,128)S(1)} %pad_maximum_fusion.2), channel_id=1, source_target_pairs={{0,2},{2,4},{3,1},{4,6},{5,3},{6,8},{7,5},{8,10},{9,7},{10,12},{11... | collective-permute-start | bytes 110600 | tf_op jit(solution)/shard_map/ppermute | solution.py:24
  119.3 6.8 %collective-permute-start.7 = (f32[2,12,256]{2,1,0:T(8,128)S(1)}, f32[2,12,256]{2,1,0:T(8,128)S(1)}, u32[]{:S(2)}, u32[]{:S(2)}) collective-permute-start(f32[2,12,256]{2,1,0:T(8,128)S(1)} %pad_maximum_fusion.4), channel_id=1, source_target_pairs={{0,2},{2,4},{3,1},{4,6},{5,3},{6,8},{7,5},{8,10},{9,7},{10,12},{11... | collective-permute-start | bytes 73736 | tf_op jit(solution)/shard_map/ppermute | solution.py:24
  121.2 8.3 %collective-permute-start.6 = (f32[2,12,256]{2,1,0:T(8,128)S(1)}, f32[2,12,256]{2,1,0:T(8,128)S(1)}, u32[]{:S(2)}, u32[]{:S(2)}) collective-permute-start(f32[2,12,256]{2,1,0:T(8,128)S(1)} %pad_maximum_fusion.4), channel_id=1, source_target_pairs={{1,3},{2,0},{3,5},{4,2},{5,7},{6,4},{7,9},{8,6},{9,11},{10,8},{11,... | collective-permute-start | bytes 73736 | tf_op jit(solution)/shard_map/ppermute | solution.py:24
  126.1 2.2 %copy-start.3 = (bf16[256,1536]{0,1:T(8,128)(2,1)S(1)}, bf16[256,1536]{0,1:T(8,128)(2,1)}, u32[]{:S(2)}) copy-start(bf16[256,1536]{0,1:T(8,128)(2,1)} %copy-done.2) | copy-start | bytes 2359300
  128.2 8.3 %slice-start = ((s8[6291456]{0:T(1024)(128)(4,1)}), s8[4194304]{0:T(1024)(128)(4,1)S(1)}, s32[]{:S(2)}) async-start(s8[6291456]{0:T(1024)(128)(4,1)} %bitcast.158), calls=%async_computation | async-start | bytes 8388608
  129.5 7.0 %slice-start.1 = ((s8[6291456]{0:T(1024)(128)(4,1)}), s8[2097152]{0:T(1024)(128)(4,1)S(1)}, s32[]{:S(2)}) async-start(s8[6291456]{0:T(1024)(128)(4,1)} %bitcast.158), calls=%async_computation.1 | async-start | bytes 4194304
  135.1 1.5 copy-start.14
  139.7 35.3 %collective-permute-start.8 = (bf16[256,12,128]{0,2,1:T(8,128)(2,1)}, bf16[256,12,128]{0,2,1:T(8,128)(2,1)}, u32[]{:S(2)}, u32[]{:S(2)}) collective-permute-start(bf16[256,12,128]{0,2,1:T(8,128)(2,1)} %multiply_bitcast_fusion.3), channel_id=1, source_target_pairs={{0,2},{2,4},{3,1},{4,6},{5,3},{6,8},{7,5},{8,10},{9,7},{10,12},{11... | collective-permute-start | bytes 2359304 | tf_op jit(solution)/shard_map/ppermute | solution.py:24
  142.9 32.1 %collective-permute-start.9 = (bf16[256,12,128]{0,2,1:T(8,128)(2,1)}, bf16[256,12,128]{0,2,1:T(8,128)(2,1)}, u32[]{:S(2)}, u32[]{:S(2)}) collective-permute-start(bf16[256,12,128]{0,2,1:T(8,128)(2,1)} %multiply_bitcast_fusion.2), channel_id=1, source_target_pairs={{1,3},{2,0},{3,5},{4,2},{5,7},{6,4},{7,9},{8,6},{9,11},{10,8},{11,... | collective-permute-start | bytes 2359304 | tf_op jit(solution)/shard_map/ppermute | solution.py:24
  146.7 4.6 %copy-start.9 = (bf16[256,1536]{0,1:T(8,128)(2,1)S(1)}, bf16[256,1536]{0,1:T(8,128)(2,1)}, u32[]{:S(2)}) copy-start(bf16[256,1536]{0,1:T(8,128)(2,1)} %copy-done.8) | copy-start | bytes 2359300
  151.3 1.2 copy-start.11
  152.4 1.7 copy-start.5
  154.1 2.4 %copy-start.6 = (f32[512,12,128]{0,2,1:T(8,128)}, f32[512,12,128]{0,2,1:T(8,128)S(1)}, u32[]{:S(2)}) copy-start(f32[512,12,128]{0,2,1:T(8,128)S(1)} %multiply_bitcast_fusion.1) | copy-start | bytes 9437188
  154.1 3.6 %copy-start.1 = (bf16[12,256,512]{1,2,0:T(8,128)(2,1)S(1)}, bf16[12,256,512]{1,2,0:T(8,128)(2,1)}, u32[]{:S(2)}) copy-start(bf16[12,256,512]{1,2,0:T(8,128)(2,1)} %get-tuple-element.22) | copy-start | bytes 9437188
  154.1 3.8 %copy-start.16 = (bf16[256,1536]{0,1:T(8,128)(2,1)S(1)}, bf16[256,1536]{0,1:T(8,128)(2,1)}, u32[]{:S(2)}) copy-start(bf16[256,1536]{0,1:T(8,128)(2,1)} %copy.210) | copy-start | bytes 2359300
  156.5 2.6 %copy-start.7 = (f32[512,12,128]{0,2,1:T(8,128)S(1)}, f32[512,12,128]{0,2,1:T(8,128)}, u32[]{:S(2)}) copy-start(f32[512,12,128]{0,2,1:T(8,128)} %fusion.19) | copy-start | bytes 9437188
  156.5 23.7 %collective-permute-start.10 = (f32[256,12,128]{0,2,1:T(8,128)}, f32[256,12,128]{0,2,1:T(8,128)}, u32[]{:S(2)}, u32[]{:S(2)}) collective-permute-start(f32[256,12,128]{0,2,1:T(8,128)} %slice_add_fusion.2), channel_id=1, source_target_pairs={{0,1},{1,0},{2,3},{3,2},{4,5},{5,4},{6,7},{7,6},{8,9},{9,8},{10,11... | collective-permute-start | bytes 4718600 | tf_op jit(solution)/shard_map/ppermute | solution.py:24
  159.1 18.9 %copy-start.4 = (f32[512,12,128]{0,2,1:T(8,128)}, f32[512,12,128]{0,2,1:T(8,128)S(1)}, u32[]{:S(2)}) copy-start(f32[512,12,128]{0,2,1:T(8,128)S(1)} %convolution_bitcast_fusion) | copy-start | bytes 9437188
  161.0 25.8 %collective-permute-start.11 = (f32[256,12,128]{0,2,1:T(8,128)}, f32[256,12,128]{0,2,1:T(8,128)}, u32[]{:S(2)}, u32[]{:S(2)}) collective-permute-start(f32[256,12,128]{0,2,1:T(8,128)} %slice_add_fusion), channel_id=1, source_target_pairs={{0,1},{1,0},{2,3},{3,2},{4,5},{5,4},{6,7},{7,6},{8,9},{9,8},{10,11... | collective-permute-start | bytes 4718600 | tf_op jit(solution)/shard_map/ppermute | solution.py:24
  180.2 6.5 %copy-start.12 = (bf16[12,256,256]{1,2,0:T(8,128)(2,1)S(1)}, bf16[12,256,256]{1,2,0:T(8,128)(2,1)}, u32[]{:S(2)}) copy-start(bf16[12,256,256]{1,2,0:T(8,128)(2,1)} %get-tuple-element.24) | copy-start | bytes 4718596

commit v4 on v3

--- a/solution.py
+++ b/solution.py
@@ -60,53 +60,35 @@
     return jnp.concatenate(tables, axis=2), jnp.concatenate(owns, axis=1)
 
 
-def local(queries, keys, values, grad_out, block_list):
-    groups = lax.axis_size("tm")
-    here = lax.axis_index("tm")
+def chunk_grads(here, groups, data, key_own, value_own, key_partner, value_partner):
     even = here % 2 == 0
     up = jnp.where(even, 1, -1)
     scaling = HDIM ** (-0.5)
-    tok, width = queries.shape
+    tok, heads, _ = key_own.shape
     blocks = FRAMES * BANDS
-    cands = block_list.shape[1]
-
-    flags = (block_list > 0).astype(jnp.bfloat16).reshape(1, blocks * cands)
-    flags = jnp.pad(flags, ((0, LIST_ROWS - 1), (0, width - blocks * cands)))
-    pack = jnp.concatenate([queries, grad_out, flags], axis=0)
-
-    far_data = down_even(pack)
-    near_data = up_even(pack)
-    partner_keys, partner_values = swap_cores((keys, values))
-
-    key_own = keys.reshape(tok, HEADS, HDIM)
-    value_own = values.reshape(tok, HEADS, HDIM)
-    key_both = jnp.concatenate([keys, partner_keys], axis=0).reshape(2 * tok, HEADS, HDIM)
-    value_both = jnp.concatenate([values, partner_values], axis=0).reshape(2 * tok, HEADS, HDIM)
+    key_both = jnp.concatenate([key_own, key_partner], axis=0)
+    value_both = jnp.concatenate([value_own, value_partner], axis=0)
 
     slots = {
-        "far": (far_data, 2 * up, "both", (2, 1), (-2, -1)),
-        "near": (near_data, -2 * up, "own", (-2,), (2,)),
-        "own": (pack, 0, "own_both", (0, -1), (0, 1)),
+        "own": (0, "both", (0, -1), (0, 1)),
+        "far": (2 * up, "both", (2, 1), (-2, -1)),
+        "near": (-2 * up, "own", (-2,), (2,)),
     }
-
     parts = {}
     stats_out = {}
-    for name in ("own", "far", "near"):
-        data, q_off, key_set, offs_e, offs_o = slots[name]
+    for name, (q_off, key_set, offs_e, offs_o) in slots.items():
+        q_h, g_h, list_rows = data[name]
         if key_set == "own":
             key_h, value_h = key_own, value_own
         else:
             key_h, value_h = key_both, value_both
         nkb = key_h.shape[0] // BLOCK
-        q_h = data[:tok].reshape(tok, HEADS, HDIM)
-        g_h = data[tok : 2 * tok].reshape(tok, HEADS, HDIM)
-        list_rows = data[2 * tok, : blocks * cands].astype(jnp.float32).reshape(blocks, cands)
         source = here + q_off
         valid = (source >= 0) & (source < groups)
         table, own = parity_tables(even, offs_e, offs_o)
-        chosen = jnp.einsum("qc,qck->qk", list_rows, table) > 0
+        chosen = jnp.einsum("qc,qck->qk", (list_rows > 0).astype(jnp.float32), table) > 0
         mask = ((chosen & valid) | own)[None, :, None, :, None]
-        shape5 = (HEADS, blocks, BLOCK, nkb, BLOCK)
+        shape5 = (heads, blocks, BLOCK, nkb, BLOCK)
         scores = (
             jnp.einsum("qhd,khd->hqk", q_h, key_h, preferred_element_type=jnp.float32) * scaling
         ).reshape(shape5)
@@ -119,7 +101,7 @@
         row_sum = jnp.sum(expd, axis=(3, 4))
         row_dot = jnp.sum(expd * grad_probs, axis=(3, 4))
         parts[name] = (q_h, g_h, key_h, mask, scores, grad_probs)
-        stats_out[name] = jnp.stack([row_max, row_sum, row_dot]).reshape(3, HEADS, tok)
+        stats_out[name] = jnp.stack([row_max, row_sum, row_dot]).reshape(3, heads, tok)
 
     stats_in = [
         (stats_out["own"], 0),
@@ -140,16 +122,16 @@
     log_total = top + jnp.log(total)
     deltas = jnp.sum(dots * scale, axis=0) / total
     final = jnp.stack([log_total, deltas])
-    finals = {"own": final, "far": down_even(final), "near": up_even(final)}
+    finals = {"far": down_even(final), "near": up_even(final)}
 
     def backward(name, got):
         q_h, g_h, key_h, mask, scores, grad_probs = parts[name]
-        lse = got[0].reshape(HEADS, blocks, BLOCK)[:, :, :, None, None]
-        dlt = got[1].reshape(HEADS, blocks, BLOCK)[:, :, :, None, None]
+        lse = got[0].reshape(heads, blocks, BLOCK)[:, :, :, None, None]
+        dlt = got[1].reshape(heads, blocks, BLOCK)[:, :, :, None, None]
         weights = jnp.where(mask, jnp.exp(scores - lse), 0.0)
         nk = key_h.shape[0]
-        weights_low = weights.astype(jnp.bfloat16).reshape(HEADS, tok, nk)
-        grad_scores = (weights * (grad_probs - dlt)).astype(jnp.bfloat16).reshape(HEADS, tok, nk)
+        weights_low = weights.astype(jnp.bfloat16).reshape(heads, tok, nk)
+        grad_scores = (weights * (grad_probs - dlt)).astype(jnp.bfloat16).reshape(heads, tok, nk)
         q_part = jnp.einsum(
             "hqk,khd->qhd", grad_scores, key_h, preferred_element_type=jnp.float32
         ) * scaling
@@ -178,14 +160,55 @@
     back_kg, back_vg = swap_cores((partner_kg, partner_vg))
     key_grad = kg_far[:tok] + kg_own[:tok] + kg_near + back_kg
     value_grad = vg_far[:tok] + vg_own[:tok] + vg_near + back_vg
-    query_grad = (
-        own_b[4] + from_far.astype(jnp.float32) + from_near.astype(jnp.float32)
-    )
-    return (
-        query_grad.reshape(tok, width).astype(jnp.bfloat16),
-        key_grad.reshape(tok, width).astype(jnp.bfloat16),
-        value_grad.reshape(tok, width).astype(jnp.bfloat16),
-    )
+    query_grad = own_b[4] + from_far.astype(jnp.float32) + from_near.astype(jnp.float32)
+    return query_grad, key_grad, value_grad
+
+
+def local(queries, keys, values, grad_out, block_list):
+    groups = lax.axis_size("tm")
+    here = lax.axis_index("tm")
+    tok, width = queries.shape
+    blocks = FRAMES * BANDS
+    chunks = 2
+    per = HEADS // chunks
+
+    def heads_of(x, c):
+        return x.reshape(tok, HEADS, HDIM)[:, c * per : (c + 1) * per]
+
+    lists = {"own": block_list, "far": down_even(block_list), "near": up_even(block_list)}
+    partner_keys, partner_values = swap_cores((keys, values))
+
+    results = []
+    held = None
+    for c in range(chunks):
+        q_c = heads_of(queries, c)
+        g_c = heads_of(grad_out, c)
+        if held is not None:
+            q_c, g_c, _ = lax.optimization_barrier((q_c, g_c, held))
+        far_q, far_g = down_even((q_c, g_c))
+        near_q, near_g = up_even((q_c, g_c))
+        held = (far_q, far_g, near_q, near_g)
+        data = {
+            "own": (q_c, g_c, lists["own"]),
+            "far": (far_q, far_g, lists["far"]),
+            "near": (near_q, near_g, lists["near"]),
+        }
+        results.append(
+            chunk_grads(
+                here,
+                groups,
+                data,
+                heads_of(keys, c),
+                heads_of(values, c),
+                heads_of(partner_keys, c),
+                heads_of(partner_values, c),
+            )
+        )
+    outs = []
+    for i in range(3):
+        joined = jnp.concatenate([r[i] for r in results], axis=1)
+        outs.append(joined.reshape(tok, width).astype(jnp.bfloat16))
+    return tuple(outs)
 
 
 def solution(mesh):

time: 194 us -> 214 us (1.10)
  starting transfers between devices: 27.1 us -> 73.4 us
  waiting for transfers between devices: 73.8 us -> 29.5 us
  matrix products: 35.9 us -> 54.7 us
  other arithmetic: 22.6 us -> 11.6 us
  local copies, waits for them, and re-layouts: 30.5 us -> 38.5 us
    ppermute x12 -> x28, starting transfers between devices: 27.1 us -> 73.4 us  [permute(): return lax.ppermute(value, 'tm', pairs)]
    ppermute x12 -> x28, waiting for transfers between devices: 73.8 us -> 29.5 us  [permute(): return lax.ppermute(value, 'tm', pairs)]
    dot_general x9 -> x15, matrix products: 16.1 us -> 33 us  [the longest x6 23.9 us: chunk_grads(): jnp.einsum('qhd,khd->hqk', g_h, value_h, preferred_element_type=jnp.float32)]
    convert_element_type x4 -> x3, other arithmetic: 12.9 us -> 3.36 us  [the longest x2 2.31 us: backward(): weights_low = weights.astype(jnp.bfloat16).reshape(heads, tok, nk)]
    unnamed x73 -> x163, local copies, waits for them, and re-layouts: 20.3 us -> 26.9 us
    concatenate x3, other arithmetic: 6.02 us -> 1.11 us  [local(): joined = jnp.concatenate([r[i] for r in results], axis=1)]
    dot_general x3 -> x6, matrix products: 5.65 us -> 2.38 us  [backward(): jnp.einsum('hqk,khd->qhd', grad_scores, key_h, preferred_element_type=jnp...]
    dot_general x3 -> x6, matrix products: 6.55 us -> 9.4 us  [key_value(): jnp.einsum('hqk,qhd->khd', grad_scores, q_h, preferred_element_type=jnp.f...]
  transfers between devices with their start and end apart: 12 -> 28, of which waited for: 3 -> 6; matrix products, arithmetic and copies ran while one was open for 29% -> 41% of each run, Pallas kernels for 0% -> 0%
where the time goes in v4:
time: 214 us; the launch traced here: 210 us
  starting transfers between devices  73.4 us (34%)
  matrix products  54.7 us (26%)
  local copies, waits for them, and re-layouts  38.5 us (18%)
  waiting for transfers between devices  29.5 us (14%)
  other arithmetic  11.6 us (5%)
    ppermute x28, starting transfers between devices, permute(): return lax.ppermute(value, 'tm', pairs)  73.4 us
    ppermute x28, waiting for transfers between devices, permute(): return lax.ppermute(value, 'tm', pairs)  29.5 us
    unnamed x163, local copies, waits for them, and re-layouts  26.9 us
    dot_general x6, matrix products, chunk_grads(): jnp.einsum('qhd,khd->hqk', g_h, value_h, preferred_element_type=jnp.float32)  23.9 us
    dot_general x6, matrix products, key_value(): jnp.einsum('hqk,qhd->khd', weights_low, g_h, preferred_element_type=jnp.f...  9.99 us
    dot_general x6, matrix products, key_value(): jnp.einsum('hqk,qhd->khd', grad_scores, q_h, preferred_element_type=jnp.f...  9.4 us
    dot_general x6, matrix products, chunk_grads(): jnp.einsum('qhd,khd->hqk', q_h, key_h, preferred_element_type=jnp.float32)  8.69 us
  transfers between devices with their start and end apart: 28, of which 6 were waited for; matrix products, arithmetic and copies ran while one was open for 41% of the time, Pallas kernels for 0%

profile of v4, /device:TPU:8, one launch (start us, length us, event | category | flops | bytes accessed | tf_op | source)
XLA Modules:
  0.0 209.9 jit_solution(1850149588560678917)
XLA Ops:
  0.6 3.4 %collective-permute-start.6 = (s32[4,30]{1,0:T(4,128)}, s32[4,30]{1,0:T(4,128)}, u32[]{:S(2)}, u32[]{:S(2)}) collective-permute-start(s32[4,30]{1,0:T(4,128)} %param.49), channel_id=1, source_target_pairs={{0,2},{2,4},{3,1},{4,6},{5,3},{6,8},{7,5},{8,10},{9,7},{10,12},{11... | collective-permute-start | bytes 1448 | tf_op jit(solution)/shard_map/ppermute | solution.py:24
  4.1 3.3 %collective-permute-start.1 = (s32[4,30]{1,0:T(4,128)}, s32[4,30]{1,0:T(4,128)}, u32[]{:S(2)}, u32[]{:S(2)}) collective-permute-start(s32[4,30]{1,0:T(4,128)} %param.49), channel_id=1, source_target_pairs={{1,3},{2,0},{3,5},{4,2},{5,7},{6,4},{7,9},{8,6},{9,11},{10,8},{11,... | collective-permute-start | bytes 1448 | tf_op jit(solution)/shard_map/ppermute | solution.py:24
  7.4 1.4 copy.166
  9.8 2.5 %collective-permute-start.8 = (bf16[256,6,128]{2,0,1:T(8,128)(2,1)}, bf16[256,6,128]{2,0,1:T(8,128)(2,1)}, u32[]{:S(2)}, u32[]{:S(2)}) collective-permute-start(bf16[256,6,128]{2,0,1:T(8,128)(2,1)} %copy.270), channel_id=1, source_target_pairs={{0,2},{2,4},{3,1},{4,6},{5,3},{6,8},{7,5},{8,10},{9,7},{10,12},{11... | collective-permute-start | bytes 1179656 | tf_op jit(solution)/shard_map/ppermute | solution.py:24
  12.3 4.2 %collective-permute-start.4 = (bf16[256,6,128]{2,0,1:T(8,128)(2,1)}, bf16[256,6,128]{2,0,1:T(8,128)(2,1)}, u32[]{:S(2)}, u32[]{:S(2)}) collective-permute-start(bf16[256,6,128]{2,0,1:T(8,128)(2,1)} %copy.270), channel_id=1, source_target_pairs={{1,3},{2,0},{3,5},{4,2},{5,7},{6,4},{7,9},{8,6},{9,11},{10,8},{11,... | collective-permute-start | bytes 1179656 | tf_op jit(solution)/shard_map/ppermute | solution.py:24
  18.0 2.8 %collective-permute-start.2 = (bf16[256,6,128]{2,0,1:T(8,128)(2,1)}, bf16[256,6,128]{2,0,1:T(8,128)(2,1)}, u32[]{:S(2)}, u32[]{:S(2)}) collective-permute-start(bf16[256,6,128]{2,0,1:T(8,128)(2,1)} %copy.267), channel_id=1, source_target_pairs={{1,3},{2,0},{3,5},{4,2},{5,7},{6,4},{7,9},{8,6},{9,11},{10,8},{11,... | collective-permute-start | bytes 1179656 | tf_op jit(solution)/shard_map/ppermute | solution.py:24
  21.8 1.1 broadcast_in_dim.166
  23.2 1.7 copy.162
  29.8 3.0 %collective-permute-start.7 = (bf16[256,6,128]{2,0,1:T(8,128)(2,1)}, bf16[256,6,128]{2,0,1:T(8,128)(2,1)S(1)}, u32[]{:S(2)}, u32[]{:S(2)}) collective-permute-start(bf16[256,6,128]{2,0,1:T(8,128)(2,1)} %copy.267), channel_id=1, source_target_pairs={{0,2},{2,4},{3,1},{4,6},{5,3},{6,8},{7,5},{8,10},{9,7},{10,12},{11... | collective-permute-start | bytes 1179656 | tf_op jit(solution)/shard_map/ppermute | solution.py:24
  34.6 4.1 %collective-permute-done.8 = bf16[256,6,128]{2,0,1:T(8,128)(2,1)} collective-permute-done((bf16[256,6,128]{2,0,1:T(8,128)(2,1)}, bf16[256,6,128]{2,0,1:T(8,128)(2,1)}, u32[]{:S(2)}, u32[]{:S(2)}) %collective-permute-start.8) | collective-permute-done | bytes 393248 | tf_op jit(solution)/shard_map/ppermute | solution.py:24
  40.2 1.1 broadcast_in_dim.169
  41.3 6.1 %collective-permute-done.2 = bf16[256,6,128]{2,0,1:T(8,128)(2,1)} collective-permute-done((bf16[256,6,128]{2,0,1:T(8,128)(2,1)}, bf16[256,6,128]{2,0,1:T(8,128)(2,1)}, u32[]{:S(2)}, u32[]{:S(2)}) %collective-permute-start.2) | collective-permute-done | bytes 393248 | tf_op jit(solution)/shard_map/ppermute | solution.py:24
  47.4 4.1 %collective-permute-start.17 = (bf16[256,6,128]{2,0,1:T(8,128)(2,1)}, bf16[256,6,128]{2,0,1:T(8,128)(2,1)}, u32[]{:S(2)}, u32[]{:S(2)}) collective-permute-start(bf16[256,6,128]{2,0,1:T(8,128)(2,1)} %copy.273), channel_id=1, source_target_pairs={{0,2},{2,4},{3,1},{4,6},{5,3},{6,8},{7,5},{8,10},{9,7},{10,12},{11... | collective-permute-start | bytes 1179656 | tf_op jit(solution)/shard_map/ppermute | solution.py:24
  51.5 2.6 %collective-permute-start.14 = (bf16[256,6,128]{2,0,1:T(8,128)(2,1)}, bf16[256,6,128]{2,0,1:T(8,128)(2,1)}, u32[]{:S(2)}, u32[]{:S(2)}) collective-permute-start(bf16[256,6,128]{2,0,1:T(8,128)(2,1)} %copy.273), channel_id=1, source_target_pairs={{1,3},{2,0},{3,5},{4,2},{5,7},{6,4},{7,9},{8,6},{9,11},{10,8},{11,... | collective-permute-start | bytes 1179656 | tf_op jit(solution)/shard_map/ppermute | solution.py:24
  54.1 4.1 %collective-permute-start.15 = (bf16[256,6,128]{2,0,1:T(8,128)(2,1)}, bf16[256,6,128]{2,0,1:T(8,128)(2,1)}, u32[]{:S(2)}, u32[]{:S(2)}) collective-permute-start(bf16[256,6,128]{2,0,1:T(8,128)(2,1)} %copy.274), channel_id=1, source_target_pairs={{1,3},{2,0},{3,5},{4,2},{5,7},{6,4},{7,9},{8,6},{9,11},{10,8},{11,... | collective-permute-start | bytes 1179656 | tf_op jit(solution)/shard_map/ppermute | solution.py:24
  58.3 1.5 select_reduce_fusion.3
  59.7 2.5 %fusion.120 = (bf16[256,6,128]{0,2,1:T(8,128)(2,1)S(1)}, bf16[256,6,128]{0,2,1:T(8,128)(2,1)}) fusion(bf16[256,12,128]{0,2,1:T(8,128)(2,1)} %bitcast.13), kind=kLoop, calls=%fused_computation.236 | loop fusion | bytes 1572864 | tf_op jit(solution)/shard_map/slice | solution.py:176
  63.2 1.2 fusion.122
  66.2 7.6 %collective-permute-done.17 = bf16[256,6,128]{2,0,1:T(8,128)(2,1)} collective-permute-done((bf16[256,6,128]{2,0,1:T(8,128)(2,1)}, bf16[256,6,128]{2,0,1:T(8,128)(2,1)}, u32[]{:S(2)}, u32[]{:S(2)}) %collective-permute-start.17) | collective-permute-done | bytes 393248 | tf_op jit(solution)/shard_map/ppermute | solution.py:24
  73.8 1.5 convolution_multiply_fusion
  75.4 3.2 %fusion.60 = (f32[6,256]{1,0:T(8,128)S(1)}, f32[6,256]{1,0:T(8,128)S(1)}, f32[6,256]{1,0:T(8,128)S(1)}, f32[6,256,256]{1,2,0:T(8,128)}) fusion(f32[6,256,256]{1,2,0:T(8,128)S(1)} %get-tuple-element.146, f32[6,256]{1,0:T(8,128)S(1)} %get-tuple-element.145, pred[256,256]{0,1:T(8,128)(4,1)S(1)} %copy-done.46, ...), kind=kOutput, calls=%fused_computation.102 | convolution fusion | flops 103804416 | bytes 5597184 | tf_op jit(solution)/shard_map/qhd,khd->hqk/dot_general | solution.py:95
  78.6 4.9 %collective-permute-start.9 = (f32[3,6,256]{2,1,0:T(8,128)S(1)}, f32[3,6,256]{2,1,0:T(8,128)S(1)}, u32[]{:S(2)}, u32[]{:S(2)}) collective-permute-start(f32[3,6,256]{2,1,0:T(8,128)S(1)} %pad_maximum_fusion.12), channel_id=1, source_target_pairs={{1,3},{2,0},{3,5},{4,2},{5,7},{6,4},{7,9},{8,6},{9,11},{10,8},{11,... | collective-permute-start | bytes 55304 | tf_op jit(solution)/shard_map/ppermute | solution.py:24
  83.5 1.6 fusion.108
  86.5 3.2 %fusion.17 = (f32[6,256]{1,0:T(8,128)S(1)}, f32[6,256]{1,0:T(8,128)S(1)}, f32[6,256]{1,0:T(8,128)S(1)}, f32[6,512,256]{2,1,0:T(8,128)}) fusion(f32[6,512,256]{2,1,0:T(8,128)S(1)} %get-tuple-element.149, f32[6,256]{1,0:T(8,128)S(1)} %get-tuple-element.148, pred[256,512]{0,1:T(8,128)(4,1)S(1)} %copy-done.44, f32[6,256,512]{1,2,0:T(8,128)S(1)} %fusion.108, ...), kind=kOutput, calls=%fused_computation.37 | convolution fusion | flops 210759168 | bytes 10774528 | tf_op jit(solution)/shard_map/qhd,khd->hqk/dot_general | solution.py:95
  89.7 1.6 fusion.107
  91.3 1.9 fusion.11
  93.2 5.1 %fusion.16 = (f32[6,256]{1,0:T(8,128)S(1)}, f32[6,256]{1,0:T(8,128)S(1)}, f32[6,256]{1,0:T(8,128)}, f32[6,512,256]{2,1,0:T(8,128)}) fusion(f32[6,512,256]{2,1,0:T(8,128)S(1)} %get-tuple-element.143, f32[6,256]{1,0:T(8,128)S(1)} %get-tuple-element.142, pred[256,512]{0,1:T(8,128)(4,1)S(1)} %copy-done.56, f32[6,256,512]{1,2,0:T(8,128)S(1)} %fusion.107, ...), kind=kOutput, calls=%fused_computation.36 | convolution fusion | flops 210759168 | bytes 10772480 | tf_op jit(solution)/shard_map/qhd,khd->hqk/dot_general | solution.py:95
  98.3 1.9 collective-permute-start.5
  100.3 4.7 %collective-permute-done.5 = f32[3,6,256]{2,1,0:T(8,128)S(1)} collective-permute-done((f32[3,6,256]{2,1,0:T(8,128)S(1)}, f32[3,6,256]{2,1,0:T(8,128)S(1)}, u32[]{:S(2)}, u32[]{:S(2)}) %collective-permute-start.5) | collective-permute-done | bytes 18464 | tf_op jit(solution)/shard_map/ppermute | solution.py:24
  105.6 1.9 collective-permute-start.10
  107.5 1.9 copy.275
  109.5 3.9 %collective-permute-start.18 = (bf16[256,6,128]{2,0,1:T(8,128)(2,1)}, bf16[256,6,128]{2,0,1:T(8,128)(2,1)}, u32[]{:S(2)}, u32[]{:S(2)}) collective-permute-start(bf16[256,6,128]{2,0,1:T(8,128)(2,1)} %copy.274), channel_id=1, source_target_pairs={{0,2},{2,4},{3,1},{4,6},{5,3},{6,8},{7,5},{8,10},{9,7},{10,12},{11... | collective-permute-start | bytes 1179656 | tf_op jit(solution)/shard_map/ppermute | solution.py:24
  113.4 1.9 copy.276
  115.3 2.9 %collective-permute-start.11 = (f32[2,6,256]{2,1,0:T(8,128)}, f32[2,6,256]{2,1,0:T(8,128)S(1)}, u32[]{:S(2)}, u32[]{:S(2)}) collective-permute-start(f32[2,6,256]{2,1,0:T(8,128)} %pad_maximum_fusion.15), channel_id=1, source_target_pairs={{0,2},{2,4},{3,1},{4,6},{5,3},{6,8},{7,5},{8,10},{9,7},{10,12},{11... | collective-permute-start | bytes 36872 | tf_op jit(solution)/shard_map/ppermute | solution.py:24
  118.9 6.4 %fusion.15 = (bf16[6,256,512]{1,2,0:T(8,128)(2,1)S(1)}, bf16[6,256,512]{1,2,0:T(8,128)(2,1)S(1)}, f32[6,256]{1,0:T(8,128)S(1)}, f32[6,256]{1,0:T(8,128)S(1)}, f32[6,256,512]{1,2,0:T(8,128)S(1)}) fusion(f32[6,512,256]{2,1,0:T(8,128)} %copy-done.43, f32[6,256]{1,0:T(8,128)S(1)} %get-tuple-element.132, pred[256,512]{0,1:T(8,128)(4,1)} %broadcast_in_dim.169, ...), kind=kOutput, calls=%fused_computation.35 | convolution fusion | flops 213906432 | bytes 17070080 | tf_op jit(solution)/shard_map/qhd,khd->hqk/dot_general | solution.py:95
  127.0 2.9 %fusion.54 = (bf16[6,256,256]{1,2,0:T(8,128)(2,1)}, bf16[6,256,256]{1,2,0:T(8,128)(2,1)S(1)}, f32[6,256]{1,0:T(8,128)S(1)}, f32[6,256]{1,0:T(8,128)S(1)}, f32[6,256,256]{1,2,0:T(8,128)S(1)}) fusion(f32[6,256,256]{1,2,0:T(8,128)S(1)} %copy-done.5, f32[6,256]{1,0:T(8,128)S(1)} %get-tuple-element.130, pred[256,256]{0,1:T(8,128)(4,1)S(1)} %copy-done.47, ...), kind=kOutput, calls=%fused_computation.96 | convolution fusion | flops 105378816 | bytes 8753152 | tf_op jit(solution)/shard_map/qhd,khd->hqk/dot_general | solution.py:95
  132.4 1.6 copy-done.38
  134.0 3.1 %fusion.19 = (f32[6,256]{1,0:T(8,128)S(1)}, f32[6,256]{1,0:T(8,128)S(1)}, bf16[6,256,512]{1,2,0:T(8,128)(2,1)S(1)}, f32[6,256,512]{1,2,0:T(8,128)S(1)}) fusion(f32[6,256,512]{1,2,0:T(8,128)S(1)} %fusion.108, f32[6,256]{1,0:T(8,128)S(1)} %get-tuple-element.72, pred[256,512]{0,1:T(8,128)(4,1)S(1)} %copy-done.45, f32[6,256]{1,0:T(8,128)S(1)} %get-tuple-element.129, ...), kind=kOutput, calls=%fused_computation.39 | convolution fusion | flops 213120000 | bytes 15497216 | tf_op jit(solution)/shard_map/qhd,khd->hqk/dot_general | solution.py:95
  139.0 3.9 %collective-permute-start.16 = (f32[3,6,256]{2,1,0:T(8,128)S(1)}, f32[3,6,256]{2,1,0:T(8,128)S(1)}, u32[]{:S(2)}, u32[]{:S(2)}) collective-permute-start(f32[3,6,256]{2,1,0:T(8,128)S(1)} %pad_maximum_fusion.13), channel_id=1, source_target_pairs={{0,2},{2,4},{3,1},{4,6},{5,3},{6,8},{7,5},{8,10},{9,7},{10,12},{11... | collective-permute-start | bytes 55304 | tf_op jit(solution)/shard_map/ppermute | solution.py:24
  142.9 2.8 %collective-permute-start.19 = (f32[3,6,256]{2,1,0:T(8,128)S(1)}, f32[3,6,256]{2,1,0:T(8,128)S(1)}, u32[]{:S(2)}, u32[]{:S(2)}) collective-permute-start(f32[3,6,256]{2,1,0:T(8,128)S(1)} %pad_maximum_fusion.14), channel_id=1, source_target_pairs={{1,3},{2,0},{3,5},{4,2},{5,7},{6,4},{7,9},{8,6},{9,11},{10,8},{11,... | collective-permute-start | bytes 55304 | tf_op jit(solution)/shard_map/ppermute | solution.py:24
  145.7 3.0 %collective-permute-start.12 = (bf16[256,6,128]{0,2,1:T(8,128)(2,1)S(1)}, bf16[256,6,128]{0,2,1:T(8,128)(2,1)S(1)}, u32[]{:S(2)}, u32[]{:S(2)}) collective-permute-start(bf16[256,6,128]{0,2,1:T(8,128)(2,1)S(1)} %fusion.53), channel_id=1, source_target_pairs={{0,2},{2,4},{3,1},{4,6},{5,3},{6,8},{7,5},{8,10},{9,7},{10,12},{11... | collective-permute-start | bytes 1179656 | tf_op jit(solution)/shard_map/ppermute | solution.py:24
  148.8 3.7 %collective-permute-start.13 = (bf16[256,6,128]{0,2,1:T(8,128)(2,1)S(1)}, bf16[256,6,128]{0,2,1:T(8,128)(2,1)S(1)}, u32[]{:S(2)}, u32[]{:S(2)}) collective-permute-start(bf16[256,6,128]{0,2,1:T(8,128)(2,1)S(1)} %fusion.43), channel_id=1, source_target_pairs={{1,3},{2,0},{3,5},{4,2},{5,7},{6,4},{7,9},{8,6},{9,11},{10,8},{11,... | collective-permute-start | bytes 1179656 | tf_op jit(solution)/shard_map/ppermute | solution.py:24
  152.5 1.7 multiply_bitcast_fusion.3
  154.2 1.2 slice_add_fusion.6
  155.4 1.7 convolution_bitcast_fusion.1
  157.2 2.1 %collective-permute-start.21 = (f32[2,6,256]{2,1,0:T(8,128)S(1)}, f32[2,6,256]{2,1,0:T(8,128)S(1)}, u32[]{:S(2)}, u32[]{:S(2)}) collective-permute-start(f32[2,6,256]{2,1,0:T(8,128)S(1)} %pad_maximum_fusion.16), channel_id=1, source_target_pairs={{0,2},{2,4},{3,1},{4,6},{5,3},{6,8},{7,5},{8,10},{9,7},{10,12},{11... | collective-permute-start | bytes 36872 | tf_op jit(solution)/shard_map/ppermute | solution.py:24
  160.4 4.9 %collective-permute-start.20 = (f32[2,6,256]{2,1,0:T(8,128)S(1)}, f32[2,6,256]{2,1,0:T(8,128)S(1)}, u32[]{:S(2)}, u32[]{:S(2)}) collective-permute-start(f32[2,6,256]{2,1,0:T(8,128)S(1)} %pad_maximum_fusion.16), channel_id=1, source_target_pairs={{1,3},{2,0},{3,5},{4,2},{5,7},{6,4},{7,9},{8,6},{9,11},{10,8},{11,... | collective-permute-start | bytes 36872 | tf_op jit(solution)/shard_map/ppermute | solution.py:24
  165.4 1.3 fusion.55
  169.4 1.9 fusion.32
  172.8 1.7 multiply_bitcast_fusion
  174.4 4.3 %collective-permute-start.22 = (bf16[256,6,128]{0,2,1:T(8,128)(2,1)S(1)}, bf16[256,6,128]{0,2,1:T(8,128)(2,1)S(1)}, u32[]{:S(2)}, u32[]{:S(2)}) collective-permute-start(bf16[256,6,128]{0,2,1:T(8,128)(2,1)S(1)} %fusion.51), channel_id=1, source_target_pairs={{0,2},{2,4},{3,1},{4,6},{5,3},{6,8},{7,5},{8,10},{9,7},{10,12},{11... | collective-permute-start | bytes 1179656 | tf_op jit(solution)/shard_map/ppermute | solution.py:24
  178.8 2.4 %collective-permute-start.23 = (bf16[256,6,128]{0,2,1:T(8,128)(2,1)S(1)}, bf16[256,6,128]{0,2,1:T(8,128)(2,1)S(1)}, u32[]{:S(2)}, u32[]{:S(2)}) collective-permute-start(bf16[256,6,128]{0,2,1:T(8,128)(2,1)S(1)} %fusion.42), channel_id=1, source_target_pairs={{1,3},{2,0},{3,5},{4,2},{5,7},{6,4},{7,9},{8,6},{9,11},{10,8},{11,... | collective-permute-start | bytes 1179656 | tf_op jit(solution)/shard_map/ppermute | solution.py:24
  181.2 1.7 multiply_bitcast_fusion.1
  182.9 1.9 convolution_bitcast_fusion
  184.8 1.3 slice_add_fusion.4
  186.1 1.1 slice_add_fusion
  187.9 6.7 %collective-permute-done.22 = bf16[256,6,128]{0,2,1:T(8,128)(2,1)S(1)} collective-permute-done((bf16[256,6,128]{0,2,1:T(8,128)(2,1)S(1)}, bf16[256,6,128]{0,2,1:T(8,128)(2,1)S(1)}, u32[]{:S(2)}, u32[]{:S(2)}) %collective-permute-start.22) | collective-permute-done | bytes 393248 | tf_op jit(solution)/shard_map/ppermute | solution.py:24
  195.1 1.2 copy.216
  197.0 2.1 %fusion.56 = bf16[256,6,128]{0,2,1:T(8,128)(2,1)S(1)} fusion(f32[256,6,128]{0,2,1:T(8,128)} %collective-permute-done.24, bf16[256,6,128]{2,0,1:T(8,128)(2,1)S(1)} %copy-done.55, bf16[6,256,256]{1,2,0:T(8,128)(2,1)S(1)} %copy-done.12, f32[512,6,128]{0,2,1:T(8,128)S(1)} %copy-done.19, f32[512,6,128]{0,2,1:T(8,128)} %copy-done.22), kind=kOutput, calls=%fused_computation.98 | convolution fusion | flops 101646336 | bytes 3932160 | tf_op jit(solution)/shard_map/hqk,qhd->khd/dot_general | solution.py:151
  199.2 1.8 fusion.59
  201.6 1.7 fusion.57
  204.2 2.5 %copy.217 = bf16[256,1536]{1,0:T(8,128)(2,1)} copy(bf16[256,1536]{0,1:T(8,128)(2,1)} %bitcast.276) | data formatting | bytes 1572864
  206.8 1.9 fusion.58
  208.8 1.2 copy.218
  (246 shorter events, 31.8 us)
Async XLA Ops:
  0.6 29.2 %collective-permute-start.6 = (s32[4,30]{1,0:T(4,128)}, s32[4,30]{1,0:T(4,128)}, u32[]{:S(2)}, u32[]{:S(2)}) collective-permute-start(s32[4,30]{1,0:T(4,128)} %param.49), channel_id=1, source_target_pairs={{0,2},{2,4},{3,1},{4,6},{5,3},{6,8},{7,5},{8,10},{9,7},{10,12},{11... | collective-permute-start | bytes 1448 | tf_op jit(solution)/shard_map/ppermute | solution.py:24
  4.1 29.6 %collective-permute-start.1 = (s32[4,30]{1,0:T(4,128)}, s32[4,30]{1,0:T(4,128)}, u32[]{:S(2)}, u32[]{:S(2)}) collective-permute-start(s32[4,30]{1,0:T(4,128)} %param.49), channel_id=1, source_target_pairs={{1,3},{2,0},{3,5},{4,2},{5,7},{6,4},{7,9},{8,6},{9,11},{10,8},{11,... | collective-permute-start | bytes 1448 | tf_op jit(solution)/shard_map/ppermute | solution.py:24
  8.8 3.5 %copy-start.39 = (bf16[256,1536]{0,1:T(8,128)(2,1)}, bf16[256,1536]{0,1:T(8,128)(2,1)S(1)}, u32[]{:S(2)}) copy-start(bf16[256,1536]{0,1:T(8,128)(2,1)S(1)} %copy.166) | copy-start | bytes 2359300
  8.8 7.8 %copy-start.58 = (bf16[256,1536]{1,0:T(8,128)(2,1)S(1)}, bf16[256,1536]{1,0:T(8,128)(2,1)}, u32[]{:S(2)}) copy-start(bf16[256,1536]{1,0:T(8,128)(2,1)} %param.45) | copy-start | bytes 2359300
  9.8 29.0 %collective-permute-start.8 = (bf16[256,6,128]{2,0,1:T(8,128)(2,1)}, bf16[256,6,128]{2,0,1:T(8,128)(2,1)}, u32[]{:S(2)}, u32[]{:S(2)}) collective-permute-start(bf16[256,6,128]{2,0,1:T(8,128)(2,1)} %copy.270), channel_id=1, source_target_pairs={{0,2},{2,4},{3,1},{4,6},{5,3},{6,8},{7,5},{8,10},{9,7},{10,12},{11... | collective-permute-start | bytes 1179656 | tf_op jit(solution)/shard_map/ppermute | solution.py:24
  12.3 28.9 %collective-permute-start.4 = (bf16[256,6,128]{2,0,1:T(8,128)(2,1)}, bf16[256,6,128]{2,0,1:T(8,128)(2,1)}, u32[]{:S(2)}, u32[]{:S(2)}) collective-permute-start(bf16[256,6,128]{2,0,1:T(8,128)(2,1)} %copy.270), channel_id=1, source_target_pairs={{1,3},{2,0},{3,5},{4,2},{5,7},{6,4},{7,9},{8,6},{9,11},{10,8},{11,... | collective-permute-start | bytes 1179656 | tf_op jit(solution)/shard_map/ppermute | solution.py:24
  16.9 6.1 %copy-start.31 = (bf16[256,1536]{0,1:T(8,128)(2,1)}, bf16[256,1536]{0,1:T(8,128)(2,1)S(1)}, u32[]{:S(2)}) copy-start(bf16[256,1536]{0,1:T(8,128)(2,1)S(1)} %copy.160) | copy-start | bytes 2359300
  16.9 4.0 %copy-start.67 = (s32[4,30]{1,0:T(4,128)S(1)}, s32[4,30]{1,0:T(4,128)}, u32[]{:S(2)}) copy-start(s32[4,30]{1,0:T(4,128)} %param.49) | copy-start | bytes 1444
  16.9 4.5 %copy-start.63 = (bf16[4,30,4]{1,2,0:T(4,128)(2,1)S(1)}, bf16[4,30,4]{1,2,0:T(4,128)(2,1)}, u32[]{:S(2)}) copy-start(bf16[4,30,4]{1,2,0:T(4,128)(2,1)} %constant.220) | copy-start | bytes 2884
  16.9 4.5 %copy-start.64 = (bf16[4,30,4]{1,2,0:T(4,128)(2,1)S(1)}, bf16[4,30,4]{1,2,0:T(4,128)(2,1)}, u32[]{:S(2)}) copy-start(bf16[4,30,4]{1,2,0:T(4,128)(2,1)} %constant.221) | copy-start | bytes 2884
  16.9 4.5 %copy-start.65 = (bf16[4,30,4]{1,2,0:T(4,128)(2,1)S(1)}, bf16[4,30,4]{1,2,0:T(4,128)(2,1)}, u32[]{:S(2)}) copy-start(bf16[4,30,4]{1,2,0:T(4,128)(2,1)} %constant.223) | copy-start | bytes 2884
  16.9 4.5 %copy-start.66 = (bf16[4,30,4]{1,2,0:T(4,128)(2,1)S(1)}, bf16[4,30,4]{1,2,0:T(4,128)(2,1)}, u32[]{:S(2)}) copy-start(bf16[4,30,4]{1,2,0:T(4,128)(2,1)} %constant.222) | copy-start | bytes 2884
  16.9 4.5 %copy-start.70 = (bf16[4,30,4]{1,2,0:T(4,128)(2,1)S(1)}, bf16[4,30,4]{1,2,0:T(4,128)(2,1)}, u32[]{:S(2)}) copy-start(bf16[4,30,4]{1,2,0:T(4,128)(2,1)} %constant.224) | copy-start | bytes 2884
  16.9 4.7 %copy-start.68 = (pred[4,8]{0,1:T(8,128)(4,1)S(1)}, pred[4,8]{0,1:T(8,128)(4,1)}, u32[]{:S(2)}) copy-start(pred[4,8]{0,1:T(8,128)(4,1)} %constant.63) | copy-start | bytes 100
  17.0 6.0 %copy-start.59 = (bf16[256,1536]{1,0:T(8,128)(2,1)S(1)}, bf16[256,1536]{1,0:T(8,128)(2,1)}, u32[]{:S(2)}) copy-start(bf16[256,1536]{1,0:T(8,128)(2,1)} %param.46) | copy-start | bytes 2359300
  18.0 29.4 %collective-permute-start.2 = (bf16[256,6,128]{2,0,1:T(8,128)(2,1)}, bf16[256,6,128]{2,0,1:T(8,128)(2,1)}, u32[]{:S(2)}, u32[]{:S(2)}) collective-permute-start(bf16[256,6,128]{2,0,1:T(8,128)(2,1)} %copy.267), channel_id=1, source_target_pairs={{1,3},{2,0},{3,5},{4,2},{5,7},{6,4},{7,9},{8,6},{9,11},{10,8},{11,... | collective-permute-start | bytes 1179656 | tf_op jit(solution)/shard_map/ppermute | solution.py:24
  23.2 35.0 %copy-start.6 = (bf16[256,1536]{0,1:T(8,128)(2,1)}, bf16[256,1536]{0,1:T(8,128)(2,1)S(1)}, u32[]{:S(2)}) copy-start(bf16[256,1536]{0,1:T(8,128)(2,1)S(1)} %copy.156) | copy-start | bytes 2359300
  24.9 8.7 %copy-start.8 = (bf16[256,1536]{0,1:T(8,128)(2,1)}, bf16[256,1536]{0,1:T(8,128)(2,1)S(1)}, u32[]{:S(2)}) copy-start(bf16[256,1536]{0,1:T(8,128)(2,1)S(1)} %copy.162) | copy-start | bytes 2359300
  27.7 12.2 %copy-start.69 = (pred[8]{0:T(512)(128)(4,1)S(1)}, pred[8]{0:T(512)(128)(4,1)}, u32[]{:S(2)}) copy-start(pred[8]{0:T(512)(128)(4,1)} %pad.1.clone) | copy-start | bytes 28
  29.8 17.5 %collective-permute-start.7 = (bf16[256,6,128]{2,0,1:T(8,128)(2,1)}, bf16[256,6,128]{2,0,1:T(8,128)(2,1)S(1)}, u32[]{:S(2)}, u32[]{:S(2)}) collective-permute-start(bf16[256,6,128]{2,0,1:T(8,128)(2,1)} %copy.267), channel_id=1, source_target_pairs={{0,2},{2,4},{3,1},{4,6},{5,3},{6,8},{7,5},{8,10},{9,7},{10,12},{11... | collective-permute-start | bytes 1179656 | tf_op jit(solution)/shard_map/ppermute | solution.py:24
  33.7 26.1 %collective-permute-start.3 = (bf16[256,1536]{0,1:T(8,128)(2,1)S(1)}, bf16[256,1536]{0,1:T(8,128)(2,1)}, u32[]{:S(2)}, u32[]{:S(2)}) collective-permute-start(bf16[256,1536]{0,1:T(8,128)(2,1)S(1)} %copy.162), channel_id=1, source_target_pairs={{0,1},{1,0},{2,3},{3,2},{4,5},{5,4},{6,7},{7,6},{8,9},{9,8},{10,11... | collective-permute-start | bytes 2359304 | tf_op jit(solution)/shard_map/ppermute | solution.py:24
  38.8 24.4 %collective-permute-start = (bf16[256,1536]{0,1:T(8,128)(2,1)S(1)}, bf16[256,1536]{0,1:T(8,128)(2,1)}, u32[]{:S(2)}, u32[]{:S(2)}) collective-permute-start(bf16[256,1536]{0,1:T(8,128)(2,1)S(1)} %copy.156), channel_id=1, source_target_pairs={{0,1},{1,0},{2,3},{3,2},{4,5},{5,4},{6,7},{7,6},{8,9},{9,8},{10,11... | collective-permute-start | bytes 2359304 | tf_op jit(solution)/shard_map/ppermute | solution.py:24
  47.4 6.8 %copy-start.54 = (bf16[256,6,128]{2,0,1:T(8,128)(2,1)}, bf16[256,6,128]{2,0,1:T(8,128)(2,1)S(1)}, u32[]{:S(2)}) copy-start(bf16[256,6,128]{2,0,1:T(8,128)(2,1)S(1)} %collective-permute-done.7) | copy-start | bytes 1179652
  47.4 26.4 %collective-permute-start.17 = (bf16[256,6,128]{2,0,1:T(8,128)(2,1)}, bf16[256,6,128]{2,0,1:T(8,128)(2,1)}, u32[]{:S(2)}, u32[]{:S(2)}) collective-permute-start(bf16[256,6,128]{2,0,1:T(8,128)(2,1)} %copy.273), channel_id=1, source_target_pairs={{0,2},{2,4},{3,1},{4,6},{5,3},{6,8},{7,5},{8,10},{9,7},{10,12},{11... | collective-permute-start | bytes 1179656 | tf_op jit(solution)/shard_map/ppermute | solution.py:24
  51.5 38.2 %collective-permute-start.14 = (bf16[256,6,128]{2,0,1:T(8,128)(2,1)}, bf16[256,6,128]{2,0,1:T(8,128)(2,1)}, u32[]{:S(2)}, u32[]{:S(2)}) collective-permute-start(bf16[256,6,128]{2,0,1:T(8,128)(2,1)} %copy.273), channel_id=1, source_target_pairs={{1,3},{2,0},{3,5},{4,2},{5,7},{6,4},{7,9},{8,6},{9,11},{10,8},{11,... | collective-permute-start | bytes 1179656 | tf_op jit(solution)/shard_map/ppermute | solution.py:24
  54.1 64.8 %collective-permute-start.15 = (bf16[256,6,128]{2,0,1:T(8,128)(2,1)}, bf16[256,6,128]{2,0,1:T(8,128)(2,1)}, u32[]{:S(2)}, u32[]{:S(2)}) collective-permute-start(bf16[256,6,128]{2,0,1:T(8,128)(2,1)} %copy.274), channel_id=1, source_target_pairs={{1,3},{2,0},{3,5},{4,2},{5,7},{6,4},{7,9},{8,6},{9,11},{10,8},{11,... | collective-permute-start | bytes 1179656 | tf_op jit(solution)/shard_map/ppermute | solution.py:24
  59.7 15.6 %copy-start.4 = (f32[6,256,256]{1,2,0:T(8,128)}, f32[6,256,256]{1,2,0:T(8,128)S(1)}, u32[]{:S(2)}) copy-start(f32[6,256,256]{1,2,0:T(8,128)S(1)} %get-tuple-element.146) | copy-start | bytes 4718596
  66.2 9.2 %copy-start.9 = (bf16[256,1536]{0,1:T(8,128)(2,1)S(1)}, bf16[256,1536]{0,1:T(8,128)(2,1)}, u32[]{:S(2)}) copy-start(bf16[256,1536]{0,1:T(8,128)(2,1)} %copy-done.8) | copy-start | bytes 2359300
  66.2 9.2 %copy-start.46 = (pred[256,256]{0,1:T(8,128)(4,1)S(1)}, pred[256,256]{0,1:T(8,128)(4,1)}, u32[]{:S(2)}) copy-start(pred[256,256]{0,1:T(8,128)(4,1)} %broadcast_in_dim.176) | copy-start | bytes 196612
  75.4 8.1 %copy-start.15 = (bf16[256,6,128]{2,0,1:T(8,128)(2,1)S(1)}, bf16[256,6,128]{2,0,1:T(8,128)(2,1)}, u32[]{:S(2)}) copy-start(bf16[256,6,128]{2,0,1:T(8,128)(2,1)} %copy.272) | copy-start | bytes 1179652
  78.6 6.5 %copy-start.32 = (bf16[256,1536]{0,1:T(8,128)(2,1)S(1)}, bf16[256,1536]{0,1:T(8,128)(2,1)}, u32[]{:S(2)}) copy-start(bf16[256,1536]{0,1:T(8,128)(2,1)} %copy-done.31) | copy-start | bytes 2359300
  78.6 6.5 %copy-start.44 = (pred[256,512]{0,1:T(8,128)(4,1)S(1)}, pred[256,512]{0,1:T(8,128)(4,1)}, u32[]{:S(2)}) copy-start(pred[256,512]{0,1:T(8,128)(4,1)} %broadcast_in_dim.166) | copy-start | bytes 393220
  78.6 6.5 %copy-start.48 = (bf16[256,6,128]{2,0,1:T(8,128)(2,1)S(1)}, bf16[256,6,128]{2,0,1:T(8,128)(2,1)}, u32[]{:S(2)}) copy-start(bf16[256,6,128]{2,0,1:T(8,128)(2,1)} %copy.265) | copy-start | bytes 1179652
  78.6 6.5 %copy-start.50 = (bf16[256,6,128]{2,0,1:T(8,128)(2,1)S(1)}, bf16[256,6,128]{2,0,1:T(8,128)(2,1)}, u32[]{:S(2)}) copy-start(bf16[256,6,128]{2,0,1:T(8,128)(2,1)} %copy.266) | copy-start | bytes 1179652
  78.6 21.6 %collective-permute-start.9 = (f32[3,6,256]{2,1,0:T(8,128)S(1)}, f32[3,6,256]{2,1,0:T(8,128)S(1)}, u32[]{:S(2)}, u32[]{:S(2)}) collective-permute-start(f32[3,6,256]{2,1,0:T(8,128)S(1)} %pad_maximum_fusion.12), channel_id=1, source_target_pairs={{1,3},{2,0},{3,5},{4,2},{5,7},{6,4},{7,9},{8,6},{9,11},{10,8},{11,... | collective-permute-start | bytes 55304 | tf_op jit(solution)/shard_map/ppermute | solution.py:24
  85.8 3.9 %copy-start.36 = (f32[6,512,256]{2,1,0:T(8,128)}, f32[6,512,256]{2,1,0:T(8,128)S(1)}, u32[]{:S(2)}) copy-start(f32[6,512,256]{2,1,0:T(8,128)S(1)} %get-tuple-element.149) | copy-start | bytes 9437188
  93.2 5.1 %copy-start.43 = (f32[6,512,256]{2,1,0:T(8,128)}, f32[6,512,256]{2,1,0:T(8,128)S(1)}, u32[]{:S(2)}) copy-start(f32[6,512,256]{2,1,0:T(8,128)S(1)} %get-tuple-element.143) | copy-start | bytes 9437188
  98.3 6.6 %collective-permute-start.5 = (f32[3,6,256]{2,1,0:T(8,128)S(1)}, f32[3,6,256]{2,1,0:T(8,128)S(1)}, u32[]{:S(2)}, u32[]{:S(2)}) collective-permute-start(f32[3,6,256]{2,1,0:T(8,128)S(1)} %pad_maximum_fusion.11), channel_id=1, source_target_pairs={{0,2},{2,4},{3,1},{4,6},{5,3},{6,8},{7,5},{8,10},{9,7},{10,12},{11... | collective-permute-start | bytes 55304 | tf_op jit(solution)/shard_map/ppermute | solution.py:24
  105.6 12.6 %collective-permute-start.10 = (f32[2,6,256]{2,1,0:T(8,128)}, f32[2,6,256]{2,1,0:T(8,128)}, u32[]{:S(2)}, u32[]{:S(2)}) collective-permute-start(f32[2,6,256]{2,1,0:T(8,128)} %pad_maximum_fusion.15), channel_id=1, source_target_pairs={{1,3},{2,0},{3,5},{4,2},{5,7},{6,4},{7,9},{8,6},{9,11},{10,8},{11,... | collective-permute-start | bytes 36872 | tf_op jit(solution)/shard_map/ppermute | solution.py:24
  109.5 16.5 %collective-permute-start.18 = (bf16[256,6,128]{2,0,1:T(8,128)(2,1)}, bf16[256,6,128]{2,0,1:T(8,128)(2,1)}, u32[]{:S(2)}, u32[]{:S(2)}) collective-permute-start(bf16[256,6,128]{2,0,1:T(8,128)(2,1)} %copy.274), channel_id=1, source_target_pairs={{0,2},{2,4},{3,1},{4,6},{5,3},{6,8},{7,5},{8,10},{9,7},{10,12},{11... | collective-permute-start | bytes 1179656 | tf_op jit(solution)/shard_map/ppermute | solution.py:24
  115.3 10.1 %collective-permute-start.11 = (f32[2,6,256]{2,1,0:T(8,128)}, f32[2,6,256]{2,1,0:T(8,128)S(1)}, u32[]{:S(2)}, u32[]{:S(2)}) collective-permute-start(f32[2,6,256]{2,1,0:T(8,128)} %pad_maximum_fusion.15), channel_id=1, source_target_pairs={{0,2},{2,4},{3,1},{4,6},{5,3},{6,8},{7,5},{8,10},{9,7},{10,12},{11... | collective-permute-start | bytes 36872 | tf_op jit(solution)/shard_map/ppermute | solution.py:24
  118.9 6.5 %copy-start.49 = (bf16[256,6,128]{2,0,1:T(8,128)(2,1)S(1)}, bf16[256,6,128]{2,0,1:T(8,128)(2,1)}, u32[]{:S(2)}) copy-start(bf16[256,6,128]{2,0,1:T(8,128)(2,1)} %copy.265) | copy-start | bytes 1179652
  118.9 6.5 %copy-start.51 = (bf16[256,6,128]{2,0,1:T(8,128)(2,1)S(1)}, bf16[256,6,128]{2,0,1:T(8,128)(2,1)}, u32[]{:S(2)}) copy-start(bf16[256,6,128]{2,0,1:T(8,128)(2,1)} %copy.266) | copy-start | bytes 1179652
  118.9 7.0 %copy-start.5 = (f32[6,256,256]{1,2,0:T(8,128)S(1)}, f32[6,256,256]{1,2,0:T(8,128)}, u32[]{:S(2)}) copy-start(f32[6,256,256]{1,2,0:T(8,128)} %copy-done.4) | copy-start | bytes 4718596
  118.9 7.0 %copy-start.17 = (f32[6,256,256]{1,2,0:T(8,128)S(1)}, f32[6,256,256]{1,2,0:T(8,128)}, u32[]{:S(2)}) copy-start(f32[6,256,256]{1,2,0:T(8,128)} %get-tuple-element.147) | copy-start | bytes 4718596
  127.0 4.2 %copy-start.37 = (f32[6,512,256]{2,1,0:T(8,128)S(1)}, f32[6,512,256]{2,1,0:T(8,128)}, u32[]{:S(2)}) copy-start(f32[6,512,256]{2,1,0:T(8,128)} %copy-done.36) | copy-start | bytes 9437188
  132.2 27.2 %copy-start.52 = (f32[512,6,128]{0,2,1:T(8,128)}, f32[512,6,128]{0,2,1:T(8,128)S(1)}, u32[]{:S(2)}) copy-start(f32[512,6,128]{0,2,1:T(8,128)S(1)} %fusion.35) | copy-start | bytes 4718596
  138.9 15.2 %copy-start.18 = (f32[512,6,128]{0,2,1:T(8,128)}, f32[512,6,128]{0,2,1:T(8,128)S(1)}, u32[]{:S(2)}) copy-start(f32[512,6,128]{0,2,1:T(8,128)S(1)} %multiply_bitcast_fusion.2) | copy-start | bytes 4718596
  139.0 18.1 %collective-permute-start.16 = (f32[3,6,256]{2,1,0:T(8,128)S(1)}, f32[3,6,256]{2,1,0:T(8,128)S(1)}, u32[]{:S(2)}, u32[]{:S(2)}) collective-permute-start(f32[3,6,256]{2,1,0:T(8,128)S(1)} %pad_maximum_fusion.13), channel_id=1, source_target_pairs={{0,2},{2,4},{3,1},{4,6},{5,3},{6,8},{7,5},{8,10},{9,7},{10,12},{11... | collective-permute-start | bytes 55304 | tf_op jit(solution)/shard_map/ppermute | solution.py:24
  142.9 14.2 %collective-permute-start.19 = (f32[3,6,256]{2,1,0:T(8,128)S(1)}, f32[3,6,256]{2,1,0:T(8,128)S(1)}, u32[]{:S(2)}, u32[]{:S(2)}) collective-permute-start(f32[3,6,256]{2,1,0:T(8,128)S(1)} %pad_maximum_fusion.14), channel_id=1, source_target_pairs={{1,3},{2,0},{3,5},{4,2},{5,7},{6,4},{7,9},{8,6},{9,11},{10,8},{11,... | collective-permute-start | bytes 55304 | tf_op jit(solution)/shard_map/ppermute | solution.py:24
  145.7 41.5 %collective-permute-start.12 = (bf16[256,6,128]{0,2,1:T(8,128)(2,1)S(1)}, bf16[256,6,128]{0,2,1:T(8,128)(2,1)S(1)}, u32[]{:S(2)}, u32[]{:S(2)}) collective-permute-start(bf16[256,6,128]{0,2,1:T(8,128)(2,1)S(1)} %fusion.53), channel_id=1, source_target_pairs={{0,2},{2,4},{3,1},{4,6},{5,3},{6,8},{7,5},{8,10},{9,7},{10,12},{11... | collective-permute-start | bytes 1179656 | tf_op jit(solution)/shard_map/ppermute | solution.py:24
  148.8 38.5 %collective-permute-start.13 = (bf16[256,6,128]{0,2,1:T(8,128)(2,1)S(1)}, bf16[256,6,128]{0,2,1:T(8,128)(2,1)S(1)}, u32[]{:S(2)}, u32[]{:S(2)}) collective-permute-start(bf16[256,6,128]{0,2,1:T(8,128)(2,1)S(1)} %fusion.43), channel_id=1, source_target_pairs={{1,3},{2,0},{3,5},{4,2},{5,7},{6,4},{7,9},{8,6},{9,11},{10,8},{11,... | collective-permute-start | bytes 1179656 | tf_op jit(solution)/shard_map/ppermute | solution.py:24
  154.2 11.2 %copy-start.22 = (f32[512,6,128]{0,2,1:T(8,128)}, f32[512,6,128]{0,2,1:T(8,128)S(1)}, u32[]{:S(2)}) copy-start(f32[512,6,128]{0,2,1:T(8,128)S(1)} %multiply_bitcast_fusion.3) | copy-start | bytes 4718596
  155.4 40.8 %collective-permute-start.24 = (f32[256,6,128]{0,2,1:T(8,128)}, f32[256,6,128]{0,2,1:T(8,128)}, u32[]{:S(2)}, u32[]{:S(2)}) collective-permute-start(f32[256,6,128]{0,2,1:T(8,128)} %slice_add_fusion.6), channel_id=1, source_target_pairs={{0,1},{1,0},{2,3},{3,2},{4,5},{5,4},{6,7},{7,6},{8,9},{9,8},{10,11... | collective-permute-start | bytes 2359304 | tf_op jit(solution)/shard_map/ppermute | solution.py:24
  157.1 8.3 %copy-start.20 = (f32[512,6,128]{0,2,1:T(8,128)}, f32[512,6,128]{0,2,1:T(8,128)S(1)}, u32[]{:S(2)}) copy-start(f32[512,6,128]{0,2,1:T(8,128)S(1)} %convolution_bitcast_fusion.1) | copy-start | bytes 4718596
  157.2 8.1 %collective-permute-start.21 = (f32[2,6,256]{2,1,0:T(8,128)S(1)}, f32[2,6,256]{2,1,0:T(8,128)S(1)}, u32[]{:S(2)}, u32[]{:S(2)}) collective-permute-start(f32[2,6,256]{2,1,0:T(8,128)S(1)} %pad_maximum_fusion.16), channel_id=1, source_target_pairs={{0,2},{2,4},{3,1},{4,6},{5,3},{6,8},{7,5},{8,10},{9,7},{10,12},{11... | collective-permute-start | bytes 36872 | tf_op jit(solution)/shard_map/ppermute | solution.py:24
  160.4 7.2 %collective-permute-start.20 = (f32[2,6,256]{2,1,0:T(8,128)S(1)}, f32[2,6,256]{2,1,0:T(8,128)S(1)}, u32[]{:S(2)}, u32[]{:S(2)}) collective-permute-start(f32[2,6,256]{2,1,0:T(8,128)S(1)} %pad_maximum_fusion.16), channel_id=1, source_target_pairs={{1,3},{2,0},{3,5},{4,2},{5,7},{6,4},{7,9},{8,6},{9,11},{10,8},{11,... | collective-permute-start | bytes 36872 | tf_op jit(solution)/shard_map/ppermute | solution.py:24
  171.2 14.9 %copy-start.29 = (f32[512,6,128]{0,2,1:T(8,128)}, f32[512,6,128]{0,2,1:T(8,128)S(1)}, u32[]{:S(2)}) copy-start(f32[512,6,128]{0,2,1:T(8,128)S(1)} %fusion.32) | copy-start | bytes 4718596
  174.4 10.4 %copy-start.25 = (f32[512,6,128]{0,2,1:T(8,128)}, f32[512,6,128]{0,2,1:T(8,128)S(1)}, u32[]{:S(2)}) copy-start(f32[512,6,128]{0,2,1:T(8,128)S(1)} %multiply_bitcast_fusion) | copy-start | bytes 4718596
  174.4 20.1 %collective-permute-start.22 = (bf16[256,6,128]{0,2,1:T(8,128)(2,1)S(1)}, bf16[256,6,128]{0,2,1:T(8,128)(2,1)S(1)}, u32[]{:S(2)}, u32[]{:S(2)}) collective-permute-start(bf16[256,6,128]{0,2,1:T(8,128)(2,1)S(1)} %fusion.51), channel_id=1, source_target_pairs={{0,2},{2,4},{3,1},{4,6},{5,3},{6,8},{7,5},{8,10},{9,7},{10,12},{11... | collective-permute-start | bytes 1179656 | tf_op jit(solution)/shard_map/ppermute | solution.py:24
  178.8 16.1 %collective-permute-start.23 = (bf16[256,6,128]{0,2,1:T(8,128)(2,1)S(1)}, bf16[256,6,128]{0,2,1:T(8,128)(2,1)S(1)}, u32[]{:S(2)}, u32[]{:S(2)}) collective-permute-start(bf16[256,6,128]{0,2,1:T(8,128)(2,1)S(1)} %fusion.42), channel_id=1, source_target_pairs={{1,3},{2,0},{3,5},{4,2},{5,7},{6,4},{7,9},{8,6},{9,11},{10,8},{11,... | collective-permute-start | bytes 1179656 | tf_op jit(solution)/shard_map/ppermute | solution.py:24
  187.2 11.9 %collective-permute-start.26 = (f32[256,6,128]{0,2,1:T(8,128)}, f32[256,6,128]{0,2,1:T(8,128)}, u32[]{:S(2)}, u32[]{:S(2)}) collective-permute-start(f32[256,6,128]{0,2,1:T(8,128)} %slice_add_fusion.2), channel_id=1, source_target_pairs={{0,1},{1,0},{2,3},{3,2},{4,5},{5,4},{6,7},{7,6},{8,9},{9,8},{10,11... | collective-permute-start | bytes 2359304 | tf_op jit(solution)/shard_map/ppermute | solution.py:24
  187.2 13.8 %collective-permute-start.25 = (f32[256,6,128]{0,2,1:T(8,128)}, f32[256,6,128]{0,2,1:T(8,128)}, u32[]{:S(2)}, u32[]{:S(2)}) collective-permute-start(f32[256,6,128]{0,2,1:T(8,128)} %slice_add_fusion.4), channel_id=1, source_target_pairs={{0,1},{1,0},{2,3},{3,2},{4,5},{5,4},{6,7},{7,6},{8,9},{9,8},{10,11... | collective-permute-start | bytes 2359304 | tf_op jit(solution)/shard_map/ppermute | solution.py:24
  194.5 12.2 %collective-permute-start.27 = (f32[256,6,128]{0,2,1:T(8,128)}, f32[256,6,128]{0,2,1:T(8,128)}, u32[]{:S(2)}, u32[]{:S(2)}) collective-permute-start(f32[256,6,128]{0,2,1:T(8,128)} %slice_add_fusion), channel_id=1, source_target_pairs={{0,1},{1,0},{2,3},{3,2},{4,5},{5,4},{6,7},{7,6},{8,9},{9,8},{10,11... | collective-permute-start | bytes 2359304 | tf_op jit(solution)/shard_map/ppermute | solution.py:24
  (35 other events, 66.7 us)

commit v5 on v3

v5 whole, which is shorter than its diff:
```python
import jax
import jax.numpy as jnp
import numpy as np
from jax import lax
from jax.experimental import pallas as pl
from jax.experimental.pallas import tpu as pltpu
from jax.sharding import PartitionSpec as P

HEADS = 12
HDIM = 128
BLOCK = 64
REACH = 2
FRAMES = 2
BANDS = 2
NEG = -1e30
LIST_ROWS = 16


def permute(value, rule):
    count = lax.axis_size("tm")
    pairs = []
    for source in range(count):
        target = rule(source)
        if 0 <= target < count:
            pairs.append((source, target))
    return lax.ppermute(value, "tm", pairs)


def swap_cores(value):
    return permute(value, lambda s: s ^ 1)


def down_even(value):
    return permute(value, lambda s: s - 2 if s % 2 == 0 else s + 2)


def up_even(value):
    return permute(value, lambda s: s + 2 if s % 2 == 0 else s - 2)


def pick_table(offset):
    blocks = FRAMES * BANDS
    slot = REACH - offset
    table = np.zeros((blocks, 30, blocks), np.float32)
    own = np.zeros((blocks, blocks), bool)
    if abs(offset) <= REACH:
        for qb in range(blocks):
            for kb in range(blocks):
                cand = (slot * FRAMES + kb // BANDS) * 3 + kb % BANDS - qb % BANDS + 1
                table[qb, cand, kb] = 1.0
                own[qb, kb] = offset == 0 and qb == kb
    return table, own


def parity_tables(even, even_offsets, odd_offsets):
    tables, owns = [], []
    for off_e, off_o in zip(even_offsets, odd_offsets):
        t_e, o_e = pick_table(off_e)
        t_o, o_o = pick_table(off_o)
        tables.append(jnp.where(even, jnp.asarray(t_e), jnp.asarray(t_o)))
        owns.append(jnp.where(even, jnp.asarray(o_e), jnp.asarray(o_o)))
    return jnp.concatenate(tables, axis=2), jnp.concatenate(owns, axis=1)


SCALE = HDIM ** (-0.5)
NT = (((1,), (1,)), ((), ()))


def slot_scores(q_ref, g_ref, k_ref, v_ref):
    q = q_ref[...]
    g = g_ref[...]
    s = lax.dot_general(k_ref[...], q, NT, preferred_element_type=jnp.float32) * SCALE
    dp = lax.dot_general(v_ref[...], g, NT, preferred_element_type=jnp.float32)
    return q, g, s, dp


def stats_kernel(q_ref, g_ref, k_ref, v_ref, m_ref, out_ref):
    _, _, s, dp = slot_scores(q_ref, g_ref, k_ref, v_ref)
    m = m_ref[...] > 0
    masked = jnp.where(m, s, NEG)
    mx = jnp.max(masked, axis=0, keepdims=True)
    e = jnp.where(m, jnp.exp(masked - mx), 0.0)
    total = jnp.sum(e, axis=0, keepdims=True)
    dot = jnp.sum(e * dp, axis=0, keepdims=True)
    out_ref[0] = jnp.concatenate([mx, total, dot], axis=0)


def back_kernel(q_ref, g_ref, k_ref, v_ref, m_ref, f_ref, dq_ref, dk_ref, dv_ref):
    q, g, s, dp = slot_scores(q_ref, g_ref, k_ref, v_ref)
    m = m_ref[...] > 0
    fin = f_ref[0]
    p = jnp.where(m, jnp.exp(s - fin[0:1]), 0.0)
    ds = (p * (dp - fin[1:2])).astype(jnp.bfloat16)
    dk_ref[...] = jnp.dot(ds, q, preferred_element_type=jnp.float32) * SCALE
    dv_ref[...] = jnp.dot(p.astype(jnp.bfloat16), g, preferred_element_type=jnp.float32)
    dq = lax.dot_general(ds, k_ref[...], (((0,), (0,)), ((), ())), preferred_element_type=jnp.float32)
    dq_ref[...] = (dq * SCALE).astype(dq_ref.dtype)


def slot_specs(q_rows, g_rows, nk, tok):
    return [
        pl.BlockSpec((tok, HDIM), lambda h: (q_rows, h)),
        pl.BlockSpec((tok, HDIM), lambda h: (g_rows, h)),
        pl.BlockSpec((nk, HDIM), lambda h: (0, h)),
        pl.BlockSpec((nk, HDIM), lambda h: (0, h)),
        pl.BlockSpec((nk, tok), lambda h: (0, 0)),
    ]


def slot_stats(q_arr, g_arr, q_rows, g_rows, key_arr, value_arr, mask_t, tok):
    nk = key_arr.shape[0]
    flops = 4 * tok * nk * HDIM * HEADS
    return pl.pallas_call(
        stats_kernel,
        grid=(HEADS,),
        in_specs=slot_specs(q_rows, g_rows, nk, tok),
        out_specs=pl.BlockSpec((1, 3, tok), lambda h: (h, 0, 0)),
        out_shape=jax.ShapeDtypeStruct((HEADS, 3, tok), jnp.float32),
        cost_estimate=pl.CostEstimate(
            flops=flops, transcendentals=tok * nk * HEADS, bytes_accessed=4 * (tok + nk) * HDIM * HEADS
        ),
    )(q_arr, g_arr, key_arr, value_arr, mask_t)


def slot_back(q_arr, g_arr, q_rows, g_rows, key_arr, value_arr, mask_t, fin, tok, dq_type):
    nk = key_arr.shape[0]
    width = HEADS * HDIM
    flops = 10 * tok * nk * HDIM * HEADS
    return pl.pallas_call(
        back_kernel,
        grid=(HEADS,),
        in_specs=slot_specs(q_rows, g_rows, nk, tok)
        + [pl.BlockSpec((1, 2, tok), lambda h: (h, 0, 0))],
        out_specs=[
            pl.BlockSpec((tok, HDIM), lambda h: (0, h)),
            pl.BlockSpec((nk, HDIM), lambda h: (0, h)),
            pl.BlockSpec((nk, HDIM), lambda h: (0, h)),
        ],
        out_shape=[
            jax.ShapeDtypeStruct((tok, width), dq_type),
            jax.ShapeDtypeStruct((nk, width), jnp.float32),
            jax.ShapeDtypeStruct((nk, width), jnp.float32),
        ],
        cost_estimate=pl.CostEstimate(
            flops=flops, transcendentals=tok * nk * HEADS, bytes_accessed=12 * (tok + nk) * HDIM * HEADS
        ),
    )(q_arr, g_arr, key_arr, value_arr, mask_t, fin)


def local(queries, keys, values, grad_out, block_list):
    groups = lax.axis_size("tm")
    here = lax.axis_index("tm")
    even = here % 2 == 0
    up = jnp.where(even, 1, -1)
    tok, width = queries.shape
    blocks = FRAMES * BANDS
    cands = block_list.shape[1]

    flags = (block_list > 0).astype(jnp.bfloat16).reshape(1, blocks * cands)
    flags = jnp.pad(flags, ((0, LIST_ROWS - 1), (0, width - blocks * cands)))
    pack = jnp.concatenate([queries, grad_out, flags], axis=0)

    far_data = down_even(pack)
    near_data = up_even(pack)
    partner_keys, partner_values = swap_cores((keys, values))
    key_both = jnp.concatenate([keys, partner_keys], axis=0)
    value_both = jnp.concatenate([values, partner_values], axis=0)

    slots = {
        "own": (queries, grad_out, 0, 0, block_list, 0, True, (0, -1), (0, 1)),
        "far": (far_data, far_data, 0, 1, None, 2 * up, True, (2, 1), (-2, -1)),
        "near": (near_data, near_data, 0, 1, None, -2 * up, False, (-2,), (2,)),
    }

    args = {}
    stats_out = {}
    for name, (q_arr, g_arr, q_rows, g_rows, rows, q_off, both, offs_e, offs_o) in slots.items():
        if rows is None:
            rows = q_arr[2 * tok, : blocks * cands].reshape(blocks, cands)
        key_arr, value_arr = (key_both, value_both) if both else (keys, values)
        nkb = key_arr.shape[0] // BLOCK
        source = here + q_off
        valid = (source >= 0) & (source < groups)
        table, own = parity_tables(even, offs_e, offs_o)
        chosen = jnp.einsum("qc,qck->qk", (rows > 0).astype(jnp.float32), table) > 0
        mask4 = (chosen & valid) | own
        mask_t = jnp.broadcast_to(
            mask4.T[:, None, :, None], (nkb, BLOCK, blocks, BLOCK)
        ).reshape(nkb * BLOCK, tok).astype(jnp.float32)
        args[name] = (q_arr, g_arr, q_rows, g_rows, key_arr, value_arr, mask_t)
        stats_out[name] = slot_stats(*args[name], tok)

    stats_in = [
        (stats_out["own"], 0),
        (up_even(stats_out["far"]), -2 * up),
        (down_even(stats_out["near"]), 2 * up),
    ]
    maxes, sums, dots = [], [], []
    for stats, offset in stats_in:
        source = here + offset
        valid = (source >= 0) & (source < groups)
        maxes.append(jnp.where(valid, stats[:, 0], NEG))
        sums.append(jnp.where(valid, stats[:, 1], 0.0))
        dots.append(jnp.where(valid, stats[:, 2], 0.0))
    maxes, sums, dots = jnp.stack(maxes), jnp.stack(sums), jnp.stack(dots)
    top = jnp.max(maxes, axis=0)
    scale = jnp.exp(maxes - top[None])
    total = jnp.sum(sums * scale, axis=0)
    log_total = top + jnp.log(total)
    deltas = jnp.sum(dots * scale, axis=0) / total
    final = jnp.stack([log_total, deltas], axis=1)
    finals = {"far": down_even(final), "near": up_even(final)}

    far_q, far_k, far_v = slot_back(*args["far"], finals["far"], tok, jnp.bfloat16)
    near_q, near_k, near_v = slot_back(*args["near"], finals["near"], tok, jnp.bfloat16)
    far_q, near_q, far_k, far_v, near_k, near_v, own_final = lax.optimization_barrier(
        (far_q, near_q, far_k, far_v, near_k, near_v, final)
    )
    from_far = up_even(far_q)
    from_near = down_even(near_q)
    own_q, own_k, own_v = slot_back(*args["own"], own_final, tok, jnp.float32)

    back_kg, back_vg = swap_cores((far_k[tok:] + own_k[tok:], far_v[tok:] + own_v[tok:]))
    key_grad = far_k[:tok] + own_k[:tok] + near_k + back_kg
    value_grad = far_v[:tok] + own_v[:tok] + near_v + back_vg
    query_grad = own_q + from_far.astype(jnp.float32) + from_near.astype(jnp.float32)
    return (
        query_grad.astype(jnp.bfloat16),
        key_grad.astype(jnp.bfloat16),
        value_grad.astype(jnp.bfloat16),
    )


def solution(mesh):
    placed = (
        P(("group", "tm"), None),
        P(("group", "tm"), None),
        P(("group", "tm"), None),
        P(("group", "tm"), None),
        P(("group", "tm"), None),
    )
    return jax.shard_map(
        local,
        mesh=mesh,
        in_specs=placed,
        out_specs=(P(("group", "tm"), None), P(("group", "tm"), None), P(("group", "tm"), None)),
        check_vma=False,
    )
```

time: 194 us -> 207 us (1.067)
  Pallas kernels: 0 us -> 65.6 us
  matrix products: 35.9 us -> 0.37 us
  local copies, waits for them, and re-layouts: 30.5 us -> 17 us
  other arithmetic: 22.6 us -> 11.9 us
  waiting for transfers between devices: 73.8 us -> 80.7 us
    pallas_call x0 -> x6, Pallas kernels: none -> 65.6 us  [the longest x3 35 us: slot_back(): pl.pallas_call(back_kernel, grid=(HEADS,), in_specs=slot_specs(q_rows, g_...]
    dot_general x18 -> x3, matrix products: 35.9 us -> 0.37 us  [local(): chosen = jnp.einsum('qc,qck->qk', (rows > 0).astype(jnp.float32), table) > 0]
    unnamed x73 -> x46, local copies, waits for them, and re-layouts: 20.3 us -> 7.06 us
    convert_element_type x4 -> x6, other arithmetic: 12.9 us -> 4.11 us  [the longest x1 1.45 us: local(): value_grad.astype(jnp.bfloat16)]
    ppermute x12, waiting for transfers between devices: 73.8 us -> 80.7 us  [permute(): return lax.ppermute(value, 'tm', pairs)]
    slice x4 -> x1, local copies, waits for them, and re-layouts: 6.33 us -> 0.94 us  [local(): dots.append(jnp.where(valid, stats[:, 2], 0.0))]
    convert_element_type x0 -> x3, local copies, waits for them, and re-layouts: none -> 3.86 us  [local(): mask_t = jnp.broadcast_to(mask4.T[:, None, :, None], (nkb, BLOCK, blocks,...]
    concatenate x2 -> x0, other arithmetic: 3.29 us -> none  [the longest x1 1.81 us: local(): jnp.concatenate([keys, partner_keys], axis=0).reshape(2 * tok, HEADS, HDIM)]
  transfers between devices with their start and end apart: 12 -> 12, of which waited for: 3 -> 4; matrix products, arithmetic and copies ran while one was open for 29% -> 9% of each run, Pallas kernels for 0% -> 20%
where the time goes in v5:
time: 207 us; the launch traced here: 204 us
  waiting for transfers between devices  80.7 us (39%)
  Pallas kernels  65.6 us (32%)
  starting transfers between devices  27.2 us (13%)
  local copies, waits for them, and re-layouts  17 us (8%)
  other arithmetic  11.9 us (6%)
    ppermute x12, waiting for transfers between devices, permute(): return lax.ppermute(value, 'tm', pairs)  80.7 us
    pallas_call x3, Pallas kernels, slot_back(): pl.pallas_call(back_kernel, grid=(HEADS,), in_specs=slot_specs(q_rows, g_...  35 us
    pallas_call x3, Pallas kernels, slot_stats(): pl.pallas_call(stats_kernel, grid=(HEADS,), in_specs=slot_specs(q_rows, g...  30.6 us
    ppermute x12, starting transfers between devices, permute(): return lax.ppermute(value, 'tm', pairs)  27.2 us
    unnamed x46, local copies, waits for them, and re-layouts  7.06 us
  transfers between devices with their start and end apart: 12, of which 4 were waited for; matrix products, arithmetic and copies ran while one was open for 9% of the time, Pallas kernels for 20%

profile of v5, /device:TPU:8, one launch (start us, length us, event | category | flops | bytes accessed | tf_op | source)
XLA Modules:
  0.0 203.9 jit_solution(5409829198067786674)
XLA Ops:
  0.6 0.7 broadcast_compare_fusion
  1.3 0.1 reshape.188
  1.4 0.0 copy-start.13
  1.4 0.0 copy-start.14
  1.4 0.0 copy-start.15
  1.5 0.0 copy-start.21
  1.5 0.0 copy-start.17
  1.5 2.7 %pad_maximum_fusion = bf16[528,1536]{1,0:T(8,128)(2,1)} fusion(bf16[16,1536]{1,0:T(8,128)(2,1)S(1)} %pad_convert_fusion, bf16[256,1536]{1,0:T(8,128)(2,1)} %g_ref.3, bf16[256,1536]{1,0:T(8,128)(2,1)} %q_ref.3), kind=kLoop, calls=%fused_computation | loop fusion | flops 4866048 | bytes 3244032 | tf_op jit(solution)/shard_map/concatenate | solution.py:161
  4.2 3.4 %collective-permute-start.4 = (bf16[528,1536]{1,0:T(8,128)(2,1)}, bf16[528,1536]{1,0:T(8,128)(2,1)S(1)}, u32[]{:S(2)}, u32[]{:S(2)}) collective-permute-start(bf16[528,1536]{1,0:T(8,128)(2,1)} %pad_maximum_fusion), channel_id=1, source_target_pairs={{0,2},{2,4},{3,1},{4,6},{5,3},{6,8},{7,5},{8,10},{9,7},{10,12},{11... | collective-permute-start | bytes 4866056 | tf_op jit(solution)/shard_map/ppermute | solution.py:26
  7.6 3.3 %collective-permute-start.2 = (bf16[528,1536]{1,0:T(8,128)(2,1)}, bf16[528,1536]{1,0:T(8,128)(2,1)}, u32[]{:S(2)}, u32[]{:S(2)}) collective-permute-start(bf16[528,1536]{1,0:T(8,128)(2,1)} %pad_maximum_fusion), channel_id=1, source_target_pairs={{1,3},{2,0},{3,5},{4,2},{5,7},{6,4},{7,9},{8,6},{9,11},{10,8},{11,... | collective-permute-start | bytes 4866056 | tf_op jit(solution)/shard_map/ppermute | solution.py:26
  11.0 0.1 collective-permute-start
  11.0 0.5 collective-permute-start.1
  11.6 0.1 fusion.7
  11.7 0.1 copy.41
  11.8 0.2 broadcast_in_dim.33
  12.0 1.4 convert_element_type.44.m_ref
  13.4 1.2 constant_dynamic-update-slice_fusion.1
  14.6 1.2 constant_dynamic-update-slice_fusion.3
  15.8 1.2 constant_dynamic-update-slice_fusion.k_ref
  17.0 1.2 copy-done.2
  18.2 1.2 constant_dynamic-update-slice_fusion.2.v_ref
  19.4 1.1 copy-done.1
  20.5 10.7 %shard_map.256 = f32[12,3,256]{2,1,0:T(4,128)} custom-call(bf16[256,1536]{1,0:T(8,128)(2,1)} %q_ref.3, bf16[256,1536]{1,0:T(8,128)(2,1)} %g_ref.3, bf16[512,1536]{1,0:T(8,128)(2,1)} %copy-done.2, bf16[512,1536]{1,0:T(8,128)(2,1)} %copy-done.1, f32[512,256]{1,0:T(8,128)} %convert_element_type.44.m_ref), custom_call_target="tpu_custom_call" | custom-call | flops 805306368 | bytes 4718592 | tf_op jit(solution)/shard_map/pallas_call | solution.py:113
  31.2 0.9 fusion.34
  32.2 46.0 %collective-permute-done.4.q_ref.g_ref = bf16[528,1536]{1,0:T(8,128)(2,1)S(1)} collective-permute-done((bf16[528,1536]{1,0:T(8,128)(2,1)}, bf16[528,1536]{1,0:T(8,128)(2,1)S(1)}, u32[]{:S(2)}, u32[]{:S(2)}) %collective-permute-start.4) | collective-permute-done | bytes 1622048 | tf_op jit(solution)/shard_map/ppermute | solution.py:26
  78.2 0.1 reshape.198
  78.3 0.1 fusion.22
  78.4 0.1 copy.45
  78.5 0.1 broadcast_in_dim.36
  78.7 1.0 convert_element_type.50.m_ref
  79.7 9.2 %shard_map.258 = f32[12,3,256]{2,1,0:T(4,128)} custom-call(bf16[528,1536]{1,0:T(8,128)(2,1)} %copy-done, bf16[528,1536]{1,0:T(8,128)(2,1)} %copy-done, bf16[256,1536]{1,0:T(8,128)(2,1)} %k_ref.3, bf16[256,1536]{1,0:T(8,128)(2,1)} %v_ref.3, f32[256,256]{1,0:T(8,128)} %convert_element_type.50.m_ref), custom_call_target="tpu_custom_call" | custom-call | flops 402653184 | bytes 3145728 | tf_op jit(solution)/shard_map/pallas_call | solution.py:113
  88.9 0.8 copy.36
  89.7 4.2 %collective-permute-start.5 = (f32[12,3,256]{2,0,1:T(8,128)S(1)}, f32[12,3,256]{2,0,1:T(8,128)S(1)}, u32[]{:S(2)}, u32[]{:S(2)}) collective-permute-start(f32[12,3,256]{2,0,1:T(8,128)S(1)} %copy.36), channel_id=1, source_target_pairs={{1,3},{2,0},{3,5},{4,2},{5,7},{6,4},{7,9},{8,6},{9,11},{10,8},{11,... | collective-permute-start | bytes 110600 | tf_op jit(solution)/shard_map/ppermute | solution.py:26
  93.9 0.7 compare_reduce_fusion.1
  94.6 0.1 reshape.196
  94.7 0.1 fusion.11
  94.8 0.1 copy.43
  94.9 0.1 convert_bitcast_fusion
  95.0 0.2 broadcast_in_dim.34
  95.2 1.4 convert_element_type.47.m_ref
  96.6 10.7 %shard_map.257 = f32[12,3,256]{2,1,0:T(4,128)} custom-call(bf16[528,1536]{1,0:T(8,128)(2,1)} %collective-permute-done.2.q_ref.g_ref, bf16[528,1536]{1,0:T(8,128)(2,1)} %collective-permute-done.2.q_ref.g_ref, bf16[512,1536]{1,0:T(8,128)(2,1)} %copy-done.2, bf16[512,1536]{1,0:T(8,128)(2,1)} %copy-done.1, f32[512,256]{1,0:T(8,128)} %convert_element_type.47.m_ref), custom_call_target="tpu_custom_call" | custom-call | flops 805306368 | bytes 4718592 | tf_op jit(solution)/shard_map/pallas_call | solution.py:113
  107.4 0.8 copy.35
  108.2 2.0 collective-permute-start.3
  110.2 4.8 %collective-permute-done.3 = f32[12,3,256]{2,0,1:T(8,128)S(1)} collective-permute-done((f32[12,3,256]{2,0,1:T(8,128)S(1)}, f32[12,3,256]{2,0,1:T(8,128)S(1)}, u32[]{:S(2)}, u32[]{:S(2)}) %collective-permute-start.3) | collective-permute-done | bytes 36896 | tf_op jit(solution)/shard_map/ppermute | solution.py:26
  115.2 1.9 collective-permute-start.7
  117.1 4.8 %collective-permute-start.6 = (f32[12,2,256]{2,1,0:T(2,128)S(1)}, f32[12,2,256]{2,1,0:T(2,128)S(1)}, u32[]{:S(2)}, u32[]{:S(2)}) collective-permute-start(f32[12,2,256]{2,1,0:T(2,128)S(1)} %pad_maximum_fusion.1.f_ref), channel_id=1, source_target_pairs={{1,3},{2,0},{3,5},{4,2},{5,7},{6,4},{7,9},{8,6},{9,11},{10,8},{11,... | collective-permute-start | bytes 73736 | tf_op jit(solution)/shard_map/ppermute | solution.py:26
  122.0 0.6 copy-done.10
  122.6 10.5 %shard_map.260 = (bf16[256,1536]{1,0:T(8,128)(2,1)}, f32[256,1536]{1,0:T(8,128)}, f32[256,1536]{1,0:T(8,128)}) custom-call(bf16[528,1536]{1,0:T(8,128)(2,1)} %copy-done, bf16[528,1536]{1,0:T(8,128)(2,1)} %copy-done, bf16[256,1536]{1,0:T(8,128)(2,1)} %k_ref.3, bf16[256,1536]{1,0:T(8,128)(2,1)} %v_ref.3, f32[256,256]{1,0:T(8,128)} %convert_element_type.50.m_ref, ...), custom_call_target="tpu_custom_call" | custom-call | flops 1006632960 | bytes 9437184 | tf_op jit(solution)/shard_map/pallas_call | solution.py:129
  133.1 0.6 copy-done.20
  133.7 12.1 %shard_map.259 = (bf16[256,1536]{1,0:T(8,128)(2,1)}, f32[512,1536]{1,0:T(8,128)}, f32[512,1536]{1,0:T(8,128)}) custom-call(bf16[528,1536]{1,0:T(8,128)(2,1)} %collective-permute-done.2.q_ref.g_ref, bf16[528,1536]{1,0:T(8,128)(2,1)} %collective-permute-done.2.q_ref.g_ref, bf16[512,1536]{1,0:T(8,128)(2,1)} %copy-done.2, bf16[512,1536]{1,0:T(8,128)(2,1)} %copy-done.1, ...), custom_call_target="tpu_custom_call" | custom-call | flops 2013265920 | bytes 14155776 | tf_op jit(solution)/shard_map/pallas_call | solution.py:129
  145.7 12.4 %shard_map.261 = (f32[256,1536]{1,0:T(8,128)}, f32[512,1536]{1,0:T(8,128)}, f32[512,1536]{1,0:T(8,128)}) custom-call(bf16[256,1536]{1,0:T(8,128)(2,1)} %q_ref.3, bf16[256,1536]{1,0:T(8,128)(2,1)} %g_ref.3, bf16[512,1536]{1,0:T(8,128)(2,1)} %copy-done.2, bf16[512,1536]{1,0:T(8,128)(2,1)} %copy-done.1, f32[512,256]{1,0:T(8,128)} %convert_element_type.44.m_ref, ...), custom_call_target="tpu_custom_call" | custom-call | flops 2013265920 | bytes 14155776 | tf_op jit(solution)/shard_map/pallas_call | solution.py:129
  158.2 1.8 slice_add_fusion
  159.9 0.1 collective-permute-start.11
  160.0 2.1 %collective-permute-start.8 = (bf16[256,1536]{1,0:T(8,128)(2,1)S(1)}, bf16[256,1536]{1,0:T(8,128)(2,1)S(1)}, u32[]{:S(2)}, u32[]{:S(2)}) collective-permute-start(bf16[256,1536]{1,0:T(8,128)(2,1)S(1)} %copy-done.19), channel_id=1, source_target_pairs={{0,2},{2,4},{3,1},{4,6},{5,3},{6,8},{7,5},{8,10},{9,7},{10,12},{11... | collective-permute-start | bytes 2359304 | tf_op jit(solution)/shard_map/ppermute | solution.py:26
  162.2 4.7 %collective-permute-start.9 = (bf16[256,1536]{1,0:T(8,128)(2,1)S(1)}, bf16[256,1536]{1,0:T(8,128)(2,1)S(1)}, u32[]{:S(2)}, u32[]{:S(2)}) collective-permute-start(bf16[256,1536]{1,0:T(8,128)(2,1)S(1)} %copy-done.18), channel_id=1, source_target_pairs={{1,3},{2,0},{3,5},{4,2},{5,7},{6,4},{7,9},{8,6},{9,11},{10,8},{11,... | collective-permute-start | bytes 2359304 | tf_op jit(solution)/shard_map/ppermute | solution.py:26
  167.0 1.8 slice_add_fusion.1
  168.8 0.1 collective-permute-start.10
  168.9 27.3 %collective-permute-done.8 = bf16[256,1536]{1,0:T(8,128)(2,1)S(1)} collective-permute-done((bf16[256,1536]{1,0:T(8,128)(2,1)S(1)}, bf16[256,1536]{1,0:T(8,128)(2,1)S(1)}, u32[]{:S(2)}, u32[]{:S(2)}) %collective-permute-start.8) | collective-permute-done | bytes 786464 | tf_op jit(solution)/shard_map/ppermute | solution.py:26
  196.2 2.5 %collective-permute-done.9 = bf16[256,1536]{1,0:T(8,128)(2,1)S(1)} collective-permute-done((bf16[256,1536]{1,0:T(8,128)(2,1)S(1)}, bf16[256,1536]{1,0:T(8,128)(2,1)S(1)}, u32[]{:S(2)}, u32[]{:S(2)}) %collective-permute-start.9) | collective-permute-done | bytes 786464 | tf_op jit(solution)/shard_map/ppermute | solution.py:26
  198.7 1.2 add_convert_fusion.2
  199.9 1.0 copy-done.6
  200.9 1.4 add_convert_fusion
  202.3 0.1 copy-done.7
  202.5 1.4 add_convert_fusion.1
  (58 shorter events, 0.3 us)
Async XLA Ops:
  1.4 10.1 %copy-start.12 = (s32[4,30]{1,0:T(4,128)S(1)}, s32[4,30]{1,0:T(4,128)}, u32[]{:S(2)}) copy-start(s32[4,30]{1,0:T(4,128)} %param.29) | copy-start | bytes 1444
  1.4 10.1 %copy-start.13 = (bf16[4,30,4]{1,2,0:T(4,128)(2,1)S(1)}, bf16[4,30,4]{1,2,0:T(4,128)(2,1)}, u32[]{:S(2)}) copy-start(bf16[4,30,4]{1,2,0:T(4,128)(2,1)} %constant.133) | copy-start | bytes 2884
  1.4 10.1 %copy-start.14 = (bf16[4,30,4]{1,2,0:T(4,128)(2,1)S(1)}, bf16[4,30,4]{1,2,0:T(4,128)(2,1)}, u32[]{:S(2)}) copy-start(bf16[4,30,4]{1,2,0:T(4,128)(2,1)} %constant.134) | copy-start | bytes 2884
  1.4 10.1 %copy-start.15 = (bf16[4,30,4]{1,2,0:T(4,128)(2,1)S(1)}, bf16[4,30,4]{1,2,0:T(4,128)(2,1)}, u32[]{:S(2)}) copy-start(bf16[4,30,4]{1,2,0:T(4,128)(2,1)} %constant.132) | copy-start | bytes 2884
  1.5 10.1 %copy-start.16 = (bf16[4,30,4]{1,2,0:T(4,128)(2,1)S(1)}, bf16[4,30,4]{1,2,0:T(4,128)(2,1)}, u32[]{:S(2)}) copy-start(bf16[4,30,4]{1,2,0:T(4,128)(2,1)} %constant.131) | copy-start | bytes 2884
  1.5 10.1 %copy-start.21 = (bf16[4,30,4]{1,2,0:T(4,128)(2,1)S(1)}, bf16[4,30,4]{1,2,0:T(4,128)(2,1)}, u32[]{:S(2)}) copy-start(bf16[4,30,4]{1,2,0:T(4,128)(2,1)} %constant.135) | copy-start | bytes 2884
  1.5 10.3 %copy-start.17 = (pred[4,8]{0,1:T(8,128)(4,1)S(1)}, pred[4,8]{0,1:T(8,128)(4,1)}, u32[]{:S(2)}) copy-start(pred[4,8]{0,1:T(8,128)(4,1)} %constant.62) | copy-start | bytes 100
  4.2 74.0 %collective-permute-start.4 = (bf16[528,1536]{1,0:T(8,128)(2,1)}, bf16[528,1536]{1,0:T(8,128)(2,1)S(1)}, u32[]{:S(2)}, u32[]{:S(2)}) collective-permute-start(bf16[528,1536]{1,0:T(8,128)(2,1)} %pad_maximum_fusion), channel_id=1, source_target_pairs={{0,2},{2,4},{3,1},{4,6},{5,3},{6,8},{7,5},{8,10},{9,7},{10,12},{11... | collective-permute-start | bytes 4866056 | tf_op jit(solution)/shard_map/ppermute | solution.py:26
  7.6 86.3 %collective-permute-start.2 = (bf16[528,1536]{1,0:T(8,128)(2,1)}, bf16[528,1536]{1,0:T(8,128)(2,1)}, u32[]{:S(2)}, u32[]{:S(2)}) collective-permute-start(bf16[528,1536]{1,0:T(8,128)(2,1)} %pad_maximum_fusion), channel_id=1, source_target_pairs={{1,3},{2,0},{3,5},{4,2},{5,7},{6,4},{7,9},{8,6},{9,11},{10,8},{11,... | collective-permute-start | bytes 4866056 | tf_op jit(solution)/shard_map/ppermute | solution.py:26
  11.0 4.9 %collective-permute-start = (bf16[256,1536]{1,0:T(8,128)(2,1)}, bf16[256,1536]{1,0:T(8,128)(2,1)}, u32[]{:S(2)}, u32[]{:S(2)}) collective-permute-start(bf16[256,1536]{1,0:T(8,128)(2,1)} %k_ref.3), channel_id=1, source_target_pairs={{0,1},{1,0},{2,3},{3,2},{4,5},{5,4},{6,7},{7,6},{8,9},{9,8},{10,11... | collective-permute-start | bytes 2359304 | tf_op jit(solution)/shard_map/ppermute | solution.py:26
  11.0 7.2 %collective-permute-start.1 = (bf16[256,1536]{1,0:T(8,128)(2,1)}, bf16[256,1536]{1,0:T(8,128)(2,1)}, u32[]{:S(2)}, u32[]{:S(2)}) collective-permute-start(bf16[256,1536]{1,0:T(8,128)(2,1)} %v_ref.3), channel_id=1, source_target_pairs={{0,1},{1,0},{2,3},{3,2},{4,5},{5,4},{6,7},{7,6},{8,9},{9,8},{10,11... | collective-permute-start | bytes 2359304 | tf_op jit(solution)/shard_map/ppermute | solution.py:26
  17.0 1.2 copy-start.2
  19.4 1.1 copy-start.1
  78.2 1.5 copy-start
  89.7 20.4 %collective-permute-start.5 = (f32[12,3,256]{2,0,1:T(8,128)S(1)}, f32[12,3,256]{2,0,1:T(8,128)S(1)}, u32[]{:S(2)}, u32[]{:S(2)}) collective-permute-start(f32[12,3,256]{2,0,1:T(8,128)S(1)} %copy.36), channel_id=1, source_target_pairs={{1,3},{2,0},{3,5},{4,2},{5,7},{6,4},{7,9},{8,6},{9,11},{10,8},{11,... | collective-permute-start | bytes 110600 | tf_op jit(solution)/shard_map/ppermute | solution.py:26
  108.2 6.9 %collective-permute-start.3 = (f32[12,3,256]{2,0,1:T(8,128)S(1)}, f32[12,3,256]{2,0,1:T(8,128)S(1)}, u32[]{:S(2)}, u32[]{:S(2)}) collective-permute-start(f32[12,3,256]{2,0,1:T(8,128)S(1)} %copy.35), channel_id=1, source_target_pairs={{0,2},{2,4},{3,1},{4,6},{5,3},{6,8},{7,5},{8,10},{9,7},{10,12},{11... | collective-permute-start | bytes 110600 | tf_op jit(solution)/shard_map/ppermute | solution.py:26
  115.2 30.5 %copy-start.11 = (f32[12,2,256]{2,1,0:T(2,128)}, f32[12,2,256]{2,1,0:T(2,128)S(1)}, u32[]{:S(2)}) copy-start(f32[12,2,256]{2,1,0:T(2,128)S(1)} %pad_maximum_fusion.1.f_ref) | copy-start | bytes 73732
  115.2 6.8 %collective-permute-start.7 = (f32[12,2,256]{2,1,0:T(2,128)S(1)}, f32[12,2,256]{2,1,0:T(2,128)S(1)}, u32[]{:S(2)}, u32[]{:S(2)}) collective-permute-start(f32[12,2,256]{2,1,0:T(2,128)S(1)} %pad_maximum_fusion.1.f_ref), channel_id=1, source_target_pairs={{0,2},{2,4},{3,1},{4,6},{5,3},{6,8},{7,5},{8,10},{9,7},{10,12},{11... | collective-permute-start | bytes 73736 | tf_op jit(solution)/shard_map/ppermute | solution.py:26
  117.1 15.9 %collective-permute-start.6 = (f32[12,2,256]{2,1,0:T(2,128)S(1)}, f32[12,2,256]{2,1,0:T(2,128)S(1)}, u32[]{:S(2)}, u32[]{:S(2)}) collective-permute-start(f32[12,2,256]{2,1,0:T(2,128)S(1)} %pad_maximum_fusion.1.f_ref), channel_id=1, source_target_pairs={{1,3},{2,0},{3,5},{4,2},{5,7},{6,4},{7,9},{8,6},{9,11},{10,8},{11,... | collective-permute-start | bytes 73736 | tf_op jit(solution)/shard_map/ppermute | solution.py:26
  122.0 0.6 copy-start.10
  133.1 0.6 copy-start.20
  145.7 12.4 %copy-start.4 = (f32[512,1536]{1,0:T(8,128)S(1)}, f32[512,1536]{1,0:T(8,128)}, u32[]{:S(2)}) copy-start(f32[512,1536]{1,0:T(8,128)} %get-tuple-element.32) | copy-start | bytes 9437188
  158.2 1.9 copy-start.19
  158.2 4.0 %copy-start.18 = (bf16[256,1536]{1,0:T(8,128)(2,1)S(1)}, bf16[256,1536]{1,0:T(8,128)(2,1)}, u32[]{:S(2)}) copy-start(bf16[256,1536]{1,0:T(8,128)(2,1)} %get-tuple-element.28) | copy-start | bytes 2359300
  158.2 8.8 %copy-start.3 = (f32[512,1536]{1,0:T(8,128)S(1)}, f32[512,1536]{1,0:T(8,128)}, u32[]{:S(2)}) copy-start(f32[512,1536]{1,0:T(8,128)} %get-tuple-element.29) | copy-start | bytes 9437188
  159.9 40.0 %collective-permute-start.11 = (f32[256,1536]{1,0:T(8,128)S(1)}, f32[256,1536]{1,0:T(8,128)S(1)}, u32[]{:S(2)}, u32[]{:S(2)}) collective-permute-start(f32[256,1536]{1,0:T(8,128)S(1)} %slice_add_fusion), channel_id=1, source_target_pairs={{0,1},{1,0},{2,3},{3,2},{4,5},{5,4},{6,7},{7,6},{8,9},{9,8},{10,11... | collective-permute-start | bytes 4718600 | tf_op jit(solution)/shard_map/ppermute | solution.py:26
  160.0 36.2 %collective-permute-start.8 = (bf16[256,1536]{1,0:T(8,128)(2,1)S(1)}, bf16[256,1536]{1,0:T(8,128)(2,1)S(1)}, u32[]{:S(2)}, u32[]{:S(2)}) collective-permute-start(bf16[256,1536]{1,0:T(8,128)(2,1)S(1)} %copy-done.19), channel_id=1, source_target_pairs={{0,2},{2,4},{3,1},{4,6},{5,3},{6,8},{7,5},{8,10},{9,7},{10,12},{11... | collective-permute-start | bytes 2359304 | tf_op jit(solution)/shard_map/ppermute | solution.py:26
  162.2 36.5 %collective-permute-start.9 = (bf16[256,1536]{1,0:T(8,128)(2,1)S(1)}, bf16[256,1536]{1,0:T(8,128)(2,1)S(1)}, u32[]{:S(2)}, u32[]{:S(2)}) collective-permute-start(bf16[256,1536]{1,0:T(8,128)(2,1)S(1)} %copy-done.18), channel_id=1, source_target_pairs={{1,3},{2,0},{3,5},{4,2},{5,7},{6,4},{7,9},{8,6},{9,11},{10,8},{11,... | collective-permute-start | bytes 2359304 | tf_op jit(solution)/shard_map/ppermute | solution.py:26
  166.9 31.8 %copy-start.9 = (f32[256,1536]{1,0:T(8,128)S(1)}, f32[256,1536]{1,0:T(8,128)}, u32[]{:S(2)}) copy-start(f32[256,1536]{1,0:T(8,128)} %get-tuple-element.26) | copy-start | bytes 4718596
  167.0 33.0 %copy-start.8 = (f32[256,1536]{1,0:T(8,128)S(1)}, f32[256,1536]{1,0:T(8,128)}, u32[]{:S(2)}) copy-start(f32[256,1536]{1,0:T(8,128)} %get-tuple-element.34) | copy-start | bytes 4718596
  168.8 33.6 %collective-permute-start.10 = (f32[256,1536]{1,0:T(8,128)S(1)}, f32[256,1536]{1,0:T(8,128)S(1)}, u32[]{:S(2)}, u32[]{:S(2)}) collective-permute-start(f32[256,1536]{1,0:T(8,128)S(1)} %slice_add_fusion.1), channel_id=1, source_target_pairs={{0,1},{1,0},{2,3},{3,2},{4,5},{5,4},{6,7},{7,6},{8,9},{9,8},{10,11... | collective-permute-start | bytes 4718600 | tf_op jit(solution)/shard_map/ppermute | solution.py:26
  198.7 2.2 %copy-start.6 = (f32[512,1536]{1,0:T(8,128)S(1)}, f32[512,1536]{1,0:T(8,128)}, u32[]{:S(2)}) copy-start(f32[512,1536]{1,0:T(8,128)} %get-tuple-element.33) | copy-start | bytes 9437188
  199.9 2.4 %copy-start.5 = (f32[512,1536]{1,0:T(8,128)S(1)}, f32[512,1536]{1,0:T(8,128)}, u32[]{:S(2)}) copy-start(f32[512,1536]{1,0:T(8,128)} %get-tuple-element.30) | copy-start | bytes 9437188
  199.9 2.6 %copy-start.7 = (f32[256,1536]{1,0:T(8,128)S(1)}, f32[256,1536]{1,0:T(8,128)}, u32[]{:S(2)}) copy-start(f32[256,1536]{1,0:T(8,128)} %get-tuple-element.31) | copy-start | bytes 4718596

commit v6 on v5

--- a/solution.py
+++ b/solution.py
@@ -211,14 +211,15 @@
     final = jnp.stack([log_total, deltas], axis=1)
     finals = {"far": down_even(final), "near": up_even(final)}
 
+    own_q, own_k, own_v = slot_back(*args["own"], final, tok, jnp.float32)
+    far_fin, near_fin, own_k, own_v = lax.optimization_barrier(
+        (finals["far"], finals["near"], own_k, own_v)
+    )
+    finals = {"far": far_fin, "near": near_fin}
     far_q, far_k, far_v = slot_back(*args["far"], finals["far"], tok, jnp.bfloat16)
     near_q, near_k, near_v = slot_back(*args["near"], finals["near"], tok, jnp.bfloat16)
-    far_q, near_q, far_k, far_v, near_k, near_v, own_final = lax.optimization_barrier(
-        (far_q, near_q, far_k, far_v, near_k, near_v, final)
-    )
     from_far = up_even(far_q)
     from_near = down_even(near_q)
-    own_q, own_k, own_v = slot_back(*args["own"], own_final, tok, jnp.float32)
 
     back_kg, back_vg = swap_cores((far_k[tok:] + own_k[tok:], far_v[tok:] + own_v[tok:]))
     key_grad = far_k[:tok] + own_k[:tok] + near_k + back_kg

time: 207 us -> 200 us (0.966)
  waiting for transfers between devices: 80.7 us -> 70.8 us
  other arithmetic: 11.9 us -> 16.1 us
    ppermute x12, waiting for transfers between devices: 80.7 us -> 70.8 us  [permute(): return lax.ppermute(value, 'tm', pairs)]
    unnamed x46 -> x42, local copies, waits for them, and re-layouts: 7.06 us -> 5.36 us
  transfers between devices with their start and end apart: 12 -> 12, of which waited for: 4 -> 4; matrix products, arithmetic and copies ran while one was open for 9% -> 11% of each run, Pallas kernels for 20% -> 27%
where the time goes in v6:
time: 200 us; the launch traced here: 196 us
  waiting for transfers between devices  70.8 us (35%)
  Pallas kernels  65.6 us (33%)
  starting transfers between devices  27.1 us (14%)
  other arithmetic  16.1 us (8%)
  local copies, waits for them, and re-layouts  15.3 us (8%)
    ppermute x12, waiting for transfers between devices, permute(): return lax.ppermute(value, 'tm', pairs)  70.8 us
    pallas_call x3, Pallas kernels, slot_back(): pl.pallas_call(back_kernel, grid=(HEADS,), in_specs=slot_specs(q_rows, g_...  34.9 us
    pallas_call x3, Pallas kernels, slot_stats(): pl.pallas_call(stats_kernel, grid=(HEADS,), in_specs=slot_specs(q_rows, g...  30.6 us
    ppermute x12, starting transfers between devices, permute(): return lax.ppermute(value, 'tm', pairs)  27.1 us
    unnamed x42, local copies, waits for them, and re-layouts  5.36 us
  transfers between devices with their start and end apart: 12, of which 4 were waited for; matrix products, arithmetic and copies ran while one was open for 11% of the time, Pallas kernels for 27%

profile of v6, /device:TPU:8, one launch (start us, length us, event | category | flops | bytes accessed | tf_op | source)
XLA Modules:
  0.0 196.3 jit_solution(7245221501763430999)
XLA Ops:
  0.6 0.7 broadcast_compare_fusion
  1.3 0.1 reshape.188
  1.4 0.0 copy-start.13
  1.4 0.0 copy-start.14
  1.4 0.0 copy-start.15
  1.5 0.0 copy-start.16
  1.5 0.0 copy-start.19
  1.5 0.0 copy-start.17
  1.5 2.7 %pad_maximum_fusion = bf16[528,1536]{1,0:T(8,128)(2,1)} fusion(bf16[16,1536]{1,0:T(8,128)(2,1)S(1)} %pad_convert_fusion, bf16[256,1536]{1,0:T(8,128)(2,1)} %g_ref.3, bf16[256,1536]{1,0:T(8,128)(2,1)} %q_ref.3), kind=kLoop, calls=%fused_computation | loop fusion | flops 4866048 | bytes 3244032 | tf_op jit(solution)/shard_map/concatenate | solution.py:161
  4.2 3.3 %collective-permute-start.2 = (bf16[528,1536]{1,0:T(8,128)(2,1)}, bf16[528,1536]{1,0:T(8,128)(2,1)}, u32[]{:S(2)}, u32[]{:S(2)}) collective-permute-start(bf16[528,1536]{1,0:T(8,128)(2,1)} %pad_maximum_fusion), channel_id=1, source_target_pairs={{1,3},{2,0},{3,5},{4,2},{5,7},{6,4},{7,9},{8,6},{9,11},{10,8},{11,... | collective-permute-start | bytes 4866056 | tf_op jit(solution)/shard_map/ppermute | solution.py:26
  7.5 2.5 %collective-permute-start.4 = (bf16[528,1536]{1,0:T(8,128)(2,1)}, bf16[528,1536]{1,0:T(8,128)(2,1)S(1)}, u32[]{:S(2)}, u32[]{:S(2)}) collective-permute-start(bf16[528,1536]{1,0:T(8,128)(2,1)} %pad_maximum_fusion), channel_id=1, source_target_pairs={{0,2},{2,4},{3,1},{4,6},{5,3},{6,8},{7,5},{8,10},{9,7},{10,12},{11... | collective-permute-start | bytes 4866056 | tf_op jit(solution)/shard_map/ppermute | solution.py:26
  10.1 0.2 collective-permute-start
  10.3 0.3 collective-permute-start.1
  10.7 0.1 fusion.7
  10.8 0.1 copy.41
  10.9 0.2 broadcast_in_dim.33
  11.2 1.4 convert_element_type.44.m_ref
  12.6 1.2 constant_dynamic-update-slice_fusion.1
  13.8 1.2 constant_dynamic-update-slice_fusion.3
  15.0 1.2 constant_dynamic-update-slice_fusion.k_ref
  16.2 1.2 copy-done.2
  17.3 1.2 constant_dynamic-update-slice_fusion.2.v_ref
  18.5 1.1 copy-done.1
  19.7 10.7 %shard_map.256 = f32[12,3,256]{2,1,0:T(4,128)} custom-call(bf16[256,1536]{1,0:T(8,128)(2,1)} %q_ref.3, bf16[256,1536]{1,0:T(8,128)(2,1)} %g_ref.3, bf16[512,1536]{1,0:T(8,128)(2,1)} %copy-done.2, bf16[512,1536]{1,0:T(8,128)(2,1)} %copy-done.1, f32[512,256]{1,0:T(8,128)} %convert_element_type.44.m_ref), custom_call_target="tpu_custom_call" | custom-call | flops 805306368 | bytes 4718592 | tf_op jit(solution)/shard_map/pallas_call | solution.py:113
  30.4 0.9 fusion.34
  31.3 47.9 %collective-permute-done.2.q_ref.g_ref = bf16[528,1536]{1,0:T(8,128)(2,1)} collective-permute-done((bf16[528,1536]{1,0:T(8,128)(2,1)}, bf16[528,1536]{1,0:T(8,128)(2,1)}, u32[]{:S(2)}, u32[]{:S(2)}) %collective-permute-start.2) | collective-permute-done | bytes 1622048 | tf_op jit(solution)/shard_map/ppermute | solution.py:26
  79.2 0.6 compare_reduce_fusion.1
  79.8 0.1 reshape.196
  79.9 0.1 fusion.11
  80.0 0.1 copy.43
  80.1 0.1 convert_bitcast_fusion
  80.2 0.2 broadcast_in_dim.35
  80.4 1.4 convert_element_type.47.m_ref
  81.8 10.7 %shard_map.257 = f32[12,3,256]{2,1,0:T(4,128)} custom-call(bf16[528,1536]{1,0:T(8,128)(2,1)} %collective-permute-done.2.q_ref.g_ref, bf16[528,1536]{1,0:T(8,128)(2,1)} %collective-permute-done.2.q_ref.g_ref, bf16[512,1536]{1,0:T(8,128)(2,1)} %copy-done.2, bf16[512,1536]{1,0:T(8,128)(2,1)} %copy-done.1, f32[512,256]{1,0:T(8,128)} %convert_element_type.47.m_ref), custom_call_target="tpu_custom_call" | custom-call | flops 805306368 | bytes 4718592 | tf_op jit(solution)/shard_map/pallas_call | solution.py:113
  92.5 0.8 copy.35
  93.3 1.9 collective-permute-start.3
  95.3 0.0 collective-permute-done.4.q_ref.g_ref
  95.3 0.1 reshape.198
  95.4 0.1 fusion.22
  95.5 0.1 copy.45
  95.6 0.1 broadcast_in_dim.36
  95.8 1.0 convert_element_type.50.m_ref
  96.8 9.2 %shard_map.258 = f32[12,3,256]{2,1,0:T(4,128)} custom-call(bf16[528,1536]{1,0:T(8,128)(2,1)} %copy-done, bf16[528,1536]{1,0:T(8,128)(2,1)} %copy-done, bf16[256,1536]{1,0:T(8,128)(2,1)} %k_ref.3, bf16[256,1536]{1,0:T(8,128)(2,1)} %v_ref.3, f32[256,256]{1,0:T(8,128)} %convert_element_type.50.m_ref), custom_call_target="tpu_custom_call" | custom-call | flops 402653184 | bytes 3145728 | tf_op jit(solution)/shard_map/pallas_call | solution.py:113
  106.0 0.8 copy.36
  106.8 4.8 %collective-permute-start.5 = (f32[12,3,256]{2,0,1:T(8,128)S(1)}, f32[12,3,256]{2,0,1:T(8,128)S(1)}, u32[]{:S(2)}, u32[]{:S(2)}) collective-permute-start(f32[12,3,256]{2,0,1:T(8,128)S(1)} %copy.36), channel_id=1, source_target_pairs={{1,3},{2,0},{3,5},{4,2},{5,7},{6,4},{7,9},{8,6},{9,11},{10,8},{11,... | collective-permute-start | bytes 110600 | tf_op jit(solution)/shard_map/ppermute | solution.py:26
  111.6 0.0 collective-permute-done.3
  111.7 2.1 %collective-permute-done.5 = f32[12,3,256]{2,0,1:T(8,128)S(1)} collective-permute-done((f32[12,3,256]{2,0,1:T(8,128)S(1)}, f32[12,3,256]{2,0,1:T(8,128)S(1)}, u32[]{:S(2)}, u32[]{:S(2)}) %collective-permute-start.5) | collective-permute-done | bytes 36896 | tf_op jit(solution)/shard_map/ppermute | solution.py:26
  114.0 4.7 %collective-permute-start.6 = (f32[12,2,256]{2,1,0:T(2,128)S(1)}, f32[12,2,256]{2,1,0:T(2,128)S(1)}, u32[]{:S(2)}, u32[]{:S(2)}) collective-permute-start(f32[12,2,256]{2,1,0:T(2,128)S(1)} %pad_maximum_fusion.1.f_ref), channel_id=1, source_target_pairs={{1,3},{2,0},{3,5},{4,2},{5,7},{6,4},{7,9},{8,6},{9,11},{10,8},{11,... | collective-permute-start | bytes 73736 | tf_op jit(solution)/shard_map/ppermute | solution.py:26
  118.7 2.0 %collective-permute-start.7 = (f32[12,2,256]{2,1,0:T(2,128)S(1)}, f32[12,2,256]{2,1,0:T(2,128)S(1)}, u32[]{:S(2)}, u32[]{:S(2)}) collective-permute-start(f32[12,2,256]{2,1,0:T(2,128)S(1)} %pad_maximum_fusion.1.f_ref), channel_id=1, source_target_pairs={{0,2},{2,4},{3,1},{4,6},{5,3},{6,8},{7,5},{8,10},{9,7},{10,12},{11... | collective-permute-start | bytes 73736 | tf_op jit(solution)/shard_map/ppermute | solution.py:26
  120.7 12.3 %shard_map.259 = (f32[256,1536]{1,0:T(8,128)}, f32[512,1536]{1,0:T(8,128)}, f32[512,1536]{1,0:T(8,128)}) custom-call(bf16[256,1536]{1,0:T(8,128)(2,1)} %q_ref.3, bf16[256,1536]{1,0:T(8,128)(2,1)} %g_ref.3, bf16[512,1536]{1,0:T(8,128)(2,1)} %copy-done.2, bf16[512,1536]{1,0:T(8,128)(2,1)} %copy-done.1, f32[512,256]{1,0:T(8,128)} %convert_element_type.44.m_ref, ...), custom_call_target="tpu_custom_call" | custom-call | flops 2013265920 | bytes 14155776 | tf_op jit(solution)/shard_map/pallas_call | solution.py:129
  133.0 0.0 collective-permute-done.6.f_ref
  133.1 0.6 copy-done.18
  133.7 12.2 %shard_map.260 = (bf16[256,1536]{1,0:T(8,128)(2,1)}, f32[512,1536]{1,0:T(8,128)}, f32[512,1536]{1,0:T(8,128)}) custom-call(bf16[528,1536]{1,0:T(8,128)(2,1)} %collective-permute-done.2.q_ref.g_ref, bf16[528,1536]{1,0:T(8,128)(2,1)} %collective-permute-done.2.q_ref.g_ref, bf16[512,1536]{1,0:T(8,128)(2,1)} %copy-done.2, bf16[512,1536]{1,0:T(8,128)(2,1)} %copy-done.1, ...), custom_call_target="tpu_custom_call" | custom-call | flops 2013265920 | bytes 14155776 | tf_op jit(solution)/shard_map/pallas_call | solution.py:129
  145.8 2.7 %slice_add_fusion = f32[256,1536]{1,0:T(8,128)} fusion(f32[512,1536]{1,0:T(8,128)S(1)} %copy-done.4, f32[512,1536]{1,0:T(8,128)} %get-tuple-element.26), kind=kLoop, calls=%fused_computation.2 | loop fusion | flops 393216 | bytes 4718592 | tf_op jit(solution)/shard_map/add | solution.py:224
  148.6 5.1 %collective-permute-start.8 = (bf16[256,1536]{1,0:T(8,128)(2,1)}, bf16[256,1536]{1,0:T(8,128)(2,1)}, u32[]{:S(2)}, u32[]{:S(2)}) collective-permute-start(bf16[256,1536]{1,0:T(8,128)(2,1)} %get-tuple-element.20), channel_id=1, source_target_pairs={{0,2},{2,4},{3,1},{4,6},{5,3},{6,8},{7,5},{8,10},{9,7},{10,12},{11... | collective-permute-start | bytes 2359304 | tf_op jit(solution)/shard_map/ppermute | solution.py:26
  153.7 10.5 %shard_map.261 = (bf16[256,1536]{1,0:T(8,128)(2,1)}, f32[256,1536]{1,0:T(8,128)}, f32[256,1536]{1,0:T(8,128)}) custom-call(bf16[528,1536]{1,0:T(8,128)(2,1)} %copy-done, bf16[528,1536]{1,0:T(8,128)(2,1)} %copy-done, bf16[256,1536]{1,0:T(8,128)(2,1)} %k_ref.3, bf16[256,1536]{1,0:T(8,128)(2,1)} %v_ref.3, f32[256,256]{1,0:T(8,128)} %convert_element_type.50.m_ref, ...), custom_call_target="tpu_custom_call" | custom-call | flops 1006632960 | bytes 9437184 | tf_op jit(solution)/shard_map/pallas_call | solution.py:129
  164.1 1.9 collective-permute-start.9
  166.1 1.8 slice_add_fusion.1
  167.9 0.3 collective-permute-start.10
  168.1 17.0 %collective-permute-done.8 = bf16[256,1536]{1,0:T(8,128)(2,1)} collective-permute-done((bf16[256,1536]{1,0:T(8,128)(2,1)}, bf16[256,1536]{1,0:T(8,128)(2,1)}, u32[]{:S(2)}, u32[]{:S(2)}) %collective-permute-start.8) | collective-permute-done | bytes 786464 | tf_op jit(solution)/shard_map/ppermute | solution.py:26
  185.2 3.7 %collective-permute-done.9 = bf16[256,1536]{1,0:T(8,128)(2,1)S(1)} collective-permute-done((bf16[256,1536]{1,0:T(8,128)(2,1)}, bf16[256,1536]{1,0:T(8,128)(2,1)S(1)}, u32[]{:S(2)}, u32[]{:S(2)}) %collective-permute-start.9) | collective-permute-done | bytes 786464 | tf_op jit(solution)/shard_map/ppermute | solution.py:26
  188.9 2.9 %add_convert_fusion.2 = bf16[256,1536]{1,0:T(8,128)(2,1)} fusion(bf16[256,1536]{1,0:T(8,128)(2,1)S(1)} %collective-permute-done.9, f32[256,1536]{1,0:T(8,128)} %get-tuple-element.16, bf16[256,1536]{1,0:T(8,128)(2,1)} %collective-permute-done.8), kind=kLoop, calls=%fused_computation.5 | loop fusion | flops 1966080 | bytes 3932160 | tf_op jit(solution)/shard_map/convert_element_type | solution.py:229
  191.9 3.0 %add_convert_fusion = bf16[256,1536]{1,0:T(8,128)(2,1)} fusion(f32[256,1536]{1,0:T(8,128)} %collective-permute-done.11, f32[256,1536]{1,0:T(8,128)S(1)} %copy-done.9, f32[512,1536]{1,0:T(8,128)S(1)} %copy-done.5, f32[512,1536]{1,0:T(8,128)S(1)} %copy-done.7), kind=kLoop, calls=%fused_computation.1 | loop fusion | flops 1572864 | bytes 7077888 | tf_op jit(solution)/shard_map/convert_element_type | solution.py:231
  194.9 1.4 add_convert_fusion.1
  (54 shorter events, 0.3 us)
Async XLA Ops:
  1.4 9.2 %copy-start.12 = (s32[4,30]{1,0:T(4,128)S(1)}, s32[4,30]{1,0:T(4,128)}, u32[]{:S(2)}) copy-start(s32[4,30]{1,0:T(4,128)} %param.29) | copy-start | bytes 1444
  1.4 9.2 %copy-start.13 = (bf16[4,30,4]{1,2,0:T(4,128)(2,1)S(1)}, bf16[4,30,4]{1,2,0:T(4,128)(2,1)}, u32[]{:S(2)}) copy-start(bf16[4,30,4]{1,2,0:T(4,128)(2,1)} %constant.132) | copy-start | bytes 2884
  1.4 9.2 %copy-start.14 = (bf16[4,30,4]{1,2,0:T(4,128)(2,1)S(1)}, bf16[4,30,4]{1,2,0:T(4,128)(2,1)}, u32[]{:S(2)}) copy-start(bf16[4,30,4]{1,2,0:T(4,128)(2,1)} %constant.131) | copy-start | bytes 2884
  1.4 9.2 %copy-start.15 = (bf16[4,30,4]{1,2,0:T(4,128)(2,1)S(1)}, bf16[4,30,4]{1,2,0:T(4,128)(2,1)}, u32[]{:S(2)}) copy-start(bf16[4,30,4]{1,2,0:T(4,128)(2,1)} %constant.134) | copy-start | bytes 2884
  1.5 9.2 %copy-start.16 = (bf16[4,30,4]{1,2,0:T(4,128)(2,1)S(1)}, bf16[4,30,4]{1,2,0:T(4,128)(2,1)}, u32[]{:S(2)}) copy-start(bf16[4,30,4]{1,2,0:T(4,128)(2,1)} %constant.133) | copy-start | bytes 2884
  1.5 9.2 %copy-start.19 = (bf16[4,30,4]{1,2,0:T(4,128)(2,1)S(1)}, bf16[4,30,4]{1,2,0:T(4,128)(2,1)}, u32[]{:S(2)}) copy-start(bf16[4,30,4]{1,2,0:T(4,128)(2,1)} %constant.135) | copy-start | bytes 2884
  1.5 9.4 %copy-start.17 = (pred[4,8]{0,1:T(8,128)(4,1)S(1)}, pred[4,8]{0,1:T(8,128)(4,1)}, u32[]{:S(2)}) copy-start(pred[4,8]{0,1:T(8,128)(4,1)} %constant.62) | copy-start | bytes 100
  4.2 74.9 %collective-permute-start.2 = (bf16[528,1536]{1,0:T(8,128)(2,1)}, bf16[528,1536]{1,0:T(8,128)(2,1)}, u32[]{:S(2)}, u32[]{:S(2)}) collective-permute-start(bf16[528,1536]{1,0:T(8,128)(2,1)} %pad_maximum_fusion), channel_id=1, source_target_pairs={{1,3},{2,0},{3,5},{4,2},{5,7},{6,4},{7,9},{8,6},{9,11},{10,8},{11,... | collective-permute-start | bytes 4866056 | tf_op jit(solution)/shard_map/ppermute | solution.py:26
  7.5 87.7 %collective-permute-start.4 = (bf16[528,1536]{1,0:T(8,128)(2,1)}, bf16[528,1536]{1,0:T(8,128)(2,1)S(1)}, u32[]{:S(2)}, u32[]{:S(2)}) collective-permute-start(bf16[528,1536]{1,0:T(8,128)(2,1)} %pad_maximum_fusion), channel_id=1, source_target_pairs={{0,2},{2,4},{3,1},{4,6},{5,3},{6,8},{7,5},{8,10},{9,7},{10,12},{11... | collective-permute-start | bytes 4866056 | tf_op jit(solution)/shard_map/ppermute | solution.py:26
  10.1 4.9 %collective-permute-start = (bf16[256,1536]{1,0:T(8,128)(2,1)}, bf16[256,1536]{1,0:T(8,128)(2,1)}, u32[]{:S(2)}, u32[]{:S(2)}) collective-permute-start(bf16[256,1536]{1,0:T(8,128)(2,1)} %k_ref.3), channel_id=1, source_target_pairs={{0,1},{1,0},{2,3},{3,2},{4,5},{5,4},{6,7},{7,6},{8,9},{9,8},{10,11... | collective-permute-start | bytes 2359304 | tf_op jit(solution)/shard_map/ppermute | solution.py:26
  10.3 7.0 %collective-permute-start.1 = (bf16[256,1536]{1,0:T(8,128)(2,1)}, bf16[256,1536]{1,0:T(8,128)(2,1)}, u32[]{:S(2)}, u32[]{:S(2)}) collective-permute-start(bf16[256,1536]{1,0:T(8,128)(2,1)} %v_ref.3), channel_id=1, source_target_pairs={{0,1},{1,0},{2,3},{3,2},{4,5},{5,4},{6,7},{7,6},{8,9},{9,8},{10,11... | collective-permute-start | bytes 2359304 | tf_op jit(solution)/shard_map/ppermute | solution.py:26
  16.1 1.2 copy-start.2
  18.5 1.1 copy-start.1
  93.3 18.3 %collective-permute-start.3 = (f32[12,3,256]{2,0,1:T(8,128)S(1)}, f32[12,3,256]{2,0,1:T(8,128)S(1)}, u32[]{:S(2)}, u32[]{:S(2)}) collective-permute-start(f32[12,3,256]{2,0,1:T(8,128)S(1)} %copy.35), channel_id=1, source_target_pairs={{0,2},{2,4},{3,1},{4,6},{5,3},{6,8},{7,5},{8,10},{9,7},{10,12},{11... | collective-permute-start | bytes 110600 | tf_op jit(solution)/shard_map/ppermute | solution.py:26
  95.3 1.5 copy-start
  106.8 7.0 %collective-permute-start.5 = (f32[12,3,256]{2,0,1:T(8,128)S(1)}, f32[12,3,256]{2,0,1:T(8,128)S(1)}, u32[]{:S(2)}, u32[]{:S(2)}) collective-permute-start(f32[12,3,256]{2,0,1:T(8,128)S(1)} %copy.36), channel_id=1, source_target_pairs={{1,3},{2,0},{3,5},{4,2},{5,7},{6,4},{7,9},{8,6},{9,11},{10,8},{11,... | collective-permute-start | bytes 110600 | tf_op jit(solution)/shard_map/ppermute | solution.py:26
  114.0 6.8 %copy-start.11 = (f32[12,2,256]{2,1,0:T(2,128)}, f32[12,2,256]{2,1,0:T(2,128)S(1)}, u32[]{:S(2)}) copy-start(f32[12,2,256]{2,1,0:T(2,128)S(1)} %pad_maximum_fusion.1.f_ref) | copy-start | bytes 73732
  114.0 19.1 %collective-permute-start.6 = (f32[12,2,256]{2,1,0:T(2,128)S(1)}, f32[12,2,256]{2,1,0:T(2,128)S(1)}, u32[]{:S(2)}, u32[]{:S(2)}) collective-permute-start(f32[12,2,256]{2,1,0:T(2,128)S(1)} %pad_maximum_fusion.1.f_ref), channel_id=1, source_target_pairs={{1,3},{2,0},{3,5},{4,2},{5,7},{6,4},{7,9},{8,6},{9,11},{10,8},{11,... | collective-permute-start | bytes 73736 | tf_op jit(solution)/shard_map/ppermute | solution.py:26
  118.7 14.4 %collective-permute-start.7 = (f32[12,2,256]{2,1,0:T(2,128)S(1)}, f32[12,2,256]{2,1,0:T(2,128)S(1)}, u32[]{:S(2)}, u32[]{:S(2)}) collective-permute-start(f32[12,2,256]{2,1,0:T(2,128)S(1)} %pad_maximum_fusion.1.f_ref), channel_id=1, source_target_pairs={{0,2},{2,4},{3,1},{4,6},{5,3},{6,8},{7,5},{8,10},{9,7},{10,12},{11... | collective-permute-start | bytes 73736 | tf_op jit(solution)/shard_map/ppermute | solution.py:26
  133.0 0.6 copy-start.18
  133.1 12.8 %copy-start.10 = (f32[12,2,256]{2,1,0:T(2,128)}, f32[12,2,256]{2,1,0:T(2,128)S(1)}, u32[]{:S(2)}) copy-start(f32[12,2,256]{2,1,0:T(2,128)S(1)} %collective-permute-done.7.f_ref) | copy-start | bytes 73732
  133.7 12.2 %copy-start.4 = (f32[512,1536]{1,0:T(8,128)S(1)}, f32[512,1536]{1,0:T(8,128)}, u32[]{:S(2)}) copy-start(f32[512,1536]{1,0:T(8,128)} %get-tuple-element.27) | copy-start | bytes 9437188
  148.6 43.3 %collective-permute-start.11 = (f32[256,1536]{1,0:T(8,128)}, f32[256,1536]{1,0:T(8,128)}, u32[]{:S(2)}, u32[]{:S(2)}) collective-permute-start(f32[256,1536]{1,0:T(8,128)} %slice_add_fusion), channel_id=1, source_target_pairs={{0,1},{1,0},{2,3},{3,2},{4,5},{5,4},{6,7},{7,6},{8,9},{9,8},{10,11... | collective-permute-start | bytes 4718600 | tf_op jit(solution)/shard_map/ppermute | solution.py:26
  148.6 17.5 %copy-start.3 = (f32[512,1536]{1,0:T(8,128)S(1)}, f32[512,1536]{1,0:T(8,128)}, u32[]{:S(2)}) copy-start(f32[512,1536]{1,0:T(8,128)} %get-tuple-element.24) | copy-start | bytes 9437188
  148.6 36.6 %collective-permute-start.8 = (bf16[256,1536]{1,0:T(8,128)(2,1)}, bf16[256,1536]{1,0:T(8,128)(2,1)}, u32[]{:S(2)}, u32[]{:S(2)}) collective-permute-start(bf16[256,1536]{1,0:T(8,128)(2,1)} %get-tuple-element.20), channel_id=1, source_target_pairs={{0,2},{2,4},{3,1},{4,6},{5,3},{6,8},{7,5},{8,10},{9,7},{10,12},{11... | collective-permute-start | bytes 2359304 | tf_op jit(solution)/shard_map/ppermute | solution.py:26
  164.1 24.8 %collective-permute-start.9 = (bf16[256,1536]{1,0:T(8,128)(2,1)}, bf16[256,1536]{1,0:T(8,128)(2,1)S(1)}, u32[]{:S(2)}, u32[]{:S(2)}) collective-permute-start(bf16[256,1536]{1,0:T(8,128)(2,1)} %get-tuple-element.22), channel_id=1, source_target_pairs={{1,3},{2,0},{3,5},{4,2},{5,7},{6,4},{7,9},{8,6},{9,11},{10,8},{11,... | collective-permute-start | bytes 2359304 | tf_op jit(solution)/shard_map/ppermute | solution.py:26
  166.1 25.8 %copy-start.7 = (f32[512,1536]{1,0:T(8,128)S(1)}, f32[512,1536]{1,0:T(8,128)}, u32[]{:S(2)}) copy-start(f32[512,1536]{1,0:T(8,128)} %get-tuple-element.26) | copy-start | bytes 9437188
  166.1 25.8 %copy-start.9 = (f32[256,1536]{1,0:T(8,128)S(1)}, f32[256,1536]{1,0:T(8,128)}, u32[]{:S(2)}) copy-start(f32[256,1536]{1,0:T(8,128)} %get-tuple-element.28) | copy-start | bytes 4718596
  167.9 27.0 %collective-permute-start.10 = (f32[256,1536]{1,0:T(8,128)S(1)}, f32[256,1536]{1,0:T(8,128)S(1)}, u32[]{:S(2)}, u32[]{:S(2)}) collective-permute-start(f32[256,1536]{1,0:T(8,128)S(1)} %slice_add_fusion.1), channel_id=1, source_target_pairs={{0,1},{1,0},{2,3},{3,2},{4,5},{5,4},{6,7},{7,6},{8,9},{9,8},{10,11... | collective-permute-start | bytes 4718600 | tf_op jit(solution)/shard_map/ppermute | solution.py:26
  188.9 3.0 %copy-start.5 = (f32[512,1536]{1,0:T(8,128)S(1)}, f32[512,1536]{1,0:T(8,128)}, u32[]{:S(2)}) copy-start(f32[512,1536]{1,0:T(8,128)} %get-tuple-element.27) | copy-start | bytes 9437188
  191.9 3.0 %copy-start.6 = (f32[512,1536]{1,0:T(8,128)S(1)}, f32[512,1536]{1,0:T(8,128)}, u32[]{:S(2)}) copy-start(f32[512,1536]{1,0:T(8,128)} %get-tuple-element.23) | copy-start | bytes 9437188
  191.9 3.0 %copy-start.8 = (f32[256,1536]{1,0:T(8,128)S(1)}, f32[256,1536]{1,0:T(8,128)}, u32[]{:S(2)}) copy-start(f32[256,1536]{1,0:T(8,128)} %get-tuple-element.25) | copy-start | bytes 4718596

commit v7 on v6

--- a/solution.py
+++ b/solution.py
@@ -64,45 +64,56 @@
 
 SCALE = HDIM ** (-0.5)
 NT = (((1,), (1,)), ((), ()))
-
-
-def slot_scores(q_ref, g_ref, k_ref, v_ref):
-    q = q_ref[...]
-    g = g_ref[...]
-    s = lax.dot_general(k_ref[...], q, NT, preferred_element_type=jnp.float32) * SCALE
-    dp = lax.dot_general(v_ref[...], g, NT, preferred_element_type=jnp.float32)
-    return q, g, s, dp
+STEP_HEADS = 4
+
+
+def slot_scores(q, g, k, v):
+    s = lax.dot_general(k, q, NT, preferred_element_type=jnp.float32) * SCALE
+    dp = lax.dot_general(v, g, NT, preferred_element_type=jnp.float32)
+    return s, dp
+
+
+def head_cols(j):
+    return slice(j * HDIM, (j + 1) * HDIM)
 
 
 def stats_kernel(q_ref, g_ref, k_ref, v_ref, m_ref, out_ref):
-    _, _, s, dp = slot_scores(q_ref, g_ref, k_ref, v_ref)
     m = m_ref[...] > 0
-    masked = jnp.where(m, s, NEG)
-    mx = jnp.max(masked, axis=0, keepdims=True)
-    e = jnp.where(m, jnp.exp(masked - mx), 0.0)
-    total = jnp.sum(e, axis=0, keepdims=True)
-    dot = jnp.sum(e * dp, axis=0, keepdims=True)
-    out_ref[0] = jnp.concatenate([mx, total, dot], axis=0)
+    for j in range(STEP_HEADS):
+        cols = head_cols(j)
+        s, dp = slot_scores(q_ref[:, cols], g_ref[:, cols], k_ref[:, cols], v_ref[:, cols])
+        masked = jnp.where(m, s, NEG)
+        mx = jnp.max(masked, axis=0, keepdims=True)
+        e = jnp.where(m, jnp.exp(masked - mx), 0.0)
+        total = jnp.sum(e, axis=0, keepdims=True)
+        dot = jnp.sum(e * dp, axis=0, keepdims=True)
+        out_ref[j] = jnp.concatenate([mx, total, dot], axis=0)
 
 
 def back_kernel(q_ref, g_ref, k_ref, v_ref, m_ref, f_ref, dq_ref, dk_ref, dv_ref):
-    q, g, s, dp = slot_scores(q_ref, g_ref, k_ref, v_ref)
     m = m_ref[...] > 0
-    fin = f_ref[0]
-    p = jnp.where(m, jnp.exp(s - fin[0:1]), 0.0)
-    ds = (p * (dp - fin[1:2])).astype(jnp.bfloat16)
-    dk_ref[...] = jnp.dot(ds, q, preferred_element_type=jnp.float32) * SCALE
-    dv_ref[...] = jnp.dot(p.astype(jnp.bfloat16), g, preferred_element_type=jnp.float32)
-    dq = lax.dot_general(ds, k_ref[...], (((0,), (0,)), ((), ())), preferred_element_type=jnp.float32)
-    dq_ref[...] = (dq * SCALE).astype(dq_ref.dtype)
+    for j in range(STEP_HEADS):
+        cols = head_cols(j)
+        q = q_ref[:, cols]
+        g = g_ref[:, cols]
+        k = k_ref[:, cols]
+        s, dp = slot_scores(q, g, k, v_ref[:, cols])
+        fin = f_ref[j]
+        p = jnp.where(m, jnp.exp(s - fin[0:1]), 0.0)
+        ds = (p * (dp - fin[1:2])).astype(jnp.bfloat16)
+        dk_ref[:, cols] = jnp.dot(ds, q, preferred_element_type=jnp.float32) * SCALE
+        dv_ref[:, cols] = jnp.dot(p.astype(jnp.bfloat16), g, preferred_element_type=jnp.float32)
+        dq = lax.dot_general(ds, k, (((0,), (0,)), ((), ())), preferred_element_type=jnp.float32)
+        dq_ref[:, cols] = (dq * SCALE).astype(dq_ref.dtype)
 
 
 def slot_specs(q_rows, g_rows, nk, tok):
+    cols = STEP_HEADS * HDIM
     return [
-        pl.BlockSpec((tok, HDIM), lambda h: (q_rows, h)),
-        pl.BlockSpec((tok, HDIM), lambda h: (g_rows, h)),
-        pl.BlockSpec((nk, HDIM), lambda h: (0, h)),
-        pl.BlockSpec((nk, HDIM), lambda h: (0, h)),
+        pl.BlockSpec((tok, cols), lambda h: (q_rows, h)),
+        pl.BlockSpec((tok, cols), lambda h: (g_rows, h)),
+        pl.BlockSpec((nk, cols), lambda h: (0, h)),
+        pl.BlockSpec((nk, cols), lambda h: (0, h)),
         pl.BlockSpec((nk, tok), lambda h: (0, 0)),
     ]
 
@@ -112,9 +123,9 @@
     flops = 4 * tok * nk * HDIM * HEADS
     return pl.pallas_call(
         stats_kernel,
-        grid=(HEADS,),
+        grid=(HEADS // STEP_HEADS,),
         in_specs=slot_specs(q_rows, g_rows, nk, tok),
-        out_specs=pl.BlockSpec((1, 3, tok), lambda h: (h, 0, 0)),
+        out_specs=pl.BlockSpec((STEP_HEADS, 3, tok), lambda h: (h, 0, 0)),
         out_shape=jax.ShapeDtypeStruct((HEADS, 3, tok), jnp.float32),
         cost_estimate=pl.CostEstimate(
             flops=flops, transcendentals=tok * nk * HEADS, bytes_accessed=4 * (tok + nk) * HDIM * HEADS
@@ -128,13 +139,13 @@
     flops = 10 * tok * nk * HDIM * HEADS
     return pl.pallas_call(
         back_kernel,
-        grid=(HEADS,),
+        grid=(HEADS // STEP_HEADS,),
         in_specs=slot_specs(q_rows, g_rows, nk, tok)
-        + [pl.BlockSpec((1, 2, tok), lambda h: (h, 0, 0))],
+        + [pl.BlockSpec((STEP_HEADS, 2, tok), lambda h: (h, 0, 0))],
         out_specs=[
-            pl.BlockSpec((tok, HDIM), lambda h: (0, h)),
-            pl.BlockSpec((nk, HDIM), lambda h: (0, h)),
-            pl.BlockSpec((nk, HDIM), lambda h: (0, h)),
+            pl.BlockSpec((tok, STEP_HEADS * HDIM), lambda h: (0, h)),
+            pl.BlockSpec((nk, STEP_HEADS * HDIM), lambda h: (0, h)),
+            pl.BlockSpec((nk, STEP_HEADS * HDIM), lambda h: (0, h)),
         ],
         out_shape=[
             jax.ShapeDtypeStruct((tok, width), dq_type),

time: 200 us -> 183 us (0.915)
  Pallas kernels: 65.6 us -> 41.7 us
  waiting for transfers between devices: 70.8 us -> 78.8 us
    pallas_call x6, Pallas kernels: 65.6 us -> 41.7 us  [the longest x3 24.6 us: slot_back(): pl.pallas_call(back_kernel, grid=(HEADS // STEP_HEADS,), in_specs=slot_sp...]
    ppermute x12, waiting for transfers between devices: 70.8 us -> 78.8 us  [permute(): return lax.ppermute(value, 'tm', pairs)]
  transfers between devices with their start and end apart: 12 -> 12, of which waited for: 4 -> 4; matrix products, arithmetic and copies ran while one was open for 11% -> 12% of each run, Pallas kernels for 27% -> 18%
where the time goes in v7:
time: 183 us; the launch traced here: 181 us
  waiting for transfers between devices  78.8 us (43%)
  Pallas kernels  41.7 us (23%)
  starting transfers between devices  27.3 us (15%)
  other arithmetic  16.1 us (9%)
  local copies, waits for them, and re-layouts  15.3 us (8%)
    ppermute x12, waiting for transfers between devices, permute(): return lax.ppermute(value, 'tm', pairs)  78.8 us
    ppermute x12, starting transfers between devices, permute(): return lax.ppermute(value, 'tm', pairs)  27.3 us
    pallas_call x3, Pallas kernels, slot_back(): pl.pallas_call(back_kernel, grid=(HEADS // STEP_HEADS,), in_specs=slot_sp...  24.6 us
    pallas_call x3, Pallas kernels, slot_stats(): pl.pallas_call(stats_kernel, grid=(HEADS // STEP_HEADS,), in_specs=slot_s...  17.1 us
    unnamed x42, local copies, waits for them, and re-layouts  5.36 us
    convert_element_type x3, local copies, waits for them, and re-layouts, local(): mask_t = jnp.broadcast_to(mask4.T[:, None, :, None], (nkb, BLOCK, blocks,...  3.86 us
  transfers between devices with their start and end apart: 12, of which 4 were waited for; matrix products, arithmetic and copies ran while one was open for 12% of the time, Pallas kernels for 18%

profile of v7, /device:TPU:8, one launch (start us, length us, event | category | flops | bytes accessed | tf_op | source)
XLA Modules:
  0.0 180.7 jit_solution(2374690076922156418)
XLA Ops:
  0.6 0.7 broadcast_compare_fusion
  1.3 0.1 reshape.188
  1.4 0.0 copy-start.13
  1.4 0.0 copy-start.14
  1.4 0.0 copy-start.15
  1.5 0.0 copy-start.16
  1.5 0.0 copy-start.19
  1.5 0.0 copy-start.17
  1.5 2.7 %pad_maximum_fusion = bf16[528,1536]{1,0:T(8,128)(2,1)} fusion(bf16[16,1536]{1,0:T(8,128)(2,1)S(1)} %pad_convert_fusion, bf16[256,1536]{1,0:T(8,128)(2,1)} %g_ref.3, bf16[256,1536]{1,0:T(8,128)(2,1)} %q_ref.3), kind=kLoop, calls=%fused_computation | loop fusion | flops 4866048 | bytes 3244032 | tf_op jit(solution)/shard_map/concatenate | solution.py:172
  4.2 3.3 %collective-permute-start.2 = (bf16[528,1536]{1,0:T(8,128)(2,1)}, bf16[528,1536]{1,0:T(8,128)(2,1)}, u32[]{:S(2)}, u32[]{:S(2)}) collective-permute-start(bf16[528,1536]{1,0:T(8,128)(2,1)} %pad_maximum_fusion), channel_id=1, source_target_pairs={{1,3},{2,0},{3,5},{4,2},{5,7},{6,4},{7,9},{8,6},{9,11},{10,8},{11,... | collective-permute-start | bytes 4866056 | tf_op jit(solution)/shard_map/ppermute | solution.py:26
  7.5 2.5 %collective-permute-start.4 = (bf16[528,1536]{1,0:T(8,128)(2,1)}, bf16[528,1536]{1,0:T(8,128)(2,1)S(1)}, u32[]{:S(2)}, u32[]{:S(2)}) collective-permute-start(bf16[528,1536]{1,0:T(8,128)(2,1)} %pad_maximum_fusion), channel_id=1, source_target_pairs={{0,2},{2,4},{3,1},{4,6},{5,3},{6,8},{7,5},{8,10},{9,7},{10,12},{11... | collective-permute-start | bytes 4866056 | tf_op jit(solution)/shard_map/ppermute | solution.py:26
  10.1 0.2 collective-permute-start
  10.3 0.3 collective-permute-start.1
  10.7 0.1 fusion.7
  10.8 0.1 copy.41
  10.9 0.2 broadcast_in_dim.33
  11.2 1.4 convert_element_type.44.m_ref
  12.6 1.2 constant_dynamic-update-slice_fusion.1
  13.8 1.2 constant_dynamic-update-slice_fusion.3
  15.0 1.2 constant_dynamic-update-slice_fusion.k_ref
  16.2 1.2 copy-done.2
  17.3 0.0 collective-permute-done.1
  17.3 1.2 constant_dynamic-update-slice_fusion.2.v_ref
  18.5 1.1 copy-done.1
  19.7 6.3 %shard_map.256 = f32[12,3,256]{2,1,0:T(4,128)} custom-call(bf16[256,1536]{1,0:T(8,128)(2,1)} %q_ref.3, bf16[256,1536]{1,0:T(8,128)(2,1)} %g_ref.3, bf16[512,1536]{1,0:T(8,128)(2,1)} %copy-done.2, bf16[512,1536]{1,0:T(8,128)(2,1)} %copy-done.1, f32[512,256]{1,0:T(8,128)} %convert_element_type.44.m_ref), custom_call_target="tpu_custom_call" | custom-call | flops 805306368 | bytes 4718592 | tf_op jit(solution)/shard_map/pallas_call | solution.py:124
  25.9 0.9 fusion.34
  26.9 52.3 %collective-permute-done.2.q_ref.g_ref = bf16[528,1536]{1,0:T(8,128)(2,1)} collective-permute-done((bf16[528,1536]{1,0:T(8,128)(2,1)}, bf16[528,1536]{1,0:T(8,128)(2,1)}, u32[]{:S(2)}, u32[]{:S(2)}) %collective-permute-start.2) | collective-permute-done | bytes 1622048 | tf_op jit(solution)/shard_map/ppermute | solution.py:26
  79.2 0.6 compare_reduce_fusion.1
  79.8 0.1 reshape.196
  79.9 0.1 fusion.11
  80.0 0.1 copy.43
  80.1 0.1 convert_bitcast_fusion
  80.2 0.2 broadcast_in_dim.35
  80.4 1.4 convert_element_type.47.m_ref
  81.8 6.3 %shard_map.257 = f32[12,3,256]{2,1,0:T(4,128)} custom-call(bf16[528,1536]{1,0:T(8,128)(2,1)} %collective-permute-done.2.q_ref.g_ref, bf16[528,1536]{1,0:T(8,128)(2,1)} %collective-permute-done.2.q_ref.g_ref, bf16[512,1536]{1,0:T(8,128)(2,1)} %copy-done.2, bf16[512,1536]{1,0:T(8,128)(2,1)} %copy-done.1, f32[512,256]{1,0:T(8,128)} %convert_element_type.47.m_ref), custom_call_target="tpu_custom_call" | custom-call | flops 805306368 | bytes 4718592 | tf_op jit(solution)/shard_map/pallas_call | solution.py:124
  88.1 0.8 copy.35
  88.9 1.9 %collective-permute-start.3 = (f32[12,3,256]{2,0,1:T(8,128)S(1)}, f32[12,3,256]{2,0,1:T(8,128)S(1)}, u32[]{:S(2)}, u32[]{:S(2)}) collective-permute-start(f32[12,3,256]{2,0,1:T(8,128)S(1)} %copy.35), channel_id=1, source_target_pairs={{0,2},{2,4},{3,1},{4,6},{5,3},{6,8},{7,5},{8,10},{9,7},{10,12},{11... | collective-permute-start | bytes 110600 | tf_op jit(solution)/shard_map/ppermute | solution.py:26
  90.8 0.0 collective-permute-done.4.q_ref.g_ref
  90.8 0.1 reshape.198
  90.9 0.1 fusion.22
  91.0 0.1 copy.45
  91.1 0.1 broadcast_in_dim.36
  91.3 1.0 convert_element_type.50.m_ref
  92.3 4.6 %shard_map.258 = f32[12,3,256]{2,1,0:T(4,128)} custom-call(bf16[528,1536]{1,0:T(8,128)(2,1)} %copy-done, bf16[528,1536]{1,0:T(8,128)(2,1)} %copy-done, bf16[256,1536]{1,0:T(8,128)(2,1)} %k_ref.3, bf16[256,1536]{1,0:T(8,128)(2,1)} %v_ref.3, f32[256,256]{1,0:T(8,128)} %convert_element_type.50.m_ref), custom_call_target="tpu_custom_call" | custom-call | flops 402653184 | bytes 3145728 | tf_op jit(solution)/shard_map/pallas_call | solution.py:124
  96.9 0.8 copy.36
  97.7 4.8 %collective-permute-start.5 = (f32[12,3,256]{2,0,1:T(8,128)S(1)}, f32[12,3,256]{2,0,1:T(8,128)S(1)}, u32[]{:S(2)}, u32[]{:S(2)}) collective-permute-start(f32[12,3,256]{2,0,1:T(8,128)S(1)} %copy.36), channel_id=1, source_target_pairs={{1,3},{2,0},{3,5},{4,2},{5,7},{6,4},{7,9},{8,6},{9,11},{10,8},{11,... | collective-permute-start | bytes 110600 | tf_op jit(solution)/shard_map/ppermute | solution.py:26
  102.6 2.1 %collective-permute-done.5 = f32[12,3,256]{2,0,1:T(8,128)S(1)} collective-permute-done((f32[12,3,256]{2,0,1:T(8,128)S(1)}, f32[12,3,256]{2,0,1:T(8,128)S(1)}, u32[]{:S(2)}, u32[]{:S(2)}) %collective-permute-start.5) | collective-permute-done | bytes 36896 | tf_op jit(solution)/shard_map/ppermute | solution.py:26
  104.9 4.7 %collective-permute-start.6 = (f32[12,2,256]{2,1,0:T(2,128)S(1)}, f32[12,2,256]{2,1,0:T(2,128)S(1)}, u32[]{:S(2)}, u32[]{:S(2)}) collective-permute-start(f32[12,2,256]{2,1,0:T(2,128)S(1)} %pad_maximum_fusion.1.f_ref), channel_id=1, source_target_pairs={{1,3},{2,0},{3,5},{4,2},{5,7},{6,4},{7,9},{8,6},{9,11},{10,8},{11,... | collective-permute-start | bytes 73736 | tf_op jit(solution)/shard_map/ppermute | solution.py:26
  109.6 2.0 %collective-permute-start.7 = (f32[12,2,256]{2,1,0:T(2,128)S(1)}, f32[12,2,256]{2,1,0:T(2,128)S(1)}, u32[]{:S(2)}, u32[]{:S(2)}) collective-permute-start(f32[12,2,256]{2,1,0:T(2,128)S(1)} %pad_maximum_fusion.1.f_ref), channel_id=1, source_target_pairs={{0,2},{2,4},{3,1},{4,6},{5,3},{6,8},{7,5},{8,10},{9,7},{10,12},{11... | collective-permute-start | bytes 73736 | tf_op jit(solution)/shard_map/ppermute | solution.py:26
  111.7 9.0 %shard_map.259 = (f32[256,1536]{1,0:T(8,128)}, f32[512,1536]{1,0:T(8,128)}, f32[512,1536]{1,0:T(8,128)}) custom-call(bf16[256,1536]{1,0:T(8,128)(2,1)} %q_ref.3, bf16[256,1536]{1,0:T(8,128)(2,1)} %g_ref.3, bf16[512,1536]{1,0:T(8,128)(2,1)} %copy-done.2, bf16[512,1536]{1,0:T(8,128)(2,1)} %copy-done.1, f32[512,256]{1,0:T(8,128)} %convert_element_type.44.m_ref, ...), custom_call_target="tpu_custom_call" | custom-call | flops 2013265920 | bytes 14155776 | tf_op jit(solution)/shard_map/pallas_call | solution.py:140
  120.6 0.0 collective-permute-done.6.f_ref
  120.7 0.6 copy-done.18
  121.3 8.9 %shard_map.260 = (bf16[256,1536]{1,0:T(8,128)(2,1)}, f32[512,1536]{1,0:T(8,128)}, f32[512,1536]{1,0:T(8,128)}) custom-call(bf16[528,1536]{1,0:T(8,128)(2,1)} %collective-permute-done.2.q_ref.g_ref, bf16[528,1536]{1,0:T(8,128)(2,1)} %collective-permute-done.2.q_ref.g_ref, bf16[512,1536]{1,0:T(8,128)(2,1)} %copy-done.2, bf16[512,1536]{1,0:T(8,128)(2,1)} %copy-done.1, ...), custom_call_target="tpu_custom_call" | custom-call | flops 2013265920 | bytes 14155776 | tf_op jit(solution)/shard_map/pallas_call | solution.py:140
  130.2 2.7 %slice_add_fusion = f32[256,1536]{1,0:T(8,128)} fusion(f32[512,1536]{1,0:T(8,128)S(1)} %copy-done.4, f32[512,1536]{1,0:T(8,128)} %get-tuple-element.26), kind=kLoop, calls=%fused_computation.2 | loop fusion | flops 393216 | bytes 4718592 | tf_op jit(solution)/shard_map/add | solution.py:235
  132.9 5.3 %collective-permute-start.8 = (bf16[256,1536]{1,0:T(8,128)(2,1)}, bf16[256,1536]{1,0:T(8,128)(2,1)}, u32[]{:S(2)}, u32[]{:S(2)}) collective-permute-start(bf16[256,1536]{1,0:T(8,128)(2,1)} %get-tuple-element.20), channel_id=1, source_target_pairs={{0,2},{2,4},{3,1},{4,6},{5,3},{6,8},{7,5},{8,10},{9,7},{10,12},{11... | collective-permute-start | bytes 2359304 | tf_op jit(solution)/shard_map/ppermute | solution.py:26
  138.2 6.8 %shard_map.261 = (bf16[256,1536]{1,0:T(8,128)(2,1)}, f32[256,1536]{1,0:T(8,128)}, f32[256,1536]{1,0:T(8,128)}) custom-call(bf16[528,1536]{1,0:T(8,128)(2,1)} %copy-done, bf16[528,1536]{1,0:T(8,128)(2,1)} %copy-done, bf16[256,1536]{1,0:T(8,128)(2,1)} %k_ref.3, bf16[256,1536]{1,0:T(8,128)(2,1)} %v_ref.3, f32[256,256]{1,0:T(8,128)} %convert_element_type.50.m_ref, ...), custom_call_target="tpu_custom_call" | custom-call | flops 1006632960 | bytes 9437184 | tf_op jit(solution)/shard_map/pallas_call | solution.py:140
  144.9 1.9 %collective-permute-start.9 = (bf16[256,1536]{1,0:T(8,128)(2,1)}, bf16[256,1536]{1,0:T(8,128)(2,1)S(1)}, u32[]{:S(2)}, u32[]{:S(2)}) collective-permute-start(bf16[256,1536]{1,0:T(8,128)(2,1)} %get-tuple-element.22), channel_id=1, source_target_pairs={{1,3},{2,0},{3,5},{4,2},{5,7},{6,4},{7,9},{8,6},{9,11},{10,8},{11,... | collective-permute-start | bytes 2359304 | tf_op jit(solution)/shard_map/ppermute | solution.py:26
  146.9 1.8 slice_add_fusion.1
  148.6 0.3 collective-permute-start.10
  148.9 23.5 %collective-permute-done.8 = bf16[256,1536]{1,0:T(8,128)(2,1)} collective-permute-done((bf16[256,1536]{1,0:T(8,128)(2,1)}, bf16[256,1536]{1,0:T(8,128)(2,1)}, u32[]{:S(2)}, u32[]{:S(2)}) %collective-permute-start.8) | collective-permute-done | bytes 786464 | tf_op jit(solution)/shard_map/ppermute | solution.py:26
  172.5 0.8 collective-permute-done.9
  173.2 2.9 %add_convert_fusion.2 = bf16[256,1536]{1,0:T(8,128)(2,1)} fusion(bf16[256,1536]{1,0:T(8,128)(2,1)S(1)} %collective-permute-done.9, f32[256,1536]{1,0:T(8,128)} %get-tuple-element.16, bf16[256,1536]{1,0:T(8,128)(2,1)} %collective-permute-done.8), kind=kLoop, calls=%fused_computation.5 | loop fusion | flops 1966080 | bytes 3932160 | tf_op jit(solution)/shard_map/convert_element_type | solution.py:240
  176.2 3.0 %add_convert_fusion = bf16[256,1536]{1,0:T(8,128)(2,1)} fusion(f32[256,1536]{1,0:T(8,128)} %collective-permute-done.11, f32[256,1536]{1,0:T(8,128)S(1)} %copy-done.9, f32[512,1536]{1,0:T(8,128)S(1)} %copy-done.5, f32[512,1536]{1,0:T(8,128)S(1)} %copy-done.7), kind=kLoop, calls=%fused_computation.1 | loop fusion | flops 1572864 | bytes 7077888 | tf_op jit(solution)/shard_map/convert_element_type | solution.py:242
  179.2 1.4 add_convert_fusion.1
  (54 shorter events, 0.3 us)
Async XLA Ops:
  1.4 9.2 %copy-start.12 = (s32[4,30]{1,0:T(4,128)S(1)}, s32[4,30]{1,0:T(4,128)}, u32[]{:S(2)}) copy-start(s32[4,30]{1,0:T(4,128)} %param.29) | copy-start | bytes 1444
  1.4 9.2 %copy-start.13 = (bf16[4,30,4]{1,2,0:T(4,128)(2,1)S(1)}, bf16[4,30,4]{1,2,0:T(4,128)(2,1)}, u32[]{:S(2)}) copy-start(bf16[4,30,4]{1,2,0:T(4,128)(2,1)} %constant.132) | copy-start | bytes 2884
  1.4 9.2 %copy-start.14 = (bf16[4,30,4]{1,2,0:T(4,128)(2,1)S(1)}, bf16[4,30,4]{1,2,0:T(4,128)(2,1)}, u32[]{:S(2)}) copy-start(bf16[4,30,4]{1,2,0:T(4,128)(2,1)} %constant.131) | copy-start | bytes 2884
  1.4 9.2 %copy-start.15 = (bf16[4,30,4]{1,2,0:T(4,128)(2,1)S(1)}, bf16[4,30,4]{1,2,0:T(4,128)(2,1)}, u32[]{:S(2)}) copy-start(bf16[4,30,4]{1,2,0:T(4,128)(2,1)} %constant.134) | copy-start | bytes 2884
  1.5 9.2 %copy-start.16 = (bf16[4,30,4]{1,2,0:T(4,128)(2,1)S(1)}, bf16[4,30,4]{1,2,0:T(4,128)(2,1)}, u32[]{:S(2)}) copy-start(bf16[4,30,4]{1,2,0:T(4,128)(2,1)} %constant.133) | copy-start | bytes 2884
  1.5 9.2 %copy-start.19 = (bf16[4,30,4]{1,2,0:T(4,128)(2,1)S(1)}, bf16[4,30,4]{1,2,0:T(4,128)(2,1)}, u32[]{:S(2)}) copy-start(bf16[4,30,4]{1,2,0:T(4,128)(2,1)} %constant.135) | copy-start | bytes 2884
  1.5 9.4 %copy-start.17 = (pred[4,8]{0,1:T(8,128)(4,1)S(1)}, pred[4,8]{0,1:T(8,128)(4,1)}, u32[]{:S(2)}) copy-start(pred[4,8]{0,1:T(8,128)(4,1)} %constant.62) | copy-start | bytes 100
  4.2 74.9 %collective-permute-start.2 = (bf16[528,1536]{1,0:T(8,128)(2,1)}, bf16[528,1536]{1,0:T(8,128)(2,1)}, u32[]{:S(2)}, u32[]{:S(2)}) collective-permute-start(bf16[528,1536]{1,0:T(8,128)(2,1)} %pad_maximum_fusion), channel_id=1, source_target_pairs={{1,3},{2,0},{3,5},{4,2},{5,7},{6,4},{7,9},{8,6},{9,11},{10,8},{11,... | collective-permute-start | bytes 4866056 | tf_op jit(solution)/shard_map/ppermute | solution.py:26
  7.5 83.3 %collective-permute-start.4 = (bf16[528,1536]{1,0:T(8,128)(2,1)}, bf16[528,1536]{1,0:T(8,128)(2,1)S(1)}, u32[]{:S(2)}, u32[]{:S(2)}) collective-permute-start(bf16[528,1536]{1,0:T(8,128)(2,1)} %pad_maximum_fusion), channel_id=1, source_target_pairs={{0,2},{2,4},{3,1},{4,6},{5,3},{6,8},{7,5},{8,10},{9,7},{10,12},{11... | collective-permute-start | bytes 4866056 | tf_op jit(solution)/shard_map/ppermute | solution.py:26
  10.1 4.9 %collective-permute-start = (bf16[256,1536]{1,0:T(8,128)(2,1)}, bf16[256,1536]{1,0:T(8,128)(2,1)}, u32[]{:S(2)}, u32[]{:S(2)}) collective-permute-start(bf16[256,1536]{1,0:T(8,128)(2,1)} %k_ref.3), channel_id=1, source_target_pairs={{0,1},{1,0},{2,3},{3,2},{4,5},{5,4},{6,7},{7,6},{8,9},{9,8},{10,11... | collective-permute-start | bytes 2359304 | tf_op jit(solution)/shard_map/ppermute | solution.py:26
  10.3 7.0 %collective-permute-start.1 = (bf16[256,1536]{1,0:T(8,128)(2,1)}, bf16[256,1536]{1,0:T(8,128)(2,1)}, u32[]{:S(2)}, u32[]{:S(2)}) collective-permute-start(bf16[256,1536]{1,0:T(8,128)(2,1)} %v_ref.3), channel_id=1, source_target_pairs={{0,1},{1,0},{2,3},{3,2},{4,5},{5,4},{6,7},{7,6},{8,9},{9,8},{10,11... | collective-permute-start | bytes 2359304 | tf_op jit(solution)/shard_map/ppermute | solution.py:26
  16.1 1.2 copy-start.2
  18.5 1.1 copy-start.1
  88.9 13.7 %collective-permute-start.3 = (f32[12,3,256]{2,0,1:T(8,128)S(1)}, f32[12,3,256]{2,0,1:T(8,128)S(1)}, u32[]{:S(2)}, u32[]{:S(2)}) collective-permute-start(f32[12,3,256]{2,0,1:T(8,128)S(1)} %copy.35), channel_id=1, source_target_pairs={{0,2},{2,4},{3,1},{4,6},{5,3},{6,8},{7,5},{8,10},{9,7},{10,12},{11... | collective-permute-start | bytes 110600 | tf_op jit(solution)/shard_map/ppermute | solution.py:26
  90.8 1.5 copy-start
  97.7 7.0 %collective-permute-start.5 = (f32[12,3,256]{2,0,1:T(8,128)S(1)}, f32[12,3,256]{2,0,1:T(8,128)S(1)}, u32[]{:S(2)}, u32[]{:S(2)}) collective-permute-start(f32[12,3,256]{2,0,1:T(8,128)S(1)} %copy.36), channel_id=1, source_target_pairs={{1,3},{2,0},{3,5},{4,2},{5,7},{6,4},{7,9},{8,6},{9,11},{10,8},{11,... | collective-permute-start | bytes 110600 | tf_op jit(solution)/shard_map/ppermute | solution.py:26
  104.9 6.8 %copy-start.11 = (f32[12,2,256]{2,1,0:T(2,128)}, f32[12,2,256]{2,1,0:T(2,128)S(1)}, u32[]{:S(2)}) copy-start(f32[12,2,256]{2,1,0:T(2,128)S(1)} %pad_maximum_fusion.1.f_ref) | copy-start | bytes 73732
  104.9 15.7 %collective-permute-start.6 = (f32[12,2,256]{2,1,0:T(2,128)S(1)}, f32[12,2,256]{2,1,0:T(2,128)S(1)}, u32[]{:S(2)}, u32[]{:S(2)}) collective-permute-start(f32[12,2,256]{2,1,0:T(2,128)S(1)} %pad_maximum_fusion.1.f_ref), channel_id=1, source_target_pairs={{1,3},{2,0},{3,5},{4,2},{5,7},{6,4},{7,9},{8,6},{9,11},{10,8},{11,... | collective-permute-start | bytes 73736 | tf_op jit(solution)/shard_map/ppermute | solution.py:26
  109.6 11.0 %collective-permute-start.7 = (f32[12,2,256]{2,1,0:T(2,128)S(1)}, f32[12,2,256]{2,1,0:T(2,128)S(1)}, u32[]{:S(2)}, u32[]{:S(2)}) collective-permute-start(f32[12,2,256]{2,1,0:T(2,128)S(1)} %pad_maximum_fusion.1.f_ref), channel_id=1, source_target_pairs={{0,2},{2,4},{3,1},{4,6},{5,3},{6,8},{7,5},{8,10},{9,7},{10,12},{11... | collective-permute-start | bytes 73736 | tf_op jit(solution)/shard_map/ppermute | solution.py:26
  120.6 0.6 copy-start.18
  120.7 9.5 %copy-start.10 = (f32[12,2,256]{2,1,0:T(2,128)}, f32[12,2,256]{2,1,0:T(2,128)S(1)}, u32[]{:S(2)}) copy-start(f32[12,2,256]{2,1,0:T(2,128)S(1)} %collective-permute-done.7.f_ref) | copy-start | bytes 73732
  121.3 8.9 %copy-start.4 = (f32[512,1536]{1,0:T(8,128)S(1)}, f32[512,1536]{1,0:T(8,128)}, u32[]{:S(2)}) copy-start(f32[512,1536]{1,0:T(8,128)} %get-tuple-element.27) | copy-start | bytes 9437188
  132.9 43.3 %collective-permute-start.11 = (f32[256,1536]{1,0:T(8,128)}, f32[256,1536]{1,0:T(8,128)}, u32[]{:S(2)}, u32[]{:S(2)}) collective-permute-start(f32[256,1536]{1,0:T(8,128)} %slice_add_fusion), channel_id=1, source_target_pairs={{0,1},{1,0},{2,3},{3,2},{4,5},{5,4},{6,7},{7,6},{8,9},{9,8},{10,11... | collective-permute-start | bytes 4718600 | tf_op jit(solution)/shard_map/ppermute | solution.py:26
  132.9 13.9 %copy-start.3 = (f32[512,1536]{1,0:T(8,128)S(1)}, f32[512,1536]{1,0:T(8,128)}, u32[]{:S(2)}) copy-start(f32[512,1536]{1,0:T(8,128)} %get-tuple-element.24) | copy-start | bytes 9437188
  132.9 39.6 %collective-permute-start.8 = (bf16[256,1536]{1,0:T(8,128)(2,1)}, bf16[256,1536]{1,0:T(8,128)(2,1)}, u32[]{:S(2)}, u32[]{:S(2)}) collective-permute-start(bf16[256,1536]{1,0:T(8,128)(2,1)} %get-tuple-element.20), channel_id=1, source_target_pairs={{0,2},{2,4},{3,1},{4,6},{5,3},{6,8},{7,5},{8,10},{9,7},{10,12},{11... | collective-permute-start | bytes 2359304 | tf_op jit(solution)/shard_map/ppermute | solution.py:26
  144.9 28.3 %collective-permute-start.9 = (bf16[256,1536]{1,0:T(8,128)(2,1)}, bf16[256,1536]{1,0:T(8,128)(2,1)S(1)}, u32[]{:S(2)}, u32[]{:S(2)}) collective-permute-start(bf16[256,1536]{1,0:T(8,128)(2,1)} %get-tuple-element.22), channel_id=1, source_target_pairs={{1,3},{2,0},{3,5},{4,2},{5,7},{6,4},{7,9},{8,6},{9,11},{10,8},{11,... | collective-permute-start | bytes 2359304 | tf_op jit(solution)/shard_map/ppermute | solution.py:26
  146.9 29.3 %copy-start.7 = (f32[512,1536]{1,0:T(8,128)S(1)}, f32[512,1536]{1,0:T(8,128)}, u32[]{:S(2)}) copy-start(f32[512,1536]{1,0:T(8,128)} %get-tuple-element.26) | copy-start | bytes 9437188
  146.9 29.3 %copy-start.9 = (f32[256,1536]{1,0:T(8,128)S(1)}, f32[256,1536]{1,0:T(8,128)}, u32[]{:S(2)}) copy-start(f32[256,1536]{1,0:T(8,128)} %get-tuple-element.28) | copy-start | bytes 4718596
  148.6 30.6 %collective-permute-start.10 = (f32[256,1536]{1,0:T(8,128)S(1)}, f32[256,1536]{1,0:T(8,128)S(1)}, u32[]{:S(2)}, u32[]{:S(2)}) collective-permute-start(f32[256,1536]{1,0:T(8,128)S(1)} %slice_add_fusion.1), channel_id=1, source_target_pairs={{0,1},{1,0},{2,3},{3,2},{4,5},{5,4},{6,7},{7,6},{8,9},{9,8},{10,11... | collective-permute-start | bytes 4718600 | tf_op jit(solution)/shard_map/ppermute | solution.py:26
  173.2 3.0 %copy-start.5 = (f32[512,1536]{1,0:T(8,128)S(1)}, f32[512,1536]{1,0:T(8,128)}, u32[]{:S(2)}) copy-start(f32[512,1536]{1,0:T(8,128)} %get-tuple-element.27) | copy-start | bytes 9437188
  176.2 3.0 %copy-start.6 = (f32[512,1536]{1,0:T(8,128)S(1)}, f32[512,1536]{1,0:T(8,128)}, u32[]{:S(2)}) copy-start(f32[512,1536]{1,0:T(8,128)} %get-tuple-element.23) | copy-start | bytes 9437188
  176.2 3.0 %copy-start.8 = (f32[256,1536]{1,0:T(8,128)S(1)}, f32[256,1536]{1,0:T(8,128)}, u32[]{:S(2)}) copy-start(f32[256,1536]{1,0:T(8,128)} %get-tuple-element.25) | copy-start | bytes 4718596

commit v8 on v7

--- a/solution.py
+++ b/solution.py
@@ -64,7 +64,7 @@
 
 SCALE = HDIM ** (-0.5)
 NT = (((1,), (1,)), ((), ()))
-STEP_HEADS = 4
+STEP_HEADS = 6
 
 
 def slot_scores(q, g, k, v):

time: 183 us -> 182 us (level)
  no operation moved by 1% of the time
where the time goes in v8:
time: 182 us; the launch traced here: 181 us
  waiting for transfers between devices  78.6 us (43%)
  Pallas kernels  41.8 us (23%)
  starting transfers between devices  27.3 us (15%)
  other arithmetic  16.1 us (9%)
  local copies, waits for them, and re-layouts  15.3 us (8%)
    ppermute x12, waiting for transfers between devices, permute(): return lax.ppermute(value, 'tm', pairs)  78.6 us
    ppermute x12, starting transfers between devices, permute(): return lax.ppermute(value, 'tm', pairs)  27.3 us
    pallas_call x3, Pallas kernels, slot_back(): pl.pallas_call(back_kernel, grid=(HEADS // STEP_HEADS,), in_specs=slot_sp...  25.1 us
    pallas_call x3, Pallas kernels, slot_stats(): pl.pallas_call(stats_kernel, grid=(HEADS // STEP_HEADS,), in_specs=slot_s...  16.7 us
    unnamed x42, local copies, waits for them, and re-layouts  5.36 us
    convert_element_type x3, local copies, waits for them, and re-layouts, local(): mask_t = jnp.broadcast_to(mask4.T[:, None, :, None], (nkb, BLOCK, blocks,...  3.86 us
  transfers between devices with their start and end apart: 12, of which 4 were waited for; matrix products, arithmetic and copies ran while one was open for 12% of the time, Pallas kernels for 18%

profile of v8, /device:TPU:8, one launch (start us, length us, event | category | flops | bytes accessed | tf_op | source)
XLA Modules:
  0.0 180.6 jit_solution(8611358640070807259)
XLA Ops:
  0.6 0.7 broadcast_compare_fusion
  1.3 0.1 reshape.188
  1.4 0.0 copy-start.13
  1.4 0.0 copy-start.14
  1.4 0.0 copy-start.15
  1.5 0.0 copy-start.16
  1.5 0.0 copy-start.19
  1.5 0.0 copy-start.17
  1.5 2.7 %pad_maximum_fusion = bf16[528,1536]{1,0:T(8,128)(2,1)} fusion(bf16[16,1536]{1,0:T(8,128)(2,1)S(1)} %pad_convert_fusion, bf16[256,1536]{1,0:T(8,128)(2,1)} %g_ref.3, bf16[256,1536]{1,0:T(8,128)(2,1)} %q_ref.3), kind=kLoop, calls=%fused_computation | loop fusion | flops 4866048 | bytes 3244032 | tf_op jit(solution)/shard_map/concatenate | solution.py:172
  4.2 3.3 %collective-permute-start.2 = (bf16[528,1536]{1,0:T(8,128)(2,1)}, bf16[528,1536]{1,0:T(8,128)(2,1)}, u32[]{:S(2)}, u32[]{:S(2)}) collective-permute-start(bf16[528,1536]{1,0:T(8,128)(2,1)} %pad_maximum_fusion), channel_id=1, source_target_pairs={{1,3},{2,0},{3,5},{4,2},{5,7},{6,4},{7,9},{8,6},{9,11},{10,8},{11,... | collective-permute-start | bytes 4866056 | tf_op jit(solution)/shard_map/ppermute | solution.py:26
  7.5 2.5 %collective-permute-start.4 = (bf16[528,1536]{1,0:T(8,128)(2,1)}, bf16[528,1536]{1,0:T(8,128)(2,1)S(1)}, u32[]{:S(2)}, u32[]{:S(2)}) collective-permute-start(bf16[528,1536]{1,0:T(8,128)(2,1)} %pad_maximum_fusion), channel_id=1, source_target_pairs={{0,2},{2,4},{3,1},{4,6},{5,3},{6,8},{7,5},{8,10},{9,7},{10,12},{11... | collective-permute-start | bytes 4866056 | tf_op jit(solution)/shard_map/ppermute | solution.py:26
  10.1 0.2 collective-permute-start
  10.3 0.3 collective-permute-start.1
  10.7 0.1 fusion.7
  10.8 0.1 copy.41
  10.9 0.2 broadcast_in_dim.33
  11.2 1.4 convert_element_type.44.m_ref
  12.6 1.2 constant_dynamic-update-slice_fusion.1
  13.8 1.2 constant_dynamic-update-slice_fusion.3
  15.0 1.2 constant_dynamic-update-slice_fusion.k_ref
  16.2 1.2 copy-done.2
  17.3 0.0 collective-permute-done.1
  17.3 1.2 constant_dynamic-update-slice_fusion.2.v_ref
  18.5 1.1 copy-done.1
  19.7 6.4 %shard_map.256 = f32[12,3,256]{2,1,0:T(4,128)} custom-call(bf16[256,1536]{1,0:T(8,128)(2,1)} %q_ref.3, bf16[256,1536]{1,0:T(8,128)(2,1)} %g_ref.3, bf16[512,1536]{1,0:T(8,128)(2,1)} %copy-done.2, bf16[512,1536]{1,0:T(8,128)(2,1)} %copy-done.1, f32[512,256]{1,0:T(8,128)} %convert_element_type.44.m_ref), custom_call_target="tpu_custom_call" | custom-call | flops 805306368 | bytes 4718592 | tf_op jit(solution)/shard_map/pallas_call | solution.py:124
  26.0 0.9 fusion.34
  27.0 52.2 %collective-permute-done.2.q_ref.g_ref = bf16[528,1536]{1,0:T(8,128)(2,1)} collective-permute-done((bf16[528,1536]{1,0:T(8,128)(2,1)}, bf16[528,1536]{1,0:T(8,128)(2,1)}, u32[]{:S(2)}, u32[]{:S(2)}) %collective-permute-start.2) | collective-permute-done | bytes 1622048 | tf_op jit(solution)/shard_map/ppermute | solution.py:26
  79.2 0.6 compare_reduce_fusion.1
  79.8 0.1 reshape.196
  79.9 0.1 fusion.11
  80.0 0.1 copy.43
  80.1 0.1 convert_bitcast_fusion
  80.2 0.2 broadcast_in_dim.35
  80.4 1.4 convert_element_type.47.m_ref
  81.8 6.3 %shard_map.257 = f32[12,3,256]{2,1,0:T(4,128)} custom-call(bf16[528,1536]{1,0:T(8,128)(2,1)} %collective-permute-done.2.q_ref.g_ref, bf16[528,1536]{1,0:T(8,128)(2,1)} %collective-permute-done.2.q_ref.g_ref, bf16[512,1536]{1,0:T(8,128)(2,1)} %copy-done.2, bf16[512,1536]{1,0:T(8,128)(2,1)} %copy-done.1, f32[512,256]{1,0:T(8,128)} %convert_element_type.47.m_ref), custom_call_target="tpu_custom_call" | custom-call | flops 805306368 | bytes 4718592 | tf_op jit(solution)/shard_map/pallas_call | solution.py:124
  88.1 0.8 copy.35
  88.9 1.9 %collective-permute-start.3 = (f32[12,3,256]{2,0,1:T(8,128)S(1)}, f32[12,3,256]{2,0,1:T(8,128)S(1)}, u32[]{:S(2)}, u32[]{:S(2)}) collective-permute-start(f32[12,3,256]{2,0,1:T(8,128)S(1)} %copy.35), channel_id=1, source_target_pairs={{0,2},{2,4},{3,1},{4,6},{5,3},{6,8},{7,5},{8,10},{9,7},{10,12},{11... | collective-permute-start | bytes 110600 | tf_op jit(solution)/shard_map/ppermute | solution.py:26
  90.8 0.0 collective-permute-done.4.q_ref.g_ref
  90.8 0.1 reshape.198
  90.9 0.1 fusion.22
  91.0 0.1 copy.45
  91.1 0.1 broadcast_in_dim.36
  91.3 1.0 convert_element_type.50.m_ref
  92.3 4.1 %shard_map.258 = f32[12,3,256]{2,1,0:T(4,128)} custom-call(bf16[528,1536]{1,0:T(8,128)(2,1)} %copy-done, bf16[528,1536]{1,0:T(8,128)(2,1)} %copy-done, bf16[256,1536]{1,0:T(8,128)(2,1)} %k_ref.3, bf16[256,1536]{1,0:T(8,128)(2,1)} %v_ref.3, f32[256,256]{1,0:T(8,128)} %convert_element_type.50.m_ref), custom_call_target="tpu_custom_call" | custom-call | flops 402653184 | bytes 3145728 | tf_op jit(solution)/shard_map/pallas_call | solution.py:124
  96.4 0.8 copy.36
  97.2 4.8 %collective-permute-start.5 = (f32[12,3,256]{2,0,1:T(8,128)S(1)}, f32[12,3,256]{2,0,1:T(8,128)S(1)}, u32[]{:S(2)}, u32[]{:S(2)}) collective-permute-start(f32[12,3,256]{2,0,1:T(8,128)S(1)} %copy.36), channel_id=1, source_target_pairs={{1,3},{2,0},{3,5},{4,2},{5,7},{6,4},{7,9},{8,6},{9,11},{10,8},{11,... | collective-permute-start | bytes 110600 | tf_op jit(solution)/shard_map/ppermute | solution.py:26
  102.1 0.0 collective-permute-done.3
  102.1 2.1 %collective-permute-done.5 = f32[12,3,256]{2,0,1:T(8,128)S(1)} collective-permute-done((f32[12,3,256]{2,0,1:T(8,128)S(1)}, f32[12,3,256]{2,0,1:T(8,128)S(1)}, u32[]{:S(2)}, u32[]{:S(2)}) %collective-permute-start.5) | collective-permute-done | bytes 36896 | tf_op jit(solution)/shard_map/ppermute | solution.py:26
  104.4 4.7 %collective-permute-start.6 = (f32[12,2,256]{2,1,0:T(2,128)S(1)}, f32[12,2,256]{2,1,0:T(2,128)S(1)}, u32[]{:S(2)}, u32[]{:S(2)}) collective-permute-start(f32[12,2,256]{2,1,0:T(2,128)S(1)} %pad_maximum_fusion.1.f_ref), channel_id=1, source_target_pairs={{1,3},{2,0},{3,5},{4,2},{5,7},{6,4},{7,9},{8,6},{9,11},{10,8},{11,... | collective-permute-start | bytes 73736 | tf_op jit(solution)/shard_map/ppermute | solution.py:26
  109.1 2.2 %collective-permute-start.7 = (f32[12,2,256]{2,1,0:T(2,128)S(1)}, f32[12,2,256]{2,1,0:T(2,128)S(1)}, u32[]{:S(2)}, u32[]{:S(2)}) collective-permute-start(f32[12,2,256]{2,1,0:T(2,128)S(1)} %pad_maximum_fusion.1.f_ref), channel_id=1, source_target_pairs={{0,2},{2,4},{3,1},{4,6},{5,3},{6,8},{7,5},{8,10},{9,7},{10,12},{11... | collective-permute-start | bytes 73736 | tf_op jit(solution)/shard_map/ppermute | solution.py:26
  111.3 9.1 %shard_map.259 = (f32[256,1536]{1,0:T(8,128)}, f32[512,1536]{1,0:T(8,128)}, f32[512,1536]{1,0:T(8,128)}) custom-call(bf16[256,1536]{1,0:T(8,128)(2,1)} %q_ref.3, bf16[256,1536]{1,0:T(8,128)(2,1)} %g_ref.3, bf16[512,1536]{1,0:T(8,128)(2,1)} %copy-done.2, bf16[512,1536]{1,0:T(8,128)(2,1)} %copy-done.1, f32[512,256]{1,0:T(8,128)} %convert_element_type.44.m_ref, ...), custom_call_target="tpu_custom_call" | custom-call | flops 2013265920 | bytes 14155776 | tf_op jit(solution)/shard_map/pallas_call | solution.py:140
  120.5 0.6 copy-done.18
  121.1 9.0 %shard_map.260 = (bf16[256,1536]{1,0:T(8,128)(2,1)}, f32[512,1536]{1,0:T(8,128)}, f32[512,1536]{1,0:T(8,128)}) custom-call(bf16[528,1536]{1,0:T(8,128)(2,1)} %collective-permute-done.2.q_ref.g_ref, bf16[528,1536]{1,0:T(8,128)(2,1)} %collective-permute-done.2.q_ref.g_ref, bf16[512,1536]{1,0:T(8,128)(2,1)} %copy-done.2, bf16[512,1536]{1,0:T(8,128)(2,1)} %copy-done.1, ...), custom_call_target="tpu_custom_call" | custom-call | flops 2013265920 | bytes 14155776 | tf_op jit(solution)/shard_map/pallas_call | solution.py:140
  130.1 2.7 %slice_add_fusion = f32[256,1536]{1,0:T(8,128)} fusion(f32[512,1536]{1,0:T(8,128)S(1)} %copy-done.4, f32[512,1536]{1,0:T(8,128)} %get-tuple-element.26), kind=kLoop, calls=%fused_computation.2 | loop fusion | flops 393216 | bytes 4718592 | tf_op jit(solution)/shard_map/add | solution.py:235
  132.8 5.1 %collective-permute-start.8 = (bf16[256,1536]{1,0:T(8,128)(2,1)}, bf16[256,1536]{1,0:T(8,128)(2,1)}, u32[]{:S(2)}, u32[]{:S(2)}) collective-permute-start(bf16[256,1536]{1,0:T(8,128)(2,1)} %get-tuple-element.20), channel_id=1, source_target_pairs={{0,2},{2,4},{3,1},{4,6},{5,3},{6,8},{7,5},{8,10},{9,7},{10,12},{11... | collective-permute-start | bytes 2359304 | tf_op jit(solution)/shard_map/ppermute | solution.py:26
  137.9 7.0 %shard_map.261 = (bf16[256,1536]{1,0:T(8,128)(2,1)}, f32[256,1536]{1,0:T(8,128)}, f32[256,1536]{1,0:T(8,128)}) custom-call(bf16[528,1536]{1,0:T(8,128)(2,1)} %copy-done, bf16[528,1536]{1,0:T(8,128)(2,1)} %copy-done, bf16[256,1536]{1,0:T(8,128)(2,1)} %k_ref.3, bf16[256,1536]{1,0:T(8,128)(2,1)} %v_ref.3, f32[256,256]{1,0:T(8,128)} %convert_element_type.50.m_ref, ...), custom_call_target="tpu_custom_call" | custom-call | flops 1006632960 | bytes 9437184 | tf_op jit(solution)/shard_map/pallas_call | solution.py:140
  144.9 1.9 %collective-permute-start.9 = (bf16[256,1536]{1,0:T(8,128)(2,1)}, bf16[256,1536]{1,0:T(8,128)(2,1)S(1)}, u32[]{:S(2)}, u32[]{:S(2)}) collective-permute-start(bf16[256,1536]{1,0:T(8,128)(2,1)} %get-tuple-element.22), channel_id=1, source_target_pairs={{1,3},{2,0},{3,5},{4,2},{5,7},{6,4},{7,9},{8,6},{9,11},{10,8},{11,... | collective-permute-start | bytes 2359304 | tf_op jit(solution)/shard_map/ppermute | solution.py:26
  146.8 1.8 slice_add_fusion.1
  148.6 0.3 collective-permute-start.10
  148.9 23.5 %collective-permute-done.8 = bf16[256,1536]{1,0:T(8,128)(2,1)} collective-permute-done((bf16[256,1536]{1,0:T(8,128)(2,1)}, bf16[256,1536]{1,0:T(8,128)(2,1)}, u32[]{:S(2)}, u32[]{:S(2)}) %collective-permute-start.8) | collective-permute-done | bytes 786464 | tf_op jit(solution)/shard_map/ppermute | solution.py:26
  172.4 0.8 collective-permute-done.9
  173.1 2.9 %add_convert_fusion.2 = bf16[256,1536]{1,0:T(8,128)(2,1)} fusion(bf16[256,1536]{1,0:T(8,128)(2,1)S(1)} %collective-permute-done.9, f32[256,1536]{1,0:T(8,128)} %get-tuple-element.16, bf16[256,1536]{1,0:T(8,128)(2,1)} %collective-permute-done.8), kind=kLoop, calls=%fused_computation.5 | loop fusion | flops 1966080 | bytes 3932160 | tf_op jit(solution)/shard_map/convert_element_type | solution.py:240
  176.1 3.0 %add_convert_fusion = bf16[256,1536]{1,0:T(8,128)(2,1)} fusion(f32[256,1536]{1,0:T(8,128)} %collective-permute-done.11, f32[256,1536]{1,0:T(8,128)S(1)} %copy-done.9, f32[512,1536]{1,0:T(8,128)S(1)} %copy-done.5, f32[512,1536]{1,0:T(8,128)S(1)} %copy-done.7), kind=kLoop, calls=%fused_computation.1 | loop fusion | flops 1572864 | bytes 7077888 | tf_op jit(solution)/shard_map/convert_element_type | solution.py:242
  179.1 1.4 add_convert_fusion.1
  (54 shorter events, 0.3 us)
Async XLA Ops:
  1.4 9.2 %copy-start.12 = (s32[4,30]{1,0:T(4,128)S(1)}, s32[4,30]{1,0:T(4,128)}, u32[]{:S(2)}) copy-start(s32[4,30]{1,0:T(4,128)} %param.29) | copy-start | bytes 1444
  1.4 9.2 %copy-start.13 = (bf16[4,30,4]{1,2,0:T(4,128)(2,1)S(1)}, bf16[4,30,4]{1,2,0:T(4,128)(2,1)}, u32[]{:S(2)}) copy-start(bf16[4,30,4]{1,2,0:T(4,128)(2,1)} %constant.132) | copy-start | bytes 2884
  1.4 9.2 %copy-start.14 = (bf16[4,30,4]{1,2,0:T(4,128)(2,1)S(1)}, bf16[4,30,4]{1,2,0:T(4,128)(2,1)}, u32[]{:S(2)}) copy-start(bf16[4,30,4]{1,2,0:T(4,128)(2,1)} %constant.131) | copy-start | bytes 2884
  1.4 9.2 %copy-start.15 = (bf16[4,30,4]{1,2,0:T(4,128)(2,1)S(1)}, bf16[4,30,4]{1,2,0:T(4,128)(2,1)}, u32[]{:S(2)}) copy-start(bf16[4,30,4]{1,2,0:T(4,128)(2,1)} %constant.134) | copy-start | bytes 2884
  1.5 9.2 %copy-start.16 = (bf16[4,30,4]{1,2,0:T(4,128)(2,1)S(1)}, bf16[4,30,4]{1,2,0:T(4,128)(2,1)}, u32[]{:S(2)}) copy-start(bf16[4,30,4]{1,2,0:T(4,128)(2,1)} %constant.133) | copy-start | bytes 2884
  1.5 9.2 %copy-start.19 = (bf16[4,30,4]{1,2,0:T(4,128)(2,1)S(1)}, bf16[4,30,4]{1,2,0:T(4,128)(2,1)}, u32[]{:S(2)}) copy-start(bf16[4,30,4]{1,2,0:T(4,128)(2,1)} %constant.135) | copy-start | bytes 2884
  1.5 9.4 %copy-start.17 = (pred[4,8]{0,1:T(8,128)(4,1)S(1)}, pred[4,8]{0,1:T(8,128)(4,1)}, u32[]{:S(2)}) copy-start(pred[4,8]{0,1:T(8,128)(4,1)} %constant.62) | copy-start | bytes 100
  4.2 74.9 %collective-permute-start.2 = (bf16[528,1536]{1,0:T(8,128)(2,1)}, bf16[528,1536]{1,0:T(8,128)(2,1)}, u32[]{:S(2)}, u32[]{:S(2)}) collective-permute-start(bf16[528,1536]{1,0:T(8,128)(2,1)} %pad_maximum_fusion), channel_id=1, source_target_pairs={{1,3},{2,0},{3,5},{4,2},{5,7},{6,4},{7,9},{8,6},{9,11},{10,8},{11,... | collective-permute-start | bytes 4866056 | tf_op jit(solution)/shard_map/ppermute | solution.py:26
  7.5 83.3 %collective-permute-start.4 = (bf16[528,1536]{1,0:T(8,128)(2,1)}, bf16[528,1536]{1,0:T(8,128)(2,1)S(1)}, u32[]{:S(2)}, u32[]{:S(2)}) collective-permute-start(bf16[528,1536]{1,0:T(8,128)(2,1)} %pad_maximum_fusion), channel_id=1, source_target_pairs={{0,2},{2,4},{3,1},{4,6},{5,3},{6,8},{7,5},{8,10},{9,7},{10,12},{11... | collective-permute-start | bytes 4866056 | tf_op jit(solution)/shard_map/ppermute | solution.py:26
  10.1 4.9 %collective-permute-start = (bf16[256,1536]{1,0:T(8,128)(2,1)}, bf16[256,1536]{1,0:T(8,128)(2,1)}, u32[]{:S(2)}, u32[]{:S(2)}) collective-permute-start(bf16[256,1536]{1,0:T(8,128)(2,1)} %k_ref.3), channel_id=1, source_target_pairs={{0,1},{1,0},{2,3},{3,2},{4,5},{5,4},{6,7},{7,6},{8,9},{9,8},{10,11... | collective-permute-start | bytes 2359304 | tf_op jit(solution)/shard_map/ppermute | solution.py:26
  10.3 7.0 %collective-permute-start.1 = (bf16[256,1536]{1,0:T(8,128)(2,1)}, bf16[256,1536]{1,0:T(8,128)(2,1)}, u32[]{:S(2)}, u32[]{:S(2)}) collective-permute-start(bf16[256,1536]{1,0:T(8,128)(2,1)} %v_ref.3), channel_id=1, source_target_pairs={{0,1},{1,0},{2,3},{3,2},{4,5},{5,4},{6,7},{7,6},{8,9},{9,8},{10,11... | collective-permute-start | bytes 2359304 | tf_op jit(solution)/shard_map/ppermute | solution.py:26
  16.1 1.2 copy-start.2
  18.5 1.1 copy-start.1
  88.9 13.2 %collective-permute-start.3 = (f32[12,3,256]{2,0,1:T(8,128)S(1)}, f32[12,3,256]{2,0,1:T(8,128)S(1)}, u32[]{:S(2)}, u32[]{:S(2)}) collective-permute-start(f32[12,3,256]{2,0,1:T(8,128)S(1)} %copy.35), channel_id=1, source_target_pairs={{0,2},{2,4},{3,1},{4,6},{5,3},{6,8},{7,5},{8,10},{9,7},{10,12},{11... | collective-permute-start | bytes 110600 | tf_op jit(solution)/shard_map/ppermute | solution.py:26
  90.8 1.5 copy-start
  97.2 7.0 %collective-permute-start.5 = (f32[12,3,256]{2,0,1:T(8,128)S(1)}, f32[12,3,256]{2,0,1:T(8,128)S(1)}, u32[]{:S(2)}, u32[]{:S(2)}) collective-permute-start(f32[12,3,256]{2,0,1:T(8,128)S(1)} %copy.36), channel_id=1, source_target_pairs={{1,3},{2,0},{3,5},{4,2},{5,7},{6,4},{7,9},{8,6},{9,11},{10,8},{11,... | collective-permute-start | bytes 110600 | tf_op jit(solution)/shard_map/ppermute | solution.py:26
  104.4 7.0 %copy-start.11 = (f32[12,2,256]{2,1,0:T(2,128)}, f32[12,2,256]{2,1,0:T(2,128)S(1)}, u32[]{:S(2)}) copy-start(f32[12,2,256]{2,1,0:T(2,128)S(1)} %pad_maximum_fusion.1.f_ref) | copy-start | bytes 73732
  104.4 16.1 %collective-permute-start.6 = (f32[12,2,256]{2,1,0:T(2,128)S(1)}, f32[12,2,256]{2,1,0:T(2,128)S(1)}, u32[]{:S(2)}, u32[]{:S(2)}) collective-permute-start(f32[12,2,256]{2,1,0:T(2,128)S(1)} %pad_maximum_fusion.1.f_ref), channel_id=1, source_target_pairs={{1,3},{2,0},{3,5},{4,2},{5,7},{6,4},{7,9},{8,6},{9,11},{10,8},{11,... | collective-permute-start | bytes 73736 | tf_op jit(solution)/shard_map/ppermute | solution.py:26
  109.1 11.4 %collective-permute-start.7 = (f32[12,2,256]{2,1,0:T(2,128)S(1)}, f32[12,2,256]{2,1,0:T(2,128)S(1)}, u32[]{:S(2)}, u32[]{:S(2)}) collective-permute-start(f32[12,2,256]{2,1,0:T(2,128)S(1)} %pad_maximum_fusion.1.f_ref), channel_id=1, source_target_pairs={{0,2},{2,4},{3,1},{4,6},{5,3},{6,8},{7,5},{8,10},{9,7},{10,12},{11... | collective-permute-start | bytes 73736 | tf_op jit(solution)/shard_map/ppermute | solution.py:26
  120.5 0.6 copy-start.18
  120.5 9.6 %copy-start.10 = (f32[12,2,256]{2,1,0:T(2,128)}, f32[12,2,256]{2,1,0:T(2,128)S(1)}, u32[]{:S(2)}) copy-start(f32[12,2,256]{2,1,0:T(2,128)S(1)} %collective-permute-done.7.f_ref) | copy-start | bytes 73732
  121.1 9.0 %copy-start.4 = (f32[512,1536]{1,0:T(8,128)S(1)}, f32[512,1536]{1,0:T(8,128)}, u32[]{:S(2)}) copy-start(f32[512,1536]{1,0:T(8,128)} %get-tuple-element.27) | copy-start | bytes 9437188
  132.8 43.3 %collective-permute-start.11 = (f32[256,1536]{1,0:T(8,128)}, f32[256,1536]{1,0:T(8,128)}, u32[]{:S(2)}, u32[]{:S(2)}) collective-permute-start(f32[256,1536]{1,0:T(8,128)} %slice_add_fusion), channel_id=1, source_target_pairs={{0,1},{1,0},{2,3},{3,2},{4,5},{5,4},{6,7},{7,6},{8,9},{9,8},{10,11... | collective-permute-start | bytes 4718600 | tf_op jit(solution)/shard_map/ppermute | solution.py:26
  132.8 14.0 %copy-start.3 = (f32[512,1536]{1,0:T(8,128)S(1)}, f32[512,1536]{1,0:T(8,128)}, u32[]{:S(2)}) copy-start(f32[512,1536]{1,0:T(8,128)} %get-tuple-element.24) | copy-start | bytes 9437188
  132.8 39.6 %collective-permute-start.8 = (bf16[256,1536]{1,0:T(8,128)(2,1)}, bf16[256,1536]{1,0:T(8,128)(2,1)}, u32[]{:S(2)}, u32[]{:S(2)}) collective-permute-start(bf16[256,1536]{1,0:T(8,128)(2,1)} %get-tuple-element.20), channel_id=1, source_target_pairs={{0,2},{2,4},{3,1},{4,6},{5,3},{6,8},{7,5},{8,10},{9,7},{10,12},{11... | collective-permute-start | bytes 2359304 | tf_op jit(solution)/shard_map/ppermute | solution.py:26
  144.9 28.3 %collective-permute-start.9 = (bf16[256,1536]{1,0:T(8,128)(2,1)}, bf16[256,1536]{1,0:T(8,128)(2,1)S(1)}, u32[]{:S(2)}, u32[]{:S(2)}) collective-permute-start(bf16[256,1536]{1,0:T(8,128)(2,1)} %get-tuple-element.22), channel_id=1, source_target_pairs={{1,3},{2,0},{3,5},{4,2},{5,7},{6,4},{7,9},{8,6},{9,11},{10,8},{11,... | collective-permute-start | bytes 2359304 | tf_op jit(solution)/shard_map/ppermute | solution.py:26
  146.8 29.3 %copy-start.7 = (f32[512,1536]{1,0:T(8,128)S(1)}, f32[512,1536]{1,0:T(8,128)}, u32[]{:S(2)}) copy-start(f32[512,1536]{1,0:T(8,128)} %get-tuple-element.26) | copy-start | bytes 9437188
  146.8 29.3 %copy-start.9 = (f32[256,1536]{1,0:T(8,128)S(1)}, f32[256,1536]{1,0:T(8,128)}, u32[]{:S(2)}) copy-start(f32[256,1536]{1,0:T(8,128)} %get-tuple-element.28) | copy-start | bytes 4718596
  148.6 30.5 %collective-permute-start.10 = (f32[256,1536]{1,0:T(8,128)S(1)}, f32[256,1536]{1,0:T(8,128)S(1)}, u32[]{:S(2)}, u32[]{:S(2)}) collective-permute-start(f32[256,1536]{1,0:T(8,128)S(1)} %slice_add_fusion.1), channel_id=1, source_target_pairs={{0,1},{1,0},{2,3},{3,2},{4,5},{5,4},{6,7},{7,6},{8,9},{9,8},{10,11... | collective-permute-start | bytes 4718600 | tf_op jit(solution)/shard_map/ppermute | solution.py:26
  173.1 3.0 %copy-start.5 = (f32[512,1536]{1,0:T(8,128)S(1)}, f32[512,1536]{1,0:T(8,128)}, u32[]{:S(2)}) copy-start(f32[512,1536]{1,0:T(8,128)} %get-tuple-element.27) | copy-start | bytes 9437188
  176.1 3.0 %copy-start.6 = (f32[512,1536]{1,0:T(8,128)S(1)}, f32[512,1536]{1,0:T(8,128)}, u32[]{:S(2)}) copy-start(f32[512,1536]{1,0:T(8,128)} %get-tuple-element.23) | copy-start | bytes 9437188
  176.1 3.0 %copy-start.8 = (f32[256,1536]{1,0:T(8,128)S(1)}, f32[256,1536]{1,0:T(8,128)}, u32[]{:S(2)}) copy-start(f32[256,1536]{1,0:T(8,128)} %get-tuple-element.25) | copy-start | bytes 4718596

commit v9 on v7

--- a/solution.py
+++ b/solution.py
@@ -233,14 +233,13 @@
     from_near = down_even(near_q)
 
     back_kg, back_vg = swap_cores((far_k[tok:] + own_k[tok:], far_v[tok:] + own_v[tok:]))
-    key_grad = far_k[:tok] + own_k[:tok] + near_k + back_kg
-    value_grad = far_v[:tok] + own_v[:tok] + near_v + back_vg
+    key_grad = (far_k[:tok] + own_k[:tok] + near_k + back_kg).astype(jnp.bfloat16)
+    value_grad = (far_v[:tok] + own_v[:tok] + near_v + back_vg).astype(jnp.bfloat16)
+    from_far, from_near, key_grad, value_grad = lax.optimization_barrier(
+        (from_far, from_near, key_grad, value_grad)
+    )
     query_grad = own_q + from_far.astype(jnp.float32) + from_near.astype(jnp.float32)
-    return (
-        query_grad.astype(jnp.bfloat16),
-        key_grad.astype(jnp.bfloat16),
-        value_grad.astype(jnp.bfloat16),
-    )
+    return query_grad.astype(jnp.bfloat16), key_grad, value_grad
 
 
 def solution(mesh):

time: 183 us -> 181 us (0.989)
  waiting for transfers between devices: 78.8 us -> 73.1 us
  other arithmetic: 16.1 us -> 20.1 us
    ppermute x12, waiting for transfers between devices: 78.8 us -> 73.1 us  [permute(): return lax.ppermute(value, 'tm', pairs)]
    convert_element_type x3, other arithmetic: 7.36 us -> 9.68 us  [the longest x1 4.37 us: local(): (far_k[:tok] + own_k[:tok] + near_k + back_kg).astype(jnp.bfloat16)]
    unnamed x42 -> x36, local copies, waits for them, and re-layouts: 5.36 us -> 5.34 us
  transfers between devices with their start and end apart: 12 -> 12, of which waited for: 4 -> 3; matrix products, arithmetic and copies ran while one was open for 12% -> 13% of each run, Pallas kernels for 18% -> 18%
where the time goes in v9:
time: 181 us; the launch traced here: 179 us
  waiting for transfers between devices  73.1 us (40%)
  Pallas kernels  41.7 us (23%)
  starting transfers between devices  27.3 us (15%)
  other arithmetic  20.1 us (11%)
  local copies, waits for them, and re-layouts  15.3 us (8%)
    ppermute x12, waiting for transfers between devices, permute(): return lax.ppermute(value, 'tm', pairs)  73.1 us
    ppermute x12, starting transfers between devices, permute(): return lax.ppermute(value, 'tm', pairs)  27.3 us
    pallas_call x3, Pallas kernels, slot_back(): pl.pallas_call(back_kernel, grid=(HEADS // STEP_HEADS,), in_specs=slot_sp...  24.6 us
    pallas_call x3, Pallas kernels, slot_stats(): pl.pallas_call(stats_kernel, grid=(HEADS // STEP_HEADS,), in_specs=slot_s...  17.1 us
    unnamed x36, local copies, waits for them, and re-layouts  5.34 us
    convert_element_type x1, other arithmetic, local(): (far_k[:tok] + own_k[:tok] + near_k + back_kg).astype(jnp.bfloat16)  4.37 us
    convert_element_type x3, local copies, waits for them, and re-layouts, local(): mask_t = jnp.broadcast_to(mask4.T[:, None, :, None], (nkb, BLOCK, blocks,...  3.88 us
  transfers between devices with their start and end apart: 12, of which 3 were waited for; matrix products, arithmetic and copies ran while one was open for 13% of the time, Pallas kernels for 18%

profile of v9, /device:TPU:8, one launch (start us, length us, event | category | flops | bytes accessed | tf_op | source)
XLA Modules:
  0.0 178.9 jit_solution(4305505545527761562)
XLA Ops:
  0.6 0.7 broadcast_compare_fusion
  1.3 0.1 reshape.188
  1.4 0.0 copy-start.10
  1.4 0.0 copy-start.11
  1.4 0.0 copy-start.12
  1.5 0.0 copy-start.13
  1.5 0.0 copy-start.16
  1.5 0.0 copy-start.14
  1.5 2.7 %pad_maximum_fusion = bf16[528,1536]{1,0:T(8,128)(2,1)} fusion(bf16[16,1536]{1,0:T(8,128)(2,1)S(1)} %pad_convert_fusion, bf16[256,1536]{1,0:T(8,128)(2,1)} %g_ref.3, bf16[256,1536]{1,0:T(8,128)(2,1)} %q_ref.3), kind=kLoop, calls=%fused_computation | loop fusion | flops 4866048 | bytes 3244032 | tf_op jit(solution)/shard_map/concatenate | solution.py:172
  4.2 3.3 %collective-permute-start.2 = (bf16[528,1536]{1,0:T(8,128)(2,1)}, bf16[528,1536]{1,0:T(8,128)(2,1)}, u32[]{:S(2)}, u32[]{:S(2)}) collective-permute-start(bf16[528,1536]{1,0:T(8,128)(2,1)} %pad_maximum_fusion), channel_id=1, source_target_pairs={{1,3},{2,0},{3,5},{4,2},{5,7},{6,4},{7,9},{8,6},{9,11},{10,8},{11,... | collective-permute-start | bytes 4866056 | tf_op jit(solution)/shard_map/ppermute | solution.py:26
  7.5 2.5 %collective-permute-start.4 = (bf16[528,1536]{1,0:T(8,128)(2,1)}, bf16[528,1536]{1,0:T(8,128)(2,1)S(1)}, u32[]{:S(2)}, u32[]{:S(2)}) collective-permute-start(bf16[528,1536]{1,0:T(8,128)(2,1)} %pad_maximum_fusion), channel_id=1, source_target_pairs={{0,2},{2,4},{3,1},{4,6},{5,3},{6,8},{7,5},{8,10},{9,7},{10,12},{11... | collective-permute-start | bytes 4866056 | tf_op jit(solution)/shard_map/ppermute | solution.py:26
  10.0 0.2 collective-permute-start
  10.3 0.3 collective-permute-start.1
  10.7 0.1 fusion.7
  10.8 0.1 copy.41
  10.9 0.2 broadcast_in_dim.33
  11.1 1.4 convert_element_type.44.m_ref
  12.5 1.2 constant_dynamic-update-slice_fusion.1
  13.7 1.2 constant_dynamic-update-slice_fusion.3
  14.9 1.2 constant_dynamic-update-slice_fusion.k_ref
  16.1 1.2 copy-done.2
  17.3 1.2 constant_dynamic-update-slice_fusion.2.v_ref
  18.5 1.1 copy-done.1
  19.6 6.3 %shard_map.256 = f32[12,3,256]{2,1,0:T(4,128)} custom-call(bf16[256,1536]{1,0:T(8,128)(2,1)} %q_ref.3, bf16[256,1536]{1,0:T(8,128)(2,1)} %g_ref.3, bf16[512,1536]{1,0:T(8,128)(2,1)} %copy-done.2, bf16[512,1536]{1,0:T(8,128)(2,1)} %copy-done.1, f32[512,256]{1,0:T(8,128)} %convert_element_type.44.m_ref), custom_call_target="tpu_custom_call" | custom-call | flops 805306368 | bytes 4718592 | tf_op jit(solution)/shard_map/pallas_call | solution.py:124
  25.9 0.9 fusion.34
  26.9 52.3 %collective-permute-done.2.q_ref.g_ref = bf16[528,1536]{1,0:T(8,128)(2,1)} collective-permute-done((bf16[528,1536]{1,0:T(8,128)(2,1)}, bf16[528,1536]{1,0:T(8,128)(2,1)}, u32[]{:S(2)}, u32[]{:S(2)}) %collective-permute-start.2) | collective-permute-done | bytes 1622048 | tf_op jit(solution)/shard_map/ppermute | solution.py:26
  79.1 0.7 compare_reduce_fusion.1
  79.8 0.1 reshape.196
  79.9 0.1 fusion.11
  80.0 0.1 copy.43
  80.1 0.1 convert_bitcast_fusion
  80.2 0.2 broadcast_in_dim.35
  80.4 1.4 convert_element_type.47.m_ref
  81.8 6.3 %shard_map.257 = f32[12,3,256]{2,1,0:T(4,128)} custom-call(bf16[528,1536]{1,0:T(8,128)(2,1)} %collective-permute-done.2.q_ref.g_ref, bf16[528,1536]{1,0:T(8,128)(2,1)} %collective-permute-done.2.q_ref.g_ref, bf16[512,1536]{1,0:T(8,128)(2,1)} %copy-done.2, bf16[512,1536]{1,0:T(8,128)(2,1)} %copy-done.1, f32[512,256]{1,0:T(8,128)} %convert_element_type.47.m_ref), custom_call_target="tpu_custom_call" | custom-call | flops 805306368 | bytes 4718592 | tf_op jit(solution)/shard_map/pallas_call | solution.py:124
  88.1 0.8 copy.35
  88.9 1.9 %collective-permute-start.3 = (f32[12,3,256]{2,0,1:T(8,128)S(1)}, f32[12,3,256]{2,0,1:T(8,128)S(1)}, u32[]{:S(2)}, u32[]{:S(2)}) collective-permute-start(f32[12,3,256]{2,0,1:T(8,128)S(1)} %copy.35), channel_id=1, source_target_pairs={{0,2},{2,4},{3,1},{4,6},{5,3},{6,8},{7,5},{8,10},{9,7},{10,12},{11... | collective-permute-start | bytes 110600 | tf_op jit(solution)/shard_map/ppermute | solution.py:26
  90.8 0.0 collective-permute-done.4.q_ref.g_ref
  90.9 0.1 reshape.198
  90.9 0.1 fusion.22
  91.1 0.1 copy.45
  91.2 0.1 broadcast_in_dim.36
  91.3 1.1 convert_element_type.50.m_ref
  92.4 4.6 %shard_map.258 = f32[12,3,256]{2,1,0:T(4,128)} custom-call(bf16[528,1536]{1,0:T(8,128)(2,1)} %copy-done, bf16[528,1536]{1,0:T(8,128)(2,1)} %copy-done, bf16[256,1536]{1,0:T(8,128)(2,1)} %k_ref.3, bf16[256,1536]{1,0:T(8,128)(2,1)} %v_ref.3, f32[256,256]{1,0:T(8,128)} %convert_element_type.50.m_ref), custom_call_target="tpu_custom_call" | custom-call | flops 402653184 | bytes 3145728 | tf_op jit(solution)/shard_map/pallas_call | solution.py:124
  97.0 0.8 copy.36
  97.8 4.8 %collective-permute-start.5 = (f32[12,3,256]{2,0,1:T(8,128)S(1)}, f32[12,3,256]{2,0,1:T(8,128)S(1)}, u32[]{:S(2)}, u32[]{:S(2)}) collective-permute-start(f32[12,3,256]{2,0,1:T(8,128)S(1)} %copy.36), channel_id=1, source_target_pairs={{1,3},{2,0},{3,5},{4,2},{5,7},{6,4},{7,9},{8,6},{9,11},{10,8},{11,... | collective-permute-start | bytes 110600 | tf_op jit(solution)/shard_map/ppermute | solution.py:26
  102.6 2.1 %collective-permute-done.5 = f32[12,3,256]{2,0,1:T(8,128)S(1)} collective-permute-done((f32[12,3,256]{2,0,1:T(8,128)S(1)}, f32[12,3,256]{2,0,1:T(8,128)S(1)}, u32[]{:S(2)}, u32[]{:S(2)}) %collective-permute-start.5) | collective-permute-done | bytes 36896 | tf_op jit(solution)/shard_map/ppermute | solution.py:26
  104.9 0.0 copy-start.8
  105.0 4.7 %collective-permute-start.6 = (f32[12,2,256]{2,1,0:T(2,128)S(1)}, f32[12,2,256]{2,1,0:T(2,128)S(1)}, u32[]{:S(2)}, u32[]{:S(2)}) collective-permute-start(f32[12,2,256]{2,1,0:T(2,128)S(1)} %pad_maximum_fusion.1.f_ref), channel_id=1, source_target_pairs={{1,3},{2,0},{3,5},{4,2},{5,7},{6,4},{7,9},{8,6},{9,11},{10,8},{11,... | collective-permute-start | bytes 73736 | tf_op jit(solution)/shard_map/ppermute | solution.py:26
  109.7 2.0 %collective-permute-start.7 = (f32[12,2,256]{2,1,0:T(2,128)S(1)}, f32[12,2,256]{2,1,0:T(2,128)S(1)}, u32[]{:S(2)}, u32[]{:S(2)}) collective-permute-start(f32[12,2,256]{2,1,0:T(2,128)S(1)} %pad_maximum_fusion.1.f_ref), channel_id=1, source_target_pairs={{0,2},{2,4},{3,1},{4,6},{5,3},{6,8},{7,5},{8,10},{9,7},{10,12},{11... | collective-permute-start | bytes 73736 | tf_op jit(solution)/shard_map/ppermute | solution.py:26
  111.7 9.0 %shard_map.259 = (f32[256,1536]{1,0:T(8,128)}, f32[512,1536]{1,0:T(8,128)}, f32[512,1536]{1,0:T(8,128)}) custom-call(bf16[256,1536]{1,0:T(8,128)(2,1)} %q_ref.3, bf16[256,1536]{1,0:T(8,128)(2,1)} %g_ref.3, bf16[512,1536]{1,0:T(8,128)(2,1)} %copy-done.2, bf16[512,1536]{1,0:T(8,128)(2,1)} %copy-done.1, f32[512,256]{1,0:T(8,128)} %convert_element_type.44.m_ref, ...), custom_call_target="tpu_custom_call" | custom-call | flops 2013265920 | bytes 14155776 | tf_op jit(solution)/shard_map/pallas_call | solution.py:140
  120.8 0.0 copy-start.15
  120.8 0.0 copy-start.7
  120.8 0.6 copy-done.15
  121.4 8.8 %shard_map.260 = (bf16[256,1536]{1,0:T(8,128)(2,1)}, f32[512,1536]{1,0:T(8,128)}, f32[512,1536]{1,0:T(8,128)}) custom-call(bf16[528,1536]{1,0:T(8,128)(2,1)} %collective-permute-done.2.q_ref.g_ref, bf16[528,1536]{1,0:T(8,128)(2,1)} %collective-permute-done.2.q_ref.g_ref, bf16[512,1536]{1,0:T(8,128)(2,1)} %copy-done.2, bf16[512,1536]{1,0:T(8,128)(2,1)} %copy-done.1, ...), custom_call_target="tpu_custom_call" | custom-call | flops 2013265920 | bytes 14155776 | tf_op jit(solution)/shard_map/pallas_call | solution.py:140
  130.2 3.4 %slice_add_fusion.1 = f32[256,1536]{1,0:T(8,128)} fusion(f32[512,1536]{1,0:T(8,128)} %get-tuple-element.28, f32[512,1536]{1,0:T(8,128)} %get-tuple-element.27), kind=kLoop, calls=%fused_computation.5 | loop fusion | flops 393216 | bytes 4718592 | tf_op jit(solution)/shard_map/add | solution.py:235
  133.5 2.7 %slice_add_fusion = f32[256,1536]{1,0:T(8,128)} fusion(f32[512,1536]{1,0:T(8,128)S(1)} %copy-done.3, f32[512,1536]{1,0:T(8,128)} %get-tuple-element.30), kind=kLoop, calls=%fused_computation.3 | loop fusion | flops 393216 | bytes 4718592 | tf_op jit(solution)/shard_map/add | solution.py:235
  136.3 0.5 collective-permute-start.11
  136.8 5.0 %collective-permute-start.8 = (bf16[256,1536]{1,0:T(8,128)(2,1)}, bf16[256,1536]{1,0:T(8,128)(2,1)}, u32[]{:S(2)}, u32[]{:S(2)}) collective-permute-start(bf16[256,1536]{1,0:T(8,128)(2,1)} %get-tuple-element.24), channel_id=1, source_target_pairs={{0,2},{2,4},{3,1},{4,6},{5,3},{6,8},{7,5},{8,10},{9,7},{10,12},{11... | collective-permute-start | bytes 2359304 | tf_op jit(solution)/shard_map/ppermute | solution.py:26
  141.8 6.8 %shard_map.261 = (bf16[256,1536]{1,0:T(8,128)(2,1)}, f32[256,1536]{1,0:T(8,128)}, f32[256,1536]{1,0:T(8,128)}) custom-call(bf16[528,1536]{1,0:T(8,128)(2,1)} %copy-done, bf16[528,1536]{1,0:T(8,128)(2,1)} %copy-done, bf16[256,1536]{1,0:T(8,128)(2,1)} %k_ref.3, bf16[256,1536]{1,0:T(8,128)(2,1)} %v_ref.3, f32[256,256]{1,0:T(8,128)} %convert_element_type.50.m_ref, ...), custom_call_target="tpu_custom_call" | custom-call | flops 1006632960 | bytes 9437184 | tf_op jit(solution)/shard_map/pallas_call | solution.py:140
  148.6 1.9 %collective-permute-start.9 = (bf16[256,1536]{1,0:T(8,128)(2,1)}, bf16[256,1536]{1,0:T(8,128)(2,1)S(1)}, u32[]{:S(2)}, u32[]{:S(2)}) collective-permute-start(bf16[256,1536]{1,0:T(8,128)(2,1)} %get-tuple-element.26), channel_id=1, source_target_pairs={{1,3},{2,0},{3,5},{4,2},{5,7},{6,4},{7,9},{8,6},{9,11},{10,8},{11,... | collective-permute-start | bytes 2359304 | tf_op jit(solution)/shard_map/ppermute | solution.py:26
  150.5 4.4 %add_convert_fusion.2 = bf16[256,1536]{1,0:T(8,128)(2,1)} fusion(f32[256,1536]{1,0:T(8,128)} %collective-permute-done.10, f32[256,1536]{1,0:T(8,128)} %get-tuple-element.29, f32[512,1536]{1,0:T(8,128)} %get-tuple-element.28, f32[512,1536]{1,0:T(8,128)} %get-tuple-element.27), kind=kLoop, calls=%fused_computation.4 | loop fusion | flops 1572864 | bytes 7077888 | tf_op jit(solution)/shard_map/convert_element_type | solution.py:236
  154.9 3.0 %add_convert_fusion.1 = bf16[256,1536]{1,0:T(8,128)(2,1)} fusion(f32[256,1536]{1,0:T(8,128)} %collective-permute-done.11, f32[256,1536]{1,0:T(8,128)S(1)} %copy-done.5, f32[512,1536]{1,0:T(8,128)S(1)} %copy-done.3, f32[512,1536]{1,0:T(8,128)S(1)} %copy-done.4), kind=kLoop, calls=%fused_computation.2 | loop fusion | flops 1572864 | bytes 7077888 | tf_op jit(solution)/shard_map/convert_element_type | solution.py:237
  157.9 18.7 %collective-permute-done.8 = bf16[256,1536]{1,0:T(8,128)(2,1)} collective-permute-done((bf16[256,1536]{1,0:T(8,128)(2,1)}, bf16[256,1536]{1,0:T(8,128)(2,1)}, u32[]{:S(2)}, u32[]{:S(2)}) %collective-permute-start.8) | collective-permute-done | bytes 786464 | tf_op jit(solution)/shard_map/ppermute | solution.py:26
  176.5 2.3 %add_convert_fusion = bf16[256,1536]{1,0:T(8,128)(2,1)} fusion(bf16[256,1536]{1,0:T(8,128)(2,1)S(1)} %collective-permute-done.9, f32[256,1536]{1,0:T(8,128)S(1)} %copy-done.6, bf16[256,1536]{1,0:T(8,128)(2,1)} %collective-permute-done.8), kind=kLoop, calls=%fused_computation.1 | loop fusion | flops 1966080 | bytes 3932160 | tf_op jit(solution)/shard_map/convert_element_type | solution.py:242
  (48 shorter events, 0.3 us)
Async XLA Ops:
  1.4 9.2 %copy-start.9 = (s32[4,30]{1,0:T(4,128)S(1)}, s32[4,30]{1,0:T(4,128)}, u32[]{:S(2)}) copy-start(s32[4,30]{1,0:T(4,128)} %param.29) | copy-start | bytes 1444
  1.4 9.2 %copy-start.10 = (bf16[4,30,4]{1,2,0:T(4,128)(2,1)S(1)}, bf16[4,30,4]{1,2,0:T(4,128)(2,1)}, u32[]{:S(2)}) copy-start(bf16[4,30,4]{1,2,0:T(4,128)(2,1)} %constant.133) | copy-start | bytes 2884
  1.4 9.2 %copy-start.11 = (bf16[4,30,4]{1,2,0:T(4,128)(2,1)S(1)}, bf16[4,30,4]{1,2,0:T(4,128)(2,1)}, u32[]{:S(2)}) copy-start(bf16[4,30,4]{1,2,0:T(4,128)(2,1)} %constant.134) | copy-start | bytes 2884
  1.4 9.2 %copy-start.12 = (bf16[4,30,4]{1,2,0:T(4,128)(2,1)S(1)}, bf16[4,30,4]{1,2,0:T(4,128)(2,1)}, u32[]{:S(2)}) copy-start(bf16[4,30,4]{1,2,0:T(4,128)(2,1)} %constant.132) | copy-start | bytes 2884
  1.5 9.2 %copy-start.13 = (bf16[4,30,4]{1,2,0:T(4,128)(2,1)S(1)}, bf16[4,30,4]{1,2,0:T(4,128)(2,1)}, u32[]{:S(2)}) copy-start(bf16[4,30,4]{1,2,0:T(4,128)(2,1)} %constant.131) | copy-start | bytes 2884
  1.5 9.2 %copy-start.16 = (bf16[4,30,4]{1,2,0:T(4,128)(2,1)S(1)}, bf16[4,30,4]{1,2,0:T(4,128)(2,1)}, u32[]{:S(2)}) copy-start(bf16[4,30,4]{1,2,0:T(4,128)(2,1)} %constant.135) | copy-start | bytes 2884
  1.5 9.4 %copy-start.14 = (pred[4,8]{0,1:T(8,128)(4,1)S(1)}, pred[4,8]{0,1:T(8,128)(4,1)}, u32[]{:S(2)}) copy-start(pred[4,8]{0,1:T(8,128)(4,1)} %constant.62) | copy-start | bytes 100
  4.2 74.9 %collective-permute-start.2 = (bf16[528,1536]{1,0:T(8,128)(2,1)}, bf16[528,1536]{1,0:T(8,128)(2,1)}, u32[]{:S(2)}, u32[]{:S(2)}) collective-permute-start(bf16[528,1536]{1,0:T(8,128)(2,1)} %pad_maximum_fusion), channel_id=1, source_target_pairs={{1,3},{2,0},{3,5},{4,2},{5,7},{6,4},{7,9},{8,6},{9,11},{10,8},{11,... | collective-permute-start | bytes 4866056 | tf_op jit(solution)/shard_map/ppermute | solution.py:26
  7.5 83.3 %collective-permute-start.4 = (bf16[528,1536]{1,0:T(8,128)(2,1)}, bf16[528,1536]{1,0:T(8,128)(2,1)S(1)}, u32[]{:S(2)}, u32[]{:S(2)}) collective-permute-start(bf16[528,1536]{1,0:T(8,128)(2,1)} %pad_maximum_fusion), channel_id=1, source_target_pairs={{0,2},{2,4},{3,1},{4,6},{5,3},{6,8},{7,5},{8,10},{9,7},{10,12},{11... | collective-permute-start | bytes 4866056 | tf_op jit(solution)/shard_map/ppermute | solution.py:26
  10.0 4.9 %collective-permute-start = (bf16[256,1536]{1,0:T(8,128)(2,1)}, bf16[256,1536]{1,0:T(8,128)(2,1)}, u32[]{:S(2)}, u32[]{:S(2)}) collective-permute-start(bf16[256,1536]{1,0:T(8,128)(2,1)} %k_ref.3), channel_id=1, source_target_pairs={{0,1},{1,0},{2,3},{3,2},{4,5},{5,4},{6,7},{7,6},{8,9},{9,8},{10,11... | collective-permute-start | bytes 2359304 | tf_op jit(solution)/shard_map/ppermute | solution.py:26
  10.3 7.0 %collective-permute-start.1 = (bf16[256,1536]{1,0:T(8,128)(2,1)}, bf16[256,1536]{1,0:T(8,128)(2,1)}, u32[]{:S(2)}, u32[]{:S(2)}) collective-permute-start(bf16[256,1536]{1,0:T(8,128)(2,1)} %v_ref.3), channel_id=1, source_target_pairs={{0,1},{1,0},{2,3},{3,2},{4,5},{5,4},{6,7},{7,6},{8,9},{9,8},{10,11... | collective-permute-start | bytes 2359304 | tf_op jit(solution)/shard_map/ppermute | solution.py:26
  16.1 1.2 copy-start.2
  18.5 1.1 copy-start.1
  88.9 13.7 %collective-permute-start.3 = (f32[12,3,256]{2,0,1:T(8,128)S(1)}, f32[12,3,256]{2,0,1:T(8,128)S(1)}, u32[]{:S(2)}, u32[]{:S(2)}) collective-permute-start(f32[12,3,256]{2,0,1:T(8,128)S(1)} %copy.35), channel_id=1, source_target_pairs={{0,2},{2,4},{3,1},{4,6},{5,3},{6,8},{7,5},{8,10},{9,7},{10,12},{11... | collective-permute-start | bytes 110600 | tf_op jit(solution)/shard_map/ppermute | solution.py:26
  90.8 1.6 copy-start
  97.8 7.0 %collective-permute-start.5 = (f32[12,3,256]{2,0,1:T(8,128)S(1)}, f32[12,3,256]{2,0,1:T(8,128)S(1)}, u32[]{:S(2)}, u32[]{:S(2)}) collective-permute-start(f32[12,3,256]{2,0,1:T(8,128)S(1)} %copy.36), channel_id=1, source_target_pairs={{1,3},{2,0},{3,5},{4,2},{5,7},{6,4},{7,9},{8,6},{9,11},{10,8},{11,... | collective-permute-start | bytes 110600 | tf_op jit(solution)/shard_map/ppermute | solution.py:26
  104.9 6.8 %copy-start.8 = (f32[12,2,256]{2,1,0:T(2,128)}, f32[12,2,256]{2,1,0:T(2,128)S(1)}, u32[]{:S(2)}) copy-start(f32[12,2,256]{2,1,0:T(2,128)S(1)} %pad_maximum_fusion.1.f_ref) | copy-start | bytes 73732
  105.0 15.8 %collective-permute-start.6 = (f32[12,2,256]{2,1,0:T(2,128)S(1)}, f32[12,2,256]{2,1,0:T(2,128)S(1)}, u32[]{:S(2)}, u32[]{:S(2)}) collective-permute-start(f32[12,2,256]{2,1,0:T(2,128)S(1)} %pad_maximum_fusion.1.f_ref), channel_id=1, source_target_pairs={{1,3},{2,0},{3,5},{4,2},{5,7},{6,4},{7,9},{8,6},{9,11},{10,8},{11,... | collective-permute-start | bytes 73736 | tf_op jit(solution)/shard_map/ppermute | solution.py:26
  109.7 11.1 %collective-permute-start.7 = (f32[12,2,256]{2,1,0:T(2,128)S(1)}, f32[12,2,256]{2,1,0:T(2,128)S(1)}, u32[]{:S(2)}, u32[]{:S(2)}) collective-permute-start(f32[12,2,256]{2,1,0:T(2,128)S(1)} %pad_maximum_fusion.1.f_ref), channel_id=1, source_target_pairs={{0,2},{2,4},{3,1},{4,6},{5,3},{6,8},{7,5},{8,10},{9,7},{10,12},{11... | collective-permute-start | bytes 73736 | tf_op jit(solution)/shard_map/ppermute | solution.py:26
  120.8 0.6 copy-start.15
  120.8 9.4 %copy-start.7 = (f32[12,2,256]{2,1,0:T(2,128)}, f32[12,2,256]{2,1,0:T(2,128)S(1)}, u32[]{:S(2)}) copy-start(f32[12,2,256]{2,1,0:T(2,128)S(1)} %collective-permute-done.7.f_ref) | copy-start | bytes 73732
  130.2 3.4 %copy-start.3 = (f32[512,1536]{1,0:T(8,128)S(1)}, f32[512,1536]{1,0:T(8,128)}, u32[]{:S(2)}) copy-start(f32[512,1536]{1,0:T(8,128)} %get-tuple-element.31) | copy-start | bytes 9437188
  133.5 16.9 %collective-permute-start.10 = (f32[256,1536]{1,0:T(8,128)}, f32[256,1536]{1,0:T(8,128)}, u32[]{:S(2)}, u32[]{:S(2)}) collective-permute-start(f32[256,1536]{1,0:T(8,128)} %slice_add_fusion.1), channel_id=1, source_target_pairs={{0,1},{1,0},{2,3},{3,2},{4,5},{5,4},{6,7},{7,6},{8,9},{9,8},{10,11... | collective-permute-start | bytes 4718600 | tf_op jit(solution)/shard_map/ppermute | solution.py:26
  136.3 18.6 %collective-permute-start.11 = (f32[256,1536]{1,0:T(8,128)}, f32[256,1536]{1,0:T(8,128)}, u32[]{:S(2)}, u32[]{:S(2)}) collective-permute-start(f32[256,1536]{1,0:T(8,128)} %slice_add_fusion), channel_id=1, source_target_pairs={{0,1},{1,0},{2,3},{3,2},{4,5},{5,4},{6,7},{7,6},{8,9},{9,8},{10,11... | collective-permute-start | bytes 4718600 | tf_op jit(solution)/shard_map/ppermute | solution.py:26
  136.8 39.7 %collective-permute-start.8 = (bf16[256,1536]{1,0:T(8,128)(2,1)}, bf16[256,1536]{1,0:T(8,128)(2,1)}, u32[]{:S(2)}, u32[]{:S(2)}) collective-permute-start(bf16[256,1536]{1,0:T(8,128)(2,1)} %get-tuple-element.24), channel_id=1, source_target_pairs={{0,2},{2,4},{3,1},{4,6},{5,3},{6,8},{7,5},{8,10},{9,7},{10,12},{11... | collective-permute-start | bytes 2359304 | tf_op jit(solution)/shard_map/ppermute | solution.py:26
  148.6 28.0 %collective-permute-start.9 = (bf16[256,1536]{1,0:T(8,128)(2,1)}, bf16[256,1536]{1,0:T(8,128)(2,1)S(1)}, u32[]{:S(2)}, u32[]{:S(2)}) collective-permute-start(bf16[256,1536]{1,0:T(8,128)(2,1)} %get-tuple-element.26), channel_id=1, source_target_pairs={{1,3},{2,0},{3,5},{4,2},{5,7},{6,4},{7,9},{8,6},{9,11},{10,8},{11,... | collective-permute-start | bytes 2359304 | tf_op jit(solution)/shard_map/ppermute | solution.py:26
  150.5 4.4 %copy-start.4 = (f32[512,1536]{1,0:T(8,128)S(1)}, f32[512,1536]{1,0:T(8,128)}, u32[]{:S(2)}) copy-start(f32[512,1536]{1,0:T(8,128)} %get-tuple-element.30) | copy-start | bytes 9437188
  150.5 4.4 %copy-start.5 = (f32[256,1536]{1,0:T(8,128)S(1)}, f32[256,1536]{1,0:T(8,128)}, u32[]{:S(2)}) copy-start(f32[256,1536]{1,0:T(8,128)} %get-tuple-element.32) | copy-start | bytes 4718596
  154.9 21.6 %copy-start.6 = (f32[256,1536]{1,0:T(8,128)S(1)}, f32[256,1536]{1,0:T(8,128)}, u32[]{:S(2)}) copy-start(f32[256,1536]{1,0:T(8,128)} %get-tuple-element.20) | copy-start | bytes 4718596

commit v10 on v9

--- a/solution.py
+++ b/solution.py
@@ -232,9 +232,14 @@
     from_far = up_even(far_q)
     from_near = down_even(near_q)
 
-    back_kg, back_vg = swap_cores((far_k[tok:] + own_k[tok:], far_v[tok:] + own_v[tok:]))
-    key_grad = (far_k[:tok] + own_k[:tok] + near_k + back_kg).astype(jnp.bfloat16)
-    value_grad = (far_v[:tok] + own_v[:tok] + near_v + back_vg).astype(jnp.bfloat16)
+    def low(x):
+        return x.astype(jnp.bfloat16).astype(jnp.float32)
+
+    back_kg, back_vg = swap_cores(
+        (low(far_k[tok:]) + low(own_k[tok:]), low(far_v[tok:]) + low(own_v[tok:]))
+    )
+    key_grad = (low(far_k[:tok]) + low(own_k[:tok]) + low(near_k) + back_kg).astype(jnp.bfloat16)
+    value_grad = (low(far_v[:tok]) + low(own_v[:tok]) + low(near_v) + back_vg).astype(jnp.bfloat16)
     from_far, from_near, key_grad, value_grad = lax.optimization_barrier(
         (from_far, from_near, key_grad, value_grad)
     )

time: 181 us -> 183 us (1.011)
    another operation x0 -> x4, other arithmetic: none -> 4.49 us
    add x2, other arithmetic: 6.11 us -> 3.12 us  [the longest x1 1.62 us: local(): low(far_k[tok:]) + low(own_k[tok:])]
    unnamed x36 -> x42, local copies, waits for them, and re-layouts: 5.34 us -> 7.22 us
  transfers between devices with their start and end apart: 12 -> 12, of which waited for: 3 -> 4; matrix products, arithmetic and copies ran while one was open for 13% -> 12% of each run, Pallas kernels for 18% -> 18%
where the time goes in v10:
time: 183 us; the launch traced here: 182 us
  waiting for transfers between devices  74.1 us (40%)
  Pallas kernels  41.7 us (23%)
  starting transfers between devices  27.1 us (15%)
  other arithmetic  20.7 us (11%)
  local copies, waits for them, and re-layouts  17.1 us (9%)
    ppermute x12, waiting for transfers between devices, permute(): return lax.ppermute(value, 'tm', pairs)  74.1 us
    ppermute x12, starting transfers between devices, permute(): return lax.ppermute(value, 'tm', pairs)  27.1 us
    pallas_call x3, Pallas kernels, slot_back(): pl.pallas_call(back_kernel, grid=(HEADS // STEP_HEADS,), in_specs=slot_sp...  24.5 us
    pallas_call x3, Pallas kernels, slot_stats(): pl.pallas_call(stats_kernel, grid=(HEADS // STEP_HEADS,), in_specs=slot_s...  17.1 us
    unnamed x42, local copies, waits for them, and re-layouts  7.22 us
    another operation x4, other arithmetic  4.49 us
    convert_element_type x3, local copies, waits for them, and re-layouts, local(): mask_t = jnp.broadcast_to(mask4.T[:, None, :, None], (nkb, BLOCK, blocks,...  3.87 us
  transfers between devices with their start and end apart: 12, of which 4 were waited for; matrix products, arithmetic and copies ran while one was open for 12% of the time, Pallas kernels for 18%

profile of v10, /device:TPU:8, one launch (start us, length us, event | category | flops | bytes accessed | tf_op | source)
XLA Modules:
  0.0 182.1 jit_solution(17682353944646974579)
XLA Ops:
  0.6 0.7 broadcast_compare_fusion
  1.3 0.1 reshape.188
  1.4 0.0 copy-start.13
  1.4 0.0 copy-start.14
  1.4 0.0 copy-start.15
  1.5 2.7 %pad_maximum_fusion = bf16[528,1536]{1,0:T(8,128)(2,1)} fusion(bf16[16,1536]{1,0:T(8,128)(2,1)S(1)} %pad_convert_fusion, bf16[256,1536]{1,0:T(8,128)(2,1)} %g_ref.3, bf16[256,1536]{1,0:T(8,128)(2,1)} %q_ref.3), kind=kLoop, calls=%fused_computation | loop fusion | flops 4866048 | bytes 3244032 | tf_op jit(solution)/shard_map/concatenate | solution.py:172
  4.2 3.4 %collective-permute-start.4 = (bf16[528,1536]{1,0:T(8,128)(2,1)}, bf16[528,1536]{1,0:T(8,128)(2,1)S(1)}, u32[]{:S(2)}, u32[]{:S(2)}) collective-permute-start(bf16[528,1536]{1,0:T(8,128)(2,1)} %pad_maximum_fusion), channel_id=1, source_target_pairs={{0,2},{2,4},{3,1},{4,6},{5,3},{6,8},{7,5},{8,10},{9,7},{10,12},{11... | collective-permute-start | bytes 4866056 | tf_op jit(solution)/shard_map/ppermute | solution.py:26
  7.6 3.3 %collective-permute-start.2 = (bf16[528,1536]{1,0:T(8,128)(2,1)}, bf16[528,1536]{1,0:T(8,128)(2,1)}, u32[]{:S(2)}, u32[]{:S(2)}) collective-permute-start(bf16[528,1536]{1,0:T(8,128)(2,1)} %pad_maximum_fusion), channel_id=1, source_target_pairs={{1,3},{2,0},{3,5},{4,2},{5,7},{6,4},{7,9},{8,6},{9,11},{10,8},{11,... | collective-permute-start | bytes 4866056 | tf_op jit(solution)/shard_map/ppermute | solution.py:26
  11.0 0.1 collective-permute-start
  11.0 0.5 collective-permute-start.1
  11.6 0.1 fusion.7
  11.7 0.1 copy.41
  11.8 0.2 broadcast_in_dim.33
  12.1 1.4 convert_element_type.88.m_ref
  13.5 1.2 constant_dynamic-update-slice_fusion.1
  14.7 1.2 constant_dynamic-update-slice_fusion.3
  15.9 1.2 constant_dynamic-update-slice_fusion.k_ref
  17.1 1.2 copy-done.2
  18.2 1.2 constant_dynamic-update-slice_fusion.2.v_ref
  19.4 1.1 copy-done.1
  20.5 6.3 %shard_map.256 = f32[12,3,256]{2,1,0:T(4,128)} custom-call(bf16[256,1536]{1,0:T(8,128)(2,1)} %q_ref.3, bf16[256,1536]{1,0:T(8,128)(2,1)} %g_ref.3, bf16[512,1536]{1,0:T(8,128)(2,1)} %copy-done.2, bf16[512,1536]{1,0:T(8,128)(2,1)} %copy-done.1, f32[512,256]{1,0:T(8,128)} %convert_element_type.88.m_ref), custom_call_target="tpu_custom_call" | custom-call | flops 805306368 | bytes 4718592 | tf_op jit(solution)/shard_map/pallas_call | solution.py:124
  26.8 0.9 fusion.34
  27.8 50.4 %collective-permute-done.4.q_ref.g_ref = bf16[528,1536]{1,0:T(8,128)(2,1)S(1)} collective-permute-done((bf16[528,1536]{1,0:T(8,128)(2,1)}, bf16[528,1536]{1,0:T(8,128)(2,1)S(1)}, u32[]{:S(2)}, u32[]{:S(2)}) %collective-permute-start.4) | collective-permute-done | bytes 1622048 | tf_op jit(solution)/shard_map/ppermute | solution.py:26
  78.2 0.1 reshape.198
  78.3 0.1 fusion.22
  78.4 0.1 copy.45
  78.5 0.1 broadcast_in_dim.36
  78.7 1.1 convert_element_type.94.m_ref
  79.7 4.6 %shard_map.258 = f32[12,3,256]{2,1,0:T(4,128)} custom-call(bf16[528,1536]{1,0:T(8,128)(2,1)} %copy-done, bf16[528,1536]{1,0:T(8,128)(2,1)} %copy-done, bf16[256,1536]{1,0:T(8,128)(2,1)} %k_ref.3, bf16[256,1536]{1,0:T(8,128)(2,1)} %v_ref.3, f32[256,256]{1,0:T(8,128)} %convert_element_type.94.m_ref), custom_call_target="tpu_custom_call" | custom-call | flops 402653184 | bytes 3145728 | tf_op jit(solution)/shard_map/pallas_call | solution.py:124
  84.3 0.8 copy.36
  85.1 4.2 %collective-permute-start.5 = (f32[12,3,256]{2,0,1:T(8,128)S(1)}, f32[12,3,256]{2,0,1:T(8,128)S(1)}, u32[]{:S(2)}, u32[]{:S(2)}) collective-permute-start(f32[12,3,256]{2,0,1:T(8,128)S(1)} %copy.36), channel_id=1, source_target_pairs={{1,3},{2,0},{3,5},{4,2},{5,7},{6,4},{7,9},{8,6},{9,11},{10,8},{11,... | collective-permute-start | bytes 110600 | tf_op jit(solution)/shard_map/ppermute | solution.py:26
  89.3 0.7 compare_reduce_fusion.1
  90.0 0.1 reshape.196
  90.1 0.1 fusion.11
  90.2 0.1 copy.43
  90.3 0.1 convert_bitcast_fusion
  90.4 0.2 broadcast_in_dim.35
  90.6 1.4 convert_element_type.91.m_ref
  92.0 6.3 %shard_map.257 = f32[12,3,256]{2,1,0:T(4,128)} custom-call(bf16[528,1536]{1,0:T(8,128)(2,1)} %collective-permute-done.2.q_ref.g_ref, bf16[528,1536]{1,0:T(8,128)(2,1)} %collective-permute-done.2.q_ref.g_ref, bf16[512,1536]{1,0:T(8,128)(2,1)} %copy-done.2, bf16[512,1536]{1,0:T(8,128)(2,1)} %copy-done.1, f32[512,256]{1,0:T(8,128)} %convert_element_type.91.m_ref), custom_call_target="tpu_custom_call" | custom-call | flops 805306368 | bytes 4718592 | tf_op jit(solution)/shard_map/pallas_call | solution.py:124
  98.3 0.8 copy.35
  99.1 2.0 %collective-permute-start.3 = (f32[12,3,256]{2,0,1:T(8,128)S(1)}, f32[12,3,256]{2,0,1:T(8,128)S(1)}, u32[]{:S(2)}, u32[]{:S(2)}) collective-permute-start(f32[12,3,256]{2,0,1:T(8,128)S(1)} %copy.35), channel_id=1, source_target_pairs={{0,2},{2,4},{3,1},{4,6},{5,3},{6,8},{7,5},{8,10},{9,7},{10,12},{11... | collective-permute-start | bytes 110600 | tf_op jit(solution)/shard_map/ppermute | solution.py:26
  101.1 4.8 %collective-permute-done.3 = f32[12,3,256]{2,0,1:T(8,128)S(1)} collective-permute-done((f32[12,3,256]{2,0,1:T(8,128)S(1)}, f32[12,3,256]{2,0,1:T(8,128)S(1)}, u32[]{:S(2)}, u32[]{:S(2)}) %collective-permute-start.3) | collective-permute-done | bytes 36896 | tf_op jit(solution)/shard_map/ppermute | solution.py:26
  106.1 1.9 %collective-permute-start.7 = (f32[12,2,256]{2,1,0:T(2,128)S(1)}, f32[12,2,256]{2,1,0:T(2,128)S(1)}, u32[]{:S(2)}, u32[]{:S(2)}) collective-permute-start(f32[12,2,256]{2,1,0:T(2,128)S(1)} %pad_maximum_fusion.1.f_ref), channel_id=1, source_target_pairs={{0,2},{2,4},{3,1},{4,6},{5,3},{6,8},{7,5},{8,10},{9,7},{10,12},{11... | collective-permute-start | bytes 73736 | tf_op jit(solution)/shard_map/ppermute | solution.py:26
  108.1 4.8 %collective-permute-start.6 = (f32[12,2,256]{2,1,0:T(2,128)S(1)}, f32[12,2,256]{2,1,0:T(2,128)S(1)}, u32[]{:S(2)}, u32[]{:S(2)}) collective-permute-start(f32[12,2,256]{2,1,0:T(2,128)S(1)} %pad_maximum_fusion.1.f_ref), channel_id=1, source_target_pairs={{1,3},{2,0},{3,5},{4,2},{5,7},{6,4},{7,9},{8,6},{9,11},{10,8},{11,... | collective-permute-start | bytes 73736 | tf_op jit(solution)/shard_map/ppermute | solution.py:26
  112.9 9.0 %shard_map.259 = (f32[256,1536]{1,0:T(8,128)}, f32[512,1536]{1,0:T(8,128)}, f32[512,1536]{1,0:T(8,128)}) custom-call(bf16[256,1536]{1,0:T(8,128)(2,1)} %q_ref.3, bf16[256,1536]{1,0:T(8,128)(2,1)} %g_ref.3, bf16[512,1536]{1,0:T(8,128)(2,1)} %copy-done.2, bf16[512,1536]{1,0:T(8,128)(2,1)} %copy-done.1, f32[512,256]{1,0:T(8,128)} %convert_element_type.88.m_ref, ...), custom_call_target="tpu_custom_call" | custom-call | flops 2013265920 | bytes 14155776 | tf_op jit(solution)/shard_map/pallas_call | solution.py:140
  121.9 2.1 %convert.25 = bf16[512,1536]{1,0:T(8,128)(2,1)S(1)} convert(f32[512,1536]{1,0:T(8,128)} %get-tuple-element.31) | non-fusion elementwise | flops 786432 | bytes 4718592 | tf_op jit(solution)/shard_map/convert.8
  124.0 8.8 %shard_map.260 = (bf16[256,1536]{1,0:T(8,128)(2,1)}, f32[512,1536]{1,0:T(8,128)}, f32[512,1536]{1,0:T(8,128)}) custom-call(bf16[528,1536]{1,0:T(8,128)(2,1)} %collective-permute-done.2.q_ref.g_ref, bf16[528,1536]{1,0:T(8,128)(2,1)} %collective-permute-done.2.q_ref.g_ref, bf16[512,1536]{1,0:T(8,128)(2,1)} %copy-done.2, bf16[512,1536]{1,0:T(8,128)(2,1)} %copy-done.1, ...), custom_call_target="tpu_custom_call" | custom-call | flops 2013265920 | bytes 14155776 | tf_op jit(solution)/shard_map/pallas_call | solution.py:140
  132.8 2.1 %convert.24 = bf16[512,1536]{1,0:T(8,128)(2,1)S(1)} convert(f32[512,1536]{1,0:T(8,128)} %get-tuple-element.30) | non-fusion elementwise | flops 786432 | bytes 4718592 | tf_op jit(solution)/shard_map/convert.9
  134.9 1.5 convert_add_fusion
  136.4 0.2 copy-done.5
  136.6 1.3 copy-done.6
  137.9 0.2 convert.23
  138.1 0.9 copy-done.7
  139.0 0.2 convert.22
  139.2 1.6 convert_add_fusion.1
  140.8 0.0 copy-done.3
  140.9 2.2 %collective-permute-start.8 = (bf16[256,1536]{1,0:T(8,128)(2,1)}, bf16[256,1536]{1,0:T(8,128)(2,1)}, u32[]{:S(2)}, u32[]{:S(2)}) collective-permute-start(bf16[256,1536]{1,0:T(8,128)(2,1)} %get-tuple-element.24), channel_id=1, source_target_pairs={{0,2},{2,4},{3,1},{4,6},{5,3},{6,8},{7,5},{8,10},{9,7},{10,12},{11... | collective-permute-start | bytes 2359304 | tf_op jit(solution)/shard_map/ppermute | solution.py:26
  143.1 6.8 %shard_map.261 = (bf16[256,1536]{1,0:T(8,128)(2,1)}, f32[256,1536]{1,0:T(8,128)}, f32[256,1536]{1,0:T(8,128)}) custom-call(bf16[528,1536]{1,0:T(8,128)(2,1)} %copy-done, bf16[528,1536]{1,0:T(8,128)(2,1)} %copy-done, bf16[256,1536]{1,0:T(8,128)(2,1)} %k_ref.3, bf16[256,1536]{1,0:T(8,128)(2,1)} %v_ref.3, f32[256,256]{1,0:T(8,128)} %convert_element_type.94.m_ref, ...), custom_call_target="tpu_custom_call" | custom-call | flops 1006632960 | bytes 9437184 | tf_op jit(solution)/shard_map/pallas_call | solution.py:140
  149.8 4.7 %collective-permute-start.9 = (bf16[256,1536]{1,0:T(8,128)(2,1)}, bf16[256,1536]{1,0:T(8,128)(2,1)S(1)}, u32[]{:S(2)}, u32[]{:S(2)}) collective-permute-start(bf16[256,1536]{1,0:T(8,128)(2,1)} %get-tuple-element.26), channel_id=1, source_target_pairs={{1,3},{2,0},{3,5},{4,2},{5,7},{6,4},{7,9},{8,6},{9,11},{10,8},{11,... | collective-permute-start | bytes 2359304 | tf_op jit(solution)/shard_map/ppermute | solution.py:26
  154.6 3.6 %add_convert_fusion.1 = bf16[256,1536]{1,0:T(8,128)(2,1)} fusion(f32[256,1536]{1,0:T(8,128)} %collective-permute-done.11, bf16[512,1536]{1,0:T(8,128)(2,1)S(1)} %convert.25, bf16[512,1536]{1,0:T(8,128)(2,1)} %copy-done.5, f32[256,1536]{1,0:T(8,128)} %get-tuple-element.32), kind=kLoop, calls=%fused_computation.2 | loop fusion | flops 3145728 | bytes 5505024 | tf_op jit(solution)/shard_map/convert_element_type | solution.py:242
  158.2 2.8 %add_convert_fusion.2 = bf16[256,1536]{1,0:T(8,128)(2,1)} fusion(f32[256,1536]{1,0:T(8,128)} %collective-permute-done.10, bf16[512,1536]{1,0:T(8,128)(2,1)S(1)} %convert.23, bf16[512,1536]{1,0:T(8,128)(2,1)S(1)} %copy-done.4, f32[256,1536]{1,0:T(8,128)S(1)} %copy-done.9), kind=kLoop, calls=%fused_computation.4 | loop fusion | flops 3145728 | bytes 5505024 | tf_op jit(solution)/shard_map/convert_element_type | solution.py:241
  161.0 15.3 %collective-permute-done.8 = bf16[256,1536]{1,0:T(8,128)(2,1)} collective-permute-done((bf16[256,1536]{1,0:T(8,128)(2,1)}, bf16[256,1536]{1,0:T(8,128)(2,1)}, u32[]{:S(2)}, u32[]{:S(2)}) %collective-permute-start.8) | collective-permute-done | bytes 786464 | tf_op jit(solution)/shard_map/ppermute | solution.py:26
  176.3 3.5 %collective-permute-done.9 = bf16[256,1536]{1,0:T(8,128)(2,1)S(1)} collective-permute-done((bf16[256,1536]{1,0:T(8,128)(2,1)}, bf16[256,1536]{1,0:T(8,128)(2,1)S(1)}, u32[]{:S(2)}, u32[]{:S(2)}) %collective-permute-start.9) | collective-permute-done | bytes 786464 | tf_op jit(solution)/shard_map/ppermute | solution.py:26
  179.8 2.4 %add_convert_fusion = bf16[256,1536]{1,0:T(8,128)(2,1)} fusion(bf16[256,1536]{1,0:T(8,128)(2,1)S(1)} %collective-permute-done.9, f32[256,1536]{1,0:T(8,128)S(1)} %copy-done.8, bf16[256,1536]{1,0:T(8,128)(2,1)} %collective-permute-done.8), kind=kLoop, calls=%fused_computation.1 | loop fusion | flops 1966080 | bytes 3932160 | tf_op jit(solution)/shard_map/convert_element_type | solution.py:247
  (58 shorter events, 0.3 us)
Async XLA Ops:
  1.4 10.1 %copy-start.12 = (s32[4,30]{1,0:T(4,128)S(1)}, s32[4,30]{1,0:T(4,128)}, u32[]{:S(2)}) copy-start(s32[4,30]{1,0:T(4,128)} %param.29) | copy-start | bytes 1444
  1.4 10.1 %copy-start.13 = (bf16[4,30,4]{1,2,0:T(4,128)(2,1)S(1)}, bf16[4,30,4]{1,2,0:T(4,128)(2,1)}, u32[]{:S(2)}) copy-start(bf16[4,30,4]{1,2,0:T(4,128)(2,1)} %constant.133) | copy-start | bytes 2884
  1.4 10.1 %copy-start.14 = (bf16[4,30,4]{1,2,0:T(4,128)(2,1)S(1)}, bf16[4,30,4]{1,2,0:T(4,128)(2,1)}, u32[]{:S(2)}) copy-start(bf16[4,30,4]{1,2,0:T(4,128)(2,1)} %constant.134) | copy-start | bytes 2884
  1.4 10.1 %copy-start.15 = (bf16[4,30,4]{1,2,0:T(4,128)(2,1)S(1)}, bf16[4,30,4]{1,2,0:T(4,128)(2,1)}, u32[]{:S(2)}) copy-start(bf16[4,30,4]{1,2,0:T(4,128)(2,1)} %constant.132) | copy-start | bytes 2884
  1.5 10.1 %copy-start.16 = (bf16[4,30,4]{1,2,0:T(4,128)(2,1)S(1)}, bf16[4,30,4]{1,2,0:T(4,128)(2,1)}, u32[]{:S(2)}) copy-start(bf16[4,30,4]{1,2,0:T(4,128)(2,1)} %constant.131) | copy-start | bytes 2884
  1.5 10.1 %copy-start.19 = (bf16[4,30,4]{1,2,0:T(4,128)(2,1)S(1)}, bf16[4,30,4]{1,2,0:T(4,128)(2,1)}, u32[]{:S(2)}) copy-start(bf16[4,30,4]{1,2,0:T(4,128)(2,1)} %constant.135) | copy-start | bytes 2884
  1.5 10.3 %copy-start.17 = (pred[4,8]{0,1:T(8,128)(4,1)S(1)}, pred[4,8]{0,1:T(8,128)(4,1)}, u32[]{:S(2)}) copy-start(pred[4,8]{0,1:T(8,128)(4,1)} %constant.62) | copy-start | bytes 100
  4.2 74.0 %collective-permute-start.4 = (bf16[528,1536]{1,0:T(8,128)(2,1)}, bf16[528,1536]{1,0:T(8,128)(2,1)S(1)}, u32[]{:S(2)}, u32[]{:S(2)}) collective-permute-start(bf16[528,1536]{1,0:T(8,128)(2,1)} %pad_maximum_fusion), channel_id=1, source_target_pairs={{0,2},{2,4},{3,1},{4,6},{5,3},{6,8},{7,5},{8,10},{9,7},{10,12},{11... | collective-permute-start | bytes 4866056 | tf_op jit(solution)/shard_map/ppermute | solution.py:26
  7.6 81.7 %collective-permute-start.2 = (bf16[528,1536]{1,0:T(8,128)(2,1)}, bf16[528,1536]{1,0:T(8,128)(2,1)}, u32[]{:S(2)}, u32[]{:S(2)}) collective-permute-start(bf16[528,1536]{1,0:T(8,128)(2,1)} %pad_maximum_fusion), channel_id=1, source_target_pairs={{1,3},{2,0},{3,5},{4,2},{5,7},{6,4},{7,9},{8,6},{9,11},{10,8},{11,... | collective-permute-start | bytes 4866056 | tf_op jit(solution)/shard_map/ppermute | solution.py:26
  11.0 4.9 %collective-permute-start = (bf16[256,1536]{1,0:T(8,128)(2,1)}, bf16[256,1536]{1,0:T(8,128)(2,1)}, u32[]{:S(2)}, u32[]{:S(2)}) collective-permute-start(bf16[256,1536]{1,0:T(8,128)(2,1)} %k_ref.3), channel_id=1, source_target_pairs={{0,1},{1,0},{2,3},{3,2},{4,5},{5,4},{6,7},{7,6},{8,9},{9,8},{10,11... | collective-permute-start | bytes 2359304 | tf_op jit(solution)/shard_map/ppermute | solution.py:26
  11.0 7.2 %collective-permute-start.1 = (bf16[256,1536]{1,0:T(8,128)(2,1)}, bf16[256,1536]{1,0:T(8,128)(2,1)}, u32[]{:S(2)}, u32[]{:S(2)}) collective-permute-start(bf16[256,1536]{1,0:T(8,128)(2,1)} %v_ref.3), channel_id=1, source_target_pairs={{0,1},{1,0},{2,3},{3,2},{4,5},{5,4},{6,7},{7,6},{8,9},{9,8},{10,11... | collective-permute-start | bytes 2359304 | tf_op jit(solution)/shard_map/ppermute | solution.py:26
  17.0 1.2 copy-start.2
  19.4 1.1 copy-start.1
  78.2 1.5 copy-start
  85.1 16.0 %collective-permute-start.5 = (f32[12,3,256]{2,0,1:T(8,128)S(1)}, f32[12,3,256]{2,0,1:T(8,128)S(1)}, u32[]{:S(2)}, u32[]{:S(2)}) collective-permute-start(f32[12,3,256]{2,0,1:T(8,128)S(1)} %copy.36), channel_id=1, source_target_pairs={{1,3},{2,0},{3,5},{4,2},{5,7},{6,4},{7,9},{8,6},{9,11},{10,8},{11,... | collective-permute-start | bytes 110600 | tf_op jit(solution)/shard_map/ppermute | solution.py:26
  99.1 6.9 %collective-permute-start.3 = (f32[12,3,256]{2,0,1:T(8,128)S(1)}, f32[12,3,256]{2,0,1:T(8,128)S(1)}, u32[]{:S(2)}, u32[]{:S(2)}) collective-permute-start(f32[12,3,256]{2,0,1:T(8,128)S(1)} %copy.35), channel_id=1, source_target_pairs={{0,2},{2,4},{3,1},{4,6},{5,3},{6,8},{7,5},{8,10},{9,7},{10,12},{11... | collective-permute-start | bytes 110600 | tf_op jit(solution)/shard_map/ppermute | solution.py:26
  106.1 6.8 %copy-start.11 = (f32[12,2,256]{2,1,0:T(2,128)}, f32[12,2,256]{2,1,0:T(2,128)S(1)}, u32[]{:S(2)}) copy-start(f32[12,2,256]{2,1,0:T(2,128)S(1)} %pad_maximum_fusion.1.f_ref) | copy-start | bytes 73732
  106.1 15.7 %collective-permute-start.7 = (f32[12,2,256]{2,1,0:T(2,128)S(1)}, f32[12,2,256]{2,1,0:T(2,128)S(1)}, u32[]{:S(2)}, u32[]{:S(2)}) collective-permute-start(f32[12,2,256]{2,1,0:T(2,128)S(1)} %pad_maximum_fusion.1.f_ref), channel_id=1, source_target_pairs={{0,2},{2,4},{3,1},{4,6},{5,3},{6,8},{7,5},{8,10},{9,7},{10,12},{11... | collective-permute-start | bytes 73736 | tf_op jit(solution)/shard_map/ppermute | solution.py:26
  108.1 13.8 %collective-permute-start.6 = (f32[12,2,256]{2,1,0:T(2,128)S(1)}, f32[12,2,256]{2,1,0:T(2,128)S(1)}, u32[]{:S(2)}, u32[]{:S(2)}) collective-permute-start(f32[12,2,256]{2,1,0:T(2,128)S(1)} %pad_maximum_fusion.1.f_ref), channel_id=1, source_target_pairs={{1,3},{2,0},{3,5},{4,2},{5,7},{6,4},{7,9},{8,6},{9,11},{10,8},{11,... | collective-permute-start | bytes 73736 | tf_op jit(solution)/shard_map/ppermute | solution.py:26
  121.9 2.1 %copy-start.10 = (f32[12,2,256]{2,1,0:T(2,128)}, f32[12,2,256]{2,1,0:T(2,128)S(1)}, u32[]{:S(2)}) copy-start(f32[12,2,256]{2,1,0:T(2,128)S(1)} %collective-permute-done.7.f_ref) | copy-start | bytes 73732
  121.9 2.1 %copy-start.18 = (f32[12,2,256]{2,1,0:T(2,128)}, f32[12,2,256]{2,1,0:T(2,128)S(1)}, u32[]{:S(2)}) copy-start(f32[12,2,256]{2,1,0:T(2,128)S(1)} %collective-permute-done.6.f_ref) | copy-start | bytes 73732
  134.9 1.7 copy-start.5
  134.9 3.0 %copy-start.6 = (f32[512,1536]{1,0:T(8,128)S(1)}, f32[512,1536]{1,0:T(8,128)}, u32[]{:S(2)}) copy-start(f32[512,1536]{1,0:T(8,128)} %get-tuple-element.28) | copy-start | bytes 9437188
  136.6 2.4 %copy-start.7 = (f32[512,1536]{1,0:T(8,128)S(1)}, f32[512,1536]{1,0:T(8,128)}, u32[]{:S(2)}) copy-start(f32[512,1536]{1,0:T(8,128)} %get-tuple-element.27) | copy-start | bytes 9437188
  136.6 18.0 %collective-permute-start.11 = (f32[256,1536]{1,0:T(8,128)}, f32[256,1536]{1,0:T(8,128)}, u32[]{:S(2)}, u32[]{:S(2)}) collective-permute-start(f32[256,1536]{1,0:T(8,128)} %convert_add_fusion), channel_id=1, source_target_pairs={{0,1},{1,0},{2,3},{3,2},{4,5},{5,4},{6,7},{7,6},{8,9},{9,8},{10,11... | collective-permute-start | bytes 4718600 | tf_op jit(solution)/shard_map/ppermute | solution.py:26
  139.2 1.7 copy-start.3
  140.9 17.3 %collective-permute-start.10 = (f32[256,1536]{1,0:T(8,128)}, f32[256,1536]{1,0:T(8,128)}, u32[]{:S(2)}, u32[]{:S(2)}) collective-permute-start(f32[256,1536]{1,0:T(8,128)} %convert_add_fusion.1), channel_id=1, source_target_pairs={{0,1},{1,0},{2,3},{3,2},{4,5},{5,4},{6,7},{7,6},{8,9},{9,8},{10,11... | collective-permute-start | bytes 4718600 | tf_op jit(solution)/shard_map/ppermute | solution.py:26
  140.9 35.4 %collective-permute-start.8 = (bf16[256,1536]{1,0:T(8,128)(2,1)}, bf16[256,1536]{1,0:T(8,128)(2,1)}, u32[]{:S(2)}, u32[]{:S(2)}) collective-permute-start(bf16[256,1536]{1,0:T(8,128)(2,1)} %get-tuple-element.24), channel_id=1, source_target_pairs={{0,2},{2,4},{3,1},{4,6},{5,3},{6,8},{7,5},{8,10},{9,7},{10,12},{11... | collective-permute-start | bytes 2359304 | tf_op jit(solution)/shard_map/ppermute | solution.py:26
  149.8 29.9 %collective-permute-start.9 = (bf16[256,1536]{1,0:T(8,128)(2,1)}, bf16[256,1536]{1,0:T(8,128)(2,1)S(1)}, u32[]{:S(2)}, u32[]{:S(2)}) collective-permute-start(bf16[256,1536]{1,0:T(8,128)(2,1)} %get-tuple-element.26), channel_id=1, source_target_pairs={{1,3},{2,0},{3,5},{4,2},{5,7},{6,4},{7,9},{8,6},{9,11},{10,8},{11,... | collective-permute-start | bytes 2359304 | tf_op jit(solution)/shard_map/ppermute | solution.py:26
  154.6 3.6 %copy-start.4 = (bf16[512,1536]{1,0:T(8,128)(2,1)S(1)}, bf16[512,1536]{1,0:T(8,128)(2,1)}, u32[]{:S(2)}) copy-start(bf16[512,1536]{1,0:T(8,128)(2,1)} %copy-done.3) | copy-start | bytes 4718596
  154.6 3.6 %copy-start.9 = (f32[256,1536]{1,0:T(8,128)S(1)}, f32[256,1536]{1,0:T(8,128)}, u32[]{:S(2)}) copy-start(f32[256,1536]{1,0:T(8,128)} %get-tuple-element.29) | copy-start | bytes 4718596
  158.2 21.6 %copy-start.8 = (f32[256,1536]{1,0:T(8,128)S(1)}, f32[256,1536]{1,0:T(8,128)}, u32[]{:S(2)}) copy-start(f32[256,1536]{1,0:T(8,128)} %get-tuple-element.20) | copy-start | bytes 4718596

commit v11 on v10

--- a/solution.py
+++ b/solution.py
@@ -169,8 +169,9 @@
 
     flags = (block_list > 0).astype(jnp.bfloat16).reshape(1, blocks * cands)
     flags = jnp.pad(flags, ((0, LIST_ROWS - 1), (0, width - blocks * cands)))
-    pack = jnp.concatenate([queries, grad_out, flags], axis=0)
-
+    far_q_data = down_even(queries)
+    near_q_data = up_even(queries)
+    pack = jnp.concatenate([grad_out, flags], axis=0)
     far_data = down_even(pack)
     near_data = up_even(pack)
     partner_keys, partner_values = swap_cores((keys, values))
@@ -179,15 +180,15 @@
 
     slots = {
         "own": (queries, grad_out, 0, 0, block_list, 0, True, (0, -1), (0, 1)),
-        "far": (far_data, far_data, 0, 1, None, 2 * up, True, (2, 1), (-2, -1)),
-        "near": (near_data, near_data, 0, 1, None, -2 * up, False, (-2,), (2,)),
+        "far": (far_q_data, far_data, 0, 0, None, 2 * up, True, (2, 1), (-2, -1)),
+        "near": (near_q_data, near_data, 0, 0, None, -2 * up, False, (-2,), (2,)),
     }
 
     args = {}
     stats_out = {}
     for name, (q_arr, g_arr, q_rows, g_rows, rows, q_off, both, offs_e, offs_o) in slots.items():
         if rows is None:
-            rows = q_arr[2 * tok, : blocks * cands].reshape(blocks, cands)
+            rows = g_arr[tok, : blocks * cands].reshape(blocks, cands)
         key_arr, value_arr = (key_both, value_both) if both else (keys, values)
         nkb = key_arr.shape[0] // BLOCK
         source = here + q_off

time: 183 us -> 181 us (0.989)
  waiting for transfers between devices: 74.1 us -> 66.1 us
  starting transfers between devices: 27.1 us -> 33.8 us
    ppermute x12 -> x14, waiting for transfers between devices: 74.1 us -> 66.1 us  [permute(): return lax.ppermute(value, 'tm', pairs)]
    ppermute x12 -> x14, starting transfers between devices: 27.1 us -> 33.8 us  [permute(): return lax.ppermute(value, 'tm', pairs)]
    unnamed x42, local copies, waits for them, and re-layouts: 7.22 us -> 4.96 us
  transfers between devices with their start and end apart: 12 -> 14, of which waited for: 4 -> 4; matrix products, arithmetic and copies ran while one was open for 12% -> 14% of each run, Pallas kernels for 18% -> 18%
where the time goes in v11:
time: 181 us; the launch traced here: 179 us
  waiting for transfers between devices  66.1 us (37%)
  Pallas kernels  42 us (23%)
  starting transfers between devices  33.8 us (19%)
  other arithmetic  20.5 us (11%)
  local copies, waits for them, and re-layouts  15.4 us (9%)
    ppermute x14, waiting for transfers between devices, permute(): return lax.ppermute(value, 'tm', pairs)  66.1 us
    ppermute x14, starting transfers between devices, permute(): return lax.ppermute(value, 'tm', pairs)  33.8 us
    pallas_call x3, Pallas kernels, slot_back(): pl.pallas_call(back_kernel, grid=(HEADS // STEP_HEADS,), in_specs=slot_sp...  24.8 us
    pallas_call x3, Pallas kernels, slot_stats(): pl.pallas_call(stats_kernel, grid=(HEADS // STEP_HEADS,), in_specs=slot_s...  17.2 us
    unnamed x42, local copies, waits for them, and re-layouts  4.96 us
    another operation x4, other arithmetic  4.49 us
    convert_element_type x3, local copies, waits for them, and re-layouts, local(): mask_t = jnp.broadcast_to(mask4.T[:, None, :, None], (nkb, BLOCK, blocks,...  3.87 us
  transfers between devices with their start and end apart: 14, of which 4 were waited for; matrix products, arithmetic and copies ran while one was open for 14% of the time, Pallas kernels for 18%

profile of v11, /device:TPU:8, one launch (start us, length us, event | category | flops | bytes accessed | tf_op | source)
XLA Modules:
  0.0 179.3 jit_solution(7223636488509608432)
XLA Ops:
  0.6 0.0 copy-start.12
  0.6 0.0 copy-start.13
  0.7 3.4 %collective-permute-start.2 = (bf16[256,1536]{1,0:T(8,128)(2,1)}, bf16[256,1536]{1,0:T(8,128)(2,1)}, u32[]{:S(2)}, u32[]{:S(2)}) collective-permute-start(bf16[256,1536]{1,0:T(8,128)(2,1)} %q_ref.3), channel_id=1, source_target_pairs={{1,3},{2,0},{3,5},{4,2},{5,7},{6,4},{7,9},{8,6},{9,11},{10,8},{11,... | collective-permute-start | bytes 2359304 | tf_op jit(solution)/shard_map/ppermute | solution.py:26
  4.2 2.5 %collective-permute-start.5 = (bf16[256,1536]{1,0:T(8,128)(2,1)}, bf16[256,1536]{1,0:T(8,128)(2,1)}, u32[]{:S(2)}, u32[]{:S(2)}) collective-permute-start(bf16[256,1536]{1,0:T(8,128)(2,1)} %q_ref.3), channel_id=1, source_target_pairs={{0,2},{2,4},{3,1},{4,6},{5,3},{6,8},{7,5},{8,10},{9,7},{10,12},{11... | collective-permute-start | bytes 2359304 | tf_op jit(solution)/shard_map/ppermute | solution.py:26
  6.7 0.2 collective-permute-start
  7.0 0.3 collective-permute-start.1
  7.3 0.7 broadcast_compare_fusion
  8.0 0.1 reshape.188
  8.1 2.1 %pad_maximum_fusion = bf16[272,1536]{1,0:T(8,128)(2,1)} fusion(bf16[16,1536]{1,0:T(8,128)(2,1)S(1)} %pad_convert_fusion, bf16[256,1536]{1,0:T(8,128)(2,1)} %g_ref.3), kind=kLoop, calls=%fused_computation.5 | loop fusion | flops 1671168 | bytes 1671168 | tf_op jit(solution)/shard_map/concatenate | solution.py:174
  10.2 4.4 %collective-permute-start.6 = (bf16[272,1536]{1,0:T(8,128)(2,1)}, bf16[272,1536]{1,0:T(8,128)(2,1)}, u32[]{:S(2)}, u32[]{:S(2)}) collective-permute-start(bf16[272,1536]{1,0:T(8,128)(2,1)} %pad_maximum_fusion), channel_id=1, source_target_pairs={{0,2},{2,4},{3,1},{4,6},{5,3},{6,8},{7,5},{8,10},{9,7},{10,12},{11... | collective-permute-start | bytes 2506760 | tf_op jit(solution)/shard_map/ppermute | solution.py:26
  14.7 0.1 fusion.7
  14.9 0.1 copy.41
  15.0 0.2 broadcast_in_dim.33
  15.2 1.4 convert_element_type.88.m_ref
  16.6 0.1 constant_dynamic-update-slice_fusion.1
  16.7 1.2 constant_dynamic-update-slice_fusion.3
  17.9 2.4 %collective-permute-start.3 = (bf16[272,1536]{1,0:T(8,128)(2,1)}, bf16[272,1536]{1,0:T(8,128)(2,1)}, u32[]{:S(2)}, u32[]{:S(2)}) collective-permute-start(bf16[272,1536]{1,0:T(8,128)(2,1)} %pad_maximum_fusion), channel_id=1, source_target_pairs={{1,3},{2,0},{3,5},{4,2},{5,7},{6,4},{7,9},{8,6},{9,11},{10,8},{11,... | collective-permute-start | bytes 2506760 | tf_op jit(solution)/shard_map/ppermute | solution.py:26
  20.3 1.2 constant_dynamic-update-slice_fusion.k_ref
  21.5 1.8 constant_dynamic-update-slice_fusion.2.v_ref
  23.3 1.1 copy-done
  24.4 6.3 %shard_map.256 = f32[12,3,256]{2,1,0:T(4,128)} custom-call(bf16[256,1536]{1,0:T(8,128)(2,1)} %q_ref.3, bf16[256,1536]{1,0:T(8,128)(2,1)} %g_ref.3, bf16[512,1536]{1,0:T(8,128)(2,1)} %copy-done.1, bf16[512,1536]{1,0:T(8,128)(2,1)} %copy-done, f32[512,256]{1,0:T(8,128)} %convert_element_type.88.m_ref), custom_call_target="tpu_custom_call" | custom-call | flops 805306368 | bytes 4718592 | tf_op jit(solution)/shard_map/pallas_call | solution.py:124
  30.7 0.9 fusion.34
  31.6 42.4 %collective-permute-done.6.g_ref = bf16[272,1536]{1,0:T(8,128)(2,1)} collective-permute-done((bf16[272,1536]{1,0:T(8,128)(2,1)}, bf16[272,1536]{1,0:T(8,128)(2,1)}, u32[]{:S(2)}, u32[]{:S(2)}) %collective-permute-start.6) | collective-permute-done | bytes 835616 | tf_op jit(solution)/shard_map/ppermute | solution.py:26
  74.0 0.6 compare_reduce_fusion
  74.7 0.1 reshape.198
  74.8 0.1 fusion.22
  74.9 0.1 copy.45
  75.0 0.1 broadcast_in_dim.36
  75.1 1.1 convert_element_type.94.m_ref
  76.2 4.6 %shard_map.258 = f32[12,3,256]{2,1,0:T(4,128)} custom-call(bf16[256,1536]{1,0:T(8,128)(2,1)} %collective-permute-done.5.q_ref, bf16[272,1536]{1,0:T(8,128)(2,1)} %collective-permute-done.6.g_ref, bf16[256,1536]{1,0:T(8,128)(2,1)} %k_ref.3, bf16[256,1536]{1,0:T(8,128)(2,1)} %v_ref.3, f32[256,256]{1,0:T(8,128)} %convert_element_type.94.m_ref), custom_call_target="tpu_custom_call" | custom-call | flops 402653184 | bytes 3145728 | tf_op jit(solution)/shard_map/pallas_call | solution.py:124
  80.8 0.8 copy.36
  81.6 4.8 %collective-permute-start.7 = (f32[12,3,256]{2,0,1:T(8,128)S(1)}, f32[12,3,256]{2,0,1:T(8,128)S(1)}, u32[]{:S(2)}, u32[]{:S(2)}) collective-permute-start(f32[12,3,256]{2,0,1:T(8,128)S(1)} %copy.36), channel_id=1, source_target_pairs={{1,3},{2,0},{3,5},{4,2},{5,7},{6,4},{7,9},{8,6},{9,11},{10,8},{11,... | collective-permute-start | bytes 110600 | tf_op jit(solution)/shard_map/ppermute | solution.py:26
  86.4 0.6 compare_reduce_fusion.1
  87.1 0.1 reshape.196
  87.2 0.1 fusion.11
  87.3 0.1 copy.43
  87.4 0.1 convert_bitcast_fusion
  87.4 0.2 broadcast_in_dim.35
  87.7 1.4 convert_element_type.91.m_ref
  89.1 6.3 %shard_map.257 = f32[12,3,256]{2,1,0:T(4,128)} custom-call(bf16[256,1536]{1,0:T(8,128)(2,1)} %collective-permute-done.2.q_ref, bf16[272,1536]{1,0:T(8,128)(2,1)} %collective-permute-done.3.g_ref, bf16[512,1536]{1,0:T(8,128)(2,1)} %copy-done.1, bf16[512,1536]{1,0:T(8,128)(2,1)} %copy-done, f32[512,256]{1,0:T(8,128)} %convert_element_type.91.m_ref), custom_call_target="tpu_custom_call" | custom-call | flops 805306368 | bytes 4718592 | tf_op jit(solution)/shard_map/pallas_call | solution.py:124
  95.3 0.8 copy.35
  96.2 1.9 %collective-permute-start.4 = (f32[12,3,256]{2,0,1:T(8,128)S(1)}, f32[12,3,256]{2,0,1:T(8,128)S(1)}, u32[]{:S(2)}, u32[]{:S(2)}) collective-permute-start(f32[12,3,256]{2,0,1:T(8,128)S(1)} %copy.35), channel_id=1, source_target_pairs={{0,2},{2,4},{3,1},{4,6},{5,3},{6,8},{7,5},{8,10},{9,7},{10,12},{11... | collective-permute-start | bytes 110600 | tf_op jit(solution)/shard_map/ppermute | solution.py:26
  98.1 4.9 %collective-permute-done.4 = f32[12,3,256]{2,0,1:T(8,128)S(1)} collective-permute-done((f32[12,3,256]{2,0,1:T(8,128)S(1)}, f32[12,3,256]{2,0,1:T(8,128)S(1)}, u32[]{:S(2)}, u32[]{:S(2)}) %collective-permute-start.4) | collective-permute-done | bytes 36896 | tf_op jit(solution)/shard_map/ppermute | solution.py:26
  103.2 1.9 %collective-permute-start.9 = (f32[12,2,256]{2,1,0:T(2,128)S(1)}, f32[12,2,256]{2,1,0:T(2,128)S(1)}, u32[]{:S(2)}, u32[]{:S(2)}) collective-permute-start(f32[12,2,256]{2,1,0:T(2,128)S(1)} %pad_maximum_fusion.1.f_ref), channel_id=1, source_target_pairs={{0,2},{2,4},{3,1},{4,6},{5,3},{6,8},{7,5},{8,10},{9,7},{10,12},{11... | collective-permute-start | bytes 73736 | tf_op jit(solution)/shard_map/ppermute | solution.py:26
  105.1 4.8 %collective-permute-start.8 = (f32[12,2,256]{2,1,0:T(2,128)S(1)}, f32[12,2,256]{2,1,0:T(2,128)S(1)}, u32[]{:S(2)}, u32[]{:S(2)}) collective-permute-start(f32[12,2,256]{2,1,0:T(2,128)S(1)} %pad_maximum_fusion.1.f_ref), channel_id=1, source_target_pairs={{1,3},{2,0},{3,5},{4,2},{5,7},{6,4},{7,9},{8,6},{9,11},{10,8},{11,... | collective-permute-start | bytes 73736 | tf_op jit(solution)/shard_map/ppermute | solution.py:26
  110.0 9.0 %shard_map.259 = (f32[256,1536]{1,0:T(8,128)}, f32[512,1536]{1,0:T(8,128)}, f32[512,1536]{1,0:T(8,128)}) custom-call(bf16[256,1536]{1,0:T(8,128)(2,1)} %q_ref.3, bf16[256,1536]{1,0:T(8,128)(2,1)} %g_ref.3, bf16[512,1536]{1,0:T(8,128)(2,1)} %copy-done.1, bf16[512,1536]{1,0:T(8,128)(2,1)} %copy-done, f32[512,256]{1,0:T(8,128)} %convert_element_type.88.m_ref, ...), custom_call_target="tpu_custom_call" | custom-call | flops 2013265920 | bytes 14155776 | tf_op jit(solution)/shard_map/pallas_call | solution.py:140
  119.0 2.1 %convert.25 = bf16[512,1536]{1,0:T(8,128)(2,1)S(1)} convert(f32[512,1536]{1,0:T(8,128)} %get-tuple-element.31) | non-fusion elementwise | flops 786432 | bytes 4718592 | tf_op jit(solution)/shard_map/convert.8
  121.1 8.9 %shard_map.260 = (bf16[256,1536]{1,0:T(8,128)(2,1)}, f32[512,1536]{1,0:T(8,128)}, f32[512,1536]{1,0:T(8,128)}) custom-call(bf16[256,1536]{1,0:T(8,128)(2,1)} %collective-permute-done.2.q_ref, bf16[272,1536]{1,0:T(8,128)(2,1)} %collective-permute-done.3.g_ref, bf16[512,1536]{1,0:T(8,128)(2,1)} %copy-done.1, bf16[512,1536]{1,0:T(8,128)(2,1)} %copy-done, ...), custom_call_target="tpu_custom_call" | custom-call | flops 2013265920 | bytes 14155776 | tf_op jit(solution)/shard_map/pallas_call | solution.py:140
  130.1 2.1 %convert.24 = bf16[512,1536]{1,0:T(8,128)(2,1)S(1)} convert(f32[512,1536]{1,0:T(8,128)} %get-tuple-element.30) | non-fusion elementwise | flops 786432 | bytes 4718592 | tf_op jit(solution)/shard_map/convert.9
  132.2 1.4 convert_add_fusion
  133.6 1.6 copy-done.5
  135.2 0.2 convert.23
  135.4 0.8 copy-done.6
  136.2 0.2 convert.22
  136.4 1.6 convert_add_fusion.1
  138.0 0.0 copy-done.2
  138.0 2.1 %collective-permute-start.10 = (bf16[256,1536]{1,0:T(8,128)(2,1)}, bf16[256,1536]{1,0:T(8,128)(2,1)}, u32[]{:S(2)}, u32[]{:S(2)}) collective-permute-start(bf16[256,1536]{1,0:T(8,128)(2,1)} %get-tuple-element.24), channel_id=1, source_target_pairs={{0,2},{2,4},{3,1},{4,6},{5,3},{6,8},{7,5},{8,10},{9,7},{10,12},{11... | collective-permute-start | bytes 2359304 | tf_op jit(solution)/shard_map/ppermute | solution.py:26
  140.1 6.8 %shard_map.261 = (bf16[256,1536]{1,0:T(8,128)(2,1)}, f32[256,1536]{1,0:T(8,128)}, f32[256,1536]{1,0:T(8,128)}) custom-call(bf16[256,1536]{1,0:T(8,128)(2,1)} %collective-permute-done.5.q_ref, bf16[272,1536]{1,0:T(8,128)(2,1)} %collective-permute-done.6.g_ref, bf16[256,1536]{1,0:T(8,128)(2,1)} %k_ref.3, bf16[256,1536]{1,0:T(8,128)(2,1)} %v_ref.3, ...), custom_call_target="tpu_custom_call" | custom-call | flops 1006632960 | bytes 9437184 | tf_op jit(solution)/shard_map/pallas_call | solution.py:140
  147.0 4.8 %collective-permute-start.11 = (bf16[256,1536]{1,0:T(8,128)(2,1)}, bf16[256,1536]{1,0:T(8,128)(2,1)S(1)}, u32[]{:S(2)}, u32[]{:S(2)}) collective-permute-start(bf16[256,1536]{1,0:T(8,128)(2,1)} %get-tuple-element.26), channel_id=1, source_target_pairs={{1,3},{2,0},{3,5},{4,2},{5,7},{6,4},{7,9},{8,6},{9,11},{10,8},{11,... | collective-permute-start | bytes 2359304 | tf_op jit(solution)/shard_map/ppermute | solution.py:26
  151.8 3.6 %add_convert_fusion.1 = bf16[256,1536]{1,0:T(8,128)(2,1)} fusion(f32[256,1536]{1,0:T(8,128)} %collective-permute-done.13, bf16[512,1536]{1,0:T(8,128)(2,1)S(1)} %convert.25, bf16[512,1536]{1,0:T(8,128)(2,1)} %copy-done.4, f32[256,1536]{1,0:T(8,128)} %get-tuple-element.32), kind=kLoop, calls=%fused_computation.1 | loop fusion | flops 3145728 | bytes 5505024 | tf_op jit(solution)/shard_map/convert_element_type | solution.py:243
  155.4 2.8 %add_convert_fusion.2 = bf16[256,1536]{1,0:T(8,128)(2,1)} fusion(f32[256,1536]{1,0:T(8,128)} %collective-permute-done.12, bf16[512,1536]{1,0:T(8,128)(2,1)S(1)} %convert.23, bf16[512,1536]{1,0:T(8,128)(2,1)S(1)} %copy-done.3, f32[256,1536]{1,0:T(8,128)S(1)} %copy-done.9), kind=kLoop, calls=%fused_computation.3 | loop fusion | flops 3145728 | bytes 5505024 | tf_op jit(solution)/shard_map/convert_element_type | solution.py:242
  158.2 15.0 %collective-permute-done.10 = bf16[256,1536]{1,0:T(8,128)(2,1)} collective-permute-done((bf16[256,1536]{1,0:T(8,128)(2,1)}, bf16[256,1536]{1,0:T(8,128)(2,1)}, u32[]{:S(2)}, u32[]{:S(2)}) %collective-permute-start.10) | collective-permute-done | bytes 786464 | tf_op jit(solution)/shard_map/ppermute | solution.py:26
  173.2 3.7 %collective-permute-done.11 = bf16[256,1536]{1,0:T(8,128)(2,1)S(1)} collective-permute-done((bf16[256,1536]{1,0:T(8,128)(2,1)}, bf16[256,1536]{1,0:T(8,128)(2,1)S(1)}, u32[]{:S(2)}, u32[]{:S(2)}) %collective-permute-start.11) | collective-permute-done | bytes 786464 | tf_op jit(solution)/shard_map/ppermute | solution.py:26
  176.9 2.4 %add_convert_fusion = bf16[256,1536]{1,0:T(8,128)(2,1)} fusion(bf16[256,1536]{1,0:T(8,128)(2,1)S(1)} %collective-permute-done.11, f32[256,1536]{1,0:T(8,128)S(1)} %copy-done.8, bf16[256,1536]{1,0:T(8,128)(2,1)} %collective-permute-done.10), kind=kLoop, calls=%fused_computation | loop fusion | flops 1966080 | bytes 3932160 | tf_op jit(solution)/shard_map/convert_element_type | solution.py:248
  (62 shorter events, 0.3 us)
Async XLA Ops:
  0.6 14.0 %copy-start.12 = (bf16[4,30,4]{1,2,0:T(4,128)(2,1)S(1)}, bf16[4,30,4]{1,2,0:T(4,128)(2,1)}, u32[]{:S(2)}) copy-start(bf16[4,30,4]{1,2,0:T(4,128)(2,1)} %constant.133) | copy-start | bytes 2884
  0.6 14.0 %copy-start.13 = (bf16[4,30,4]{1,2,0:T(4,128)(2,1)S(1)}, bf16[4,30,4]{1,2,0:T(4,128)(2,1)}, u32[]{:S(2)}) copy-start(bf16[4,30,4]{1,2,0:T(4,128)(2,1)} %constant.134) | copy-start | bytes 2884
  0.7 14.0 %copy-start.14 = (bf16[4,30,4]{1,2,0:T(4,128)(2,1)S(1)}, bf16[4,30,4]{1,2,0:T(4,128)(2,1)}, u32[]{:S(2)}) copy-start(bf16[4,30,4]{1,2,0:T(4,128)(2,1)} %constant.132) | copy-start | bytes 2884
  0.7 14.0 %copy-start.15 = (bf16[4,30,4]{1,2,0:T(4,128)(2,1)S(1)}, bf16[4,30,4]{1,2,0:T(4,128)(2,1)}, u32[]{:S(2)}) copy-start(bf16[4,30,4]{1,2,0:T(4,128)(2,1)} %constant.131) | copy-start | bytes 2884
  0.7 14.0 %copy-start.19 = (bf16[4,30,4]{1,2,0:T(4,128)(2,1)S(1)}, bf16[4,30,4]{1,2,0:T(4,128)(2,1)}, u32[]{:S(2)}) copy-start(bf16[4,30,4]{1,2,0:T(4,128)(2,1)} %constant.135) | copy-start | bytes 2884
  0.7 14.3 %copy-start.16 = (pred[4,8]{0,1:T(8,128)(4,1)S(1)}, pred[4,8]{0,1:T(8,128)(4,1)}, u32[]{:S(2)}) copy-start(pred[4,8]{0,1:T(8,128)(4,1)} %constant.62) | copy-start | bytes 100
  0.7 13.9 %copy-start.11 = (s32[4,30]{1,0:T(4,128)S(1)}, s32[4,30]{1,0:T(4,128)}, u32[]{:S(2)}) copy-start(s32[4,30]{1,0:T(4,128)} %param.29) | copy-start | bytes 1444
  0.7 88.4 %collective-permute-start.2 = (bf16[256,1536]{1,0:T(8,128)(2,1)}, bf16[256,1536]{1,0:T(8,128)(2,1)}, u32[]{:S(2)}, u32[]{:S(2)}) collective-permute-start(bf16[256,1536]{1,0:T(8,128)(2,1)} %q_ref.3), channel_id=1, source_target_pairs={{1,3},{2,0},{3,5},{4,2},{5,7},{6,4},{7,9},{8,6},{9,11},{10,8},{11,... | collective-permute-start | bytes 2359304 | tf_op jit(solution)/shard_map/ppermute | solution.py:26
  4.2 72.0 %collective-permute-start.5 = (bf16[256,1536]{1,0:T(8,128)(2,1)}, bf16[256,1536]{1,0:T(8,128)(2,1)}, u32[]{:S(2)}, u32[]{:S(2)}) collective-permute-start(bf16[256,1536]{1,0:T(8,128)(2,1)} %q_ref.3), channel_id=1, source_target_pairs={{0,2},{2,4},{3,1},{4,6},{5,3},{6,8},{7,5},{8,10},{9,7},{10,12},{11... | collective-permute-start | bytes 2359304 | tf_op jit(solution)/shard_map/ppermute | solution.py:26
  6.7 11.1 %collective-permute-start = (bf16[256,1536]{1,0:T(8,128)(2,1)}, bf16[256,1536]{1,0:T(8,128)(2,1)}, u32[]{:S(2)}, u32[]{:S(2)}) collective-permute-start(bf16[256,1536]{1,0:T(8,128)(2,1)} %k_ref.3), channel_id=1, source_target_pairs={{0,1},{1,0},{2,3},{3,2},{4,5},{5,4},{6,7},{7,6},{8,9},{9,8},{10,11... | collective-permute-start | bytes 2359304 | tf_op jit(solution)/shard_map/ppermute | solution.py:26
  7.0 14.5 %collective-permute-start.1 = (bf16[256,1536]{1,0:T(8,128)(2,1)}, bf16[256,1536]{1,0:T(8,128)(2,1)}, u32[]{:S(2)}, u32[]{:S(2)}) collective-permute-start(bf16[256,1536]{1,0:T(8,128)(2,1)} %v_ref.3), channel_id=1, source_target_pairs={{0,1},{1,0},{2,3},{3,2},{4,5},{5,4},{6,7},{7,6},{8,9},{9,8},{10,11... | collective-permute-start | bytes 2359304 | tf_op jit(solution)/shard_map/ppermute | solution.py:26
  10.2 6.4 %copy-start.7 = (bf16[256,1536]{1,0:T(8,128)(2,1)S(1)}, bf16[256,1536]{1,0:T(8,128)(2,1)}, u32[]{:S(2)}) copy-start(bf16[256,1536]{1,0:T(8,128)(2,1)} %k_ref.3) | copy-start | bytes 2359300
  10.2 63.9 %collective-permute-start.6 = (bf16[272,1536]{1,0:T(8,128)(2,1)}, bf16[272,1536]{1,0:T(8,128)(2,1)}, u32[]{:S(2)}, u32[]{:S(2)}) collective-permute-start(bf16[272,1536]{1,0:T(8,128)(2,1)} %pad_maximum_fusion), channel_id=1, source_target_pairs={{0,2},{2,4},{3,1},{4,6},{5,3},{6,8},{7,5},{8,10},{9,7},{10,12},{11... | collective-permute-start | bytes 2506760 | tf_op jit(solution)/shard_map/ppermute | solution.py:26
  17.9 68.6 %collective-permute-start.3 = (bf16[272,1536]{1,0:T(8,128)(2,1)}, bf16[272,1536]{1,0:T(8,128)(2,1)}, u32[]{:S(2)}, u32[]{:S(2)}) collective-permute-start(bf16[272,1536]{1,0:T(8,128)(2,1)} %pad_maximum_fusion), channel_id=1, source_target_pairs={{1,3},{2,0},{3,5},{4,2},{5,7},{6,4},{7,9},{8,6},{9,11},{10,8},{11,... | collective-permute-start | bytes 2506760 | tf_op jit(solution)/shard_map/ppermute | solution.py:26
  21.5 1.8 copy-start.1
  23.3 1.2 copy-start
  81.6 16.5 %collective-permute-start.7 = (f32[12,3,256]{2,0,1:T(8,128)S(1)}, f32[12,3,256]{2,0,1:T(8,128)S(1)}, u32[]{:S(2)}, u32[]{:S(2)}) collective-permute-start(f32[12,3,256]{2,0,1:T(8,128)S(1)} %copy.36), channel_id=1, source_target_pairs={{1,3},{2,0},{3,5},{4,2},{5,7},{6,4},{7,9},{8,6},{9,11},{10,8},{11,... | collective-permute-start | bytes 110600 | tf_op jit(solution)/shard_map/ppermute | solution.py:26
  96.2 6.9 %collective-permute-start.4 = (f32[12,3,256]{2,0,1:T(8,128)S(1)}, f32[12,3,256]{2,0,1:T(8,128)S(1)}, u32[]{:S(2)}, u32[]{:S(2)}) collective-permute-start(f32[12,3,256]{2,0,1:T(8,128)S(1)} %copy.35), channel_id=1, source_target_pairs={{0,2},{2,4},{3,1},{4,6},{5,3},{6,8},{7,5},{8,10},{9,7},{10,12},{11... | collective-permute-start | bytes 110600 | tf_op jit(solution)/shard_map/ppermute | solution.py:26
  103.2 6.8 %copy-start.10 = (f32[12,2,256]{2,1,0:T(2,128)}, f32[12,2,256]{2,1,0:T(2,128)S(1)}, u32[]{:S(2)}) copy-start(f32[12,2,256]{2,1,0:T(2,128)S(1)} %pad_maximum_fusion.1.f_ref) | copy-start | bytes 73732
  103.2 15.8 %collective-permute-start.9 = (f32[12,2,256]{2,1,0:T(2,128)S(1)}, f32[12,2,256]{2,1,0:T(2,128)S(1)}, u32[]{:S(2)}, u32[]{:S(2)}) collective-permute-start(f32[12,2,256]{2,1,0:T(2,128)S(1)} %pad_maximum_fusion.1.f_ref), channel_id=1, source_target_pairs={{0,2},{2,4},{3,1},{4,6},{5,3},{6,8},{7,5},{8,10},{9,7},{10,12},{11... | collective-permute-start | bytes 73736 | tf_op jit(solution)/shard_map/ppermute | solution.py:26
  105.1 13.9 %collective-permute-start.8 = (f32[12,2,256]{2,1,0:T(2,128)S(1)}, f32[12,2,256]{2,1,0:T(2,128)S(1)}, u32[]{:S(2)}, u32[]{:S(2)}) collective-permute-start(f32[12,2,256]{2,1,0:T(2,128)S(1)} %pad_maximum_fusion.1.f_ref), channel_id=1, source_target_pairs={{1,3},{2,0},{3,5},{4,2},{5,7},{6,4},{7,9},{8,6},{9,11},{10,8},{11,... | collective-permute-start | bytes 73736 | tf_op jit(solution)/shard_map/ppermute | solution.py:26
  119.0 2.1 %copy-start.17 = (f32[12,2,256]{2,1,0:T(2,128)}, f32[12,2,256]{2,1,0:T(2,128)S(1)}, u32[]{:S(2)}) copy-start(f32[12,2,256]{2,1,0:T(2,128)S(1)} %collective-permute-done.9.f_ref) | copy-start | bytes 73732
  119.0 2.1 %copy-start.18 = (f32[12,2,256]{2,1,0:T(2,128)}, f32[12,2,256]{2,1,0:T(2,128)S(1)}, u32[]{:S(2)}) copy-start(f32[12,2,256]{2,1,0:T(2,128)S(1)} %collective-permute-done.8.f_ref) | copy-start | bytes 73732
  132.1 3.2 %copy-start.4 = (bf16[512,1536]{1,0:T(8,128)(2,1)}, bf16[512,1536]{1,0:T(8,128)(2,1)S(1)}, u32[]{:S(2)}) copy-start(bf16[512,1536]{1,0:T(8,128)(2,1)S(1)} %convert.24) | copy-start | bytes 4718596
  132.1 3.0 %copy-start.5 = (f32[512,1536]{1,0:T(8,128)S(1)}, f32[512,1536]{1,0:T(8,128)}, u32[]{:S(2)}) copy-start(f32[512,1536]{1,0:T(8,128)} %get-tuple-element.28) | copy-start | bytes 9437188
  133.6 2.6 %copy-start.6 = (f32[512,1536]{1,0:T(8,128)S(1)}, f32[512,1536]{1,0:T(8,128)}, u32[]{:S(2)}) copy-start(f32[512,1536]{1,0:T(8,128)} %get-tuple-element.27) | copy-start | bytes 9437188
  133.6 18.2 %collective-permute-start.13 = (f32[256,1536]{1,0:T(8,128)}, f32[256,1536]{1,0:T(8,128)}, u32[]{:S(2)}, u32[]{:S(2)}) collective-permute-start(f32[256,1536]{1,0:T(8,128)} %convert_add_fusion), channel_id=1, source_target_pairs={{0,1},{1,0},{2,3},{3,2},{4,5},{5,4},{6,7},{7,6},{8,9},{9,8},{10,11... | collective-permute-start | bytes 4718600 | tf_op jit(solution)/shard_map/ppermute | solution.py:26
  136.4 1.6 copy-start.2
  138.0 17.4 %collective-permute-start.12 = (f32[256,1536]{1,0:T(8,128)}, f32[256,1536]{1,0:T(8,128)}, u32[]{:S(2)}, u32[]{:S(2)}) collective-permute-start(f32[256,1536]{1,0:T(8,128)} %convert_add_fusion.1), channel_id=1, source_target_pairs={{0,1},{1,0},{2,3},{3,2},{4,5},{5,4},{6,7},{7,6},{8,9},{9,8},{10,11... | collective-permute-start | bytes 4718600 | tf_op jit(solution)/shard_map/ppermute | solution.py:26
  138.0 35.2 %collective-permute-start.10 = (bf16[256,1536]{1,0:T(8,128)(2,1)}, bf16[256,1536]{1,0:T(8,128)(2,1)}, u32[]{:S(2)}, u32[]{:S(2)}) collective-permute-start(bf16[256,1536]{1,0:T(8,128)(2,1)} %get-tuple-element.24), channel_id=1, source_target_pairs={{0,2},{2,4},{3,1},{4,6},{5,3},{6,8},{7,5},{8,10},{9,7},{10,12},{11... | collective-permute-start | bytes 2359304 | tf_op jit(solution)/shard_map/ppermute | solution.py:26
  147.0 29.9 %collective-permute-start.11 = (bf16[256,1536]{1,0:T(8,128)(2,1)}, bf16[256,1536]{1,0:T(8,128)(2,1)S(1)}, u32[]{:S(2)}, u32[]{:S(2)}) collective-permute-start(bf16[256,1536]{1,0:T(8,128)(2,1)} %get-tuple-element.26), channel_id=1, source_target_pairs={{1,3},{2,0},{3,5},{4,2},{5,7},{6,4},{7,9},{8,6},{9,11},{10,8},{11,... | collective-permute-start | bytes 2359304 | tf_op jit(solution)/shard_map/ppermute | solution.py:26
  151.8 3.6 %copy-start.3 = (bf16[512,1536]{1,0:T(8,128)(2,1)S(1)}, bf16[512,1536]{1,0:T(8,128)(2,1)}, u32[]{:S(2)}) copy-start(bf16[512,1536]{1,0:T(8,128)(2,1)} %copy-done.2) | copy-start | bytes 4718596
  151.8 3.6 %copy-start.9 = (f32[256,1536]{1,0:T(8,128)S(1)}, f32[256,1536]{1,0:T(8,128)}, u32[]{:S(2)}) copy-start(f32[256,1536]{1,0:T(8,128)} %get-tuple-element.29) | copy-start | bytes 4718596
  155.4 21.5 %copy-start.8 = (f32[256,1536]{1,0:T(8,128)S(1)}, f32[256,1536]{1,0:T(8,128)}, u32[]{:S(2)}) copy-start(f32[256,1536]{1,0:T(8,128)} %get-tuple-element.20) | copy-start | bytes 4718596

commit v12 on v11

--- a/solution.py
+++ b/solution.py
@@ -105,6 +105,33 @@
         dv_ref[:, cols] = jnp.dot(p.astype(jnp.bfloat16), g, preferred_element_type=jnp.float32)
         dq = lax.dot_general(ds, k, (((0,), (0,)), ((), ())), preferred_element_type=jnp.float32)
         dq_ref[:, cols] = (dq * SCALE).astype(dq_ref.dtype)
+
+
+def dq_kernel(q_ref, g_ref, k_ref, v_ref, m_ref, f_ref, dq_ref):
+    m = m_ref[...] > 0
+    for j in range(STEP_HEADS):
+        cols = head_cols(j)
+        k = k_ref[:, cols]
+        s, dp = slot_scores(q_ref[:, cols], g_ref[:, cols], k, v_ref[:, cols])
+        fin = f_ref[j]
+        p = jnp.where(m, jnp.exp(s - fin[0:1]), 0.0)
+        ds = (p * (dp - fin[1:2])).astype(jnp.bfloat16)
+        dq = lax.dot_general(ds, k, (((0,), (0,)), ((), ())), preferred_element_type=jnp.float32)
+        dq_ref[:, cols] = (dq * SCALE).astype(dq_ref.dtype)
+
+
+def kv_kernel(q_ref, g_ref, k_ref, v_ref, m_ref, f_ref, dk_ref, dv_ref):
+    m = m_ref[...] > 0
+    for j in range(STEP_HEADS):
+        cols = head_cols(j)
+        q = q_ref[:, cols]
+        g = g_ref[:, cols]
+        s, dp = slot_scores(q, g, k_ref[:, cols], v_ref[:, cols])
+        fin = f_ref[j]
+        p = jnp.where(m, jnp.exp(s - fin[0:1]), 0.0)
+        ds = (p * (dp - fin[1:2])).astype(jnp.bfloat16)
+        dk_ref[:, cols] = jnp.dot(ds, q, preferred_element_type=jnp.float32) * SCALE
+        dv_ref[:, cols] = jnp.dot(p.astype(jnp.bfloat16), g, preferred_element_type=jnp.float32)
 
 
 def slot_specs(q_rows, g_rows, nk, tok):
@@ -158,6 +185,24 @@
     )(q_arr, g_arr, key_arr, value_arr, mask_t, fin)
 
 
+def slot_part(kernel, q_arr, g_arr, q_rows, g_rows, key_arr, value_arr, mask_t, fin, tok, outs):
+    nk = key_arr.shape[0]
+    cols = STEP_HEADS * HDIM
+    rows = {"q": tok, "k": nk, "v": nk}
+    flops = 6 * tok * nk * HDIM * HEADS
+    return pl.pallas_call(
+        kernel,
+        grid=(HEADS // STEP_HEADS,),
+        in_specs=slot_specs(q_rows, g_rows, nk, tok)
+        + [pl.BlockSpec((STEP_HEADS, 2, tok), lambda h: (h, 0, 0))],
+        out_specs=[pl.BlockSpec((rows[o], cols), lambda h: (0, h)) for o, _ in outs],
+        out_shape=[jax.ShapeDtypeStruct((rows[o], HEADS * HDIM), t) for o, t in outs],
+        cost_estimate=pl.CostEstimate(
+            flops=flops, transcendentals=tok * nk * HEADS, bytes_accessed=6 * (tok + nk) * HDIM * HEADS
+        ),
+    )(q_arr, g_arr, key_arr, value_arr, mask_t, fin)
+
+
 def local(queries, keys, values, grad_out, block_list):
     groups = lax.axis_size("tm")
     here = lax.axis_index("tm")
@@ -229,7 +274,10 @@
     )
     finals = {"far": far_fin, "near": near_fin}
     far_q, far_k, far_v = slot_back(*args["far"], finals["far"], tok, jnp.bfloat16)
-    near_q, near_k, near_v = slot_back(*args["near"], finals["near"], tok, jnp.bfloat16)
+    (near_q,) = slot_part(dq_kernel, *args["near"], finals["near"], tok, [("q", jnp.bfloat16)])
+    near_k, near_v = slot_part(
+        kv_kernel, *args["near"], finals["near"], tok, [("k", jnp.float32), ("v", jnp.float32)]
+    )
     from_far = up_even(far_q)
     from_near = down_even(near_q)
 

time: 181 us -> 187 us (1.033)
  Pallas kernels: 42 us -> 47.9 us
  waiting for transfers between devices: 66.1 us -> 68.2 us
    pallas_call x0 -> x2, Pallas kernels: none -> 12.7 us  [slot_part(): pl.pallas_call(kernel, grid=(HEADS // STEP_HEADS,), in_specs=slot_specs(q...]
    pallas_call x3 -> x2, Pallas kernels: 24.8 us -> 18 us  [slot_back(): pl.pallas_call(back_kernel, grid=(HEADS // STEP_HEADS,), in_specs=slot_sp...]
    ppermute x14, waiting for transfers between devices: 66.1 us -> 68.2 us  [permute(): return lax.ppermute(value, 'tm', pairs)]
    unnamed x42 -> x46, local copies, waits for them, and re-layouts: 4.96 us -> 5.01 us
  transfers between devices with their start and end apart: 14 -> 14, of which waited for: 4 -> 3; matrix products, arithmetic and copies ran while one was open for 14% -> 12% of each run, Pallas kernels for 18% -> 21%
where the time goes in v12:
time: 187 us; the launch traced here: 186 us
  waiting for transfers between devices  68.2 us (36%)
  Pallas kernels  47.9 us (26%)
  starting transfers between devices  32.9 us (18%)
  other arithmetic  20.3 us (11%)
  local copies, waits for them, and re-layouts  14.9 us (8%)
    ppermute x14, waiting for transfers between devices, permute(): return lax.ppermute(value, 'tm', pairs)  68.2 us
    ppermute x14, starting transfers between devices, permute(): return lax.ppermute(value, 'tm', pairs)  32.9 us
    pallas_call x2, Pallas kernels, slot_back(): pl.pallas_call(back_kernel, grid=(HEADS // STEP_HEADS,), in_specs=slot_sp...  18 us
    pallas_call x3, Pallas kernels, slot_stats(): pl.pallas_call(stats_kernel, grid=(HEADS // STEP_HEADS,), in_specs=slot_s...  17.2 us
    pallas_call x2, Pallas kernels, slot_part(): pl.pallas_call(kernel, grid=(HEADS // STEP_HEADS,), in_specs=slot_specs(q...  12.7 us
    unnamed x46, local copies, waits for them, and re-layouts  5.01 us
    another operation x4, other arithmetic  4.49 us
    convert_element_type x3, local copies, waits for them, and re-layouts, local(): mask_t = jnp.broadcast_to(mask4.T[:, None, :, None], (nkb, BLOCK, blocks,...  3.85 us
  transfers between devices with their start and end apart: 14, of which 3 were waited for; matrix products, arithmetic and copies ran while one was open for 12% of the time, Pallas kernels for 21%

profile of v12, /device:TPU:8, one launch (start us, length us, event | category | flops | bytes accessed | tf_op | source)
XLA Modules:
  0.0 185.7 jit_solution(14578104675269640185)
XLA Ops:
  0.6 0.0 copy-start.16
  0.7 0.0 copy-start.17
  0.7 3.4 %collective-permute-start.2 = (bf16[256,1536]{1,0:T(8,128)(2,1)}, bf16[256,1536]{1,0:T(8,128)(2,1)}, u32[]{:S(2)}, u32[]{:S(2)}) collective-permute-start(bf16[256,1536]{1,0:T(8,128)(2,1)} %q_ref.3), channel_id=1, source_target_pairs={{1,3},{2,0},{3,5},{4,2},{5,7},{6,4},{7,9},{8,6},{9,11},{10,8},{11,... | collective-permute-start | bytes 2359304 | tf_op jit(solution)/shard_map/ppermute | solution.py:26
  4.2 2.5 %collective-permute-start.5 = (bf16[256,1536]{1,0:T(8,128)(2,1)}, bf16[256,1536]{1,0:T(8,128)(2,1)}, u32[]{:S(2)}, u32[]{:S(2)}) collective-permute-start(bf16[256,1536]{1,0:T(8,128)(2,1)} %q_ref.3), channel_id=1, source_target_pairs={{0,2},{2,4},{3,1},{4,6},{5,3},{6,8},{7,5},{8,10},{9,7},{10,12},{11... | collective-permute-start | bytes 2359304 | tf_op jit(solution)/shard_map/ppermute | solution.py:26
  6.7 0.2 collective-permute-start
  7.0 0.3 collective-permute-start.1
  7.3 0.7 broadcast_compare_fusion
  8.0 0.1 reshape.188
  8.1 2.1 %pad_maximum_fusion = bf16[272,1536]{1,0:T(8,128)(2,1)} fusion(bf16[16,1536]{1,0:T(8,128)(2,1)S(1)} %pad_convert_fusion, bf16[256,1536]{1,0:T(8,128)(2,1)} %g_ref.3), kind=kLoop, calls=%fused_computation.5 | loop fusion | flops 1671168 | bytes 1671168 | tf_op jit(solution)/shard_map/concatenate | solution.py:219
  10.2 4.4 %collective-permute-start.6 = (bf16[272,1536]{1,0:T(8,128)(2,1)}, bf16[272,1536]{1,0:T(8,128)(2,1)}, u32[]{:S(2)}, u32[]{:S(2)}) collective-permute-start(bf16[272,1536]{1,0:T(8,128)(2,1)} %pad_maximum_fusion), channel_id=1, source_target_pairs={{0,2},{2,4},{3,1},{4,6},{5,3},{6,8},{7,5},{8,10},{9,7},{10,12},{11... | collective-permute-start | bytes 2506760 | tf_op jit(solution)/shard_map/ppermute | solution.py:26
  14.7 0.1 fusion.7
  14.9 0.1 copy.41
  15.0 0.2 broadcast_in_dim.33
  15.2 1.4 convert_element_type.88.m_ref
  16.6 0.1 constant_dynamic-update-slice_fusion.1
  16.7 0.1 constant_dynamic-update-slice_fusion.3
  16.8 2.4 %collective-permute-start.3 = (bf16[272,1536]{1,0:T(8,128)(2,1)}, bf16[272,1536]{1,0:T(8,128)(2,1)S(1)}, u32[]{:S(2)}, u32[]{:S(2)}) collective-permute-start(bf16[272,1536]{1,0:T(8,128)(2,1)} %pad_maximum_fusion), channel_id=1, source_target_pairs={{1,3},{2,0},{3,5},{4,2},{5,7},{6,4},{7,9},{8,6},{9,11},{10,8},{11,... | collective-permute-start | bytes 2506760 | tf_op jit(solution)/shard_map/ppermute | solution.py:26
  19.2 1.2 constant_dynamic-update-slice_fusion.k_ref
  20.4 1.2 copy-done.3
  21.6 1.2 constant_dynamic-update-slice_fusion.2.v_ref
  22.8 1.1 copy-done.2
  23.9 6.3 %shard_map.256 = f32[12,3,256]{2,1,0:T(4,128)} custom-call(bf16[256,1536]{1,0:T(8,128)(2,1)} %q_ref.3, bf16[256,1536]{1,0:T(8,128)(2,1)} %g_ref.3, bf16[512,1536]{1,0:T(8,128)(2,1)} %copy-done.3, bf16[512,1536]{1,0:T(8,128)(2,1)} %copy-done.2, f32[512,256]{1,0:T(8,128)} %convert_element_type.88.m_ref), custom_call_target="tpu_custom_call" | custom-call | flops 805306368 | bytes 4718592 | tf_op jit(solution)/shard_map/pallas_call | solution.py:151
  30.2 0.9 fusion.34
  31.1 42.9 %collective-permute-done.6.g_ref = bf16[272,1536]{1,0:T(8,128)(2,1)} collective-permute-done((bf16[272,1536]{1,0:T(8,128)(2,1)}, bf16[272,1536]{1,0:T(8,128)(2,1)}, u32[]{:S(2)}, u32[]{:S(2)}) %collective-permute-start.6) | collective-permute-done | bytes 835616 | tf_op jit(solution)/shard_map/ppermute | solution.py:26
  74.0 0.7 compare_reduce_fusion
  74.7 0.1 reshape.198
  74.8 0.1 fusion.22
  75.0 0.1 copy.45
  75.1 0.1 broadcast_in_dim.36
  75.2 1.0 convert_element_type.94.m_ref
  76.2 4.6 %shard_map.258 = f32[12,3,256]{2,1,0:T(4,128)} custom-call(bf16[256,1536]{1,0:T(8,128)(2,1)} %collective-permute-done.5.q_ref, bf16[272,1536]{1,0:T(8,128)(2,1)} %collective-permute-done.6.g_ref, bf16[256,1536]{1,0:T(8,128)(2,1)} %k_ref.5, bf16[256,1536]{1,0:T(8,128)(2,1)} %v_ref.5, f32[256,256]{1,0:T(8,128)} %convert_element_type.94.m_ref), custom_call_target="tpu_custom_call" | custom-call | flops 402653184 | bytes 3145728 | tf_op jit(solution)/shard_map/pallas_call | solution.py:151
  80.9 0.8 copy.36
  81.7 4.8 %collective-permute-start.7 = (f32[12,3,256]{2,0,1:T(8,128)S(1)}, f32[12,3,256]{2,0,1:T(8,128)S(1)}, u32[]{:S(2)}, u32[]{:S(2)}) collective-permute-start(f32[12,3,256]{2,0,1:T(8,128)S(1)} %copy.36), channel_id=1, source_target_pairs={{1,3},{2,0},{3,5},{4,2},{5,7},{6,4},{7,9},{8,6},{9,11},{10,8},{11,... | collective-permute-start | bytes 110600 | tf_op jit(solution)/shard_map/ppermute | solution.py:26
  86.5 0.1 reshape.196
  86.6 0.1 fusion.11
  86.7 0.1 copy.43
  86.8 0.1 convert_bitcast_fusion
  86.9 0.2 broadcast_in_dim.35
  87.1 1.4 convert_element_type.91.m_ref
  88.5 6.3 %shard_map.257 = f32[12,3,256]{2,1,0:T(4,128)} custom-call(bf16[256,1536]{1,0:T(8,128)(2,1)} %collective-permute-done.2.q_ref, bf16[272,1536]{1,0:T(8,128)(2,1)} %copy-done.11, bf16[512,1536]{1,0:T(8,128)(2,1)} %copy-done.3, bf16[512,1536]{1,0:T(8,128)(2,1)} %copy-done.2, f32[512,256]{1,0:T(8,128)} %convert_element_type.91.m_ref), custom_call_target="tpu_custom_call" | custom-call | flops 805306368 | bytes 4718592 | tf_op jit(solution)/shard_map/pallas_call | solution.py:151
  94.8 0.8 copy.35
  95.6 1.9 %collective-permute-start.4 = (f32[12,3,256]{2,0,1:T(8,128)S(1)}, f32[12,3,256]{2,0,1:T(8,128)S(1)}, u32[]{:S(2)}, u32[]{:S(2)}) collective-permute-start(f32[12,3,256]{2,0,1:T(8,128)S(1)} %copy.35), channel_id=1, source_target_pairs={{0,2},{2,4},{3,1},{4,6},{5,3},{6,8},{7,5},{8,10},{9,7},{10,12},{11... | collective-permute-start | bytes 110600 | tf_op jit(solution)/shard_map/ppermute | solution.py:26
  97.5 4.9 %collective-permute-done.4 = f32[12,3,256]{2,0,1:T(8,128)S(1)} collective-permute-done((f32[12,3,256]{2,0,1:T(8,128)S(1)}, f32[12,3,256]{2,0,1:T(8,128)S(1)}, u32[]{:S(2)}, u32[]{:S(2)}) %collective-permute-start.4) | collective-permute-done | bytes 36896 | tf_op jit(solution)/shard_map/ppermute | solution.py:26
  102.6 1.9 %collective-permute-start.9 = (f32[12,2,256]{2,1,0:T(2,128)S(1)}, f32[12,2,256]{2,1,0:T(2,128)S(1)}, u32[]{:S(2)}, u32[]{:S(2)}) collective-permute-start(f32[12,2,256]{2,1,0:T(2,128)S(1)} %pad_maximum_fusion.1.f_ref), channel_id=1, source_target_pairs={{0,2},{2,4},{3,1},{4,6},{5,3},{6,8},{7,5},{8,10},{9,7},{10,12},{11... | collective-permute-start | bytes 73736 | tf_op jit(solution)/shard_map/ppermute | solution.py:26
  104.6 5.0 %collective-permute-start.8 = (f32[12,2,256]{2,1,0:T(2,128)S(1)}, f32[12,2,256]{2,1,0:T(2,128)S(1)}, u32[]{:S(2)}, u32[]{:S(2)}) collective-permute-start(f32[12,2,256]{2,1,0:T(2,128)S(1)} %pad_maximum_fusion.1.f_ref), channel_id=1, source_target_pairs={{1,3},{2,0},{3,5},{4,2},{5,7},{6,4},{7,9},{8,6},{9,11},{10,8},{11,... | collective-permute-start | bytes 73736 | tf_op jit(solution)/shard_map/ppermute | solution.py:26
  109.6 9.1 %shard_map.259 = (f32[256,1536]{1,0:T(8,128)}, f32[512,1536]{1,0:T(8,128)}, f32[512,1536]{1,0:T(8,128)}) custom-call(bf16[256,1536]{1,0:T(8,128)(2,1)} %q_ref.3, bf16[256,1536]{1,0:T(8,128)(2,1)} %g_ref.3, bf16[512,1536]{1,0:T(8,128)(2,1)} %copy-done.3, bf16[512,1536]{1,0:T(8,128)(2,1)} %copy-done.2, f32[512,256]{1,0:T(8,128)} %convert_element_type.88.m_ref, ...), custom_call_target="tpu_custom_call" | custom-call | flops 2013265920 | bytes 14155776 | tf_op jit(solution)/shard_map/pallas_call | solution.py:167
  118.7 2.1 %convert.23 = bf16[512,1536]{1,0:T(8,128)(2,1)S(1)} convert(f32[512,1536]{1,0:T(8,128)} %get-tuple-element.26) | non-fusion elementwise | flops 786432 | bytes 4718592 | tf_op jit(solution)/shard_map/convert.12
  120.8 9.0 %shard_map.260 = (bf16[256,1536]{1,0:T(8,128)(2,1)}, f32[512,1536]{1,0:T(8,128)}, f32[512,1536]{1,0:T(8,128)}) custom-call(bf16[256,1536]{1,0:T(8,128)(2,1)} %collective-permute-done.2.q_ref, bf16[272,1536]{1,0:T(8,128)(2,1)} %copy-done.11, bf16[512,1536]{1,0:T(8,128)(2,1)} %copy-done.3, bf16[512,1536]{1,0:T(8,128)(2,1)} %copy-done.2, ...), custom_call_target="tpu_custom_call" | custom-call | flops 2013265920 | bytes 14155776 | tf_op jit(solution)/shard_map/pallas_call | solution.py:167
  129.8 2.1 %convert.22 = bf16[512,1536]{1,0:T(8,128)(2,1)S(1)} convert(f32[512,1536]{1,0:T(8,128)} %get-tuple-element.25) | non-fusion elementwise | flops 786432 | bytes 4718592 | tf_op jit(solution)/shard_map/convert.13
  131.9 1.4 convert_add_fusion.1
  133.3 1.6 copy-done.7
  134.9 0.2 convert.25
  135.1 0.8 copy-done.8
  135.9 0.2 convert.24
  136.1 1.6 convert_add_fusion
  137.7 0.1 copy-done.4
  137.8 6.4 %shard_map.261 = bf16[256,1536]{1,0:T(8,128)(2,1)} custom-call(bf16[256,1536]{1,0:T(8,128)(2,1)} %collective-permute-done.5.q_ref, bf16[272,1536]{1,0:T(8,128)(2,1)} %collective-permute-done.6.g_ref, bf16[256,1536]{1,0:T(8,128)(2,1)} %k_ref.5, bf16[256,1536]{1,0:T(8,128)(2,1)} %v_ref.5, f32[256,256]{1,0:T(8,128)} %convert_element_type.94.m_ref, ...), custom_call_target="tpu_custom_call" | custom-call | flops 603979776 | bytes 4718592 | tf_op jit(solution)/shard_map/pallas_call | solution.py:193
  144.2 1.9 %collective-permute-start.11 = (bf16[256,1536]{1,0:T(8,128)(2,1)}, bf16[256,1536]{1,0:T(8,128)(2,1)}, u32[]{:S(2)}, u32[]{:S(2)}) collective-permute-start(bf16[256,1536]{1,0:T(8,128)(2,1)} %shard_map.261), channel_id=1, source_target_pairs={{1,3},{2,0},{3,5},{4,2},{5,7},{6,4},{7,9},{8,6},{9,11},{10,8},{11,... | collective-permute-start | bytes 2359304 | tf_op jit(solution)/shard_map/ppermute | solution.py:26
  146.1 3.9 %collective-permute-start.10 = (bf16[256,1536]{1,0:T(8,128)(2,1)}, bf16[256,1536]{1,0:T(8,128)(2,1)}, u32[]{:S(2)}, u32[]{:S(2)}) collective-permute-start(bf16[256,1536]{1,0:T(8,128)(2,1)} %get-tuple-element.23), channel_id=1, source_target_pairs={{0,2},{2,4},{3,1},{4,6},{5,3},{6,8},{7,5},{8,10},{9,7},{10,12},{11... | collective-permute-start | bytes 2359304 | tf_op jit(solution)/shard_map/ppermute | solution.py:26
  150.0 6.3 %shard_map.262 = (f32[256,1536]{1,0:T(8,128)}, f32[256,1536]{1,0:T(8,128)}) custom-call(bf16[256,1536]{1,0:T(8,128)(2,1)} %collective-permute-done.5.q_ref, bf16[272,1536]{1,0:T(8,128)(2,1)} %collective-permute-done.6.g_ref, bf16[256,1536]{1,0:T(8,128)(2,1)} %k_ref.5, bf16[256,1536]{1,0:T(8,128)(2,1)} %v_ref.5, f32[256,256]{1,0:T(8,128)} %convert_element_type.94.m_ref, ...), custom_call_target="tpu_custom_call" | custom-call | flops 603979776 | bytes 4718592 | tf_op jit(solution)/shard_map/pallas_call | solution.py:193
  156.3 3.6 %add_convert_fusion.2 = bf16[256,1536]{1,0:T(8,128)(2,1)} fusion(f32[256,1536]{1,0:T(8,128)} %collective-permute-done.12, bf16[512,1536]{1,0:T(8,128)(2,1)S(1)} %convert.23, bf16[512,1536]{1,0:T(8,128)(2,1)} %copy-done.6, f32[256,1536]{1,0:T(8,128)} %get-tuple-element.27), kind=kLoop, calls=%fused_computation.3 | loop fusion | flops 3145728 | bytes 5505024 | tf_op jit(solution)/shard_map/convert_element_type | solution.py:290
  159.9 2.8 %add_convert_fusion.1 = bf16[256,1536]{1,0:T(8,128)(2,1)} fusion(f32[256,1536]{1,0:T(8,128)} %collective-permute-done.13, bf16[512,1536]{1,0:T(8,128)(2,1)S(1)} %convert.25, bf16[512,1536]{1,0:T(8,128)(2,1)S(1)} %copy-done.5, f32[256,1536]{1,0:T(8,128)S(1)} %copy-done.10), kind=kLoop, calls=%fused_computation.1 | loop fusion | flops 3145728 | bytes 5505024 | tf_op jit(solution)/shard_map/convert_element_type | solution.py:291
  162.8 20.3 %collective-permute-done.11 = bf16[256,1536]{1,0:T(8,128)(2,1)} collective-permute-done((bf16[256,1536]{1,0:T(8,128)(2,1)}, bf16[256,1536]{1,0:T(8,128)(2,1)}, u32[]{:S(2)}, u32[]{:S(2)}) %collective-permute-start.11) | collective-permute-done | bytes 786464 | tf_op jit(solution)/shard_map/ppermute | solution.py:26
  183.1 2.6 %add_convert_fusion = bf16[256,1536]{1,0:T(8,128)(2,1)} fusion(bf16[256,1536]{1,0:T(8,128)(2,1)} %collective-permute-done.11, f32[256,1536]{1,0:T(8,128)S(1)} %copy-done.9, bf16[256,1536]{1,0:T(8,128)(2,1)} %collective-permute-done.10), kind=kLoop, calls=%fused_computation | loop fusion | flops 1966080 | bytes 3932160 | tf_op jit(solution)/shard_map/convert_element_type | solution.py:296
  (67 shorter events, 0.3 us)
Async XLA Ops:
  0.6 14.1 %copy-start.15 = (bf16[4,30,4]{1,2,0:T(4,128)(2,1)S(1)}, bf16[4,30,4]{1,2,0:T(4,128)(2,1)}, u32[]{:S(2)}) copy-start(bf16[4,30,4]{1,2,0:T(4,128)(2,1)} %constant.133) | copy-start | bytes 2884
  0.6 14.0 %copy-start.16 = (bf16[4,30,4]{1,2,0:T(4,128)(2,1)S(1)}, bf16[4,30,4]{1,2,0:T(4,128)(2,1)}, u32[]{:S(2)}) copy-start(bf16[4,30,4]{1,2,0:T(4,128)(2,1)} %constant.134) | copy-start | bytes 2884
  0.7 14.0 %copy-start.17 = (bf16[4,30,4]{1,2,0:T(4,128)(2,1)S(1)}, bf16[4,30,4]{1,2,0:T(4,128)(2,1)}, u32[]{:S(2)}) copy-start(bf16[4,30,4]{1,2,0:T(4,128)(2,1)} %constant.132) | copy-start | bytes 2884
  0.7 14.0 %copy-start.18 = (bf16[4,30,4]{1,2,0:T(4,128)(2,1)S(1)}, bf16[4,30,4]{1,2,0:T(4,128)(2,1)}, u32[]{:S(2)}) copy-start(bf16[4,30,4]{1,2,0:T(4,128)(2,1)} %constant.131) | copy-start | bytes 2884
  0.7 14.1 %copy-start.21 = (bf16[4,30,4]{1,2,0:T(4,128)(2,1)S(1)}, bf16[4,30,4]{1,2,0:T(4,128)(2,1)}, u32[]{:S(2)}) copy-start(bf16[4,30,4]{1,2,0:T(4,128)(2,1)} %constant.135) | copy-start | bytes 2884
  0.7 14.3 %copy-start.19 = (pred[4,8]{0,1:T(8,128)(4,1)S(1)}, pred[4,8]{0,1:T(8,128)(4,1)}, u32[]{:S(2)}) copy-start(pred[4,8]{0,1:T(8,128)(4,1)} %constant.62) | copy-start | bytes 100
  0.7 13.9 %copy-start.14 = (s32[4,30]{1,0:T(4,128)S(1)}, s32[4,30]{1,0:T(4,128)}, u32[]{:S(2)}) copy-start(s32[4,30]{1,0:T(4,128)} %param.29) | copy-start | bytes 1444
  0.7 87.8 %collective-permute-start.2 = (bf16[256,1536]{1,0:T(8,128)(2,1)}, bf16[256,1536]{1,0:T(8,128)(2,1)}, u32[]{:S(2)}, u32[]{:S(2)}) collective-permute-start(bf16[256,1536]{1,0:T(8,128)(2,1)} %q_ref.3), channel_id=1, source_target_pairs={{1,3},{2,0},{3,5},{4,2},{5,7},{6,4},{7,9},{8,6},{9,11},{10,8},{11,... | collective-permute-start | bytes 2359304 | tf_op jit(solution)/shard_map/ppermute | solution.py:26
  4.2 72.1 %collective-permute-start.5 = (bf16[256,1536]{1,0:T(8,128)(2,1)}, bf16[256,1536]{1,0:T(8,128)(2,1)}, u32[]{:S(2)}, u32[]{:S(2)}) collective-permute-start(bf16[256,1536]{1,0:T(8,128)(2,1)} %q_ref.3), channel_id=1, source_target_pairs={{0,2},{2,4},{3,1},{4,6},{5,3},{6,8},{7,5},{8,10},{9,7},{10,12},{11... | collective-permute-start | bytes 2359304 | tf_op jit(solution)/shard_map/ppermute | solution.py:26
  6.7 10.0 %collective-permute-start = (bf16[256,1536]{1,0:T(8,128)(2,1)}, bf16[256,1536]{1,0:T(8,128)(2,1)}, u32[]{:S(2)}, u32[]{:S(2)}) collective-permute-start(bf16[256,1536]{1,0:T(8,128)(2,1)} %k_ref.5), channel_id=1, source_target_pairs={{0,1},{1,0},{2,3},{3,2},{4,5},{5,4},{6,7},{7,6},{8,9},{9,8},{10,11... | collective-permute-start | bytes 2359304 | tf_op jit(solution)/shard_map/ppermute | solution.py:26
  7.0 14.6 %collective-permute-start.1 = (bf16[256,1536]{1,0:T(8,128)(2,1)}, bf16[256,1536]{1,0:T(8,128)(2,1)}, u32[]{:S(2)}, u32[]{:S(2)}) collective-permute-start(bf16[256,1536]{1,0:T(8,128)(2,1)} %v_ref.5), channel_id=1, source_target_pairs={{0,1},{1,0},{2,3},{3,2},{4,5},{5,4},{6,7},{7,6},{8,9},{9,8},{10,11... | collective-permute-start | bytes 2359304 | tf_op jit(solution)/shard_map/ppermute | solution.py:26
  10.2 6.4 %copy-start = (bf16[256,1536]{1,0:T(8,128)(2,1)S(1)}, bf16[256,1536]{1,0:T(8,128)(2,1)}, u32[]{:S(2)}) copy-start(bf16[256,1536]{1,0:T(8,128)(2,1)} %k_ref.5) | copy-start | bytes 2359300
  10.2 63.9 %collective-permute-start.6 = (bf16[272,1536]{1,0:T(8,128)(2,1)}, bf16[272,1536]{1,0:T(8,128)(2,1)}, u32[]{:S(2)}, u32[]{:S(2)}) collective-permute-start(bf16[272,1536]{1,0:T(8,128)(2,1)} %pad_maximum_fusion), channel_id=1, source_target_pairs={{0,2},{2,4},{3,1},{4,6},{5,3},{6,8},{7,5},{8,10},{9,7},{10,12},{11... | collective-permute-start | bytes 2506760 | tf_op jit(solution)/shard_map/ppermute | solution.py:26
  15.2 1.5 copy-start.1
  16.8 69.7 %collective-permute-start.3 = (bf16[272,1536]{1,0:T(8,128)(2,1)}, bf16[272,1536]{1,0:T(8,128)(2,1)S(1)}, u32[]{:S(2)}, u32[]{:S(2)}) collective-permute-start(bf16[272,1536]{1,0:T(8,128)(2,1)} %pad_maximum_fusion), channel_id=1, source_target_pairs={{1,3},{2,0},{3,5},{4,2},{5,7},{6,4},{7,9},{8,6},{9,11},{10,8},{11,... | collective-permute-start | bytes 2506760 | tf_op jit(solution)/shard_map/ppermute | solution.py:26
  20.4 1.2 copy-start.3
  22.7 1.2 copy-start.2
  81.7 15.9 %collective-permute-start.7 = (f32[12,3,256]{2,0,1:T(8,128)S(1)}, f32[12,3,256]{2,0,1:T(8,128)S(1)}, u32[]{:S(2)}, u32[]{:S(2)}) collective-permute-start(f32[12,3,256]{2,0,1:T(8,128)S(1)} %copy.36), channel_id=1, source_target_pairs={{1,3},{2,0},{3,5},{4,2},{5,7},{6,4},{7,9},{8,6},{9,11},{10,8},{11,... | collective-permute-start | bytes 110600 | tf_op jit(solution)/shard_map/ppermute | solution.py:26
  86.5 2.0 %copy-start.11 = (bf16[272,1536]{1,0:T(8,128)(2,1)}, bf16[272,1536]{1,0:T(8,128)(2,1)S(1)}, u32[]{:S(2)}) copy-start(bf16[272,1536]{1,0:T(8,128)(2,1)S(1)} %collective-permute-done.3.g_ref) | copy-start | bytes 2506756
  95.6 6.9 %collective-permute-start.4 = (f32[12,3,256]{2,0,1:T(8,128)S(1)}, f32[12,3,256]{2,0,1:T(8,128)S(1)}, u32[]{:S(2)}, u32[]{:S(2)}) collective-permute-start(f32[12,3,256]{2,0,1:T(8,128)S(1)} %copy.35), channel_id=1, source_target_pairs={{0,2},{2,4},{3,1},{4,6},{5,3},{6,8},{7,5},{8,10},{9,7},{10,12},{11... | collective-permute-start | bytes 110600 | tf_op jit(solution)/shard_map/ppermute | solution.py:26
  102.6 7.0 %copy-start.13 = (f32[12,2,256]{2,1,0:T(2,128)}, f32[12,2,256]{2,1,0:T(2,128)S(1)}, u32[]{:S(2)}) copy-start(f32[12,2,256]{2,1,0:T(2,128)S(1)} %pad_maximum_fusion.1.f_ref) | copy-start | bytes 73732
  102.6 16.0 %collective-permute-start.9 = (f32[12,2,256]{2,1,0:T(2,128)S(1)}, f32[12,2,256]{2,1,0:T(2,128)S(1)}, u32[]{:S(2)}, u32[]{:S(2)}) collective-permute-start(f32[12,2,256]{2,1,0:T(2,128)S(1)} %pad_maximum_fusion.1.f_ref), channel_id=1, source_target_pairs={{0,2},{2,4},{3,1},{4,6},{5,3},{6,8},{7,5},{8,10},{9,7},{10,12},{11... | collective-permute-start | bytes 73736 | tf_op jit(solution)/shard_map/ppermute | solution.py:26
  104.6 14.1 %collective-permute-start.8 = (f32[12,2,256]{2,1,0:T(2,128)S(1)}, f32[12,2,256]{2,1,0:T(2,128)S(1)}, u32[]{:S(2)}, u32[]{:S(2)}) collective-permute-start(f32[12,2,256]{2,1,0:T(2,128)S(1)} %pad_maximum_fusion.1.f_ref), channel_id=1, source_target_pairs={{1,3},{2,0},{3,5},{4,2},{5,7},{6,4},{7,9},{8,6},{9,11},{10,8},{11,... | collective-permute-start | bytes 73736 | tf_op jit(solution)/shard_map/ppermute | solution.py:26
  118.7 2.1 %copy-start.12 = (f32[12,2,256]{2,1,0:T(2,128)}, f32[12,2,256]{2,1,0:T(2,128)S(1)}, u32[]{:S(2)}) copy-start(f32[12,2,256]{2,1,0:T(2,128)S(1)} %collective-permute-done.9.f_ref) | copy-start | bytes 73732
  118.7 2.1 %copy-start.20 = (f32[12,2,256]{2,1,0:T(2,128)}, f32[12,2,256]{2,1,0:T(2,128)S(1)}, u32[]{:S(2)}) copy-start(f32[12,2,256]{2,1,0:T(2,128)S(1)} %collective-permute-done.8.f_ref) | copy-start | bytes 73732
  131.8 3.2 %copy-start.6 = (bf16[512,1536]{1,0:T(8,128)(2,1)}, bf16[512,1536]{1,0:T(8,128)(2,1)S(1)}, u32[]{:S(2)}) copy-start(bf16[512,1536]{1,0:T(8,128)(2,1)S(1)} %convert.22) | copy-start | bytes 4718596
  131.8 3.0 %copy-start.7 = (f32[512,1536]{1,0:T(8,128)S(1)}, f32[512,1536]{1,0:T(8,128)}, u32[]{:S(2)}) copy-start(f32[512,1536]{1,0:T(8,128)} %get-tuple-element.29) | copy-start | bytes 9437188
  133.3 2.6 %copy-start.8 = (f32[512,1536]{1,0:T(8,128)S(1)}, f32[512,1536]{1,0:T(8,128)}, u32[]{:S(2)}) copy-start(f32[512,1536]{1,0:T(8,128)} %get-tuple-element.28) | copy-start | bytes 9437188
  133.3 23.0 %collective-permute-start.12 = (f32[256,1536]{1,0:T(8,128)}, f32[256,1536]{1,0:T(8,128)}, u32[]{:S(2)}, u32[]{:S(2)}) collective-permute-start(f32[256,1536]{1,0:T(8,128)} %convert_add_fusion.1), channel_id=1, source_target_pairs={{0,1},{1,0},{2,3},{3,2},{4,5},{5,4},{6,7},{7,6},{8,9},{9,8},{10,11... | collective-permute-start | bytes 4718600 | tf_op jit(solution)/shard_map/ppermute | solution.py:26
  136.1 1.7 copy-start.4
  137.8 22.1 %collective-permute-start.13 = (f32[256,1536]{1,0:T(8,128)}, f32[256,1536]{1,0:T(8,128)}, u32[]{:S(2)}, u32[]{:S(2)}) collective-permute-start(f32[256,1536]{1,0:T(8,128)} %convert_add_fusion), channel_id=1, source_target_pairs={{0,1},{1,0},{2,3},{3,2},{4,5},{5,4},{6,7},{7,6},{8,9},{9,8},{10,11... | collective-permute-start | bytes 4718600 | tf_op jit(solution)/shard_map/ppermute | solution.py:26
  144.2 38.9 %collective-permute-start.11 = (bf16[256,1536]{1,0:T(8,128)(2,1)}, bf16[256,1536]{1,0:T(8,128)(2,1)}, u32[]{:S(2)}, u32[]{:S(2)}) collective-permute-start(bf16[256,1536]{1,0:T(8,128)(2,1)} %shard_map.261), channel_id=1, source_target_pairs={{1,3},{2,0},{3,5},{4,2},{5,7},{6,4},{7,9},{8,6},{9,11},{10,8},{11,... | collective-permute-start | bytes 2359304 | tf_op jit(solution)/shard_map/ppermute | solution.py:26
  146.1 37.0 %collective-permute-start.10 = (bf16[256,1536]{1,0:T(8,128)(2,1)}, bf16[256,1536]{1,0:T(8,128)(2,1)}, u32[]{:S(2)}, u32[]{:S(2)}) collective-permute-start(bf16[256,1536]{1,0:T(8,128)(2,1)} %get-tuple-element.23), channel_id=1, source_target_pairs={{0,2},{2,4},{3,1},{4,6},{5,3},{6,8},{7,5},{8,10},{9,7},{10,12},{11... | collective-permute-start | bytes 2359304 | tf_op jit(solution)/shard_map/ppermute | solution.py:26
  156.3 3.6 %copy-start.5 = (bf16[512,1536]{1,0:T(8,128)(2,1)S(1)}, bf16[512,1536]{1,0:T(8,128)(2,1)}, u32[]{:S(2)}) copy-start(bf16[512,1536]{1,0:T(8,128)(2,1)} %copy-done.4) | copy-start | bytes 4718596
  156.3 3.6 %copy-start.10 = (f32[256,1536]{1,0:T(8,128)S(1)}, f32[256,1536]{1,0:T(8,128)}, u32[]{:S(2)}) copy-start(f32[256,1536]{1,0:T(8,128)} %get-tuple-element.30) | copy-start | bytes 4718596
  159.9 23.1 %copy-start.9 = (f32[256,1536]{1,0:T(8,128)S(1)}, f32[256,1536]{1,0:T(8,128)}, u32[]{:S(2)}) copy-start(f32[256,1536]{1,0:T(8,128)} %get-tuple-element.19) | copy-start | bytes 4718596

commit v13 on v11

--- a/solution.py
+++ b/solution.py
@@ -86,8 +86,17 @@
         mx = jnp.max(masked, axis=0, keepdims=True)
         e = jnp.where(m, jnp.exp(masked - mx), 0.0)
         total = jnp.sum(e, axis=0, keepdims=True)
-        dot = jnp.sum(e * dp, axis=0, keepdims=True)
-        out_ref[j] = jnp.concatenate([mx, total, dot], axis=0)
+        out_ref[j] = jnp.concatenate([mx, total], axis=0)
+
+
+def delta_kernel(q_ref, g_ref, k_ref, v_ref, m_ref, f_ref, out_ref):
+    m = m_ref[...] > 0
+    for j in range(STEP_HEADS):
+        cols = head_cols(j)
+        s, dp = slot_scores(q_ref[:, cols], g_ref[:, cols], k_ref[:, cols], v_ref[:, cols])
+        p = jnp.where(m, jnp.exp(s - f_ref[j]), 0.0)
+        low = lax.reduce_precision(p, exponent_bits=8, mantissa_bits=7)
+        out_ref[j] = jnp.sum(low * dp, axis=0, keepdims=True)
 
 
 def back_kernel(q_ref, g_ref, k_ref, v_ref, m_ref, f_ref, dq_ref, dk_ref, dv_ref):
@@ -125,12 +134,28 @@
         stats_kernel,
         grid=(HEADS // STEP_HEADS,),
         in_specs=slot_specs(q_rows, g_rows, nk, tok),
-        out_specs=pl.BlockSpec((STEP_HEADS, 3, tok), lambda h: (h, 0, 0)),
-        out_shape=jax.ShapeDtypeStruct((HEADS, 3, tok), jnp.float32),
+        out_specs=pl.BlockSpec((STEP_HEADS, 2, tok), lambda h: (h, 0, 0)),
+        out_shape=jax.ShapeDtypeStruct((HEADS, 2, tok), jnp.float32),
         cost_estimate=pl.CostEstimate(
             flops=flops, transcendentals=tok * nk * HEADS, bytes_accessed=4 * (tok + nk) * HDIM * HEADS
         ),
     )(q_arr, g_arr, key_arr, value_arr, mask_t)
+
+
+def slot_delta(q_arr, g_arr, q_rows, g_rows, key_arr, value_arr, mask_t, lse, tok):
+    nk = key_arr.shape[0]
+    flops = 4 * tok * nk * HDIM * HEADS
+    return pl.pallas_call(
+        delta_kernel,
+        grid=(HEADS // STEP_HEADS,),
+        in_specs=slot_specs(q_rows, g_rows, nk, tok)
+        + [pl.BlockSpec((STEP_HEADS, 1, tok), lambda h: (h, 0, 0))],
+        out_specs=pl.BlockSpec((STEP_HEADS, 1, tok), lambda h: (h, 0, 0)),
+        out_shape=jax.ShapeDtypeStruct((HEADS, 1, tok), jnp.float32),
+        cost_estimate=pl.CostEstimate(
+            flops=flops, transcendentals=tok * nk * HEADS, bytes_accessed=4 * (tok + nk) * HDIM * HEADS
+        ),
+    )(q_arr, g_arr, key_arr, value_arr, mask_t, lse)
 
 
 def slot_back(q_arr, g_arr, q_rows, g_rows, key_arr, value_arr, mask_t, fin, tok, dq_type):
@@ -207,20 +232,20 @@
         (up_even(stats_out["far"]), -2 * up),
         (down_even(stats_out["near"]), 2 * up),
     ]
-    maxes, sums, dots = [], [], []
+    maxes, sums = [], []
     for stats, offset in stats_in:
         source = here + offset
         valid = (source >= 0) & (source < groups)
         maxes.append(jnp.where(valid, stats[:, 0], NEG))
         sums.append(jnp.where(valid, stats[:, 1], 0.0))
-        dots.append(jnp.where(valid, stats[:, 2], 0.0))
-    maxes, sums, dots = jnp.stack(maxes), jnp.stack(sums), jnp.stack(dots)
+    maxes, sums = jnp.stack(maxes), jnp.stack(sums)
     top = jnp.max(maxes, axis=0)
-    scale = jnp.exp(maxes - top[None])
-    total = jnp.sum(sums * scale, axis=0)
-    log_total = top + jnp.log(total)
-    deltas = jnp.sum(dots * scale, axis=0) / total
-    final = jnp.stack([log_total, deltas], axis=1)
+    total = jnp.sum(sums * jnp.exp(maxes - top[None]), axis=0)
+    log_total = (top + jnp.log(total))[:, None, :]
+    lses = {"own": log_total, "far": down_even(log_total), "near": up_even(log_total)}
+    parts = {name: slot_delta(*args[name], lses[name], tok) for name in slots}
+    deltas = parts["own"] + up_even(parts["far"]) + down_even(parts["near"])
+    final = jnp.concatenate([log_total, deltas], axis=1)
     finals = {"far": down_even(final), "near": up_even(final)}
 
     own_q, own_k, own_v = slot_back(*args["own"], final, tok, jnp.float32)

time: 181 us -> 216 us (1.19)
  Pallas kernels: 42 us -> 58 us
  starting transfers between devices: 33.8 us -> 46.8 us
  waiting for transfers between devices: 66.1 us -> 69.9 us
    pallas_call x0 -> x3, Pallas kernels: none -> 17.6 us  [slot_delta(): pl.pallas_call(delta_kernel, grid=(HEADS // STEP_HEADS,), in_specs=slot_s...]
    ppermute x14 -> x18, starting transfers between devices: 33.8 us -> 46.8 us  [permute(): return lax.ppermute(value, 'tm', pairs)]
    ppermute x14 -> x18, waiting for transfers between devices: 66.1 us -> 69.9 us  [permute(): return lax.ppermute(value, 'tm', pairs)]
    unnamed x42 -> x51, local copies, waits for them, and re-layouts: 4.96 us -> 5.11 us
    another operation x5 -> x4, other arithmetic: 4.51 us -> 4.49 us
  transfers between devices with their start and end apart: 14 -> 18, of which waited for: 4 -> 3; matrix products, arithmetic and copies ran while one was open for 14% -> 11% of each run, Pallas kernels for 18% -> 23%
where the time goes in v13:
time: 216 us; the launch traced here: 213 us
  waiting for transfers between devices  69.9 us (32%)
  Pallas kernels  58 us (27%)
  starting transfers between devices  46.8 us (22%)
  other arithmetic  22.2 us (10%)
  local copies, waits for them, and re-layouts  14.9 us (7%)
    ppermute x18, waiting for transfers between devices, permute(): return lax.ppermute(value, 'tm', pairs)  69.9 us
    ppermute x18, starting transfers between devices, permute(): return lax.ppermute(value, 'tm', pairs)  46.8 us
    pallas_call x3, Pallas kernels, slot_back(): pl.pallas_call(back_kernel, grid=(HEADS // STEP_HEADS,), in_specs=slot_sp...  24.7 us
    pallas_call x3, Pallas kernels, slot_delta(): pl.pallas_call(delta_kernel, grid=(HEADS // STEP_HEADS,), in_specs=slot_s...  17.6 us
    pallas_call x3, Pallas kernels, slot_stats(): pl.pallas_call(stats_kernel, grid=(HEADS // STEP_HEADS,), in_specs=slot_s...  15.6 us
    unnamed x51, local copies, waits for them, and re-layouts  5.11 us
    convert_element_type x3, local copies, waits for them, and re-layouts, local(): mask_t = jnp.broadcast_to(mask4.T[:, None, :, None], (nkb, BLOCK, blocks,...  4.91 us
    another operation x4, other arithmetic  4.49 us
  transfers between devices with their start and end apart: 18, of which 3 were waited for; matrix products, arithmetic and copies ran while one was open for 11% of the time, Pallas kernels for 23%

profile of v13, /device:TPU:8, one launch (start us, length us, event | category | flops | bytes accessed | tf_op | source)
XLA Modules:
  0.0 213.4 jit_solution(3076304787946910266)
XLA Ops:
  0.6 3.6 %collective-permute-start.5 = (bf16[256,1536]{1,0:T(8,128)(2,1)}, bf16[256,1536]{1,0:T(8,128)(2,1)}, u32[]{:S(2)}, u32[]{:S(2)}) collective-permute-start(bf16[256,1536]{1,0:T(8,128)(2,1)} %q_ref.5), channel_id=1, source_target_pairs={{0,2},{2,4},{3,1},{4,6},{5,3},{6,8},{7,5},{8,10},{9,7},{10,12},{11... | collective-permute-start | bytes 2359304 | tf_op jit(solution)/shard_map/ppermute | solution.py:26
  4.2 3.3 %collective-permute-start.2 = (bf16[256,1536]{1,0:T(8,128)(2,1)}, bf16[256,1536]{1,0:T(8,128)(2,1)}, u32[]{:S(2)}, u32[]{:S(2)}) collective-permute-start(bf16[256,1536]{1,0:T(8,128)(2,1)} %q_ref.5), channel_id=1, source_target_pairs={{1,3},{2,0},{3,5},{4,2},{5,7},{6,4},{7,9},{8,6},{9,11},{10,8},{11,... | collective-permute-start | bytes 2359304 | tf_op jit(solution)/shard_map/ppermute | solution.py:26
  7.6 0.5 collective-permute-start.1
  8.1 0.7 broadcast_compare_fusion
  8.8 0.1 reshape.137
  9.0 2.1 pad_maximum_fusion
  11.1 2.5 %collective-permute-start.6 = (bf16[272,1536]{1,0:T(8,128)(2,1)}, bf16[272,1536]{1,0:T(8,128)(2,1)}, u32[]{:S(2)}, u32[]{:S(2)}) collective-permute-start(bf16[272,1536]{1,0:T(8,128)(2,1)} %pad_maximum_fusion), channel_id=1, source_target_pairs={{0,2},{2,4},{3,1},{4,6},{5,3},{6,8},{7,5},{8,10},{9,7},{10,12},{11... | collective-permute-start | bytes 2506760 | tf_op jit(solution)/shard_map/ppermute | solution.py:26
  13.8 0.1 fusion.2
  14.0 0.2 broadcast_in_dim.31
  14.3 1.4 convert_element_type.88.m_ref
  15.7 1.2 constant_dynamic-update-slice_fusion.3
  16.9 4.2 %collective-permute-start.3 = (bf16[272,1536]{1,0:T(8,128)(2,1)}, bf16[272,1536]{1,0:T(8,128)(2,1)}, u32[]{:S(2)}, u32[]{:S(2)}) collective-permute-start(bf16[272,1536]{1,0:T(8,128)(2,1)} %pad_maximum_fusion), channel_id=1, source_target_pairs={{1,3},{2,0},{3,5},{4,2},{5,7},{6,4},{7,9},{8,6},{9,11},{10,8},{11,... | collective-permute-start | bytes 2506760 | tf_op jit(solution)/shard_map/ppermute | solution.py:26
  21.1 1.2 constant_dynamic-update-slice_fusion.k_ref
  22.3 1.8 constant_dynamic-update-slice_fusion.2.v_ref
  24.1 50.7 %collective-permute-done.6.g_ref = bf16[272,1536]{1,0:T(8,128)(2,1)} collective-permute-done((bf16[272,1536]{1,0:T(8,128)(2,1)}, bf16[272,1536]{1,0:T(8,128)(2,1)}, u32[]{:S(2)}, u32[]{:S(2)}) %collective-permute-start.6) | collective-permute-done | bytes 835616 | tf_op jit(solution)/shard_map/ppermute | solution.py:26
  74.8 0.6 compare_reduce_fusion
  75.4 0.1 reshape.147
  75.5 0.1 fusion.13
  75.6 0.1 copy.33
  75.7 0.9 broadcast_in_dim.34
  76.7 2.1 convert_element_type.94.m_ref
  78.8 4.3 %shard_map.258 = f32[12,2,256]{2,1,0:T(2,128)} custom-call(bf16[256,1536]{1,0:T(8,128)(2,1)} %collective-permute-done.5.q_ref, bf16[272,1536]{1,0:T(8,128)(2,1)} %collective-permute-done.6.g_ref, bf16[256,1536]{1,0:T(8,128)(2,1)} %k_ref.5, bf16[256,1536]{1,0:T(8,128)(2,1)} %v_ref.5, f32[256,256]{1,0:T(8,128)} %convert_element_type.94.m_ref), custom_call_target="tpu_custom_call" | custom-call | flops 402653184 | bytes 3145728 | tf_op jit(solution)/shard_map/pallas_call | solution.py:133
  83.1 4.3 %collective-permute-start.7 = (f32[12,2,256]{2,1,0:T(2,128)}, f32[12,2,256]{2,1,0:T(2,128)S(1)}, u32[]{:S(2)}, u32[]{:S(2)}) collective-permute-start(f32[12,2,256]{2,1,0:T(2,128)} %shard_map.258), channel_id=1, source_target_pairs={{1,3},{2,0},{3,5},{4,2},{5,7},{6,4},{7,9},{8,6},{9,11},{10,8},{11,... | collective-permute-start | bytes 73736 | tf_op jit(solution)/shard_map/ppermute | solution.py:26
  87.4 0.6 compare_reduce_fusion.1
  88.1 0.1 reshape.145
  88.2 0.1 fusion.6
  88.5 0.2 broadcast_in_dim.33
  88.7 1.4 convert_element_type.91.m_ref
  90.1 5.6 %shard_map.257 = f32[12,2,256]{2,1,0:T(2,128)} custom-call(bf16[256,1536]{1,0:T(8,128)(2,1)} %collective-permute-done.2.q_ref, bf16[272,1536]{1,0:T(8,128)(2,1)} %collective-permute-done.3.g_ref, bf16[512,1536]{1,0:T(8,128)(2,1)} %copy-done, bf16[512,1536]{1,0:T(8,128)(2,1)} %copy-done.1, f32[512,256]{1,0:T(8,128)} %convert_element_type.91.m_ref), custom_call_target="tpu_custom_call" | custom-call | flops 805306368 | bytes 4718592 | tf_op jit(solution)/shard_map/pallas_call | solution.py:133
  95.7 2.0 collective-permute-start.4
  97.7 5.6 %shard_map.256 = f32[12,2,256]{2,1,0:T(2,128)} custom-call(bf16[256,1536]{1,0:T(8,128)(2,1)} %q_ref.5, bf16[256,1536]{1,0:T(8,128)(2,1)} %g_ref.5, bf16[512,1536]{1,0:T(8,128)(2,1)} %copy-done, bf16[512,1536]{1,0:T(8,128)(2,1)} %copy-done.1, f32[512,256]{1,0:T(8,128)} %convert_element_type.88.m_ref), custom_call_target="tpu_custom_call" | custom-call | flops 805306368 | bytes 4718592 | tf_op jit(solution)/shard_map/pallas_call | solution.py:133
  103.4 0.9 fusion.22
  104.3 0.1 fusion
  104.5 4.8 %collective-permute-start.10 = (f32[12,1,256]{2,1,0:T(1,128)S(1)}, f32[12,1,256]{2,1,0:T(1,128)S(1)}, u32[]{:S(2)}, u32[]{:S(2)}) collective-permute-start(f32[12,1,256]{2,1,0:T(1,128)S(1)} %reshape_add_fusion.f_ref), channel_id=1, source_target_pairs={{0,2},{2,4},{3,1},{4,6},{5,3},{6,8},{7,5},{8,10},{9,7},{10,12},{11... | collective-permute-start | bytes 36872 | tf_op jit(solution)/shard_map/ppermute | solution.py:26
  109.3 1.9 collective-permute-start.8
  111.3 0.6 copy-done.13
  111.8 4.8 %shard_map.261 = f32[12,1,256]{2,1,0:T(1,128)} custom-call(bf16[256,1536]{1,0:T(8,128)(2,1)} %collective-permute-done.5.q_ref, bf16[272,1536]{1,0:T(8,128)(2,1)} %collective-permute-done.6.g_ref, bf16[256,1536]{1,0:T(8,128)(2,1)} %k_ref.5, bf16[256,1536]{1,0:T(8,128)(2,1)} %v_ref.5, f32[256,256]{1,0:T(8,128)} %convert_element_type.94.m_ref, ...), custom_call_target="tpu_custom_call" | custom-call | flops 402653184 | bytes 3145728 | tf_op jit(solution)/shard_map/pallas_call | solution.py:148
  116.6 3.8 %collective-permute-start.11 = (f32[12,1,256]{2,1,0:T(1,128)}, f32[12,1,256]{2,1,0:T(1,128)S(1)}, u32[]{:S(2)}, u32[]{:S(2)}) collective-permute-start(f32[12,1,256]{2,1,0:T(1,128)} %shard_map.261), channel_id=1, source_target_pairs={{1,3},{2,0},{3,5},{4,2},{5,7},{6,4},{7,9},{8,6},{9,11},{10,8},{11,... | collective-permute-start | bytes 36872 | tf_op jit(solution)/shard_map/ppermute | solution.py:26
  120.5 0.6 copy-done.14
  121.1 6.4 %shard_map.260 = f32[12,1,256]{2,1,0:T(1,128)} custom-call(bf16[256,1536]{1,0:T(8,128)(2,1)} %collective-permute-done.2.q_ref, bf16[272,1536]{1,0:T(8,128)(2,1)} %collective-permute-done.3.g_ref, bf16[512,1536]{1,0:T(8,128)(2,1)} %copy-done, bf16[512,1536]{1,0:T(8,128)(2,1)} %copy-done.1, f32[512,256]{1,0:T(8,128)} %convert_element_type.91.m_ref, ...), custom_call_target="tpu_custom_call" | custom-call | flops 805306368 | bytes 4718592 | tf_op jit(solution)/shard_map/pallas_call | solution.py:148
  127.5 2.1 %collective-permute-start.9 = (f32[12,1,256]{2,1,0:T(1,128)}, f32[12,1,256]{2,1,0:T(1,128)S(1)}, u32[]{:S(2)}, u32[]{:S(2)}) collective-permute-start(f32[12,1,256]{2,1,0:T(1,128)} %shard_map.260), channel_id=1, source_target_pairs={{0,2},{2,4},{3,1},{4,6},{5,3},{6,8},{7,5},{8,10},{9,7},{10,12},{11... | collective-permute-start | bytes 36872 | tf_op jit(solution)/shard_map/ppermute | solution.py:26
  129.6 6.4 %shard_map.259 = f32[12,1,256]{2,1,0:T(1,128)} custom-call(bf16[256,1536]{1,0:T(8,128)(2,1)} %q_ref.5, bf16[256,1536]{1,0:T(8,128)(2,1)} %g_ref.5, bf16[512,1536]{1,0:T(8,128)(2,1)} %copy-done, bf16[512,1536]{1,0:T(8,128)(2,1)} %copy-done.1, f32[512,256]{1,0:T(8,128)} %convert_element_type.88.m_ref, f32[12,1,256]{2,1,0:T(1,128)} %copy-done.10), custom_call_target="tpu_custom_call" | custom-call | flops 805306368 | bytes 4718592 | tf_op jit(solution)/shard_map/pallas_call | solution.py:148
  136.1 0.7 add_add_fusion
  136.8 4.8 %collective-permute-start.13 = (f32[12,2,256]{2,1,0:T(2,128)S(1)}, f32[12,2,256]{2,1,0:T(2,128)S(1)}, u32[]{:S(2)}, u32[]{:S(2)}) collective-permute-start(f32[12,2,256]{2,1,0:T(2,128)S(1)} %pad_maximum_fusion.1.f_ref), channel_id=1, source_target_pairs={{0,2},{2,4},{3,1},{4,6},{5,3},{6,8},{7,5},{8,10},{9,7},{10,12},{11... | collective-permute-start | bytes 73736 | tf_op jit(solution)/shard_map/ppermute | solution.py:26
  141.7 2.1 collective-permute-start.12
  143.8 9.0 %shard_map.262 = (f32[256,1536]{1,0:T(8,128)}, f32[512,1536]{1,0:T(8,128)}, f32[512,1536]{1,0:T(8,128)}) custom-call(bf16[256,1536]{1,0:T(8,128)(2,1)} %q_ref.5, bf16[256,1536]{1,0:T(8,128)(2,1)} %g_ref.5, bf16[512,1536]{1,0:T(8,128)(2,1)} %copy-done, bf16[512,1536]{1,0:T(8,128)(2,1)} %copy-done.1, f32[512,256]{1,0:T(8,128)} %convert_element_type.88.m_ref, ...), custom_call_target="tpu_custom_call" | custom-call | flops 2013265920 | bytes 14155776 | tf_op jit(solution)/shard_map/pallas_call | solution.py:165
  152.8 2.1 convert.25
  154.9 8.9 %shard_map.263 = (bf16[256,1536]{1,0:T(8,128)(2,1)}, f32[512,1536]{1,0:T(8,128)}, f32[512,1536]{1,0:T(8,128)}) custom-call(bf16[256,1536]{1,0:T(8,128)(2,1)} %collective-permute-done.2.q_ref, bf16[272,1536]{1,0:T(8,128)(2,1)} %collective-permute-done.3.g_ref, bf16[512,1536]{1,0:T(8,128)(2,1)} %copy-done, bf16[512,1536]{1,0:T(8,128)(2,1)} %copy-done.1, ...), custom_call_target="tpu_custom_call" | custom-call | flops 2013265920 | bytes 14155776 | tf_op jit(solution)/shard_map/pallas_call | solution.py:165
  163.8 2.1 convert.24
  165.9 1.4 convert_add_fusion
  167.3 0.3 copy-done.5
  167.6 1.3 copy-done.6
  168.9 0.2 convert.23
  169.1 0.9 copy-done.7
  170.0 0.2 convert.22
  170.2 1.6 convert_add_fusion.1
  171.8 3.9 %collective-permute-start.14 = (bf16[256,1536]{1,0:T(8,128)(2,1)}, bf16[256,1536]{1,0:T(8,128)(2,1)}, u32[]{:S(2)}, u32[]{:S(2)}) collective-permute-start(bf16[256,1536]{1,0:T(8,128)(2,1)} %get-tuple-element.24), channel_id=1, source_target_pairs={{0,2},{2,4},{3,1},{4,6},{5,3},{6,8},{7,5},{8,10},{9,7},{10,12},{11... | collective-permute-start | bytes 2359304 | tf_op jit(solution)/shard_map/ppermute | solution.py:26
  175.7 6.8 %shard_map.264 = (bf16[256,1536]{1,0:T(8,128)(2,1)}, f32[256,1536]{1,0:T(8,128)}, f32[256,1536]{1,0:T(8,128)}) custom-call(bf16[256,1536]{1,0:T(8,128)(2,1)} %collective-permute-done.5.q_ref, bf16[272,1536]{1,0:T(8,128)(2,1)} %collective-permute-done.6.g_ref, bf16[256,1536]{1,0:T(8,128)(2,1)} %k_ref.5, bf16[256,1536]{1,0:T(8,128)(2,1)} %v_ref.5, ...), custom_call_target="tpu_custom_call" | custom-call | flops 1006632960 | bytes 9437184 | tf_op jit(solution)/shard_map/pallas_call | solution.py:165
  182.6 2.8 %collective-permute-start.15 = (bf16[256,1536]{1,0:T(8,128)(2,1)}, bf16[256,1536]{1,0:T(8,128)(2,1)S(1)}, u32[]{:S(2)}, u32[]{:S(2)}) collective-permute-start(bf16[256,1536]{1,0:T(8,128)(2,1)} %get-tuple-element.26), channel_id=1, source_target_pairs={{1,3},{2,0},{3,5},{4,2},{5,7},{6,4},{7,9},{8,6},{9,11},{10,8},{11,... | collective-permute-start | bytes 2359304 | tf_op jit(solution)/shard_map/ppermute | solution.py:26
  185.4 3.6 %add_convert_fusion.1 = bf16[256,1536]{1,0:T(8,128)(2,1)} fusion(f32[256,1536]{1,0:T(8,128)} %collective-permute-done.17, bf16[512,1536]{1,0:T(8,128)(2,1)S(1)} %convert.25, bf16[512,1536]{1,0:T(8,128)(2,1)} %copy-done.5, f32[256,1536]{1,0:T(8,128)} %get-tuple-element.32), kind=kLoop, calls=%fused_computation.1 | loop fusion | flops 3145728 | bytes 5505024 | tf_op jit(solution)/shard_map/convert_element_type | solution.py:268
  189.0 2.8 %add_convert_fusion.2 = bf16[256,1536]{1,0:T(8,128)(2,1)} fusion(f32[256,1536]{1,0:T(8,128)} %collective-permute-done.16, bf16[512,1536]{1,0:T(8,128)(2,1)S(1)} %convert.23, bf16[512,1536]{1,0:T(8,128)(2,1)S(1)} %copy-done.4, f32[256,1536]{1,0:T(8,128)S(1)} %copy-done.9), kind=kLoop, calls=%fused_computation.3 | loop fusion | flops 3145728 | bytes 5505024 | tf_op jit(solution)/shard_map/convert_element_type | solution.py:267
  191.9 18.4 %collective-permute-done.14 = bf16[256,1536]{1,0:T(8,128)(2,1)} collective-permute-done((bf16[256,1536]{1,0:T(8,128)(2,1)}, bf16[256,1536]{1,0:T(8,128)(2,1)}, u32[]{:S(2)}, u32[]{:S(2)}) %collective-permute-start.14) | collective-permute-done | bytes 786464 | tf_op jit(solution)/shard_map/ppermute | solution.py:26
  210.2 0.8 collective-permute-done.15
  211.0 2.4 %add_convert_fusion = bf16[256,1536]{1,0:T(8,128)(2,1)} fusion(bf16[256,1536]{1,0:T(8,128)(2,1)S(1)} %collective-permute-done.15, f32[256,1536]{1,0:T(8,128)S(1)} %copy-done.8, bf16[256,1536]{1,0:T(8,128)(2,1)} %collective-permute-done.14), kind=kLoop, calls=%fused_computation | loop fusion | flops 1966080 | bytes 3932160 | tf_op jit(solution)/shard_map/convert_element_type | solution.py:273
  (76 shorter events, 0.7 us)
Async XLA Ops:
  0.6 13.0 %copy-start.2 = (bf16[256,1536]{1,0:T(8,128)(2,1)S(1)}, bf16[256,1536]{1,0:T(8,128)(2,1)}, u32[]{:S(2)}) copy-start(bf16[256,1536]{1,0:T(8,128)(2,1)} %k_ref.5) | copy-start | bytes 2359300
  0.6 78.1 %collective-permute-start.5 = (bf16[256,1536]{1,0:T(8,128)(2,1)}, bf16[256,1536]{1,0:T(8,128)(2,1)}, u32[]{:S(2)}, u32[]{:S(2)}) collective-permute-start(bf16[256,1536]{1,0:T(8,128)(2,1)} %q_ref.5), channel_id=1, source_target_pairs={{0,2},{2,4},{3,1},{4,6},{5,3},{6,8},{7,5},{8,10},{9,7},{10,12},{11... | collective-permute-start | bytes 2359304 | tf_op jit(solution)/shard_map/ppermute | solution.py:26
  4.2 85.9 %collective-permute-start.2 = (bf16[256,1536]{1,0:T(8,128)(2,1)}, bf16[256,1536]{1,0:T(8,128)(2,1)}, u32[]{:S(2)}, u32[]{:S(2)}) collective-permute-start(bf16[256,1536]{1,0:T(8,128)(2,1)} %q_ref.5), channel_id=1, source_target_pairs={{1,3},{2,0},{3,5},{4,2},{5,7},{6,4},{7,9},{8,6},{9,11},{10,8},{11,... | collective-permute-start | bytes 2359304 | tf_op jit(solution)/shard_map/ppermute | solution.py:26
  7.5 9.3 %collective-permute-start = (bf16[256,1536]{1,0:T(8,128)(2,1)}, bf16[256,1536]{1,0:T(8,128)(2,1)}, u32[]{:S(2)}, u32[]{:S(2)}) collective-permute-start(bf16[256,1536]{1,0:T(8,128)(2,1)} %k_ref.5), channel_id=1, source_target_pairs={{0,1},{1,0},{2,3},{3,2},{4,5},{5,4},{6,7},{7,6},{8,9},{9,8},{10,11... | collective-permute-start | bytes 2359304 | tf_op jit(solution)/shard_map/ppermute | solution.py:26
  7.6 14.7 %collective-permute-start.1 = (bf16[256,1536]{1,0:T(8,128)(2,1)}, bf16[256,1536]{1,0:T(8,128)(2,1)}, u32[]{:S(2)}, u32[]{:S(2)}) collective-permute-start(bf16[256,1536]{1,0:T(8,128)(2,1)} %v_ref.5), channel_id=1, source_target_pairs={{0,1},{1,0},{2,3},{3,2},{4,5},{5,4},{6,7},{7,6},{8,9},{9,8},{10,11... | collective-permute-start | bytes 2359304 | tf_op jit(solution)/shard_map/ppermute | solution.py:26
  8.9 4.8 %copy-start.16 = (bf16[4,30,4]{1,2,0:T(4,128)(2,1)S(1)}, bf16[4,30,4]{1,2,0:T(4,128)(2,1)}, u32[]{:S(2)}) copy-start(bf16[4,30,4]{1,2,0:T(4,128)(2,1)} %constant.123) | copy-start | bytes 2884
  8.9 4.8 %copy-start.17 = (bf16[4,30,4]{1,2,0:T(4,128)(2,1)S(1)}, bf16[4,30,4]{1,2,0:T(4,128)(2,1)}, u32[]{:S(2)}) copy-start(bf16[4,30,4]{1,2,0:T(4,128)(2,1)} %constant.124) | copy-start | bytes 2884
  8.9 4.8 %copy-start.18 = (bf16[4,30,4]{1,2,0:T(4,128)(2,1)S(1)}, bf16[4,30,4]{1,2,0:T(4,128)(2,1)}, u32[]{:S(2)}) copy-start(bf16[4,30,4]{1,2,0:T(4,128)(2,1)} %constant.122) | copy-start | bytes 2884
  8.9 4.8 %copy-start.19 = (bf16[4,30,4]{1,2,0:T(4,128)(2,1)S(1)}, bf16[4,30,4]{1,2,0:T(4,128)(2,1)}, u32[]{:S(2)}) copy-start(bf16[4,30,4]{1,2,0:T(4,128)(2,1)} %constant.121) | copy-start | bytes 2884
  8.9 4.8 %copy-start.15 = (s32[4,30]{1,0:T(4,128)S(1)}, s32[4,30]{1,0:T(4,128)}, u32[]{:S(2)}) copy-start(s32[4,30]{1,0:T(4,128)} %param.29) | copy-start | bytes 1444
  9.0 4.8 %copy-start.23 = (bf16[4,30,4]{1,2,0:T(4,128)(2,1)S(1)}, bf16[4,30,4]{1,2,0:T(4,128)(2,1)}, u32[]{:S(2)}) copy-start(bf16[4,30,4]{1,2,0:T(4,128)(2,1)} %constant.125) | copy-start | bytes 2884
  9.0 5.1 %copy-start.20 = (pred[4,8]{0,1:T(8,128)(4,1)S(1)}, pred[4,8]{0,1:T(8,128)(4,1)}, u32[]{:S(2)}) copy-start(pred[4,8]{0,1:T(8,128)(4,1)} %constant.62) | copy-start | bytes 100
  11.1 63.7 %collective-permute-start.6 = (bf16[272,1536]{1,0:T(8,128)(2,1)}, bf16[272,1536]{1,0:T(8,128)(2,1)}, u32[]{:S(2)}, u32[]{:S(2)}) collective-permute-start(bf16[272,1536]{1,0:T(8,128)(2,1)} %pad_maximum_fusion), channel_id=1, source_target_pairs={{0,2},{2,4},{3,1},{4,6},{5,3},{6,8},{7,5},{8,10},{9,7},{10,12},{11... | collective-permute-start | bytes 2506760 | tf_op jit(solution)/shard_map/ppermute | solution.py:26
  16.9 70.6 %collective-permute-start.3 = (bf16[272,1536]{1,0:T(8,128)(2,1)}, bf16[272,1536]{1,0:T(8,128)(2,1)}, u32[]{:S(2)}, u32[]{:S(2)}) collective-permute-start(bf16[272,1536]{1,0:T(8,128)(2,1)} %pad_maximum_fusion), channel_id=1, source_target_pairs={{1,3},{2,0},{3,5},{4,2},{5,7},{6,4},{7,9},{8,6},{9,11},{10,8},{11,... | collective-permute-start | bytes 2506760 | tf_op jit(solution)/shard_map/ppermute | solution.py:26
  22.3 60.8 %copy-start = (bf16[512,1536]{1,0:T(8,128)(2,1)}, bf16[512,1536]{1,0:T(8,128)(2,1)S(1)}, u32[]{:S(2)}) copy-start(bf16[512,1536]{1,0:T(8,128)(2,1)S(1)} %constant_dynamic-update-slice_fusion.k_ref) | copy-start | bytes 4718596
  24.0 59.1 %copy-start.1 = (bf16[512,1536]{1,0:T(8,128)(2,1)}, bf16[512,1536]{1,0:T(8,128)(2,1)S(1)}, u32[]{:S(2)}) copy-start(bf16[512,1536]{1,0:T(8,128)(2,1)S(1)} %constant_dynamic-update-slice_fusion.2.v_ref) | copy-start | bytes 4718596
  83.1 20.3 %collective-permute-start.7 = (f32[12,2,256]{2,1,0:T(2,128)}, f32[12,2,256]{2,1,0:T(2,128)S(1)}, u32[]{:S(2)}, u32[]{:S(2)}) collective-permute-start(f32[12,2,256]{2,1,0:T(2,128)} %shard_map.258), channel_id=1, source_target_pairs={{1,3},{2,0},{3,5},{4,2},{5,7},{6,4},{7,9},{8,6},{9,11},{10,8},{11,... | collective-permute-start | bytes 73736 | tf_op jit(solution)/shard_map/ppermute | solution.py:26
  95.7 7.7 %collective-permute-start.4 = (f32[12,2,256]{2,1,0:T(2,128)}, f32[12,2,256]{2,1,0:T(2,128)S(1)}, u32[]{:S(2)}, u32[]{:S(2)}) collective-permute-start(f32[12,2,256]{2,1,0:T(2,128)} %shard_map.257), channel_id=1, source_target_pairs={{0,2},{2,4},{3,1},{4,6},{5,3},{6,8},{7,5},{8,10},{9,7},{10,12},{11... | collective-permute-start | bytes 73736 | tf_op jit(solution)/shard_map/ppermute | solution.py:26
  104.4 12.2 %copy-start.10 = (f32[12,1,256]{2,1,0:T(1,128)}, f32[12,1,256]{2,1,0:T(1,128)S(1)}, u32[]{:S(2)}) copy-start(f32[12,1,256]{2,1,0:T(1,128)S(1)} %reshape_add_fusion.f_ref) | copy-start | bytes 36868
  104.5 6.8 %collective-permute-start.10 = (f32[12,1,256]{2,1,0:T(1,128)S(1)}, f32[12,1,256]{2,1,0:T(1,128)S(1)}, u32[]{:S(2)}, u32[]{:S(2)}) collective-permute-start(f32[12,1,256]{2,1,0:T(1,128)S(1)} %reshape_add_fusion.f_ref), channel_id=1, source_target_pairs={{0,2},{2,4},{3,1},{4,6},{5,3},{6,8},{7,5},{8,10},{9,7},{10,12},{11... | collective-permute-start | bytes 36872 | tf_op jit(solution)/shard_map/ppermute | solution.py:26
  109.3 11.2 %collective-permute-start.8 = (f32[12,1,256]{2,1,0:T(1,128)S(1)}, f32[12,1,256]{2,1,0:T(1,128)S(1)}, u32[]{:S(2)}, u32[]{:S(2)}) collective-permute-start(f32[12,1,256]{2,1,0:T(1,128)S(1)} %reshape_add_fusion.f_ref), channel_id=1, source_target_pairs={{1,3},{2,0},{3,5},{4,2},{5,7},{6,4},{7,9},{8,6},{9,11},{10,8},{11,... | collective-permute-start | bytes 36872 | tf_op jit(solution)/shard_map/ppermute | solution.py:26
  111.2 0.6 copy-start.13
  116.6 19.4 %collective-permute-start.11 = (f32[12,1,256]{2,1,0:T(1,128)}, f32[12,1,256]{2,1,0:T(1,128)S(1)}, u32[]{:S(2)}, u32[]{:S(2)}) collective-permute-start(f32[12,1,256]{2,1,0:T(1,128)} %shard_map.261), channel_id=1, source_target_pairs={{1,3},{2,0},{3,5},{4,2},{5,7},{6,4},{7,9},{8,6},{9,11},{10,8},{11,... | collective-permute-start | bytes 36872 | tf_op jit(solution)/shard_map/ppermute | solution.py:26
  120.5 0.6 copy-start.14
  127.5 9.3 %copy-start.11 = (f32[12,1,256]{2,1,0:T(1,128)S(1)}, f32[12,1,256]{2,1,0:T(1,128)}, u32[]{:S(2)}) copy-start(f32[12,1,256]{2,1,0:T(1,128)} %copy-done.10) | copy-start | bytes 36868
  127.5 8.6 %collective-permute-start.9 = (f32[12,1,256]{2,1,0:T(1,128)}, f32[12,1,256]{2,1,0:T(1,128)S(1)}, u32[]{:S(2)}, u32[]{:S(2)}) collective-permute-start(f32[12,1,256]{2,1,0:T(1,128)} %shard_map.260), channel_id=1, source_target_pairs={{0,2},{2,4},{3,1},{4,6},{5,3},{6,8},{7,5},{8,10},{9,7},{10,12},{11... | collective-permute-start | bytes 36872 | tf_op jit(solution)/shard_map/ppermute | solution.py:26
  136.8 7.0 %copy-start.12 = (f32[12,2,256]{2,1,0:T(2,128)}, f32[12,2,256]{2,1,0:T(2,128)S(1)}, u32[]{:S(2)}) copy-start(f32[12,2,256]{2,1,0:T(2,128)S(1)} %pad_maximum_fusion.1.f_ref) | copy-start | bytes 73732
  136.8 16.0 %collective-permute-start.13 = (f32[12,2,256]{2,1,0:T(2,128)S(1)}, f32[12,2,256]{2,1,0:T(2,128)S(1)}, u32[]{:S(2)}, u32[]{:S(2)}) collective-permute-start(f32[12,2,256]{2,1,0:T(2,128)S(1)} %pad_maximum_fusion.1.f_ref), channel_id=1, source_target_pairs={{0,2},{2,4},{3,1},{4,6},{5,3},{6,8},{7,5},{8,10},{9,7},{10,12},{11... | collective-permute-start | bytes 73736 | tf_op jit(solution)/shard_map/ppermute | solution.py:26
  141.7 11.2 %collective-permute-start.12 = (f32[12,2,256]{2,1,0:T(2,128)S(1)}, f32[12,2,256]{2,1,0:T(2,128)S(1)}, u32[]{:S(2)}, u32[]{:S(2)}) collective-permute-start(f32[12,2,256]{2,1,0:T(2,128)S(1)} %pad_maximum_fusion.1.f_ref), channel_id=1, source_target_pairs={{1,3},{2,0},{3,5},{4,2},{5,7},{6,4},{7,9},{8,6},{9,11},{10,8},{11,... | collective-permute-start | bytes 73736 | tf_op jit(solution)/shard_map/ppermute | solution.py:26
  152.8 2.1 copy-start.21
  152.8 2.1 copy-start.22
  165.9 1.7 copy-start.5
  165.9 3.0 %copy-start.6 = (f32[512,1536]{1,0:T(8,128)S(1)}, f32[512,1536]{1,0:T(8,128)}, u32[]{:S(2)}) copy-start(f32[512,1536]{1,0:T(8,128)} %get-tuple-element.28) | copy-start | bytes 9437188
  167.6 2.4 %copy-start.7 = (f32[512,1536]{1,0:T(8,128)S(1)}, f32[512,1536]{1,0:T(8,128)}, u32[]{:S(2)}) copy-start(f32[512,1536]{1,0:T(8,128)} %get-tuple-element.27) | copy-start | bytes 9437188
  167.6 17.8 %collective-permute-start.17 = (f32[256,1536]{1,0:T(8,128)}, f32[256,1536]{1,0:T(8,128)}, u32[]{:S(2)}, u32[]{:S(2)}) collective-permute-start(f32[256,1536]{1,0:T(8,128)} %convert_add_fusion), channel_id=1, source_target_pairs={{0,1},{1,0},{2,3},{3,2},{4,5},{5,4},{6,7},{7,6},{8,9},{9,8},{10,11... | collective-permute-start | bytes 4718600 | tf_op jit(solution)/shard_map/ppermute | solution.py:26
  170.2 1.6 copy-start.3
  171.8 17.2 %collective-permute-start.16 = (f32[256,1536]{1,0:T(8,128)}, f32[256,1536]{1,0:T(8,128)}, u32[]{:S(2)}, u32[]{:S(2)}) collective-permute-start(f32[256,1536]{1,0:T(8,128)} %convert_add_fusion.1), channel_id=1, source_target_pairs={{0,1},{1,0},{2,3},{3,2},{4,5},{5,4},{6,7},{7,6},{8,9},{9,8},{10,11... | collective-permute-start | bytes 4718600 | tf_op jit(solution)/shard_map/ppermute | solution.py:26
  171.8 38.4 %collective-permute-start.14 = (bf16[256,1536]{1,0:T(8,128)(2,1)}, bf16[256,1536]{1,0:T(8,128)(2,1)}, u32[]{:S(2)}, u32[]{:S(2)}) collective-permute-start(bf16[256,1536]{1,0:T(8,128)(2,1)} %get-tuple-element.24), channel_id=1, source_target_pairs={{0,2},{2,4},{3,1},{4,6},{5,3},{6,8},{7,5},{8,10},{9,7},{10,12},{11... | collective-permute-start | bytes 2359304 | tf_op jit(solution)/shard_map/ppermute | solution.py:26
  182.6 28.4 %collective-permute-start.15 = (bf16[256,1536]{1,0:T(8,128)(2,1)}, bf16[256,1536]{1,0:T(8,128)(2,1)S(1)}, u32[]{:S(2)}, u32[]{:S(2)}) collective-permute-start(bf16[256,1536]{1,0:T(8,128)(2,1)} %get-tuple-element.26), channel_id=1, source_target_pairs={{1,3},{2,0},{3,5},{4,2},{5,7},{6,4},{7,9},{8,6},{9,11},{10,8},{11,... | collective-permute-start | bytes 2359304 | tf_op jit(solution)/shard_map/ppermute | solution.py:26
  185.4 3.6 %copy-start.4 = (bf16[512,1536]{1,0:T(8,128)(2,1)S(1)}, bf16[512,1536]{1,0:T(8,128)(2,1)}, u32[]{:S(2)}) copy-start(bf16[512,1536]{1,0:T(8,128)(2,1)} %copy-done.3) | copy-start | bytes 4718596
  185.4 3.6 %copy-start.9 = (f32[256,1536]{1,0:T(8,128)S(1)}, f32[256,1536]{1,0:T(8,128)}, u32[]{:S(2)}) copy-start(f32[256,1536]{1,0:T(8,128)} %get-tuple-element.29) | copy-start | bytes 4718596
  189.0 22.0 %copy-start.8 = (f32[256,1536]{1,0:T(8,128)S(1)}, f32[256,1536]{1,0:T(8,128)}, u32[]{:S(2)}) copy-start(f32[256,1536]{1,0:T(8,128)} %get-tuple-element.20) | copy-start | bytes 4718596

commit v14 on v13

--- a/solution.py
+++ b/solution.py
@@ -211,7 +211,14 @@
 
     args = {}
     stats_out = {}
-    for name, (q_arr, g_arr, q_rows, g_rows, rows, q_off, both, offs_e, offs_o) in slots.items():
+    for name in ("own", "far", "near"):
+        if name == "far":
+            fq, fg, nq, ng, stats_out["own"] = lax.optimization_barrier(
+                (far_q_data, far_data, near_q_data, near_data, stats_out["own"])
+            )
+            slots["far"] = (fq, fg) + slots["far"][2:]
+            slots["near"] = (nq, ng) + slots["near"][2:]
+        q_arr, g_arr, q_rows, g_rows, rows, q_off, both, offs_e, offs_o = slots[name]
         if rows is None:
             rows = g_arr[tok, : blocks * cands].reshape(blocks, cands)
         key_arr, value_arr = (key_both, value_both) if both else (keys, values)

time: 216 us -> 214 us (level)
    unnamed x51 -> x53, local copies, waits for them, and re-layouts: 5.11 us -> 6.17 us
  transfers between devices with their start and end apart: 18 -> 18, of which waited for: 3 -> 6; matrix products, arithmetic and copies ran while one was open for 11% -> 8% of each run, Pallas kernels for 23% -> 21%
where the time goes in v14:
time: 214 us; the launch traced here: 212 us
  waiting for transfers between devices  70.8 us (33%)
  Pallas kernels  57.8 us (27%)
  starting transfers between devices  46.5 us (22%)
  other arithmetic  21.4 us (10%)
  local copies, waits for them, and re-layouts  14.1 us (7%)
    ppermute x18, waiting for transfers between devices, permute(): return lax.ppermute(value, 'tm', pairs)  70.8 us
    ppermute x18, starting transfers between devices, permute(): return lax.ppermute(value, 'tm', pairs)  46.5 us
    pallas_call x3, Pallas kernels, slot_back(): pl.pallas_call(back_kernel, grid=(HEADS // STEP_HEADS,), in_specs=slot_sp...  24.6 us
    pallas_call x3, Pallas kernels, slot_delta(): pl.pallas_call(delta_kernel, grid=(HEADS // STEP_HEADS,), in_specs=slot_s...  17.6 us
    pallas_call x3, Pallas kernels, slot_stats(): pl.pallas_call(stats_kernel, grid=(HEADS // STEP_HEADS,), in_specs=slot_s...  15.6 us
    unnamed x53, local copies, waits for them, and re-layouts  6.17 us
    another operation x4, other arithmetic  4.49 us
  transfers between devices with their start and end apart: 18, of which 6 were waited for; matrix products, arithmetic and copies ran while one was open for 8% of the time, Pallas kernels for 21%

profile of v14, /device:TPU:8, one launch (start us, length us, event | category | flops | bytes accessed | tf_op | source)
XLA Modules:
  0.0 212.3 jit_solution(6926989637394521415)
XLA Ops:
  0.7 0.8 broadcast_compare_fusion
  1.5 0.1 reshape.137
  1.6 2.1 pad_maximum_fusion
  3.7 3.4 %collective-permute-start.5 = (bf16[272,1536]{1,0:T(8,128)(2,1)}, bf16[272,1536]{1,0:T(8,128)(2,1)}, u32[]{:S(2)}, u32[]{:S(2)}) collective-permute-start(bf16[272,1536]{1,0:T(8,128)(2,1)} %pad_maximum_fusion), channel_id=1, source_target_pairs={{0,2},{2,4},{3,1},{4,6},{5,3},{6,8},{7,5},{8,10},{9,7},{10,12},{11... | collective-permute-start | bytes 2506760 | tf_op jit(solution)/shard_map/ppermute | solution.py:26
  7.1 3.3 %collective-permute-start.3 = (bf16[272,1536]{1,0:T(8,128)(2,1)}, bf16[272,1536]{1,0:T(8,128)(2,1)}, u32[]{:S(2)}, u32[]{:S(2)}) collective-permute-start(bf16[272,1536]{1,0:T(8,128)(2,1)} %pad_maximum_fusion), channel_id=1, source_target_pairs={{1,3},{2,0},{3,5},{4,2},{5,7},{6,4},{7,9},{8,6},{9,11},{10,8},{11,... | collective-permute-start | bytes 2506760 | tf_op jit(solution)/shard_map/ppermute | solution.py:26
  10.4 2.5 %collective-permute-start.4 = (bf16[256,1536]{1,0:T(8,128)(2,1)}, bf16[256,1536]{1,0:T(8,128)(2,1)}, u32[]{:S(2)}, u32[]{:S(2)}) collective-permute-start(bf16[256,1536]{1,0:T(8,128)(2,1)} %q_ref.5), channel_id=1, source_target_pairs={{0,2},{2,4},{3,1},{4,6},{5,3},{6,8},{7,5},{8,10},{9,7},{10,12},{11... | collective-permute-start | bytes 2359304 | tf_op jit(solution)/shard_map/ppermute | solution.py:26
  13.1 0.5 collective-permute-start.1
  13.7 0.1 fusion.2
  13.9 0.2 broadcast_in_dim.31
  14.1 1.4 convert_element_type.88.m_ref
  15.6 0.2 collective-permute-done
  15.8 4.2 %collective-permute-start.2 = (bf16[256,1536]{1,0:T(8,128)(2,1)}, bf16[256,1536]{1,0:T(8,128)(2,1)}, u32[]{:S(2)}, u32[]{:S(2)}) collective-permute-start(bf16[256,1536]{1,0:T(8,128)(2,1)} %q_ref.5), channel_id=1, source_target_pairs={{1,3},{2,0},{3,5},{4,2},{5,7},{6,4},{7,9},{8,6},{9,11},{10,8},{11,... | collective-permute-start | bytes 2359304 | tf_op jit(solution)/shard_map/ppermute | solution.py:26
  20.0 1.2 constant_dynamic-update-slice_fusion.3
  21.2 1.2 constant_dynamic-update-slice_fusion.k_ref
  22.4 1.8 constant_dynamic-update-slice_fusion.2.v_ref
  24.2 1.1 copy-done.1
  25.3 5.6 %shard_map.256 = f32[12,2,256]{2,1,0:T(2,128)} custom-call(bf16[256,1536]{1,0:T(8,128)(2,1)} %q_ref.5, bf16[256,1536]{1,0:T(8,128)(2,1)} %g_ref.5, bf16[512,1536]{1,0:T(8,128)(2,1)} %copy-done, bf16[512,1536]{1,0:T(8,128)(2,1)} %copy-done.1, f32[512,256]{1,0:T(8,128)} %convert_element_type.88.m_ref), custom_call_target="tpu_custom_call" | custom-call | flops 805306368 | bytes 4718592 | tf_op jit(solution)/shard_map/pallas_call | solution.py:133
  31.0 46.7 %collective-permute-done.4.q_ref = bf16[256,1536]{1,0:T(8,128)(2,1)} collective-permute-done((bf16[256,1536]{1,0:T(8,128)(2,1)}, bf16[256,1536]{1,0:T(8,128)(2,1)}, u32[]{:S(2)}, u32[]{:S(2)}) %collective-permute-start.4) | collective-permute-done | bytes 786464 | tf_op jit(solution)/shard_map/ppermute | solution.py:26
  77.7 0.2 collective-permute-done.2.q_ref
  77.9 0.6 compare_reduce_fusion.1
  78.5 0.6 compare_reduce_fusion
  79.2 0.1 fusion.13
  79.3 0.1 copy.33
  79.5 0.1 fusion.6
  79.7 0.1 broadcast_in_dim.34
  79.9 1.1 convert_element_type.94.m_ref
  80.9 4.3 %shard_map.258 = f32[12,2,256]{2,1,0:T(2,128)} custom-call(bf16[256,1536]{1,0:T(8,128)(2,1)} %collective-permute-done.4.q_ref, bf16[272,1536]{1,0:T(8,128)(2,1)} %collective-permute-done.5.g_ref, bf16[256,1536]{1,0:T(8,128)(2,1)} %k_ref.5, bf16[256,1536]{1,0:T(8,128)(2,1)} %v_ref.5, f32[256,256]{1,0:T(8,128)} %convert_element_type.94.m_ref), custom_call_target="tpu_custom_call" | custom-call | flops 402653184 | bytes 3145728 | tf_op jit(solution)/shard_map/pallas_call | solution.py:133
  85.3 4.1 %collective-permute-start.7 = (f32[12,2,256]{2,1,0:T(2,128)}, f32[12,2,256]{2,1,0:T(2,128)S(1)}, u32[]{:S(2)}, u32[]{:S(2)}) collective-permute-start(f32[12,2,256]{2,1,0:T(2,128)} %shard_map.258), channel_id=1, source_target_pairs={{1,3},{2,0},{3,5},{4,2},{5,7},{6,4},{7,9},{8,6},{9,11},{10,8},{11,... | collective-permute-start | bytes 73736 | tf_op jit(solution)/shard_map/ppermute | solution.py:26
  89.5 0.2 broadcast_in_dim.33
  89.7 1.4 convert_element_type.91.m_ref
  91.1 5.6 %shard_map.257 = f32[12,2,256]{2,1,0:T(2,128)} custom-call(bf16[256,1536]{1,0:T(8,128)(2,1)} %collective-permute-done.2.q_ref, bf16[272,1536]{1,0:T(8,128)(2,1)} %collective-permute-done.3.g_ref, bf16[512,1536]{1,0:T(8,128)(2,1)} %copy-done, bf16[512,1536]{1,0:T(8,128)(2,1)} %copy-done.1, f32[512,256]{1,0:T(8,128)} %convert_element_type.91.m_ref), custom_call_target="tpu_custom_call" | custom-call | flops 805306368 | bytes 4718592 | tf_op jit(solution)/shard_map/pallas_call | solution.py:133
  96.7 2.0 collective-permute-start.6
  98.8 4.8 %collective-permute-done.6 = f32[12,2,256]{2,1,0:T(2,128)S(1)} collective-permute-done((f32[12,2,256]{2,1,0:T(2,128)}, f32[12,2,256]{2,1,0:T(2,128)S(1)}, u32[]{:S(2)}, u32[]{:S(2)}) %collective-permute-start.6) | collective-permute-done | bytes 24608 | tf_op jit(solution)/shard_map/ppermute | solution.py:26
  103.7 0.1 fusion
  103.8 1.9 collective-permute-start.10
  105.8 4.8 %collective-permute-start.8 = (f32[12,1,256]{2,1,0:T(1,128)S(1)}, f32[12,1,256]{2,1,0:T(1,128)S(1)}, u32[]{:S(2)}, u32[]{:S(2)}) collective-permute-start(f32[12,1,256]{2,1,0:T(1,128)S(1)} %reshape_add_fusion.f_ref), channel_id=1, source_target_pairs={{1,3},{2,0},{3,5},{4,2},{5,7},{6,4},{7,9},{8,6},{9,11},{10,8},{11,... | collective-permute-start | bytes 36872 | tf_op jit(solution)/shard_map/ppermute | solution.py:26
  110.6 0.6 copy-done.14
  111.2 4.8 %shard_map.261 = f32[12,1,256]{2,1,0:T(1,128)} custom-call(bf16[256,1536]{1,0:T(8,128)(2,1)} %collective-permute-done.4.q_ref, bf16[272,1536]{1,0:T(8,128)(2,1)} %collective-permute-done.5.g_ref, bf16[256,1536]{1,0:T(8,128)(2,1)} %k_ref.5, bf16[256,1536]{1,0:T(8,128)(2,1)} %v_ref.5, f32[256,256]{1,0:T(8,128)} %convert_element_type.94.m_ref, ...), custom_call_target="tpu_custom_call" | custom-call | flops 402653184 | bytes 3145728 | tf_op jit(solution)/shard_map/pallas_call | solution.py:148
  116.0 1.9 collective-permute-start.11
  117.9 0.6 copy-done.15
  118.5 6.4 %shard_map.260 = f32[12,1,256]{2,1,0:T(1,128)} custom-call(bf16[256,1536]{1,0:T(8,128)(2,1)} %collective-permute-done.2.q_ref, bf16[272,1536]{1,0:T(8,128)(2,1)} %collective-permute-done.3.g_ref, bf16[512,1536]{1,0:T(8,128)(2,1)} %copy-done, bf16[512,1536]{1,0:T(8,128)(2,1)} %copy-done.1, f32[512,256]{1,0:T(8,128)} %convert_element_type.91.m_ref, ...), custom_call_target="tpu_custom_call" | custom-call | flops 805306368 | bytes 4718592 | tf_op jit(solution)/shard_map/pallas_call | solution.py:148
  124.9 4.0 %collective-permute-start.9 = (f32[12,1,256]{2,1,0:T(1,128)}, f32[12,1,256]{2,1,0:T(1,128)S(1)}, u32[]{:S(2)}, u32[]{:S(2)}) collective-permute-start(f32[12,1,256]{2,1,0:T(1,128)} %shard_map.260), channel_id=1, source_target_pairs={{0,2},{2,4},{3,1},{4,6},{5,3},{6,8},{7,5},{8,10},{9,7},{10,12},{11... | collective-permute-start | bytes 36872 | tf_op jit(solution)/shard_map/ppermute | solution.py:26
  129.0 6.4 %shard_map.259 = f32[12,1,256]{2,1,0:T(1,128)} custom-call(bf16[256,1536]{1,0:T(8,128)(2,1)} %q_ref.5, bf16[256,1536]{1,0:T(8,128)(2,1)} %g_ref.5, bf16[512,1536]{1,0:T(8,128)(2,1)} %copy-done, bf16[512,1536]{1,0:T(8,128)(2,1)} %copy-done.1, f32[512,256]{1,0:T(8,128)} %convert_element_type.88.m_ref, f32[12,1,256]{2,1,0:T(1,128)} %copy-done.10), custom_call_target="tpu_custom_call" | custom-call | flops 805306368 | bytes 4718592 | tf_op jit(solution)/shard_map/pallas_call | solution.py:148
  135.4 0.7 add_add_fusion
  136.2 2.9 %collective-permute-start.13 = (f32[12,2,256]{2,1,0:T(2,128)S(1)}, f32[12,2,256]{2,1,0:T(2,128)S(1)}, u32[]{:S(2)}, u32[]{:S(2)}) collective-permute-start(f32[12,2,256]{2,1,0:T(2,128)S(1)} %pad_maximum_fusion.1.f_ref), channel_id=1, source_target_pairs={{0,2},{2,4},{3,1},{4,6},{5,3},{6,8},{7,5},{8,10},{9,7},{10,12},{11... | collective-permute-start | bytes 73736 | tf_op jit(solution)/shard_map/ppermute | solution.py:26
  139.1 4.0 %collective-permute-start.12 = (f32[12,2,256]{2,1,0:T(2,128)S(1)}, f32[12,2,256]{2,1,0:T(2,128)S(1)}, u32[]{:S(2)}, u32[]{:S(2)}) collective-permute-start(f32[12,2,256]{2,1,0:T(2,128)S(1)} %pad_maximum_fusion.1.f_ref), channel_id=1, source_target_pairs={{1,3},{2,0},{3,5},{4,2},{5,7},{6,4},{7,9},{8,6},{9,11},{10,8},{11,... | collective-permute-start | bytes 73736 | tf_op jit(solution)/shard_map/ppermute | solution.py:26
  143.1 9.0 %shard_map.262 = (f32[256,1536]{1,0:T(8,128)}, f32[512,1536]{1,0:T(8,128)}, f32[512,1536]{1,0:T(8,128)}) custom-call(bf16[256,1536]{1,0:T(8,128)(2,1)} %q_ref.5, bf16[256,1536]{1,0:T(8,128)(2,1)} %g_ref.5, bf16[512,1536]{1,0:T(8,128)(2,1)} %copy-done, bf16[512,1536]{1,0:T(8,128)(2,1)} %copy-done.1, f32[512,256]{1,0:T(8,128)} %convert_element_type.88.m_ref, ...), custom_call_target="tpu_custom_call" | custom-call | flops 2013265920 | bytes 14155776 | tf_op jit(solution)/shard_map/pallas_call | solution.py:165
  152.1 2.1 convert.25
  154.2 8.8 %shard_map.263 = (bf16[256,1536]{1,0:T(8,128)(2,1)}, f32[512,1536]{1,0:T(8,128)}, f32[512,1536]{1,0:T(8,128)}) custom-call(bf16[256,1536]{1,0:T(8,128)(2,1)} %collective-permute-done.2.q_ref, bf16[272,1536]{1,0:T(8,128)(2,1)} %collective-permute-done.3.g_ref, bf16[512,1536]{1,0:T(8,128)(2,1)} %copy-done, bf16[512,1536]{1,0:T(8,128)(2,1)} %copy-done.1, ...), custom_call_target="tpu_custom_call" | custom-call | flops 2013265920 | bytes 14155776 | tf_op jit(solution)/shard_map/pallas_call | solution.py:165
  163.1 2.1 convert.24
  165.1 1.4 convert_add_fusion
  166.5 1.6 copy-done.6
  168.2 0.2 convert.23
  168.3 0.8 copy-done.7
  169.2 0.2 convert.22
  169.4 1.6 convert_add_fusion.1
  171.0 2.0 collective-permute-start.14
  173.0 6.8 %shard_map.264 = (bf16[256,1536]{1,0:T(8,128)(2,1)}, f32[256,1536]{1,0:T(8,128)}, f32[256,1536]{1,0:T(8,128)}) custom-call(bf16[256,1536]{1,0:T(8,128)(2,1)} %collective-permute-done.4.q_ref, bf16[272,1536]{1,0:T(8,128)(2,1)} %collective-permute-done.5.g_ref, bf16[256,1536]{1,0:T(8,128)(2,1)} %k_ref.5, bf16[256,1536]{1,0:T(8,128)(2,1)} %v_ref.5, ...), custom_call_target="tpu_custom_call" | custom-call | flops 1006632960 | bytes 9437184 | tf_op jit(solution)/shard_map/pallas_call | solution.py:165
  179.8 4.7 %collective-permute-start.15 = (bf16[256,1536]{1,0:T(8,128)(2,1)}, bf16[256,1536]{1,0:T(8,128)(2,1)S(1)}, u32[]{:S(2)}, u32[]{:S(2)}) collective-permute-start(bf16[256,1536]{1,0:T(8,128)(2,1)} %get-tuple-element.36), channel_id=1, source_target_pairs={{1,3},{2,0},{3,5},{4,2},{5,7},{6,4},{7,9},{8,6},{9,11},{10,8},{11,... | collective-permute-start | bytes 2359304 | tf_op jit(solution)/shard_map/ppermute | solution.py:26
  184.6 3.6 %add_convert_fusion.1 = bf16[256,1536]{1,0:T(8,128)(2,1)} fusion(f32[256,1536]{1,0:T(8,128)} %collective-permute-done.17, bf16[512,1536]{1,0:T(8,128)(2,1)S(1)} %convert.25, bf16[512,1536]{1,0:T(8,128)(2,1)} %copy-done.5, f32[256,1536]{1,0:T(8,128)} %get-tuple-element.42), kind=kLoop, calls=%fused_computation.1 | loop fusion | flops 3145728 | bytes 5505024 | tf_op jit(solution)/shard_map/convert_element_type | solution.py:275
  188.2 2.8 %add_convert_fusion.2 = bf16[256,1536]{1,0:T(8,128)(2,1)} fusion(f32[256,1536]{1,0:T(8,128)} %collective-permute-done.16, bf16[512,1536]{1,0:T(8,128)(2,1)S(1)} %convert.23, bf16[512,1536]{1,0:T(8,128)(2,1)S(1)} %copy-done.4, f32[256,1536]{1,0:T(8,128)S(1)} %copy-done.9), kind=kLoop, calls=%fused_computation.3 | loop fusion | flops 3145728 | bytes 5505024 | tf_op jit(solution)/shard_map/convert_element_type | solution.py:274
  191.0 15.5 %collective-permute-done.14 = bf16[256,1536]{1,0:T(8,128)(2,1)} collective-permute-done((bf16[256,1536]{1,0:T(8,128)(2,1)}, bf16[256,1536]{1,0:T(8,128)(2,1)}, u32[]{:S(2)}, u32[]{:S(2)}) %collective-permute-start.14) | collective-permute-done | bytes 786464 | tf_op jit(solution)/shard_map/ppermute | solution.py:26
  206.5 3.4 %collective-permute-done.15 = bf16[256,1536]{1,0:T(8,128)(2,1)S(1)} collective-permute-done((bf16[256,1536]{1,0:T(8,128)(2,1)}, bf16[256,1536]{1,0:T(8,128)(2,1)S(1)}, u32[]{:S(2)}, u32[]{:S(2)}) %collective-permute-start.15) | collective-permute-done | bytes 786464 | tf_op jit(solution)/shard_map/ppermute | solution.py:26
  209.9 2.4 %add_convert_fusion = bf16[256,1536]{1,0:T(8,128)(2,1)} fusion(bf16[256,1536]{1,0:T(8,128)(2,1)S(1)} %collective-permute-done.15, f32[256,1536]{1,0:T(8,128)S(1)} %copy-done.8, bf16[256,1536]{1,0:T(8,128)(2,1)} %collective-permute-done.14), kind=kLoop, calls=%fused_computation | loop fusion | flops 1966080 | bytes 3932160 | tf_op jit(solution)/shard_map/convert_element_type | solution.py:280
  (78 shorter events, 0.9 us)
Async XLA Ops:
  0.6 12.9 %copy-start.17 = (bf16[4,30,4]{1,2,0:T(4,128)(2,1)S(1)}, bf16[4,30,4]{1,2,0:T(4,128)(2,1)}, u32[]{:S(2)}) copy-start(bf16[4,30,4]{1,2,0:T(4,128)(2,1)} %constant.124) | copy-start | bytes 2884
  0.6 12.9 %copy-start.18 = (bf16[4,30,4]{1,2,0:T(4,128)(2,1)S(1)}, bf16[4,30,4]{1,2,0:T(4,128)(2,1)}, u32[]{:S(2)}) copy-start(bf16[4,30,4]{1,2,0:T(4,128)(2,1)} %constant.125) | copy-start | bytes 2884
  0.7 12.9 %copy-start.19 = (bf16[4,30,4]{1,2,0:T(4,128)(2,1)S(1)}, bf16[4,30,4]{1,2,0:T(4,128)(2,1)}, u32[]{:S(2)}) copy-start(bf16[4,30,4]{1,2,0:T(4,128)(2,1)} %constant.122) | copy-start | bytes 2884
  0.7 12.9 %copy-start.20 = (bf16[4,30,4]{1,2,0:T(4,128)(2,1)S(1)}, bf16[4,30,4]{1,2,0:T(4,128)(2,1)}, u32[]{:S(2)}) copy-start(bf16[4,30,4]{1,2,0:T(4,128)(2,1)} %constant.121) | copy-start | bytes 2884
  0.7 12.9 %copy-start.16 = (s32[4,30]{1,0:T(4,128)S(1)}, s32[4,30]{1,0:T(4,128)}, u32[]{:S(2)}) copy-start(s32[4,30]{1,0:T(4,128)} %param.29) | copy-start | bytes 1444
  0.7 12.3 %copy-start.2 = (bf16[256,1536]{1,0:T(8,128)(2,1)S(1)}, bf16[256,1536]{1,0:T(8,128)(2,1)}, u32[]{:S(2)}) copy-start(bf16[256,1536]{1,0:T(8,128)(2,1)} %k_ref.5) | copy-start | bytes 2359300
  1.6 12.1 %copy-start.24 = (bf16[4,30,4]{1,2,0:T(4,128)(2,1)S(1)}, bf16[4,30,4]{1,2,0:T(4,128)(2,1)}, u32[]{:S(2)}) copy-start(bf16[4,30,4]{1,2,0:T(4,128)(2,1)} %constant.123) | copy-start | bytes 2884
  1.6 12.3 %copy-start.21 = (pred[4,8]{0,1:T(8,128)(4,1)S(1)}, pred[4,8]{0,1:T(8,128)(4,1)}, u32[]{:S(2)}) copy-start(pred[4,8]{0,1:T(8,128)(4,1)} %constant.62) | copy-start | bytes 100
  3.7 74.1 %collective-permute-start.5 = (bf16[272,1536]{1,0:T(8,128)(2,1)}, bf16[272,1536]{1,0:T(8,128)(2,1)}, u32[]{:S(2)}, u32[]{:S(2)}) collective-permute-start(bf16[272,1536]{1,0:T(8,128)(2,1)} %pad_maximum_fusion), channel_id=1, source_target_pairs={{0,2},{2,4},{3,1},{4,6},{5,3},{6,8},{7,5},{8,10},{9,7},{10,12},{11... | collective-permute-start | bytes 2506760 | tf_op jit(solution)/shard_map/ppermute | solution.py:26
  7.1 70.7 %collective-permute-start.3 = (bf16[272,1536]{1,0:T(8,128)(2,1)}, bf16[272,1536]{1,0:T(8,128)(2,1)}, u32[]{:S(2)}, u32[]{:S(2)}) collective-permute-start(bf16[272,1536]{1,0:T(8,128)(2,1)} %pad_maximum_fusion), channel_id=1, source_target_pairs={{1,3},{2,0},{3,5},{4,2},{5,7},{6,4},{7,9},{8,6},{9,11},{10,8},{11,... | collective-permute-start | bytes 2506760 | tf_op jit(solution)/shard_map/ppermute | solution.py:26
  10.4 67.2 %collective-permute-start.4 = (bf16[256,1536]{1,0:T(8,128)(2,1)}, bf16[256,1536]{1,0:T(8,128)(2,1)}, u32[]{:S(2)}, u32[]{:S(2)}) collective-permute-start(bf16[256,1536]{1,0:T(8,128)(2,1)} %q_ref.5), channel_id=1, source_target_pairs={{0,2},{2,4},{3,1},{4,6},{5,3},{6,8},{7,5},{8,10},{9,7},{10,12},{11... | collective-permute-start | bytes 2359304 | tf_op jit(solution)/shard_map/ppermute | solution.py:26
  13.0 2.8 %collective-permute-start = (bf16[256,1536]{1,0:T(8,128)(2,1)S(1)}, bf16[256,1536]{1,0:T(8,128)(2,1)}, u32[]{:S(2)}, u32[]{:S(2)}) collective-permute-start(bf16[256,1536]{1,0:T(8,128)(2,1)S(1)} %copy-done.2), channel_id=1, source_target_pairs={{0,1},{1,0},{2,3},{3,2},{4,5},{5,4},{6,7},{7,6},{8,9},{9,8},{10,11... | collective-permute-start | bytes 2359304 | tf_op jit(solution)/shard_map/ppermute | solution.py:26
  13.1 9.3 %collective-permute-start.1 = (bf16[256,1536]{1,0:T(8,128)(2,1)}, bf16[256,1536]{1,0:T(8,128)(2,1)}, u32[]{:S(2)}, u32[]{:S(2)}) collective-permute-start(bf16[256,1536]{1,0:T(8,128)(2,1)} %v_ref.5), channel_id=1, source_target_pairs={{0,1},{1,0},{2,3},{3,2},{4,5},{5,4},{6,7},{7,6},{8,9},{9,8},{10,11... | collective-permute-start | bytes 2359304 | tf_op jit(solution)/shard_map/ppermute | solution.py:26
  15.8 62.0 %collective-permute-start.2 = (bf16[256,1536]{1,0:T(8,128)(2,1)}, bf16[256,1536]{1,0:T(8,128)(2,1)}, u32[]{:S(2)}, u32[]{:S(2)}) collective-permute-start(bf16[256,1536]{1,0:T(8,128)(2,1)} %q_ref.5), channel_id=1, source_target_pairs={{1,3},{2,0},{3,5},{4,2},{5,7},{6,4},{7,9},{8,6},{9,11},{10,8},{11,... | collective-permute-start | bytes 2359304 | tf_op jit(solution)/shard_map/ppermute | solution.py:26
  22.4 1.8 copy-start
  24.2 1.1 copy-start.1
  85.3 13.5 %collective-permute-start.7 = (f32[12,2,256]{2,1,0:T(2,128)}, f32[12,2,256]{2,1,0:T(2,128)S(1)}, u32[]{:S(2)}, u32[]{:S(2)}) collective-permute-start(f32[12,2,256]{2,1,0:T(2,128)} %shard_map.258), channel_id=1, source_target_pairs={{1,3},{2,0},{3,5},{4,2},{5,7},{6,4},{7,9},{8,6},{9,11},{10,8},{11,... | collective-permute-start | bytes 73736 | tf_op jit(solution)/shard_map/ppermute | solution.py:26
  91.1 12.5 %copy-start.12 = (f32[12,2,256]{2,1,0:T(2,128)S(1)}, f32[12,2,256]{2,1,0:T(2,128)}, u32[]{:S(2)}) copy-start(f32[12,2,256]{2,1,0:T(2,128)} %shard_map.256) | copy-start | bytes 73732
  96.7 6.8 %collective-permute-start.6 = (f32[12,2,256]{2,1,0:T(2,128)}, f32[12,2,256]{2,1,0:T(2,128)S(1)}, u32[]{:S(2)}, u32[]{:S(2)}) collective-permute-start(f32[12,2,256]{2,1,0:T(2,128)} %shard_map.257), channel_id=1, source_target_pairs={{0,2},{2,4},{3,1},{4,6},{5,3},{6,8},{7,5},{8,10},{9,7},{10,12},{11... | collective-permute-start | bytes 73736 | tf_op jit(solution)/shard_map/ppermute | solution.py:26
  103.8 12.2 %copy-start.10 = (f32[12,1,256]{2,1,0:T(1,128)}, f32[12,1,256]{2,1,0:T(1,128)S(1)}, u32[]{:S(2)}) copy-start(f32[12,1,256]{2,1,0:T(1,128)S(1)} %reshape_add_fusion.f_ref) | copy-start | bytes 36868
  103.8 6.8 %collective-permute-start.10 = (f32[12,1,256]{2,1,0:T(1,128)S(1)}, f32[12,1,256]{2,1,0:T(1,128)S(1)}, u32[]{:S(2)}, u32[]{:S(2)}) collective-permute-start(f32[12,1,256]{2,1,0:T(1,128)S(1)} %reshape_add_fusion.f_ref), channel_id=1, source_target_pairs={{0,2},{2,4},{3,1},{4,6},{5,3},{6,8},{7,5},{8,10},{9,7},{10,12},{11... | collective-permute-start | bytes 36872 | tf_op jit(solution)/shard_map/ppermute | solution.py:26
  105.8 12.1 %collective-permute-start.8 = (f32[12,1,256]{2,1,0:T(1,128)S(1)}, f32[12,1,256]{2,1,0:T(1,128)S(1)}, u32[]{:S(2)}, u32[]{:S(2)}) collective-permute-start(f32[12,1,256]{2,1,0:T(1,128)S(1)} %reshape_add_fusion.f_ref), channel_id=1, source_target_pairs={{1,3},{2,0},{3,5},{4,2},{5,7},{6,4},{7,9},{8,6},{9,11},{10,8},{11,... | collective-permute-start | bytes 36872 | tf_op jit(solution)/shard_map/ppermute | solution.py:26
  110.6 0.6 copy-start.14
  116.0 19.4 %collective-permute-start.11 = (f32[12,1,256]{2,1,0:T(1,128)}, f32[12,1,256]{2,1,0:T(1,128)S(1)}, u32[]{:S(2)}, u32[]{:S(2)}) collective-permute-start(f32[12,1,256]{2,1,0:T(1,128)} %shard_map.261), channel_id=1, source_target_pairs={{1,3},{2,0},{3,5},{4,2},{5,7},{6,4},{7,9},{8,6},{9,11},{10,8},{11,... | collective-permute-start | bytes 36872 | tf_op jit(solution)/shard_map/ppermute | solution.py:26
  117.9 0.6 copy-start.15
  124.9 11.2 %copy-start.11 = (f32[12,1,256]{2,1,0:T(1,128)S(1)}, f32[12,1,256]{2,1,0:T(1,128)}, u32[]{:S(2)}) copy-start(f32[12,1,256]{2,1,0:T(1,128)} %copy-done.10) | copy-start | bytes 36868
  124.9 10.5 %collective-permute-start.9 = (f32[12,1,256]{2,1,0:T(1,128)}, f32[12,1,256]{2,1,0:T(1,128)S(1)}, u32[]{:S(2)}, u32[]{:S(2)}) collective-permute-start(f32[12,1,256]{2,1,0:T(1,128)} %shard_map.260), channel_id=1, source_target_pairs={{0,2},{2,4},{3,1},{4,6},{5,3},{6,8},{7,5},{8,10},{9,7},{10,12},{11... | collective-permute-start | bytes 36872 | tf_op jit(solution)/shard_map/ppermute | solution.py:26
  136.2 7.0 %copy-start.13 = (f32[12,2,256]{2,1,0:T(2,128)}, f32[12,2,256]{2,1,0:T(2,128)S(1)}, u32[]{:S(2)}) copy-start(f32[12,2,256]{2,1,0:T(2,128)S(1)} %pad_maximum_fusion.1.f_ref) | copy-start | bytes 73732
  136.2 15.9 %collective-permute-start.13 = (f32[12,2,256]{2,1,0:T(2,128)S(1)}, f32[12,2,256]{2,1,0:T(2,128)S(1)}, u32[]{:S(2)}, u32[]{:S(2)}) collective-permute-start(f32[12,2,256]{2,1,0:T(2,128)S(1)} %pad_maximum_fusion.1.f_ref), channel_id=1, source_target_pairs={{0,2},{2,4},{3,1},{4,6},{5,3},{6,8},{7,5},{8,10},{9,7},{10,12},{11... | collective-permute-start | bytes 73736 | tf_op jit(solution)/shard_map/ppermute | solution.py:26
  139.1 13.0 %collective-permute-start.12 = (f32[12,2,256]{2,1,0:T(2,128)S(1)}, f32[12,2,256]{2,1,0:T(2,128)S(1)}, u32[]{:S(2)}, u32[]{:S(2)}) collective-permute-start(f32[12,2,256]{2,1,0:T(2,128)S(1)} %pad_maximum_fusion.1.f_ref), channel_id=1, source_target_pairs={{1,3},{2,0},{3,5},{4,2},{5,7},{6,4},{7,9},{8,6},{9,11},{10,8},{11,... | collective-permute-start | bytes 73736 | tf_op jit(solution)/shard_map/ppermute | solution.py:26
  152.1 2.1 copy-start.22
  152.1 2.1 copy-start.23
  165.1 3.2 %copy-start.5 = (bf16[512,1536]{1,0:T(8,128)(2,1)}, bf16[512,1536]{1,0:T(8,128)(2,1)S(1)}, u32[]{:S(2)}) copy-start(bf16[512,1536]{1,0:T(8,128)(2,1)S(1)} %convert.24) | copy-start | bytes 4718596
  165.1 3.0 %copy-start.6 = (f32[512,1536]{1,0:T(8,128)S(1)}, f32[512,1536]{1,0:T(8,128)}, u32[]{:S(2)}) copy-start(f32[512,1536]{1,0:T(8,128)} %get-tuple-element.38) | copy-start | bytes 9437188
  166.5 2.6 %copy-start.7 = (f32[512,1536]{1,0:T(8,128)S(1)}, f32[512,1536]{1,0:T(8,128)}, u32[]{:S(2)}) copy-start(f32[512,1536]{1,0:T(8,128)} %get-tuple-element.37) | copy-start | bytes 9437188
  166.5 18.0 %collective-permute-start.17 = (f32[256,1536]{1,0:T(8,128)}, f32[256,1536]{1,0:T(8,128)}, u32[]{:S(2)}, u32[]{:S(2)}) collective-permute-start(f32[256,1536]{1,0:T(8,128)} %convert_add_fusion), channel_id=1, source_target_pairs={{0,1},{1,0},{2,3},{3,2},{4,5},{5,4},{6,7},{7,6},{8,9},{9,8},{10,11... | collective-permute-start | bytes 4718600 | tf_op jit(solution)/shard_map/ppermute | solution.py:26
  169.4 1.6 copy-start.3
  171.0 17.2 %collective-permute-start.16 = (f32[256,1536]{1,0:T(8,128)}, f32[256,1536]{1,0:T(8,128)}, u32[]{:S(2)}, u32[]{:S(2)}) collective-permute-start(f32[256,1536]{1,0:T(8,128)} %convert_add_fusion.1), channel_id=1, source_target_pairs={{0,1},{1,0},{2,3},{3,2},{4,5},{5,4},{6,7},{7,6},{8,9},{9,8},{10,11... | collective-permute-start | bytes 4718600 | tf_op jit(solution)/shard_map/ppermute | solution.py:26
  171.0 35.5 %collective-permute-start.14 = (bf16[256,1536]{1,0:T(8,128)(2,1)}, bf16[256,1536]{1,0:T(8,128)(2,1)}, u32[]{:S(2)}, u32[]{:S(2)}) collective-permute-start(bf16[256,1536]{1,0:T(8,128)(2,1)} %get-tuple-element.34), channel_id=1, source_target_pairs={{0,2},{2,4},{3,1},{4,6},{5,3},{6,8},{7,5},{8,10},{9,7},{10,12},{11... | collective-permute-start | bytes 2359304 | tf_op jit(solution)/shard_map/ppermute | solution.py:26
  179.8 30.0 %collective-permute-start.15 = (bf16[256,1536]{1,0:T(8,128)(2,1)}, bf16[256,1536]{1,0:T(8,128)(2,1)S(1)}, u32[]{:S(2)}, u32[]{:S(2)}) collective-permute-start(bf16[256,1536]{1,0:T(8,128)(2,1)} %get-tuple-element.36), channel_id=1, source_target_pairs={{1,3},{2,0},{3,5},{4,2},{5,7},{6,4},{7,9},{8,6},{9,11},{10,8},{11,... | collective-permute-start | bytes 2359304 | tf_op jit(solution)/shard_map/ppermute | solution.py:26
  184.6 3.6 %copy-start.4 = (bf16[512,1536]{1,0:T(8,128)(2,1)S(1)}, bf16[512,1536]{1,0:T(8,128)(2,1)}, u32[]{:S(2)}) copy-start(bf16[512,1536]{1,0:T(8,128)(2,1)} %copy-done.3) | copy-start | bytes 4718596
  184.6 3.6 %copy-start.9 = (f32[256,1536]{1,0:T(8,128)S(1)}, f32[256,1536]{1,0:T(8,128)}, u32[]{:S(2)}) copy-start(f32[256,1536]{1,0:T(8,128)} %get-tuple-element.39) | copy-start | bytes 4718596
  188.2 21.7 %copy-start.8 = (f32[256,1536]{1,0:T(8,128)S(1)}, f32[256,1536]{1,0:T(8,128)}, u32[]{:S(2)}) copy-start(f32[256,1536]{1,0:T(8,128)} %get-tuple-element.30) | copy-start | bytes 4718596

commit v15 on v14

--- a/solution.py
+++ b/solution.py
@@ -77,11 +77,12 @@
     return slice(j * HDIM, (j + 1) * HDIM)
 
 
-def stats_kernel(q_ref, g_ref, k_ref, v_ref, m_ref, out_ref):
+def stats_kernel(q_ref, k_ref, m_ref, out_ref):
     m = m_ref[...] > 0
     for j in range(STEP_HEADS):
         cols = head_cols(j)
-        s, dp = slot_scores(q_ref[:, cols], g_ref[:, cols], k_ref[:, cols], v_ref[:, cols])
+        s = lax.dot_general(k_ref[:, cols], q_ref[:, cols], NT, preferred_element_type=jnp.float32)
+        s = s * SCALE
         masked = jnp.where(m, s, NEG)
         mx = jnp.max(masked, axis=0, keepdims=True)
         e = jnp.where(m, jnp.exp(masked - mx), 0.0)
@@ -129,17 +130,17 @@
 
 def slot_stats(q_arr, g_arr, q_rows, g_rows, key_arr, value_arr, mask_t, tok):
     nk = key_arr.shape[0]
-    flops = 4 * tok * nk * HDIM * HEADS
+    flops = 2 * tok * nk * HDIM * HEADS
     return pl.pallas_call(
         stats_kernel,
         grid=(HEADS // STEP_HEADS,),
-        in_specs=slot_specs(q_rows, g_rows, nk, tok),
+        in_specs=[slot_specs(q_rows, g_rows, nk, tok)[i] for i in (0, 2, 4)],
         out_specs=pl.BlockSpec((STEP_HEADS, 2, tok), lambda h: (h, 0, 0)),
         out_shape=jax.ShapeDtypeStruct((HEADS, 2, tok), jnp.float32),
         cost_estimate=pl.CostEstimate(
             flops=flops, transcendentals=tok * nk * HEADS, bytes_accessed=4 * (tok + nk) * HDIM * HEADS
         ),
-    )(q_arr, g_arr, key_arr, value_arr, mask_t)
+    )(q_arr, key_arr, mask_t)
 
 
 def slot_delta(q_arr, g_arr, q_rows, g_rows, key_arr, value_arr, mask_t, lse, tok):

time: 214 us -> 211 us (0.986)
    unnamed x53 -> x57, local copies, waits for them, and re-layouts: 6.17 us -> 5.09 us
  transfers between devices with their start and end apart: 18 -> 18, of which waited for: 6 -> 8; matrix products, arithmetic and copies ran while one was open for 8% -> 10% of each run, Pallas kernels for 21% -> 23%
where the time goes in v15:
time: 211 us; the launch traced here: 210 us
  waiting for transfers between devices  71.8 us (34%)
  Pallas kernels  56.4 us (27%)
  starting transfers between devices  46.3 us (22%)
  other arithmetic  21.4 us (10%)
  local copies, waits for them, and re-layouts  12.4 us (6%)
    ppermute x18, waiting for transfers between devices, permute(): return lax.ppermute(value, 'tm', pairs)  71.8 us
    ppermute x18, starting transfers between devices, permute(): return lax.ppermute(value, 'tm', pairs)  46.3 us
    pallas_call x3, Pallas kernels, slot_back(): pl.pallas_call(back_kernel, grid=(HEADS // STEP_HEADS,), in_specs=slot_sp...  24.8 us
    pallas_call x3, Pallas kernels, slot_delta(): pl.pallas_call(delta_kernel, grid=(HEADS // STEP_HEADS,), in_specs=slot_s...  17.6 us
    pallas_call x3, Pallas kernels, slot_stats(): pl.pallas_call(stats_kernel, grid=(HEADS // STEP_HEADS,), in_specs=[slot_...  14 us
    unnamed x57, local copies, waits for them, and re-layouts  5.09 us
    another operation x4, other arithmetic  4.49 us
  transfers between devices with their start and end apart: 18, of which 8 were waited for; matrix products, arithmetic and copies ran while one was open for 10% of the time, Pallas kernels for 23%

profile of v15, /device:TPU:8, one launch (start us, length us, event | category | flops | bytes accessed | tf_op | source)
XLA Modules:
  0.0 209.9 jit_solution(10226048075200828520)
XLA Ops:
  0.7 3.6 %collective-permute-start.4 = (bf16[256,1536]{1,0:T(8,128)(2,1)}, bf16[256,1536]{1,0:T(8,128)(2,1)S(1)}, u32[]{:S(2)}, u32[]{:S(2)}) collective-permute-start(bf16[256,1536]{1,0:T(8,128)(2,1)} %q_ref.5), channel_id=1, source_target_pairs={{0,2},{2,4},{3,1},{4,6},{5,3},{6,8},{7,5},{8,10},{9,7},{10,12},{11... | collective-permute-start | bytes 2359304 | tf_op jit(solution)/shard_map/ppermute | solution.py:26
  4.3 3.3 %collective-permute-start.2 = (bf16[256,1536]{1,0:T(8,128)(2,1)}, bf16[256,1536]{1,0:T(8,128)(2,1)}, u32[]{:S(2)}, u32[]{:S(2)}) collective-permute-start(bf16[256,1536]{1,0:T(8,128)(2,1)} %q_ref.5), channel_id=1, source_target_pairs={{1,3},{2,0},{3,5},{4,2},{5,7},{6,4},{7,9},{8,6},{9,11},{10,8},{11,... | collective-permute-start | bytes 2359304 | tf_op jit(solution)/shard_map/ppermute | solution.py:26
  7.6 0.7 broadcast_compare_fusion
  8.4 2.1 pad_maximum_fusion
  10.5 2.5 %collective-permute-start.5 = (bf16[272,1536]{1,0:T(8,128)(2,1)}, bf16[272,1536]{1,0:T(8,128)(2,1)}, u32[]{:S(2)}, u32[]{:S(2)}) collective-permute-start(bf16[272,1536]{1,0:T(8,128)(2,1)} %pad_maximum_fusion), channel_id=1, source_target_pairs={{0,2},{2,4},{3,1},{4,6},{5,3},{6,8},{7,5},{8,10},{9,7},{10,12},{11... | collective-permute-start | bytes 2506760 | tf_op jit(solution)/shard_map/ppermute | solution.py:26
  13.0 4.2 %collective-permute-start.3 = (bf16[272,1536]{1,0:T(8,128)(2,1)}, bf16[272,1536]{1,0:T(8,128)(2,1)}, u32[]{:S(2)}, u32[]{:S(2)}) collective-permute-start(bf16[272,1536]{1,0:T(8,128)(2,1)} %pad_maximum_fusion), channel_id=1, source_target_pairs={{1,3},{2,0},{3,5},{4,2},{5,7},{6,4},{7,9},{8,6},{9,11},{10,8},{11,... | collective-permute-start | bytes 2506760 | tf_op jit(solution)/shard_map/ppermute | solution.py:26
  17.4 0.1 fusion.2
  17.7 0.2 broadcast_in_dim.31
  17.9 1.4 convert_element_type.88.m_ref
  19.3 0.4 collective-permute-done
  19.7 0.1 collective-permute-start.1
  19.9 1.2 constant_dynamic-update-slice_fusion.k_ref
  21.1 1.1 copy-done.1
  22.2 5.1 %shard_map.256 = f32[12,2,256]{2,1,0:T(2,128)} custom-call(bf16[256,1536]{1,0:T(8,128)(2,1)} %q_ref.5, bf16[512,1536]{1,0:T(8,128)(2,1)} %copy-done.1, f32[512,256]{1,0:T(8,128)} %convert_element_type.88.m_ref), custom_call_target="tpu_custom_call" | custom-call | flops 402653184 | bytes 4718592 | tf_op jit(solution)/shard_map/pallas_call | solution.py:134
  27.3 29.7 %collective-permute-done.4.q_ref = bf16[256,1536]{1,0:T(8,128)(2,1)S(1)} collective-permute-done((bf16[256,1536]{1,0:T(8,128)(2,1)}, bf16[256,1536]{1,0:T(8,128)(2,1)S(1)}, u32[]{:S(2)}, u32[]{:S(2)}) %collective-permute-start.4) | collective-permute-done | bytes 786464 | tf_op jit(solution)/shard_map/ppermute | solution.py:26
  57.0 2.4 %collective-permute-done.2.q_ref = bf16[256,1536]{1,0:T(8,128)(2,1)} collective-permute-done((bf16[256,1536]{1,0:T(8,128)(2,1)}, bf16[256,1536]{1,0:T(8,128)(2,1)}, u32[]{:S(2)}, u32[]{:S(2)}) %collective-permute-start.2) | collective-permute-done | bytes 786464 | tf_op jit(solution)/shard_map/ppermute | solution.py:26
  59.3 15.5 %collective-permute-done.5.g_ref = bf16[272,1536]{1,0:T(8,128)(2,1)} collective-permute-done((bf16[272,1536]{1,0:T(8,128)(2,1)}, bf16[272,1536]{1,0:T(8,128)(2,1)}, u32[]{:S(2)}, u32[]{:S(2)}) %collective-permute-start.5) | collective-permute-done | bytes 835616 | tf_op jit(solution)/shard_map/ppermute | solution.py:26
  74.9 0.2 collective-permute-done.3.g_ref
  75.0 0.6 compare_reduce_fusion.1
  75.7 0.7 compare_reduce_fusion
  76.4 0.1 fusion.13
  76.7 0.1 fusion.6
  76.9 0.1 broadcast_in_dim.34
  77.1 1.1 convert_element_type.94.m_ref
  78.2 3.8 %shard_map.258 = f32[12,2,256]{2,1,0:T(2,128)} custom-call(bf16[256,1536]{1,0:T(8,128)(2,1)} %copy-done.8, bf16[256,1536]{1,0:T(8,128)(2,1)} %k_ref.5, f32[256,256]{1,0:T(8,128)} %convert_element_type.94.m_ref), custom_call_target="tpu_custom_call" | custom-call | flops 201326592 | bytes 3145728 | tf_op jit(solution)/shard_map/pallas_call | solution.py:134
  82.0 4.1 %collective-permute-start.7 = (f32[12,2,256]{2,1,0:T(2,128)}, f32[12,2,256]{2,1,0:T(2,128)S(1)}, u32[]{:S(2)}, u32[]{:S(2)}) collective-permute-start(f32[12,2,256]{2,1,0:T(2,128)} %shard_map.258), channel_id=1, source_target_pairs={{1,3},{2,0},{3,5},{4,2},{5,7},{6,4},{7,9},{8,6},{9,11},{10,8},{11,... | collective-permute-start | bytes 73736 | tf_op jit(solution)/shard_map/ppermute | solution.py:26
  86.2 0.2 broadcast_in_dim.33
  86.4 1.4 convert_element_type.91.m_ref
  87.8 5.1 %shard_map.257 = f32[12,2,256]{2,1,0:T(2,128)} custom-call(bf16[256,1536]{1,0:T(8,128)(2,1)} %collective-permute-done.2.q_ref, bf16[512,1536]{1,0:T(8,128)(2,1)} %copy-done.1, f32[512,256]{1,0:T(8,128)} %convert_element_type.91.m_ref), custom_call_target="tpu_custom_call" | custom-call | flops 402653184 | bytes 4718592 | tf_op jit(solution)/shard_map/pallas_call | solution.py:134
  93.0 2.0 collective-permute-start.6
  95.0 4.7 %collective-permute-done.6 = f32[12,2,256]{2,1,0:T(2,128)S(1)} collective-permute-done((f32[12,2,256]{2,1,0:T(2,128)}, f32[12,2,256]{2,1,0:T(2,128)S(1)}, u32[]{:S(2)}, u32[]{:S(2)}) %collective-permute-start.6) | collective-permute-done | bytes 24608 | tf_op jit(solution)/shard_map/ppermute | solution.py:26
  99.9 0.1 fusion
  100.0 1.9 collective-permute-start.10
  102.0 1.2 constant_dynamic-update-slice_fusion.2.v_ref
  103.2 4.8 %collective-permute-start.8 = (f32[12,1,256]{2,1,0:T(1,128)S(1)}, f32[12,1,256]{2,1,0:T(1,128)S(1)}, u32[]{:S(2)}, u32[]{:S(2)}) collective-permute-start(f32[12,1,256]{2,1,0:T(1,128)S(1)} %reshape_add_fusion.f_ref), channel_id=1, source_target_pairs={{1,3},{2,0},{3,5},{4,2},{5,7},{6,4},{7,9},{8,6},{9,11},{10,8},{11,... | collective-permute-start | bytes 36872 | tf_op jit(solution)/shard_map/ppermute | solution.py:26
  108.0 0.6 copy-done.16
  108.6 4.8 %shard_map.261 = f32[12,1,256]{2,1,0:T(1,128)} custom-call(bf16[256,1536]{1,0:T(8,128)(2,1)} %copy-done.8, bf16[272,1536]{1,0:T(8,128)(2,1)} %collective-permute-done.5.g_ref, bf16[256,1536]{1,0:T(8,128)(2,1)} %k_ref.5, bf16[256,1536]{1,0:T(8,128)(2,1)} %v_ref.3, f32[256,256]{1,0:T(8,128)} %convert_element_type.94.m_ref, f32[12,1,256]{2,1,0:T(1,128)} %copy-done.16), custom_call_target="tpu_custom_call" | custom-call | flops 402653184 | bytes 3145728 | tf_op jit(solution)/shard_map/pallas_call | solution.py:149
  113.4 1.9 collective-permute-start.11
  115.4 0.6 copy-done.17
  115.9 6.4 %shard_map.260 = f32[12,1,256]{2,1,0:T(1,128)} custom-call(bf16[256,1536]{1,0:T(8,128)(2,1)} %collective-permute-done.2.q_ref, bf16[272,1536]{1,0:T(8,128)(2,1)} %collective-permute-done.3.g_ref, bf16[512,1536]{1,0:T(8,128)(2,1)} %copy-done.1, bf16[512,1536]{1,0:T(8,128)(2,1)} %copy-done, f32[512,256]{1,0:T(8,128)} %convert_element_type.91.m_ref, ...), custom_call_target="tpu_custom_call" | custom-call | flops 805306368 | bytes 4718592 | tf_op jit(solution)/shard_map/pallas_call | solution.py:149
  122.3 4.0 %collective-permute-start.9 = (f32[12,1,256]{2,1,0:T(1,128)}, f32[12,1,256]{2,1,0:T(1,128)S(1)}, u32[]{:S(2)}, u32[]{:S(2)}) collective-permute-start(f32[12,1,256]{2,1,0:T(1,128)} %shard_map.260), channel_id=1, source_target_pairs={{0,2},{2,4},{3,1},{4,6},{5,3},{6,8},{7,5},{8,10},{9,7},{10,12},{11... | collective-permute-start | bytes 36872 | tf_op jit(solution)/shard_map/ppermute | solution.py:26
  126.4 6.4 %shard_map.259 = f32[12,1,256]{2,1,0:T(1,128)} custom-call(bf16[256,1536]{1,0:T(8,128)(2,1)} %q_ref.5, bf16[256,1536]{1,0:T(8,128)(2,1)} %g_ref.3, bf16[512,1536]{1,0:T(8,128)(2,1)} %copy-done.1, bf16[512,1536]{1,0:T(8,128)(2,1)} %copy-done, f32[512,256]{1,0:T(8,128)} %convert_element_type.88.m_ref, f32[12,1,256]{2,1,0:T(1,128)} %copy-done.12), custom_call_target="tpu_custom_call" | custom-call | flops 805306368 | bytes 4718592 | tf_op jit(solution)/shard_map/pallas_call | solution.py:149
  132.8 0.7 add_add_fusion
  133.6 2.9 %collective-permute-start.13 = (f32[12,2,256]{2,1,0:T(2,128)S(1)}, f32[12,2,256]{2,1,0:T(2,128)S(1)}, u32[]{:S(2)}, u32[]{:S(2)}) collective-permute-start(f32[12,2,256]{2,1,0:T(2,128)S(1)} %pad_maximum_fusion.1.f_ref), channel_id=1, source_target_pairs={{0,2},{2,4},{3,1},{4,6},{5,3},{6,8},{7,5},{8,10},{9,7},{10,12},{11... | collective-permute-start | bytes 73736 | tf_op jit(solution)/shard_map/ppermute | solution.py:26
  136.5 4.0 %collective-permute-start.12 = (f32[12,2,256]{2,1,0:T(2,128)S(1)}, f32[12,2,256]{2,1,0:T(2,128)S(1)}, u32[]{:S(2)}, u32[]{:S(2)}) collective-permute-start(f32[12,2,256]{2,1,0:T(2,128)S(1)} %pad_maximum_fusion.1.f_ref), channel_id=1, source_target_pairs={{1,3},{2,0},{3,5},{4,2},{5,7},{6,4},{7,9},{8,6},{9,11},{10,8},{11,... | collective-permute-start | bytes 73736 | tf_op jit(solution)/shard_map/ppermute | solution.py:26
  140.5 9.0 %shard_map.262 = (f32[256,1536]{1,0:T(8,128)}, f32[512,1536]{1,0:T(8,128)}, f32[512,1536]{1,0:T(8,128)}) custom-call(bf16[256,1536]{1,0:T(8,128)(2,1)} %q_ref.5, bf16[256,1536]{1,0:T(8,128)(2,1)} %g_ref.3, bf16[512,1536]{1,0:T(8,128)(2,1)} %copy-done.1, bf16[512,1536]{1,0:T(8,128)(2,1)} %copy-done, f32[512,256]{1,0:T(8,128)} %convert_element_type.88.m_ref, ...), custom_call_target="tpu_custom_call" | custom-call | flops 2013265920 | bytes 14155776 | tf_op jit(solution)/shard_map/pallas_call | solution.py:166
  149.6 2.1 convert.25
  151.7 8.9 %shard_map.263 = (bf16[256,1536]{1,0:T(8,128)(2,1)}, f32[512,1536]{1,0:T(8,128)}, f32[512,1536]{1,0:T(8,128)}) custom-call(bf16[256,1536]{1,0:T(8,128)(2,1)} %collective-permute-done.2.q_ref, bf16[272,1536]{1,0:T(8,128)(2,1)} %collective-permute-done.3.g_ref, bf16[512,1536]{1,0:T(8,128)(2,1)} %copy-done.1, bf16[512,1536]{1,0:T(8,128)(2,1)} %copy-done, ...), custom_call_target="tpu_custom_call" | custom-call | flops 2013265920 | bytes 14155776 | tf_op jit(solution)/shard_map/pallas_call | solution.py:166
  160.6 2.1 convert.24
  162.7 1.4 convert_add_fusion
  164.1 0.3 copy-done.5
  164.4 1.3 copy-done.6
  165.7 0.2 convert.23
  165.9 0.9 copy-done.7
  166.8 0.2 convert.22
  167.0 1.6 convert_add_fusion.1
  168.6 2.0 collective-permute-start.14
  170.6 6.8 %shard_map.264 = (bf16[256,1536]{1,0:T(8,128)(2,1)}, f32[256,1536]{1,0:T(8,128)}, f32[256,1536]{1,0:T(8,128)}) custom-call(bf16[256,1536]{1,0:T(8,128)(2,1)} %copy-done.8, bf16[272,1536]{1,0:T(8,128)(2,1)} %collective-permute-done.5.g_ref, bf16[256,1536]{1,0:T(8,128)(2,1)} %k_ref.5, bf16[256,1536]{1,0:T(8,128)(2,1)} %v_ref.3, ...), custom_call_target="tpu_custom_call" | custom-call | flops 1006632960 | bytes 9437184 | tf_op jit(solution)/shard_map/pallas_call | solution.py:166
  177.5 4.7 %collective-permute-start.15 = (bf16[256,1536]{1,0:T(8,128)(2,1)}, bf16[256,1536]{1,0:T(8,128)(2,1)S(1)}, u32[]{:S(2)}, u32[]{:S(2)}) collective-permute-start(bf16[256,1536]{1,0:T(8,128)(2,1)} %get-tuple-element.36), channel_id=1, source_target_pairs={{1,3},{2,0},{3,5},{4,2},{5,7},{6,4},{7,9},{8,6},{9,11},{10,8},{11,... | collective-permute-start | bytes 2359304 | tf_op jit(solution)/shard_map/ppermute | solution.py:26
  182.2 3.6 %add_convert_fusion.1 = bf16[256,1536]{1,0:T(8,128)(2,1)} fusion(f32[256,1536]{1,0:T(8,128)} %collective-permute-done.17, bf16[512,1536]{1,0:T(8,128)(2,1)S(1)} %convert.25, bf16[512,1536]{1,0:T(8,128)(2,1)} %copy-done.5, f32[256,1536]{1,0:T(8,128)} %get-tuple-element.42), kind=kLoop, calls=%fused_computation.1 | loop fusion | flops 3145728 | bytes 5505024 | tf_op jit(solution)/shard_map/convert_element_type | solution.py:276
  185.8 2.8 %add_convert_fusion.2 = bf16[256,1536]{1,0:T(8,128)(2,1)} fusion(f32[256,1536]{1,0:T(8,128)} %collective-permute-done.16, bf16[512,1536]{1,0:T(8,128)(2,1)S(1)} %convert.23, bf16[512,1536]{1,0:T(8,128)(2,1)S(1)} %copy-done.4, f32[256,1536]{1,0:T(8,128)S(1)} %copy-done.11), kind=kLoop, calls=%fused_computation.3 | loop fusion | flops 3145728 | bytes 5505024 | tf_op jit(solution)/shard_map/convert_element_type | solution.py:275
  188.7 15.5 %collective-permute-done.14 = bf16[256,1536]{1,0:T(8,128)(2,1)} collective-permute-done((bf16[256,1536]{1,0:T(8,128)(2,1)}, bf16[256,1536]{1,0:T(8,128)(2,1)}, u32[]{:S(2)}, u32[]{:S(2)}) %collective-permute-start.14) | collective-permute-done | bytes 786464 | tf_op jit(solution)/shard_map/ppermute | solution.py:26
  204.1 3.4 %collective-permute-done.15 = bf16[256,1536]{1,0:T(8,128)(2,1)S(1)} collective-permute-done((bf16[256,1536]{1,0:T(8,128)(2,1)}, bf16[256,1536]{1,0:T(8,128)(2,1)S(1)}, u32[]{:S(2)}, u32[]{:S(2)}) %collective-permute-start.15) | collective-permute-done | bytes 786464 | tf_op jit(solution)/shard_map/ppermute | solution.py:26
  207.5 2.4 %add_convert_fusion = bf16[256,1536]{1,0:T(8,128)(2,1)} fusion(bf16[256,1536]{1,0:T(8,128)(2,1)S(1)} %collective-permute-done.15, f32[256,1536]{1,0:T(8,128)S(1)} %copy-done.10, bf16[256,1536]{1,0:T(8,128)(2,1)} %collective-permute-done.14), kind=kLoop, calls=%fused_computation | loop fusion | flops 1966080 | bytes 3932160 | tf_op jit(solution)/shard_map/convert_element_type | solution.py:281
  (82 shorter events, 1.2 us)
Async XLA Ops:
  0.6 16.7 %copy-start.19 = (bf16[4,30,4]{1,2,0:T(4,128)(2,1)S(1)}, bf16[4,30,4]{1,2,0:T(4,128)(2,1)}, u32[]{:S(2)}) copy-start(bf16[4,30,4]{1,2,0:T(4,128)(2,1)} %constant.124) | copy-start | bytes 2884
  0.6 16.7 %copy-start.20 = (bf16[4,30,4]{1,2,0:T(4,128)(2,1)S(1)}, bf16[4,30,4]{1,2,0:T(4,128)(2,1)}, u32[]{:S(2)}) copy-start(bf16[4,30,4]{1,2,0:T(4,128)(2,1)} %constant.125) | copy-start | bytes 2884
  0.7 16.7 %copy-start.21 = (bf16[4,30,4]{1,2,0:T(4,128)(2,1)S(1)}, bf16[4,30,4]{1,2,0:T(4,128)(2,1)}, u32[]{:S(2)}) copy-start(bf16[4,30,4]{1,2,0:T(4,128)(2,1)} %constant.122) | copy-start | bytes 2884
  0.7 16.7 %copy-start.22 = (bf16[4,30,4]{1,2,0:T(4,128)(2,1)S(1)}, bf16[4,30,4]{1,2,0:T(4,128)(2,1)}, u32[]{:S(2)}) copy-start(bf16[4,30,4]{1,2,0:T(4,128)(2,1)} %constant.121) | copy-start | bytes 2884
  0.7 16.7 %copy-start.26 = (bf16[4,30,4]{1,2,0:T(4,128)(2,1)S(1)}, bf16[4,30,4]{1,2,0:T(4,128)(2,1)}, u32[]{:S(2)}) copy-start(bf16[4,30,4]{1,2,0:T(4,128)(2,1)} %constant.123) | copy-start | bytes 2884
  0.7 17.0 %copy-start.23 = (pred[4,8]{0,1:T(8,128)(4,1)S(1)}, pred[4,8]{0,1:T(8,128)(4,1)}, u32[]{:S(2)}) copy-start(pred[4,8]{0,1:T(8,128)(4,1)} %constant.62) | copy-start | bytes 100
  0.7 16.7 %copy-start.18 = (s32[4,30]{1,0:T(4,128)S(1)}, s32[4,30]{1,0:T(4,128)}, u32[]{:S(2)}) copy-start(s32[4,30]{1,0:T(4,128)} %param.29) | copy-start | bytes 1444
  0.7 16.5 %copy-start.2 = (bf16[256,1536]{1,0:T(8,128)(2,1)S(1)}, bf16[256,1536]{1,0:T(8,128)(2,1)}, u32[]{:S(2)}) copy-start(bf16[256,1536]{1,0:T(8,128)(2,1)} %k_ref.5) | copy-start | bytes 2359300
  0.7 56.2 %collective-permute-start.4 = (bf16[256,1536]{1,0:T(8,128)(2,1)}, bf16[256,1536]{1,0:T(8,128)(2,1)S(1)}, u32[]{:S(2)}, u32[]{:S(2)}) collective-permute-start(bf16[256,1536]{1,0:T(8,128)(2,1)} %q_ref.5), channel_id=1, source_target_pairs={{0,2},{2,4},{3,1},{4,6},{5,3},{6,8},{7,5},{8,10},{9,7},{10,12},{11... | collective-permute-start | bytes 2359304 | tf_op jit(solution)/shard_map/ppermute | solution.py:26
  4.3 55.0 %collective-permute-start.2 = (bf16[256,1536]{1,0:T(8,128)(2,1)}, bf16[256,1536]{1,0:T(8,128)(2,1)}, u32[]{:S(2)}, u32[]{:S(2)}) collective-permute-start(bf16[256,1536]{1,0:T(8,128)(2,1)} %q_ref.5), channel_id=1, source_target_pairs={{1,3},{2,0},{3,5},{4,2},{5,7},{6,4},{7,9},{8,6},{9,11},{10,8},{11,... | collective-permute-start | bytes 2359304 | tf_op jit(solution)/shard_map/ppermute | solution.py:26
  10.5 64.4 %collective-permute-start.5 = (bf16[272,1536]{1,0:T(8,128)(2,1)}, bf16[272,1536]{1,0:T(8,128)(2,1)}, u32[]{:S(2)}, u32[]{:S(2)}) collective-permute-start(bf16[272,1536]{1,0:T(8,128)(2,1)} %pad_maximum_fusion), channel_id=1, source_target_pairs={{0,2},{2,4},{3,1},{4,6},{5,3},{6,8},{7,5},{8,10},{9,7},{10,12},{11... | collective-permute-start | bytes 2506760 | tf_op jit(solution)/shard_map/ppermute | solution.py:26
  13.0 62.0 %collective-permute-start.3 = (bf16[272,1536]{1,0:T(8,128)(2,1)}, bf16[272,1536]{1,0:T(8,128)(2,1)}, u32[]{:S(2)}, u32[]{:S(2)}) collective-permute-start(bf16[272,1536]{1,0:T(8,128)(2,1)} %pad_maximum_fusion), channel_id=1, source_target_pairs={{1,3},{2,0},{3,5},{4,2},{5,7},{6,4},{7,9},{8,6},{9,11},{10,8},{11,... | collective-permute-start | bytes 2506760 | tf_op jit(solution)/shard_map/ppermute | solution.py:26
  17.3 2.5 %collective-permute-start = (bf16[256,1536]{1,0:T(8,128)(2,1)S(1)}, bf16[256,1536]{1,0:T(8,128)(2,1)}, u32[]{:S(2)}, u32[]{:S(2)}) collective-permute-start(bf16[256,1536]{1,0:T(8,128)(2,1)S(1)} %copy-done.2), channel_id=1, source_target_pairs={{0,1},{1,0},{2,3},{3,2},{4,5},{5,4},{6,7},{7,6},{8,9},{9,8},{10,11... | collective-permute-start | bytes 2359304 | tf_op jit(solution)/shard_map/ppermute | solution.py:26
  19.7 82.2 %collective-permute-start.1 = (bf16[256,1536]{1,0:T(8,128)(2,1)}, bf16[256,1536]{1,0:T(8,128)(2,1)}, u32[]{:S(2)}, u32[]{:S(2)}) collective-permute-start(bf16[256,1536]{1,0:T(8,128)(2,1)} %v_ref.3), channel_id=1, source_target_pairs={{0,1},{1,0},{2,3},{3,2},{4,5},{5,4},{6,7},{7,6},{8,9},{9,8},{10,11... | collective-permute-start | bytes 2359304 | tf_op jit(solution)/shard_map/ppermute | solution.py:26
  21.1 1.1 copy-start.1
  57.0 21.2 %copy-start.8 = (bf16[256,1536]{1,0:T(8,128)(2,1)}, bf16[256,1536]{1,0:T(8,128)(2,1)S(1)}, u32[]{:S(2)}) copy-start(bf16[256,1536]{1,0:T(8,128)(2,1)S(1)} %collective-permute-done.4.q_ref) | copy-start | bytes 2359300
  82.0 13.0 %collective-permute-start.7 = (f32[12,2,256]{2,1,0:T(2,128)}, f32[12,2,256]{2,1,0:T(2,128)S(1)}, u32[]{:S(2)}, u32[]{:S(2)}) collective-permute-start(f32[12,2,256]{2,1,0:T(2,128)} %shard_map.258), channel_id=1, source_target_pairs={{1,3},{2,0},{3,5},{4,2},{5,7},{6,4},{7,9},{8,6},{9,11},{10,8},{11,... | collective-permute-start | bytes 73736 | tf_op jit(solution)/shard_map/ppermute | solution.py:26
  87.8 7.1 %copy-start.9 = (bf16[256,1536]{1,0:T(8,128)(2,1)S(1)}, bf16[256,1536]{1,0:T(8,128)(2,1)}, u32[]{:S(2)}) copy-start(bf16[256,1536]{1,0:T(8,128)(2,1)} %v_ref.3) | copy-start | bytes 2359300
  87.8 12.0 %copy-start.14 = (f32[12,2,256]{2,1,0:T(2,128)S(1)}, f32[12,2,256]{2,1,0:T(2,128)}, u32[]{:S(2)}) copy-start(f32[12,2,256]{2,1,0:T(2,128)} %shard_map.256) | copy-start | bytes 73732
  93.0 6.8 %collective-permute-start.6 = (f32[12,2,256]{2,1,0:T(2,128)}, f32[12,2,256]{2,1,0:T(2,128)S(1)}, u32[]{:S(2)}, u32[]{:S(2)}) collective-permute-start(f32[12,2,256]{2,1,0:T(2,128)} %shard_map.257), channel_id=1, source_target_pairs={{0,2},{2,4},{3,1},{4,6},{5,3},{6,8},{7,5},{8,10},{9,7},{10,12},{11... | collective-permute-start | bytes 73736 | tf_op jit(solution)/shard_map/ppermute | solution.py:26
  100.0 13.4 %copy-start.12 = (f32[12,1,256]{2,1,0:T(1,128)}, f32[12,1,256]{2,1,0:T(1,128)S(1)}, u32[]{:S(2)}) copy-start(f32[12,1,256]{2,1,0:T(1,128)S(1)} %reshape_add_fusion.f_ref) | copy-start | bytes 36868
  100.0 8.0 %collective-permute-start.10 = (f32[12,1,256]{2,1,0:T(1,128)S(1)}, f32[12,1,256]{2,1,0:T(1,128)S(1)}, u32[]{:S(2)}, u32[]{:S(2)}) collective-permute-start(f32[12,1,256]{2,1,0:T(1,128)S(1)} %reshape_add_fusion.f_ref), channel_id=1, source_target_pairs={{0,2},{2,4},{3,1},{4,6},{5,3},{6,8},{7,5},{8,10},{9,7},{10,12},{11... | collective-permute-start | bytes 36872 | tf_op jit(solution)/shard_map/ppermute | solution.py:26
  103.2 10.2 %copy-start = (bf16[512,1536]{1,0:T(8,128)(2,1)}, bf16[512,1536]{1,0:T(8,128)(2,1)S(1)}, u32[]{:S(2)}) copy-start(bf16[512,1536]{1,0:T(8,128)(2,1)S(1)} %constant_dynamic-update-slice_fusion.2.v_ref) | copy-start | bytes 4718596
  103.2 12.2 %collective-permute-start.8 = (f32[12,1,256]{2,1,0:T(1,128)S(1)}, f32[12,1,256]{2,1,0:T(1,128)S(1)}, u32[]{:S(2)}, u32[]{:S(2)}) collective-permute-start(f32[12,1,256]{2,1,0:T(1,128)S(1)} %reshape_add_fusion.f_ref), channel_id=1, source_target_pairs={{1,3},{2,0},{3,5},{4,2},{5,7},{6,4},{7,9},{8,6},{9,11},{10,8},{11,... | collective-permute-start | bytes 36872 | tf_op jit(solution)/shard_map/ppermute | solution.py:26
  108.0 0.6 copy-start.16
  113.4 19.4 %collective-permute-start.11 = (f32[12,1,256]{2,1,0:T(1,128)}, f32[12,1,256]{2,1,0:T(1,128)S(1)}, u32[]{:S(2)}, u32[]{:S(2)}) collective-permute-start(f32[12,1,256]{2,1,0:T(1,128)} %shard_map.261), channel_id=1, source_target_pairs={{1,3},{2,0},{3,5},{4,2},{5,7},{6,4},{7,9},{8,6},{9,11},{10,8},{11,... | collective-permute-start | bytes 36872 | tf_op jit(solution)/shard_map/ppermute | solution.py:26
  115.3 0.6 copy-start.17
  122.3 11.2 %copy-start.13 = (f32[12,1,256]{2,1,0:T(1,128)S(1)}, f32[12,1,256]{2,1,0:T(1,128)}, u32[]{:S(2)}) copy-start(f32[12,1,256]{2,1,0:T(1,128)} %copy-done.12) | copy-start | bytes 36868
  122.3 10.5 %collective-permute-start.9 = (f32[12,1,256]{2,1,0:T(1,128)}, f32[12,1,256]{2,1,0:T(1,128)S(1)}, u32[]{:S(2)}, u32[]{:S(2)}) collective-permute-start(f32[12,1,256]{2,1,0:T(1,128)} %shard_map.260), channel_id=1, source_target_pairs={{0,2},{2,4},{3,1},{4,6},{5,3},{6,8},{7,5},{8,10},{9,7},{10,12},{11... | collective-permute-start | bytes 36872 | tf_op jit(solution)/shard_map/ppermute | solution.py:26
  133.6 7.0 %copy-start.15 = (f32[12,2,256]{2,1,0:T(2,128)}, f32[12,2,256]{2,1,0:T(2,128)S(1)}, u32[]{:S(2)}) copy-start(f32[12,2,256]{2,1,0:T(2,128)S(1)} %pad_maximum_fusion.1.f_ref) | copy-start | bytes 73732
  133.6 16.0 %collective-permute-start.13 = (f32[12,2,256]{2,1,0:T(2,128)S(1)}, f32[12,2,256]{2,1,0:T(2,128)S(1)}, u32[]{:S(2)}, u32[]{:S(2)}) collective-permute-start(f32[12,2,256]{2,1,0:T(2,128)S(1)} %pad_maximum_fusion.1.f_ref), channel_id=1, source_target_pairs={{0,2},{2,4},{3,1},{4,6},{5,3},{6,8},{7,5},{8,10},{9,7},{10,12},{11... | collective-permute-start | bytes 73736 | tf_op jit(solution)/shard_map/ppermute | solution.py:26
  136.5 13.1 %collective-permute-start.12 = (f32[12,2,256]{2,1,0:T(2,128)S(1)}, f32[12,2,256]{2,1,0:T(2,128)S(1)}, u32[]{:S(2)}, u32[]{:S(2)}) collective-permute-start(f32[12,2,256]{2,1,0:T(2,128)S(1)} %pad_maximum_fusion.1.f_ref), channel_id=1, source_target_pairs={{1,3},{2,0},{3,5},{4,2},{5,7},{6,4},{7,9},{8,6},{9,11},{10,8},{11,... | collective-permute-start | bytes 73736 | tf_op jit(solution)/shard_map/ppermute | solution.py:26
  149.6 2.1 %copy-start.24 = (f32[12,2,256]{2,1,0:T(2,128)}, f32[12,2,256]{2,1,0:T(2,128)S(1)}, u32[]{:S(2)}) copy-start(f32[12,2,256]{2,1,0:T(2,128)S(1)} %collective-permute-done.13.f_ref) | copy-start | bytes 73732
  149.6 2.1 copy-start.25
  162.7 1.7 copy-start.5
  162.7 3.0 %copy-start.6 = (f32[512,1536]{1,0:T(8,128)S(1)}, f32[512,1536]{1,0:T(8,128)}, u32[]{:S(2)}) copy-start(f32[512,1536]{1,0:T(8,128)} %get-tuple-element.38) | copy-start | bytes 9437188
  164.3 2.4 %copy-start.7 = (f32[512,1536]{1,0:T(8,128)S(1)}, f32[512,1536]{1,0:T(8,128)}, u32[]{:S(2)}) copy-start(f32[512,1536]{1,0:T(8,128)} %get-tuple-element.37) | copy-start | bytes 9437188
  164.3 17.8 %collective-permute-start.17 = (f32[256,1536]{1,0:T(8,128)}, f32[256,1536]{1,0:T(8,128)}, u32[]{:S(2)}, u32[]{:S(2)}) collective-permute-start(f32[256,1536]{1,0:T(8,128)} %convert_add_fusion), channel_id=1, source_target_pairs={{0,1},{1,0},{2,3},{3,2},{4,5},{5,4},{6,7},{7,6},{8,9},{9,8},{10,11... | collective-permute-start | bytes 4718600 | tf_op jit(solution)/shard_map/ppermute | solution.py:26
  167.0 1.7 copy-start.3
  168.6 17.2 %collective-permute-start.16 = (f32[256,1536]{1,0:T(8,128)}, f32[256,1536]{1,0:T(8,128)}, u32[]{:S(2)}, u32[]{:S(2)}) collective-permute-start(f32[256,1536]{1,0:T(8,128)} %convert_add_fusion.1), channel_id=1, source_target_pairs={{0,1},{1,0},{2,3},{3,2},{4,5},{5,4},{6,7},{7,6},{8,9},{9,8},{10,11... | collective-permute-start | bytes 4718600 | tf_op jit(solution)/shard_map/ppermute | solution.py:26
  168.6 35.5 %collective-permute-start.14 = (bf16[256,1536]{1,0:T(8,128)(2,1)}, bf16[256,1536]{1,0:T(8,128)(2,1)}, u32[]{:S(2)}, u32[]{:S(2)}) collective-permute-start(bf16[256,1536]{1,0:T(8,128)(2,1)} %get-tuple-element.34), channel_id=1, source_target_pairs={{0,2},{2,4},{3,1},{4,6},{5,3},{6,8},{7,5},{8,10},{9,7},{10,12},{11... | collective-permute-start | bytes 2359304 | tf_op jit(solution)/shard_map/ppermute | solution.py:26
  177.5 30.0 %collective-permute-start.15 = (bf16[256,1536]{1,0:T(8,128)(2,1)}, bf16[256,1536]{1,0:T(8,128)(2,1)S(1)}, u32[]{:S(2)}, u32[]{:S(2)}) collective-permute-start(bf16[256,1536]{1,0:T(8,128)(2,1)} %get-tuple-element.36), channel_id=1, source_target_pairs={{1,3},{2,0},{3,5},{4,2},{5,7},{6,4},{7,9},{8,6},{9,11},{10,8},{11,... | collective-permute-start | bytes 2359304 | tf_op jit(solution)/shard_map/ppermute | solution.py:26
  182.2 3.6 %copy-start.4 = (bf16[512,1536]{1,0:T(8,128)(2,1)S(1)}, bf16[512,1536]{1,0:T(8,128)(2,1)}, u32[]{:S(2)}) copy-start(bf16[512,1536]{1,0:T(8,128)(2,1)} %copy-done.3) | copy-start | bytes 4718596
  182.2 3.6 %copy-start.11 = (f32[256,1536]{1,0:T(8,128)S(1)}, f32[256,1536]{1,0:T(8,128)}, u32[]{:S(2)}) copy-start(f32[256,1536]{1,0:T(8,128)} %get-tuple-element.39) | copy-start | bytes 4718596
  185.8 21.7 %copy-start.10 = (f32[256,1536]{1,0:T(8,128)S(1)}, f32[256,1536]{1,0:T(8,128)}, u32[]{:S(2)}) copy-start(f32[256,1536]{1,0:T(8,128)} %get-tuple-element.30) | copy-start | bytes 4718596

commit v16 on v15

--- a/solution.py
+++ b/solution.py
@@ -111,8 +111,10 @@
         fin = f_ref[j]
         p = jnp.where(m, jnp.exp(s - fin[0:1]), 0.0)
         ds = (p * (dp - fin[1:2])).astype(jnp.bfloat16)
-        dk_ref[:, cols] = jnp.dot(ds, q, preferred_element_type=jnp.float32) * SCALE
-        dv_ref[:, cols] = jnp.dot(p.astype(jnp.bfloat16), g, preferred_element_type=jnp.float32)
+        dk = jnp.dot(ds, q, preferred_element_type=jnp.float32) * SCALE
+        dk_ref[:, cols] = dk.astype(dk_ref.dtype)
+        dv = jnp.dot(p.astype(jnp.bfloat16), g, preferred_element_type=jnp.float32)
+        dv_ref[:, cols] = dv.astype(dv_ref.dtype)
         dq = lax.dot_general(ds, k, (((0,), (0,)), ((), ())), preferred_element_type=jnp.float32)
         dq_ref[:, cols] = (dq * SCALE).astype(dq_ref.dtype)
 
@@ -175,8 +177,8 @@
         ],
         out_shape=[
             jax.ShapeDtypeStruct((tok, width), dq_type),
-            jax.ShapeDtypeStruct((nk, width), jnp.float32),
-            jax.ShapeDtypeStruct((nk, width), jnp.float32),
+            jax.ShapeDtypeStruct((nk, width), jnp.bfloat16),
+            jax.ShapeDtypeStruct((nk, width), jnp.bfloat16),
         ],
         cost_estimate=pl.CostEstimate(
             flops=flops, transcendentals=tok * nk * HEADS, bytes_accessed=12 * (tok + nk) * HDIM * HEADS

time: 211 us -> 211 us (level)
  waiting for transfers between devices: 71.8 us -> 79.9 us
  other arithmetic: 21.4 us -> 15.6 us
    ppermute x18, waiting for transfers between devices: 71.8 us -> 79.9 us  [permute(): return lax.ppermute(value, 'tm', pairs)]
    another operation x4 -> x0, other arithmetic: 4.49 us -> none
    unnamed x57 -> x51, local copies, waits for them, and re-layouts: 5.09 us -> 4.28 us
  transfers between devices with their start and end apart: 18 -> 18, of which waited for: 8 -> 7; matrix products, arithmetic and copies ran while one was open for 10% -> 10% of each run, Pallas kernels for 23% -> 22%
where the time goes in v16:
time: 211 us; the launch traced here: 209 us
  waiting for transfers between devices  79.9 us (38%)
  Pallas kernels  54.7 us (26%)
  starting transfers between devices  45.9 us (22%)
  other arithmetic  15.6 us (7%)
  local copies, waits for them, and re-layouts  11.6 us (5%)
    ppermute x18, waiting for transfers between devices, permute(): return lax.ppermute(value, 'tm', pairs)  79.9 us
    ppermute x18, starting transfers between devices, permute(): return lax.ppermute(value, 'tm', pairs)  45.9 us
    pallas_call x3, Pallas kernels, slot_back(): pl.pallas_call(back_kernel, grid=(HEADS // STEP_HEADS,), in_specs=slot_sp...  23.1 us
    pallas_call x3, Pallas kernels, slot_delta(): pl.pallas_call(delta_kernel, grid=(HEADS // STEP_HEADS,), in_specs=slot_s...  17.6 us
    pallas_call x3, Pallas kernels, slot_stats(): pl.pallas_call(stats_kernel, grid=(HEADS // STEP_HEADS,), in_specs=[slot_...  14 us
    unnamed x51, local copies, waits for them, and re-layouts  4.28 us
  transfers between devices with their start and end apart: 18, of which 7 were waited for; matrix products, arithmetic and copies ran while one was open for 10% of the time, Pallas kernels for 22%

profile of v16, /device:TPU:8, one launch (start us, length us, event | category | flops | bytes accessed | tf_op | source)
XLA Modules:
  0.0 209.3 jit_solution(4981528528258024529)
XLA Ops:
  0.7 3.6 %collective-permute-start.4 = (bf16[256,1536]{1,0:T(8,128)(2,1)}, bf16[256,1536]{1,0:T(8,128)(2,1)}, u32[]{:S(2)}, u32[]{:S(2)}) collective-permute-start(bf16[256,1536]{1,0:T(8,128)(2,1)} %q_ref.5), channel_id=1, source_target_pairs={{0,2},{2,4},{3,1},{4,6},{5,3},{6,8},{7,5},{8,10},{9,7},{10,12},{11... | collective-permute-start | bytes 2359304 | tf_op jit(solution)/shard_map/ppermute | solution.py:26
  4.3 3.3 %collective-permute-start.2 = (bf16[256,1536]{1,0:T(8,128)(2,1)}, bf16[256,1536]{1,0:T(8,128)(2,1)}, u32[]{:S(2)}, u32[]{:S(2)}) collective-permute-start(bf16[256,1536]{1,0:T(8,128)(2,1)} %q_ref.5), channel_id=1, source_target_pairs={{1,3},{2,0},{3,5},{4,2},{5,7},{6,4},{7,9},{8,6},{9,11},{10,8},{11,... | collective-permute-start | bytes 2359304 | tf_op jit(solution)/shard_map/ppermute | solution.py:26
  7.6 0.7 broadcast_compare_fusion
  8.3 0.1 reshape.137
  8.4 1.2 pad_maximum_fusion
  9.6 2.5 %collective-permute-start.5 = (bf16[272,1536]{1,0:T(8,128)(2,1)S(1)}, bf16[272,1536]{1,0:T(8,128)(2,1)}, u32[]{:S(2)}, u32[]{:S(2)}) collective-permute-start(bf16[272,1536]{1,0:T(8,128)(2,1)S(1)} %pad_maximum_fusion), channel_id=1, source_target_pairs={{0,2},{2,4},{3,1},{4,6},{5,3},{6,8},{7,5},{8,10},{9,7},{10,12},{11... | collective-permute-start | bytes 2506760 | tf_op jit(solution)/shard_map/ppermute | solution.py:26
  12.1 4.2 %collective-permute-start.3 = (bf16[272,1536]{1,0:T(8,128)(2,1)S(1)}, bf16[272,1536]{1,0:T(8,128)(2,1)}, u32[]{:S(2)}, u32[]{:S(2)}) collective-permute-start(bf16[272,1536]{1,0:T(8,128)(2,1)S(1)} %pad_maximum_fusion), channel_id=1, source_target_pairs={{1,3},{2,0},{3,5},{4,2},{5,7},{6,4},{7,9},{8,6},{9,11},{10,8},{11,... | collective-permute-start | bytes 2506760 | tf_op jit(solution)/shard_map/ppermute | solution.py:26
  16.6 0.1 fusion.2
  16.8 0.2 broadcast_in_dim.31
  17.0 1.4 convert_element_type.74.m_ref
  18.5 0.4 collective-permute-done
  18.9 0.1 collective-permute-start.1
  19.0 1.2 constant_dynamic-update-slice_fusion.k_ref
  20.2 1.1 copy-done.1
  21.3 5.1 %shard_map.256 = f32[12,2,256]{2,1,0:T(2,128)} custom-call(bf16[256,1536]{1,0:T(8,128)(2,1)} %q_ref.5, bf16[512,1536]{1,0:T(8,128)(2,1)} %copy-done.1, f32[512,256]{1,0:T(8,128)} %convert_element_type.74.m_ref), custom_call_target="tpu_custom_call" | custom-call | flops 402653184 | bytes 4718592 | tf_op jit(solution)/shard_map/pallas_call | solution.py:136
  26.4 30.6 %collective-permute-done.4.q_ref = bf16[256,1536]{1,0:T(8,128)(2,1)} collective-permute-done((bf16[256,1536]{1,0:T(8,128)(2,1)}, bf16[256,1536]{1,0:T(8,128)(2,1)}, u32[]{:S(2)}, u32[]{:S(2)}) %collective-permute-start.4) | collective-permute-done | bytes 786464 | tf_op jit(solution)/shard_map/ppermute | solution.py:26
  57.0 2.4 %collective-permute-done.2.q_ref = bf16[256,1536]{1,0:T(8,128)(2,1)} collective-permute-done((bf16[256,1536]{1,0:T(8,128)(2,1)}, bf16[256,1536]{1,0:T(8,128)(2,1)}, u32[]{:S(2)}, u32[]{:S(2)}) %collective-permute-start.2) | collective-permute-done | bytes 786464 | tf_op jit(solution)/shard_map/ppermute | solution.py:26
  59.3 15.4 %collective-permute-done.5.g_ref = bf16[272,1536]{1,0:T(8,128)(2,1)} collective-permute-done((bf16[272,1536]{1,0:T(8,128)(2,1)S(1)}, bf16[272,1536]{1,0:T(8,128)(2,1)}, u32[]{:S(2)}, u32[]{:S(2)}) %collective-permute-start.5) | collective-permute-done | bytes 835616 | tf_op jit(solution)/shard_map/ppermute | solution.py:26
  74.8 0.3 collective-permute-done.3.g_ref
  75.0 0.7 compare_reduce_fusion.1
  75.7 0.6 compare_reduce_fusion
  76.3 0.1 reshape.147
  76.4 0.1 fusion.13
  76.5 0.1 copy.33
  76.6 0.1 reshape.145
  76.7 0.1 fusion.6
  76.8 0.1 copy.31
  76.9 0.1 broadcast_in_dim.34
  77.1 1.1 convert_element_type.80.m_ref
  78.1 3.8 %shard_map.258 = f32[12,2,256]{2,1,0:T(2,128)} custom-call(bf16[256,1536]{1,0:T(8,128)(2,1)} %collective-permute-done.4.q_ref, bf16[256,1536]{1,0:T(8,128)(2,1)} %k_ref.5, f32[256,256]{1,0:T(8,128)} %convert_element_type.80.m_ref), custom_call_target="tpu_custom_call" | custom-call | flops 201326592 | bytes 3145728 | tf_op jit(solution)/shard_map/pallas_call | solution.py:136
  82.0 4.1 %collective-permute-start.7 = (f32[12,2,256]{2,1,0:T(2,128)}, f32[12,2,256]{2,1,0:T(2,128)S(1)}, u32[]{:S(2)}, u32[]{:S(2)}) collective-permute-start(f32[12,2,256]{2,1,0:T(2,128)} %shard_map.258), channel_id=1, source_target_pairs={{1,3},{2,0},{3,5},{4,2},{5,7},{6,4},{7,9},{8,6},{9,11},{10,8},{11,... | collective-permute-start | bytes 73736 | tf_op jit(solution)/shard_map/ppermute | solution.py:26
  86.2 0.2 broadcast_in_dim.33
  86.4 1.4 convert_element_type.77.m_ref
  87.8 5.1 %shard_map.257 = f32[12,2,256]{2,1,0:T(2,128)} custom-call(bf16[256,1536]{1,0:T(8,128)(2,1)} %collective-permute-done.2.q_ref, bf16[512,1536]{1,0:T(8,128)(2,1)} %copy-done.1, f32[512,256]{1,0:T(8,128)} %convert_element_type.77.m_ref), custom_call_target="tpu_custom_call" | custom-call | flops 402653184 | bytes 4718592 | tf_op jit(solution)/shard_map/pallas_call | solution.py:136
  92.9 2.0 collective-permute-start.6
  94.9 1.2 constant_dynamic-update-slice_fusion.3
  96.1 3.6 %collective-permute-done.6 = f32[12,2,256]{2,1,0:T(2,128)S(1)} collective-permute-done((f32[12,2,256]{2,1,0:T(2,128)}, f32[12,2,256]{2,1,0:T(2,128)S(1)}, u32[]{:S(2)}, u32[]{:S(2)}) %collective-permute-start.6) | collective-permute-done | bytes 24608 | tf_op jit(solution)/shard_map/ppermute | solution.py:26
  99.8 0.1 fusion
  99.9 1.9 collective-permute-start.10
  101.9 1.2 constant_dynamic-update-slice_fusion.2.v_ref
  103.1 4.8 %collective-permute-start.8 = (f32[12,1,256]{2,1,0:T(1,128)S(1)}, f32[12,1,256]{2,1,0:T(1,128)S(1)}, u32[]{:S(2)}, u32[]{:S(2)}) collective-permute-start(f32[12,1,256]{2,1,0:T(1,128)S(1)} %reshape_add_fusion.f_ref), channel_id=1, source_target_pairs={{1,3},{2,0},{3,5},{4,2},{5,7},{6,4},{7,9},{8,6},{9,11},{10,8},{11,... | collective-permute-start | bytes 36872 | tf_op jit(solution)/shard_map/ppermute | solution.py:26
  107.9 0.6 copy-done.13
  108.5 4.8 %shard_map.261 = f32[12,1,256]{2,1,0:T(1,128)} custom-call(bf16[256,1536]{1,0:T(8,128)(2,1)} %collective-permute-done.4.q_ref, bf16[272,1536]{1,0:T(8,128)(2,1)} %collective-permute-done.5.g_ref, bf16[256,1536]{1,0:T(8,128)(2,1)} %k_ref.5, bf16[256,1536]{1,0:T(8,128)(2,1)} %v_ref.3, f32[256,256]{1,0:T(8,128)} %convert_element_type.80.m_ref, ...), custom_call_target="tpu_custom_call" | custom-call | flops 402653184 | bytes 3145728 | tf_op jit(solution)/shard_map/pallas_call | solution.py:151
  113.3 1.9 collective-permute-start.11
  115.3 0.6 copy-done.14
  115.9 6.4 %shard_map.260 = f32[12,1,256]{2,1,0:T(1,128)} custom-call(bf16[256,1536]{1,0:T(8,128)(2,1)} %collective-permute-done.2.q_ref, bf16[272,1536]{1,0:T(8,128)(2,1)} %collective-permute-done.3.g_ref, bf16[512,1536]{1,0:T(8,128)(2,1)} %copy-done.1, bf16[512,1536]{1,0:T(8,128)(2,1)} %copy-done, f32[512,256]{1,0:T(8,128)} %convert_element_type.77.m_ref, ...), custom_call_target="tpu_custom_call" | custom-call | flops 805306368 | bytes 4718592 | tf_op jit(solution)/shard_map/pallas_call | solution.py:151
  122.3 4.0 %collective-permute-start.9 = (f32[12,1,256]{2,1,0:T(1,128)}, f32[12,1,256]{2,1,0:T(1,128)S(1)}, u32[]{:S(2)}, u32[]{:S(2)}) collective-permute-start(f32[12,1,256]{2,1,0:T(1,128)} %shard_map.260), channel_id=1, source_target_pairs={{0,2},{2,4},{3,1},{4,6},{5,3},{6,8},{7,5},{8,10},{9,7},{10,12},{11... | collective-permute-start | bytes 36872 | tf_op jit(solution)/shard_map/ppermute | solution.py:26
  126.3 6.4 %shard_map.259 = f32[12,1,256]{2,1,0:T(1,128)} custom-call(bf16[256,1536]{1,0:T(8,128)(2,1)} %q_ref.5, bf16[256,1536]{1,0:T(8,128)(2,1)} %g_ref.3, bf16[512,1536]{1,0:T(8,128)(2,1)} %copy-done.1, bf16[512,1536]{1,0:T(8,128)(2,1)} %copy-done, f32[512,256]{1,0:T(8,128)} %convert_element_type.74.m_ref, f32[12,1,256]{2,1,0:T(1,128)} %copy-done.9), custom_call_target="tpu_custom_call" | custom-call | flops 805306368 | bytes 4718592 | tf_op jit(solution)/shard_map/pallas_call | solution.py:151
  132.8 0.7 add_add_fusion
  133.5 2.9 %collective-permute-start.13 = (f32[12,2,256]{2,1,0:T(2,128)S(1)}, f32[12,2,256]{2,1,0:T(2,128)S(1)}, u32[]{:S(2)}, u32[]{:S(2)}) collective-permute-start(f32[12,2,256]{2,1,0:T(2,128)S(1)} %pad_maximum_fusion.1.f_ref), channel_id=1, source_target_pairs={{0,2},{2,4},{3,1},{4,6},{5,3},{6,8},{7,5},{8,10},{9,7},{10,12},{11... | collective-permute-start | bytes 73736 | tf_op jit(solution)/shard_map/ppermute | solution.py:26
  136.5 4.0 %collective-permute-start.12 = (f32[12,2,256]{2,1,0:T(2,128)S(1)}, f32[12,2,256]{2,1,0:T(2,128)S(1)}, u32[]{:S(2)}, u32[]{:S(2)}) collective-permute-start(f32[12,2,256]{2,1,0:T(2,128)S(1)} %pad_maximum_fusion.1.f_ref), channel_id=1, source_target_pairs={{1,3},{2,0},{3,5},{4,2},{5,7},{6,4},{7,9},{8,6},{9,11},{10,8},{11,... | collective-permute-start | bytes 73736 | tf_op jit(solution)/shard_map/ppermute | solution.py:26
  140.5 8.3 %shard_map.262 = (f32[256,1536]{1,0:T(8,128)}, bf16[512,1536]{1,0:T(8,128)(2,1)}, bf16[512,1536]{1,0:T(8,128)(2,1)}) custom-call(bf16[256,1536]{1,0:T(8,128)(2,1)} %q_ref.5, bf16[256,1536]{1,0:T(8,128)(2,1)} %g_ref.3, bf16[512,1536]{1,0:T(8,128)(2,1)} %copy-done.1, bf16[512,1536]{1,0:T(8,128)(2,1)} %copy-done, f32[512,256]{1,0:T(8,128)} %convert_element_type.74.m_ref, ...), custom_call_target="tpu_custom_call" | custom-call | flops 2013265920 | bytes 14155776 | tf_op jit(solution)/shard_map/pallas_call | solution.py:168
  148.8 0.6 copy-done.22
  149.4 8.3 %shard_map.263 = (bf16[256,1536]{1,0:T(8,128)(2,1)}, bf16[512,1536]{1,0:T(8,128)(2,1)}, bf16[512,1536]{1,0:T(8,128)(2,1)}) custom-call(bf16[256,1536]{1,0:T(8,128)(2,1)} %collective-permute-done.2.q_ref, bf16[272,1536]{1,0:T(8,128)(2,1)} %collective-permute-done.3.g_ref, bf16[512,1536]{1,0:T(8,128)(2,1)} %copy-done.1, bf16[512,1536]{1,0:T(8,128)(2,1)} %copy-done, ...), custom_call_target="tpu_custom_call" | custom-call | flops 2013265920 | bytes 14155776 | tf_op jit(solution)/shard_map/pallas_call | solution.py:168
  157.8 2.7 %convert_add_fusion = f32[256,1536]{1,0:T(8,128)} fusion(bf16[512,1536]{1,0:T(8,128)(2,1)S(1)} %copy-done.4, bf16[512,1536]{1,0:T(8,128)(2,1)} %get-tuple-element.40), kind=kLoop, calls=%fused_computation.2 | loop fusion | flops 1179648 | bytes 3145728 | tf_op jit(solution)/shard_map/add | solution.py:275
  160.4 1.4 convert_add_fusion.1
  161.9 0.5 collective-permute-start.16
  162.4 6.5 %shard_map.264 = (bf16[256,1536]{1,0:T(8,128)(2,1)}, bf16[256,1536]{1,0:T(8,128)(2,1)}, bf16[256,1536]{1,0:T(8,128)(2,1)}) custom-call(bf16[256,1536]{1,0:T(8,128)(2,1)} %collective-permute-done.4.q_ref, bf16[272,1536]{1,0:T(8,128)(2,1)} %collective-permute-done.5.g_ref, bf16[256,1536]{1,0:T(8,128)(2,1)} %k_ref.5, bf16[256,1536]{1,0:T(8,128)(2,1)} %v_ref.3, ...), custom_call_target="tpu_custom_call" | custom-call | flops 1006632960 | bytes 9437184 | tf_op jit(solution)/shard_map/pallas_call | solution.py:168
  168.9 1.9 collective-permute-start.15
  170.8 3.9 %collective-permute-start.14 = (bf16[256,1536]{1,0:T(8,128)(2,1)}, bf16[256,1536]{1,0:T(8,128)(2,1)S(1)}, u32[]{:S(2)}, u32[]{:S(2)}) collective-permute-start(bf16[256,1536]{1,0:T(8,128)(2,1)} %get-tuple-element.34), channel_id=1, source_target_pairs={{0,2},{2,4},{3,1},{4,6},{5,3},{6,8},{7,5},{8,10},{9,7},{10,12},{11... | collective-permute-start | bytes 2359304 | tf_op jit(solution)/shard_map/ppermute | solution.py:26
  174.7 3.3 %add_convert_fusion.1 = bf16[256,1536]{1,0:T(8,128)(2,1)} fusion(f32[256,1536]{1,0:T(8,128)} %collective-permute-done.17, bf16[256,1536]{1,0:T(8,128)(2,1)} %get-tuple-element.42, bf16[512,1536]{1,0:T(8,128)(2,1)S(1)} %copy-done.4, bf16[512,1536]{1,0:T(8,128)(2,1)} %get-tuple-element.40), kind=kLoop, calls=%fused_computation.1 | loop fusion | flops 2752512 | bytes 4718592 | tf_op jit(solution)/shard_map/convert_element_type | solution.py:278
  178.0 2.8 %add_convert_fusion.2 = bf16[256,1536]{1,0:T(8,128)(2,1)} fusion(f32[256,1536]{1,0:T(8,128)} %collective-permute-done.16, bf16[256,1536]{1,0:T(8,128)(2,1)S(1)} %copy-done.8, bf16[512,1536]{1,0:T(8,128)(2,1)S(1)} %copy-done.3, bf16[512,1536]{1,0:T(8,128)(2,1)S(1)} %copy-done.6), kind=kLoop, calls=%fused_computation.3 | loop fusion | flops 2752512 | bytes 4718592 | tf_op jit(solution)/shard_map/convert_element_type | solution.py:277
  180.8 27.2 %collective-permute-done.15 = bf16[256,1536]{1,0:T(8,128)(2,1)S(1)} collective-permute-done((bf16[256,1536]{1,0:T(8,128)(2,1)}, bf16[256,1536]{1,0:T(8,128)(2,1)S(1)}, u32[]{:S(2)}, u32[]{:S(2)}) %collective-permute-start.15) | collective-permute-done | bytes 786464 | tf_op jit(solution)/shard_map/ppermute | solution.py:26
  208.1 1.2 add_convert_fusion
  (72 shorter events, 0.6 us)
Async XLA Ops:
  0.6 15.8 %copy-start.16 = (bf16[4,30,4]{1,2,0:T(4,128)(2,1)S(1)}, bf16[4,30,4]{1,2,0:T(4,128)(2,1)}, u32[]{:S(2)}) copy-start(bf16[4,30,4]{1,2,0:T(4,128)(2,1)} %constant.124) | copy-start | bytes 2884
  0.6 15.8 %copy-start.17 = (bf16[4,30,4]{1,2,0:T(4,128)(2,1)S(1)}, bf16[4,30,4]{1,2,0:T(4,128)(2,1)}, u32[]{:S(2)}) copy-start(bf16[4,30,4]{1,2,0:T(4,128)(2,1)} %constant.125) | copy-start | bytes 2884
  0.7 15.8 %copy-start.18 = (bf16[4,30,4]{1,2,0:T(4,128)(2,1)S(1)}, bf16[4,30,4]{1,2,0:T(4,128)(2,1)}, u32[]{:S(2)}) copy-start(bf16[4,30,4]{1,2,0:T(4,128)(2,1)} %constant.122) | copy-start | bytes 2884
  0.7 15.8 %copy-start.19 = (bf16[4,30,4]{1,2,0:T(4,128)(2,1)S(1)}, bf16[4,30,4]{1,2,0:T(4,128)(2,1)}, u32[]{:S(2)}) copy-start(bf16[4,30,4]{1,2,0:T(4,128)(2,1)} %constant.121) | copy-start | bytes 2884
  0.7 15.9 %copy-start.23 = (bf16[4,30,4]{1,2,0:T(4,128)(2,1)S(1)}, bf16[4,30,4]{1,2,0:T(4,128)(2,1)}, u32[]{:S(2)}) copy-start(bf16[4,30,4]{1,2,0:T(4,128)(2,1)} %constant.123) | copy-start | bytes 2884
  0.7 16.1 %copy-start.20 = (pred[4,8]{0,1:T(8,128)(4,1)S(1)}, pred[4,8]{0,1:T(8,128)(4,1)}, u32[]{:S(2)}) copy-start(pred[4,8]{0,1:T(8,128)(4,1)} %constant.62) | copy-start | bytes 100
  0.7 15.8 %copy-start.15 = (s32[4,30]{1,0:T(4,128)S(1)}, s32[4,30]{1,0:T(4,128)}, u32[]{:S(2)}) copy-start(s32[4,30]{1,0:T(4,128)} %param.29) | copy-start | bytes 1444
  0.7 15.6 %copy-start.2 = (bf16[256,1536]{1,0:T(8,128)(2,1)S(1)}, bf16[256,1536]{1,0:T(8,128)(2,1)}, u32[]{:S(2)}) copy-start(bf16[256,1536]{1,0:T(8,128)(2,1)} %k_ref.5) | copy-start | bytes 2359300
  0.7 56.2 %collective-permute-start.4 = (bf16[256,1536]{1,0:T(8,128)(2,1)}, bf16[256,1536]{1,0:T(8,128)(2,1)}, u32[]{:S(2)}, u32[]{:S(2)}) collective-permute-start(bf16[256,1536]{1,0:T(8,128)(2,1)} %q_ref.5), channel_id=1, source_target_pairs={{0,2},{2,4},{3,1},{4,6},{5,3},{6,8},{7,5},{8,10},{9,7},{10,12},{11... | collective-permute-start | bytes 2359304 | tf_op jit(solution)/shard_map/ppermute | solution.py:26
  4.3 55.0 %collective-permute-start.2 = (bf16[256,1536]{1,0:T(8,128)(2,1)}, bf16[256,1536]{1,0:T(8,128)(2,1)}, u32[]{:S(2)}, u32[]{:S(2)}) collective-permute-start(bf16[256,1536]{1,0:T(8,128)(2,1)} %q_ref.5), channel_id=1, source_target_pairs={{1,3},{2,0},{3,5},{4,2},{5,7},{6,4},{7,9},{8,6},{9,11},{10,8},{11,... | collective-permute-start | bytes 2359304 | tf_op jit(solution)/shard_map/ppermute | solution.py:26
  9.6 65.2 %collective-permute-start.5 = (bf16[272,1536]{1,0:T(8,128)(2,1)S(1)}, bf16[272,1536]{1,0:T(8,128)(2,1)}, u32[]{:S(2)}, u32[]{:S(2)}) collective-permute-start(bf16[272,1536]{1,0:T(8,128)(2,1)S(1)} %pad_maximum_fusion), channel_id=1, source_target_pairs={{0,2},{2,4},{3,1},{4,6},{5,3},{6,8},{7,5},{8,10},{9,7},{10,12},{11... | collective-permute-start | bytes 2506760 | tf_op jit(solution)/shard_map/ppermute | solution.py:26
  12.1 62.9 %collective-permute-start.3 = (bf16[272,1536]{1,0:T(8,128)(2,1)S(1)}, bf16[272,1536]{1,0:T(8,128)(2,1)}, u32[]{:S(2)}, u32[]{:S(2)}) collective-permute-start(bf16[272,1536]{1,0:T(8,128)(2,1)S(1)} %pad_maximum_fusion), channel_id=1, source_target_pairs={{1,3},{2,0},{3,5},{4,2},{5,7},{6,4},{7,9},{8,6},{9,11},{10,8},{11,... | collective-permute-start | bytes 2506760 | tf_op jit(solution)/shard_map/ppermute | solution.py:26
  16.4 2.5 %collective-permute-start = (bf16[256,1536]{1,0:T(8,128)(2,1)S(1)}, bf16[256,1536]{1,0:T(8,128)(2,1)}, u32[]{:S(2)}, u32[]{:S(2)}) collective-permute-start(bf16[256,1536]{1,0:T(8,128)(2,1)S(1)} %copy-done.2), channel_id=1, source_target_pairs={{0,1},{1,0},{2,3},{3,2},{4,5},{5,4},{6,7},{7,6},{8,9},{9,8},{10,11... | collective-permute-start | bytes 2359304 | tf_op jit(solution)/shard_map/ppermute | solution.py:26
  18.9 83.0 %collective-permute-start.1 = (bf16[256,1536]{1,0:T(8,128)(2,1)}, bf16[256,1536]{1,0:T(8,128)(2,1)}, u32[]{:S(2)}, u32[]{:S(2)}) collective-permute-start(bf16[256,1536]{1,0:T(8,128)(2,1)} %v_ref.3), channel_id=1, source_target_pairs={{0,1},{1,0},{2,3},{3,2},{4,5},{5,4},{6,7},{7,6},{8,9},{9,8},{10,11... | collective-permute-start | bytes 2359304 | tf_op jit(solution)/shard_map/ppermute | solution.py:26
  20.2 1.2 copy-start.1
  82.0 14.1 %collective-permute-start.7 = (f32[12,2,256]{2,1,0:T(2,128)}, f32[12,2,256]{2,1,0:T(2,128)S(1)}, u32[]{:S(2)}, u32[]{:S(2)}) collective-permute-start(f32[12,2,256]{2,1,0:T(2,128)} %shard_map.258), channel_id=1, source_target_pairs={{1,3},{2,0},{3,5},{4,2},{5,7},{6,4},{7,9},{8,6},{9,11},{10,8},{11,... | collective-permute-start | bytes 73736 | tf_op jit(solution)/shard_map/ppermute | solution.py:26
  87.8 11.9 %copy-start.11 = (f32[12,2,256]{2,1,0:T(2,128)S(1)}, f32[12,2,256]{2,1,0:T(2,128)}, u32[]{:S(2)}) copy-start(f32[12,2,256]{2,1,0:T(2,128)} %shard_map.256) | copy-start | bytes 73732
  92.9 6.8 %collective-permute-start.6 = (f32[12,2,256]{2,1,0:T(2,128)}, f32[12,2,256]{2,1,0:T(2,128)S(1)}, u32[]{:S(2)}, u32[]{:S(2)}) collective-permute-start(f32[12,2,256]{2,1,0:T(2,128)} %shard_map.257), channel_id=1, source_target_pairs={{0,2},{2,4},{3,1},{4,6},{5,3},{6,8},{7,5},{8,10},{9,7},{10,12},{11... | collective-permute-start | bytes 73736 | tf_op jit(solution)/shard_map/ppermute | solution.py:26
  99.9 13.4 %copy-start.9 = (f32[12,1,256]{2,1,0:T(1,128)}, f32[12,1,256]{2,1,0:T(1,128)S(1)}, u32[]{:S(2)}) copy-start(f32[12,1,256]{2,1,0:T(1,128)S(1)} %reshape_add_fusion.f_ref) | copy-start | bytes 36868
  99.9 8.0 %collective-permute-start.10 = (f32[12,1,256]{2,1,0:T(1,128)S(1)}, f32[12,1,256]{2,1,0:T(1,128)S(1)}, u32[]{:S(2)}, u32[]{:S(2)}) collective-permute-start(f32[12,1,256]{2,1,0:T(1,128)S(1)} %reshape_add_fusion.f_ref), channel_id=1, source_target_pairs={{0,2},{2,4},{3,1},{4,6},{5,3},{6,8},{7,5},{8,10},{9,7},{10,12},{11... | collective-permute-start | bytes 36872 | tf_op jit(solution)/shard_map/ppermute | solution.py:26
  103.1 10.3 %copy-start = (bf16[512,1536]{1,0:T(8,128)(2,1)}, bf16[512,1536]{1,0:T(8,128)(2,1)S(1)}, u32[]{:S(2)}) copy-start(bf16[512,1536]{1,0:T(8,128)(2,1)S(1)} %constant_dynamic-update-slice_fusion.2.v_ref) | copy-start | bytes 4718596
  103.1 12.2 %collective-permute-start.8 = (f32[12,1,256]{2,1,0:T(1,128)S(1)}, f32[12,1,256]{2,1,0:T(1,128)S(1)}, u32[]{:S(2)}, u32[]{:S(2)}) collective-permute-start(f32[12,1,256]{2,1,0:T(1,128)S(1)} %reshape_add_fusion.f_ref), channel_id=1, source_target_pairs={{1,3},{2,0},{3,5},{4,2},{5,7},{6,4},{7,9},{8,6},{9,11},{10,8},{11,... | collective-permute-start | bytes 36872 | tf_op jit(solution)/shard_map/ppermute | solution.py:26
  107.9 0.6 copy-start.13
  113.3 19.4 %collective-permute-start.11 = (f32[12,1,256]{2,1,0:T(1,128)}, f32[12,1,256]{2,1,0:T(1,128)S(1)}, u32[]{:S(2)}, u32[]{:S(2)}) collective-permute-start(f32[12,1,256]{2,1,0:T(1,128)} %shard_map.261), channel_id=1, source_target_pairs={{1,3},{2,0},{3,5},{4,2},{5,7},{6,4},{7,9},{8,6},{9,11},{10,8},{11,... | collective-permute-start | bytes 36872 | tf_op jit(solution)/shard_map/ppermute | solution.py:26
  115.3 0.6 copy-start.14
  122.3 11.2 %copy-start.10 = (f32[12,1,256]{2,1,0:T(1,128)S(1)}, f32[12,1,256]{2,1,0:T(1,128)}, u32[]{:S(2)}) copy-start(f32[12,1,256]{2,1,0:T(1,128)} %copy-done.9) | copy-start | bytes 36868
  122.3 10.5 %collective-permute-start.9 = (f32[12,1,256]{2,1,0:T(1,128)}, f32[12,1,256]{2,1,0:T(1,128)S(1)}, u32[]{:S(2)}, u32[]{:S(2)}) collective-permute-start(f32[12,1,256]{2,1,0:T(1,128)} %shard_map.260), channel_id=1, source_target_pairs={{0,2},{2,4},{3,1},{4,6},{5,3},{6,8},{7,5},{8,10},{9,7},{10,12},{11... | collective-permute-start | bytes 36872 | tf_op jit(solution)/shard_map/ppermute | solution.py:26
  133.5 7.0 %copy-start.12 = (f32[12,2,256]{2,1,0:T(2,128)}, f32[12,2,256]{2,1,0:T(2,128)S(1)}, u32[]{:S(2)}) copy-start(f32[12,2,256]{2,1,0:T(2,128)S(1)} %pad_maximum_fusion.1.f_ref) | copy-start | bytes 73732
  133.5 15.2 %collective-permute-start.13 = (f32[12,2,256]{2,1,0:T(2,128)S(1)}, f32[12,2,256]{2,1,0:T(2,128)S(1)}, u32[]{:S(2)}, u32[]{:S(2)}) collective-permute-start(f32[12,2,256]{2,1,0:T(2,128)S(1)} %pad_maximum_fusion.1.f_ref), channel_id=1, source_target_pairs={{0,2},{2,4},{3,1},{4,6},{5,3},{6,8},{7,5},{8,10},{9,7},{10,12},{11... | collective-permute-start | bytes 73736 | tf_op jit(solution)/shard_map/ppermute | solution.py:26
  136.5 12.3 %collective-permute-start.12 = (f32[12,2,256]{2,1,0:T(2,128)S(1)}, f32[12,2,256]{2,1,0:T(2,128)S(1)}, u32[]{:S(2)}, u32[]{:S(2)}) collective-permute-start(f32[12,2,256]{2,1,0:T(2,128)S(1)} %pad_maximum_fusion.1.f_ref), channel_id=1, source_target_pairs={{1,3},{2,0},{3,5},{4,2},{5,7},{6,4},{7,9},{8,6},{9,11},{10,8},{11,... | collective-permute-start | bytes 73736 | tf_op jit(solution)/shard_map/ppermute | solution.py:26
  148.8 8.9 %copy-start.21 = (f32[12,2,256]{2,1,0:T(2,128)}, f32[12,2,256]{2,1,0:T(2,128)S(1)}, u32[]{:S(2)}) copy-start(f32[12,2,256]{2,1,0:T(2,128)S(1)} %collective-permute-done.13.f_ref) | copy-start | bytes 73732
  148.8 0.6 copy-start.22
  149.4 8.3 %copy-start.4 = (bf16[512,1536]{1,0:T(8,128)(2,1)S(1)}, bf16[512,1536]{1,0:T(8,128)(2,1)}, u32[]{:S(2)}) copy-start(bf16[512,1536]{1,0:T(8,128)(2,1)} %get-tuple-element.41) | copy-start | bytes 4718596
  157.7 2.7 %copy-start.3 = (bf16[512,1536]{1,0:T(8,128)(2,1)S(1)}, bf16[512,1536]{1,0:T(8,128)(2,1)}, u32[]{:S(2)}) copy-start(bf16[512,1536]{1,0:T(8,128)(2,1)} %get-tuple-element.38) | copy-start | bytes 4718596
  157.7 2.7 %copy-start.5 = (bf16[512,1536]{1,0:T(8,128)(2,1)S(1)}, bf16[512,1536]{1,0:T(8,128)(2,1)}, u32[]{:S(2)}) copy-start(bf16[512,1536]{1,0:T(8,128)(2,1)} %get-tuple-element.37) | copy-start | bytes 4718596
  160.4 14.3 %collective-permute-start.17 = (f32[256,1536]{1,0:T(8,128)}, f32[256,1536]{1,0:T(8,128)}, u32[]{:S(2)}, u32[]{:S(2)}) collective-permute-start(f32[256,1536]{1,0:T(8,128)} %convert_add_fusion), channel_id=1, source_target_pairs={{0,1},{1,0},{2,3},{3,2},{4,5},{5,4},{6,7},{7,6},{8,9},{9,8},{10,11... | collective-permute-start | bytes 4718600 | tf_op jit(solution)/shard_map/ppermute | solution.py:26
  161.9 16.1 %collective-permute-start.16 = (f32[256,1536]{1,0:T(8,128)}, f32[256,1536]{1,0:T(8,128)}, u32[]{:S(2)}, u32[]{:S(2)}) collective-permute-start(f32[256,1536]{1,0:T(8,128)} %convert_add_fusion.1), channel_id=1, source_target_pairs={{0,1},{1,0},{2,3},{3,2},{4,5},{5,4},{6,7},{7,6},{8,9},{9,8},{10,11... | collective-permute-start | bytes 4718600 | tf_op jit(solution)/shard_map/ppermute | solution.py:26
  168.9 39.2 %collective-permute-start.15 = (bf16[256,1536]{1,0:T(8,128)(2,1)}, bf16[256,1536]{1,0:T(8,128)(2,1)S(1)}, u32[]{:S(2)}, u32[]{:S(2)}) collective-permute-start(bf16[256,1536]{1,0:T(8,128)(2,1)} %get-tuple-element.36), channel_id=1, source_target_pairs={{1,3},{2,0},{3,5},{4,2},{5,7},{6,4},{7,9},{8,6},{9,11},{10,8},{11,... | collective-permute-start | bytes 2359304 | tf_op jit(solution)/shard_map/ppermute | solution.py:26
  170.8 37.3 %collective-permute-start.14 = (bf16[256,1536]{1,0:T(8,128)(2,1)}, bf16[256,1536]{1,0:T(8,128)(2,1)S(1)}, u32[]{:S(2)}, u32[]{:S(2)}) collective-permute-start(bf16[256,1536]{1,0:T(8,128)(2,1)} %get-tuple-element.34), channel_id=1, source_target_pairs={{0,2},{2,4},{3,1},{4,6},{5,3},{6,8},{7,5},{8,10},{9,7},{10,12},{11... | collective-permute-start | bytes 2359304 | tf_op jit(solution)/shard_map/ppermute | solution.py:26
  174.7 3.3 %copy-start.6 = (bf16[512,1536]{1,0:T(8,128)(2,1)S(1)}, bf16[512,1536]{1,0:T(8,128)(2,1)}, u32[]{:S(2)}) copy-start(bf16[512,1536]{1,0:T(8,128)(2,1)} %get-tuple-element.37) | copy-start | bytes 4718596
  174.7 3.3 %copy-start.8 = (bf16[256,1536]{1,0:T(8,128)(2,1)S(1)}, bf16[256,1536]{1,0:T(8,128)(2,1)}, u32[]{:S(2)}) copy-start(bf16[256,1536]{1,0:T(8,128)(2,1)} %get-tuple-element.39) | copy-start | bytes 2359300
  178.0 30.1 %copy-start.7 = (f32[256,1536]{1,0:T(8,128)S(1)}, f32[256,1536]{1,0:T(8,128)}, u32[]{:S(2)}) copy-start(f32[256,1536]{1,0:T(8,128)} %get-tuple-element.30) | copy-start | bytes 4718596

commit v17 on v15

--- a/solution.py
+++ b/solution.py
@@ -64,7 +64,7 @@
 
 SCALE = HDIM ** (-0.5)
 NT = (((1,), (1,)), ((), ()))
-STEP_HEADS = 4
+STEP_HEADS = 6
 
 
 def slot_scores(q, g, k, v):

time: 211 us -> 210 us (level)
  transfers between devices with their start and end apart: 18 -> 18, of which waited for: 8 -> 8; matrix products, arithmetic and copies ran while one was open for 10% -> 10% of each run, Pallas kernels for 23% -> 22%
where the time goes in v17:
time: 210 us; the launch traced here: 209 us
  waiting for transfers between devices  72 us (34%)
  Pallas kernels  55.3 us (26%)
  starting transfers between devices  46.3 us (22%)
  other arithmetic  21.4 us (10%)
  local copies, waits for them, and re-layouts  12.4 us (6%)
    ppermute x18, waiting for transfers between devices, permute(): return lax.ppermute(value, 'tm', pairs)  72 us
    ppermute x18, starting transfers between devices, permute(): return lax.ppermute(value, 'tm', pairs)  46.3 us
    pallas_call x3, Pallas kernels, slot_back(): pl.pallas_call(back_kernel, grid=(HEADS // STEP_HEADS,), in_specs=slot_sp...  25 us
    pallas_call x3, Pallas kernels, slot_delta(): pl.pallas_call(delta_kernel, grid=(HEADS // STEP_HEADS,), in_specs=slot_s...  17.4 us
    pallas_call x3, Pallas kernels, slot_stats(): pl.pallas_call(stats_kernel, grid=(HEADS // STEP_HEADS,), in_specs=[slot_...  12.9 us
    unnamed x57, local copies, waits for them, and re-layouts  5.09 us
    another operation x4, other arithmetic  4.49 us
  transfers between devices with their start and end apart: 18, of which 8 were waited for; matrix products, arithmetic and copies ran while one was open for 10% of the time, Pallas kernels for 22%

profile of v17, /device:TPU:8, one launch (start us, length us, event | category | flops | bytes accessed | tf_op | source)
XLA Modules:
  0.0 209.1 jit_solution(17439915938031110802)
XLA Ops:
  0.7 3.6 %collective-permute-start.4 = (bf16[256,1536]{1,0:T(8,128)(2,1)}, bf16[256,1536]{1,0:T(8,128)(2,1)S(1)}, u32[]{:S(2)}, u32[]{:S(2)}) collective-permute-start(bf16[256,1536]{1,0:T(8,128)(2,1)} %q_ref.5), channel_id=1, source_target_pairs={{0,2},{2,4},{3,1},{4,6},{5,3},{6,8},{7,5},{8,10},{9,7},{10,12},{11... | collective-permute-start | bytes 2359304 | tf_op jit(solution)/shard_map/ppermute | solution.py:26
  4.3 3.3 %collective-permute-start.2 = (bf16[256,1536]{1,0:T(8,128)(2,1)}, bf16[256,1536]{1,0:T(8,128)(2,1)}, u32[]{:S(2)}, u32[]{:S(2)}) collective-permute-start(bf16[256,1536]{1,0:T(8,128)(2,1)} %q_ref.5), channel_id=1, source_target_pairs={{1,3},{2,0},{3,5},{4,2},{5,7},{6,4},{7,9},{8,6},{9,11},{10,8},{11,... | collective-permute-start | bytes 2359304 | tf_op jit(solution)/shard_map/ppermute | solution.py:26
  7.6 0.7 broadcast_compare_fusion
  8.4 2.1 pad_maximum_fusion
  10.5 2.5 %collective-permute-start.5 = (bf16[272,1536]{1,0:T(8,128)(2,1)}, bf16[272,1536]{1,0:T(8,128)(2,1)}, u32[]{:S(2)}, u32[]{:S(2)}) collective-permute-start(bf16[272,1536]{1,0:T(8,128)(2,1)} %pad_maximum_fusion), channel_id=1, source_target_pairs={{0,2},{2,4},{3,1},{4,6},{5,3},{6,8},{7,5},{8,10},{9,7},{10,12},{11... | collective-permute-start | bytes 2506760 | tf_op jit(solution)/shard_map/ppermute | solution.py:26
  13.0 4.2 %collective-permute-start.3 = (bf16[272,1536]{1,0:T(8,128)(2,1)}, bf16[272,1536]{1,0:T(8,128)(2,1)}, u32[]{:S(2)}, u32[]{:S(2)}) collective-permute-start(bf16[272,1536]{1,0:T(8,128)(2,1)} %pad_maximum_fusion), channel_id=1, source_target_pairs={{1,3},{2,0},{3,5},{4,2},{5,7},{6,4},{7,9},{8,6},{9,11},{10,8},{11,... | collective-permute-start | bytes 2506760 | tf_op jit(solution)/shard_map/ppermute | solution.py:26
  17.4 0.1 fusion.2
  17.7 0.2 broadcast_in_dim.31
  17.9 1.4 convert_element_type.88.m_ref
  19.3 0.4 collective-permute-done
  19.7 0.1 collective-permute-start.1
  19.9 1.2 constant_dynamic-update-slice_fusion.k_ref
  21.1 1.1 copy-done.1
  22.2 4.7 %shard_map.256 = f32[12,2,256]{2,1,0:T(2,128)} custom-call(bf16[256,1536]{1,0:T(8,128)(2,1)} %q_ref.5, bf16[512,1536]{1,0:T(8,128)(2,1)} %copy-done.1, f32[512,256]{1,0:T(8,128)} %convert_element_type.88.m_ref), custom_call_target="tpu_custom_call" | custom-call | flops 402653184 | bytes 4718592 | tf_op jit(solution)/shard_map/pallas_call | solution.py:134
  26.9 30.0 %collective-permute-done.4.q_ref = bf16[256,1536]{1,0:T(8,128)(2,1)S(1)} collective-permute-done((bf16[256,1536]{1,0:T(8,128)(2,1)}, bf16[256,1536]{1,0:T(8,128)(2,1)S(1)}, u32[]{:S(2)}, u32[]{:S(2)}) %collective-permute-start.4) | collective-permute-done | bytes 786464 | tf_op jit(solution)/shard_map/ppermute | solution.py:26
  57.0 2.4 %collective-permute-done.2.q_ref = bf16[256,1536]{1,0:T(8,128)(2,1)} collective-permute-done((bf16[256,1536]{1,0:T(8,128)(2,1)}, bf16[256,1536]{1,0:T(8,128)(2,1)}, u32[]{:S(2)}, u32[]{:S(2)}) %collective-permute-start.2) | collective-permute-done | bytes 786464 | tf_op jit(solution)/shard_map/ppermute | solution.py:26
  59.3 15.5 %collective-permute-done.5.g_ref = bf16[272,1536]{1,0:T(8,128)(2,1)} collective-permute-done((bf16[272,1536]{1,0:T(8,128)(2,1)}, bf16[272,1536]{1,0:T(8,128)(2,1)}, u32[]{:S(2)}, u32[]{:S(2)}) %collective-permute-start.5) | collective-permute-done | bytes 835616 | tf_op jit(solution)/shard_map/ppermute | solution.py:26
  74.9 0.2 collective-permute-done.3.g_ref
  75.0 0.6 compare_reduce_fusion.1
  75.7 0.7 compare_reduce_fusion
  76.4 0.1 fusion.13
  76.7 0.1 fusion.6
  76.9 0.1 broadcast_in_dim.34
  77.1 1.1 convert_element_type.94.m_ref
  78.2 3.3 %shard_map.258 = f32[12,2,256]{2,1,0:T(2,128)} custom-call(bf16[256,1536]{1,0:T(8,128)(2,1)} %copy-done.8, bf16[256,1536]{1,0:T(8,128)(2,1)} %k_ref.5, f32[256,256]{1,0:T(8,128)} %convert_element_type.94.m_ref), custom_call_target="tpu_custom_call" | custom-call | flops 201326592 | bytes 3145728 | tf_op jit(solution)/shard_map/pallas_call | solution.py:134
  81.5 4.1 %collective-permute-start.7 = (f32[12,2,256]{2,1,0:T(2,128)}, f32[12,2,256]{2,1,0:T(2,128)S(1)}, u32[]{:S(2)}, u32[]{:S(2)}) collective-permute-start(f32[12,2,256]{2,1,0:T(2,128)} %shard_map.258), channel_id=1, source_target_pairs={{1,3},{2,0},{3,5},{4,2},{5,7},{6,4},{7,9},{8,6},{9,11},{10,8},{11,... | collective-permute-start | bytes 73736 | tf_op jit(solution)/shard_map/ppermute | solution.py:26
  85.7 0.2 broadcast_in_dim.33
  85.9 1.4 convert_element_type.91.m_ref
  87.3 4.8 %shard_map.257 = f32[12,2,256]{2,1,0:T(2,128)} custom-call(bf16[256,1536]{1,0:T(8,128)(2,1)} %collective-permute-done.2.q_ref, bf16[512,1536]{1,0:T(8,128)(2,1)} %copy-done.1, f32[512,256]{1,0:T(8,128)} %convert_element_type.91.m_ref), custom_call_target="tpu_custom_call" | custom-call | flops 402653184 | bytes 4718592 | tf_op jit(solution)/shard_map/pallas_call | solution.py:134
  92.1 2.0 collective-permute-start.6
  94.2 4.7 %collective-permute-done.6 = f32[12,2,256]{2,1,0:T(2,128)S(1)} collective-permute-done((f32[12,2,256]{2,1,0:T(2,128)}, f32[12,2,256]{2,1,0:T(2,128)S(1)}, u32[]{:S(2)}, u32[]{:S(2)}) %collective-permute-start.6) | collective-permute-done | bytes 24608 | tf_op jit(solution)/shard_map/ppermute | solution.py:26
  99.0 0.1 fusion
  99.2 1.9 collective-permute-start.10
  101.1 1.2 constant_dynamic-update-slice_fusion.2.v_ref
  102.3 4.8 %collective-permute-start.8 = (f32[12,1,256]{2,1,0:T(1,128)S(1)}, f32[12,1,256]{2,1,0:T(1,128)S(1)}, u32[]{:S(2)}, u32[]{:S(2)}) collective-permute-start(f32[12,1,256]{2,1,0:T(1,128)S(1)} %reshape_add_fusion.f_ref), channel_id=1, source_target_pairs={{1,3},{2,0},{3,5},{4,2},{5,7},{6,4},{7,9},{8,6},{9,11},{10,8},{11,... | collective-permute-start | bytes 36872 | tf_op jit(solution)/shard_map/ppermute | solution.py:26
  107.2 0.6 copy-done.16
  107.8 4.3 %shard_map.261 = f32[12,1,256]{2,1,0:T(1,128)} custom-call(bf16[256,1536]{1,0:T(8,128)(2,1)} %copy-done.8, bf16[272,1536]{1,0:T(8,128)(2,1)} %collective-permute-done.5.g_ref, bf16[256,1536]{1,0:T(8,128)(2,1)} %k_ref.5, bf16[256,1536]{1,0:T(8,128)(2,1)} %v_ref.3, f32[256,256]{1,0:T(8,128)} %convert_element_type.94.m_ref, f32[12,1,256]{2,1,0:T(1,128)} %copy-done.16), custom_call_target="tpu_custom_call" | custom-call | flops 402653184 | bytes 3145728 | tf_op jit(solution)/shard_map/pallas_call | solution.py:149
  112.1 1.9 collective-permute-start.11
  114.0 0.6 copy-done.17
  114.6 6.5 %shard_map.260 = f32[12,1,256]{2,1,0:T(1,128)} custom-call(bf16[256,1536]{1,0:T(8,128)(2,1)} %collective-permute-done.2.q_ref, bf16[272,1536]{1,0:T(8,128)(2,1)} %collective-permute-done.3.g_ref, bf16[512,1536]{1,0:T(8,128)(2,1)} %copy-done.1, bf16[512,1536]{1,0:T(8,128)(2,1)} %copy-done, f32[512,256]{1,0:T(8,128)} %convert_element_type.91.m_ref, ...), custom_call_target="tpu_custom_call" | custom-call | flops 805306368 | bytes 4718592 | tf_op jit(solution)/shard_map/pallas_call | solution.py:149
  121.2 4.2 %collective-permute-start.9 = (f32[12,1,256]{2,1,0:T(1,128)}, f32[12,1,256]{2,1,0:T(1,128)S(1)}, u32[]{:S(2)}, u32[]{:S(2)}) collective-permute-start(f32[12,1,256]{2,1,0:T(1,128)} %shard_map.260), channel_id=1, source_target_pairs={{0,2},{2,4},{3,1},{4,6},{5,3},{6,8},{7,5},{8,10},{9,7},{10,12},{11... | collective-permute-start | bytes 36872 | tf_op jit(solution)/shard_map/ppermute | solution.py:26
  125.4 6.5 %shard_map.259 = f32[12,1,256]{2,1,0:T(1,128)} custom-call(bf16[256,1536]{1,0:T(8,128)(2,1)} %q_ref.5, bf16[256,1536]{1,0:T(8,128)(2,1)} %g_ref.3, bf16[512,1536]{1,0:T(8,128)(2,1)} %copy-done.1, bf16[512,1536]{1,0:T(8,128)(2,1)} %copy-done, f32[512,256]{1,0:T(8,128)} %convert_element_type.88.m_ref, f32[12,1,256]{2,1,0:T(1,128)} %copy-done.12), custom_call_target="tpu_custom_call" | custom-call | flops 805306368 | bytes 4718592 | tf_op jit(solution)/shard_map/pallas_call | solution.py:149
  131.9 0.7 add_add_fusion
  132.7 2.9 %collective-permute-start.13 = (f32[12,2,256]{2,1,0:T(2,128)S(1)}, f32[12,2,256]{2,1,0:T(2,128)S(1)}, u32[]{:S(2)}, u32[]{:S(2)}) collective-permute-start(f32[12,2,256]{2,1,0:T(2,128)S(1)} %pad_maximum_fusion.1.f_ref), channel_id=1, source_target_pairs={{0,2},{2,4},{3,1},{4,6},{5,3},{6,8},{7,5},{8,10},{9,7},{10,12},{11... | collective-permute-start | bytes 73736 | tf_op jit(solution)/shard_map/ppermute | solution.py:26
  135.6 3.8 %collective-permute-start.12 = (f32[12,2,256]{2,1,0:T(2,128)S(1)}, f32[12,2,256]{2,1,0:T(2,128)S(1)}, u32[]{:S(2)}, u32[]{:S(2)}) collective-permute-start(f32[12,2,256]{2,1,0:T(2,128)S(1)} %pad_maximum_fusion.1.f_ref), channel_id=1, source_target_pairs={{1,3},{2,0},{3,5},{4,2},{5,7},{6,4},{7,9},{8,6},{9,11},{10,8},{11,... | collective-permute-start | bytes 73736 | tf_op jit(solution)/shard_map/ppermute | solution.py:26
  139.5 9.1 %shard_map.262 = (f32[256,1536]{1,0:T(8,128)}, f32[512,1536]{1,0:T(8,128)}, f32[512,1536]{1,0:T(8,128)}) custom-call(bf16[256,1536]{1,0:T(8,128)(2,1)} %q_ref.5, bf16[256,1536]{1,0:T(8,128)(2,1)} %g_ref.3, bf16[512,1536]{1,0:T(8,128)(2,1)} %copy-done.1, bf16[512,1536]{1,0:T(8,128)(2,1)} %copy-done, f32[512,256]{1,0:T(8,128)} %convert_element_type.88.m_ref, ...), custom_call_target="tpu_custom_call" | custom-call | flops 2013265920 | bytes 14155776 | tf_op jit(solution)/shard_map/pallas_call | solution.py:166
  148.7 2.1 convert.25
  150.8 9.0 %shard_map.263 = (bf16[256,1536]{1,0:T(8,128)(2,1)}, f32[512,1536]{1,0:T(8,128)}, f32[512,1536]{1,0:T(8,128)}) custom-call(bf16[256,1536]{1,0:T(8,128)(2,1)} %collective-permute-done.2.q_ref, bf16[272,1536]{1,0:T(8,128)(2,1)} %collective-permute-done.3.g_ref, bf16[512,1536]{1,0:T(8,128)(2,1)} %copy-done.1, bf16[512,1536]{1,0:T(8,128)(2,1)} %copy-done, ...), custom_call_target="tpu_custom_call" | custom-call | flops 2013265920 | bytes 14155776 | tf_op jit(solution)/shard_map/pallas_call | solution.py:166
  159.8 2.1 convert.24
  161.9 1.4 convert_add_fusion
  163.3 0.3 copy-done.5
  163.5 1.3 copy-done.6
  164.9 0.2 convert.23
  165.1 0.9 copy-done.7
  166.0 0.2 convert.22
  166.2 1.6 convert_add_fusion.1
  167.8 2.0 collective-permute-start.14
  169.8 6.9 %shard_map.264 = (bf16[256,1536]{1,0:T(8,128)(2,1)}, f32[256,1536]{1,0:T(8,128)}, f32[256,1536]{1,0:T(8,128)}) custom-call(bf16[256,1536]{1,0:T(8,128)(2,1)} %copy-done.8, bf16[272,1536]{1,0:T(8,128)(2,1)} %collective-permute-done.5.g_ref, bf16[256,1536]{1,0:T(8,128)(2,1)} %k_ref.5, bf16[256,1536]{1,0:T(8,128)(2,1)} %v_ref.3, ...), custom_call_target="tpu_custom_call" | custom-call | flops 1006632960 | bytes 9437184 | tf_op jit(solution)/shard_map/pallas_call | solution.py:166
  176.7 4.7 %collective-permute-start.15 = (bf16[256,1536]{1,0:T(8,128)(2,1)}, bf16[256,1536]{1,0:T(8,128)(2,1)S(1)}, u32[]{:S(2)}, u32[]{:S(2)}) collective-permute-start(bf16[256,1536]{1,0:T(8,128)(2,1)} %get-tuple-element.36), channel_id=1, source_target_pairs={{1,3},{2,0},{3,5},{4,2},{5,7},{6,4},{7,9},{8,6},{9,11},{10,8},{11,... | collective-permute-start | bytes 2359304 | tf_op jit(solution)/shard_map/ppermute | solution.py:26
  181.5 3.6 %add_convert_fusion.1 = bf16[256,1536]{1,0:T(8,128)(2,1)} fusion(f32[256,1536]{1,0:T(8,128)} %collective-permute-done.17, bf16[512,1536]{1,0:T(8,128)(2,1)S(1)} %convert.25, bf16[512,1536]{1,0:T(8,128)(2,1)} %copy-done.5, f32[256,1536]{1,0:T(8,128)} %get-tuple-element.42), kind=kLoop, calls=%fused_computation.1 | loop fusion | flops 3145728 | bytes 5505024 | tf_op jit(solution)/shard_map/convert_element_type | solution.py:276
  185.1 2.8 %add_convert_fusion.2 = bf16[256,1536]{1,0:T(8,128)(2,1)} fusion(f32[256,1536]{1,0:T(8,128)} %collective-permute-done.16, bf16[512,1536]{1,0:T(8,128)(2,1)S(1)} %convert.23, bf16[512,1536]{1,0:T(8,128)(2,1)S(1)} %copy-done.4, f32[256,1536]{1,0:T(8,128)S(1)} %copy-done.11), kind=kLoop, calls=%fused_computation.3 | loop fusion | flops 3145728 | bytes 5505024 | tf_op jit(solution)/shard_map/convert_element_type | solution.py:275
  187.9 15.4 %collective-permute-done.14 = bf16[256,1536]{1,0:T(8,128)(2,1)} collective-permute-done((bf16[256,1536]{1,0:T(8,128)(2,1)}, bf16[256,1536]{1,0:T(8,128)(2,1)}, u32[]{:S(2)}, u32[]{:S(2)}) %collective-permute-start.14) | collective-permute-done | bytes 786464 | tf_op jit(solution)/shard_map/ppermute | solution.py:26
  203.3 3.4 %collective-permute-done.15 = bf16[256,1536]{1,0:T(8,128)(2,1)S(1)} collective-permute-done((bf16[256,1536]{1,0:T(8,128)(2,1)}, bf16[256,1536]{1,0:T(8,128)(2,1)S(1)}, u32[]{:S(2)}, u32[]{:S(2)}) %collective-permute-start.15) | collective-permute-done | bytes 786464 | tf_op jit(solution)/shard_map/ppermute | solution.py:26
  206.7 2.4 %add_convert_fusion = bf16[256,1536]{1,0:T(8,128)(2,1)} fusion(bf16[256,1536]{1,0:T(8,128)(2,1)S(1)} %collective-permute-done.15, f32[256,1536]{1,0:T(8,128)S(1)} %copy-done.10, bf16[256,1536]{1,0:T(8,128)(2,1)} %collective-permute-done.14), kind=kLoop, calls=%fused_computation | loop fusion | flops 1966080 | bytes 3932160 | tf_op jit(solution)/shard_map/convert_element_type | solution.py:281
  (82 shorter events, 1.2 us)
Async XLA Ops:
  0.6 16.7 %copy-start.19 = (bf16[4,30,4]{1,2,0:T(4,128)(2,1)S(1)}, bf16[4,30,4]{1,2,0:T(4,128)(2,1)}, u32[]{:S(2)}) copy-start(bf16[4,30,4]{1,2,0:T(4,128)(2,1)} %constant.124) | copy-start | bytes 2884
  0.6 16.7 %copy-start.20 = (bf16[4,30,4]{1,2,0:T(4,128)(2,1)S(1)}, bf16[4,30,4]{1,2,0:T(4,128)(2,1)}, u32[]{:S(2)}) copy-start(bf16[4,30,4]{1,2,0:T(4,128)(2,1)} %constant.125) | copy-start | bytes 2884
  0.7 16.7 %copy-start.21 = (bf16[4,30,4]{1,2,0:T(4,128)(2,1)S(1)}, bf16[4,30,4]{1,2,0:T(4,128)(2,1)}, u32[]{:S(2)}) copy-start(bf16[4,30,4]{1,2,0:T(4,128)(2,1)} %constant.122) | copy-start | bytes 2884
  0.7 16.7 %copy-start.22 = (bf16[4,30,4]{1,2,0:T(4,128)(2,1)S(1)}, bf16[4,30,4]{1,2,0:T(4,128)(2,1)}, u32[]{:S(2)}) copy-start(bf16[4,30,4]{1,2,0:T(4,128)(2,1)} %constant.121) | copy-start | bytes 2884
  0.7 16.7 %copy-start.26 = (bf16[4,30,4]{1,2,0:T(4,128)(2,1)S(1)}, bf16[4,30,4]{1,2,0:T(4,128)(2,1)}, u32[]{:S(2)}) copy-start(bf16[4,30,4]{1,2,0:T(4,128)(2,1)} %constant.123) | copy-start | bytes 2884
  0.7 17.0 %copy-start.23 = (pred[4,8]{0,1:T(8,128)(4,1)S(1)}, pred[4,8]{0,1:T(8,128)(4,1)}, u32[]{:S(2)}) copy-start(pred[4,8]{0,1:T(8,128)(4,1)} %constant.62) | copy-start | bytes 100
  0.7 16.7 %copy-start.18 = (s32[4,30]{1,0:T(4,128)S(1)}, s32[4,30]{1,0:T(4,128)}, u32[]{:S(2)}) copy-start(s32[4,30]{1,0:T(4,128)} %param.29) | copy-start | bytes 1444
  0.7 16.5 %copy-start.2 = (bf16[256,1536]{1,0:T(8,128)(2,1)S(1)}, bf16[256,1536]{1,0:T(8,128)(2,1)}, u32[]{:S(2)}) copy-start(bf16[256,1536]{1,0:T(8,128)(2,1)} %k_ref.5) | copy-start | bytes 2359300
  0.7 56.2 %collective-permute-start.4 = (bf16[256,1536]{1,0:T(8,128)(2,1)}, bf16[256,1536]{1,0:T(8,128)(2,1)S(1)}, u32[]{:S(2)}, u32[]{:S(2)}) collective-permute-start(bf16[256,1536]{1,0:T(8,128)(2,1)} %q_ref.5), channel_id=1, source_target_pairs={{0,2},{2,4},{3,1},{4,6},{5,3},{6,8},{7,5},{8,10},{9,7},{10,12},{11... | collective-permute-start | bytes 2359304 | tf_op jit(solution)/shard_map/ppermute | solution.py:26
  4.3 55.0 %collective-permute-start.2 = (bf16[256,1536]{1,0:T(8,128)(2,1)}, bf16[256,1536]{1,0:T(8,128)(2,1)}, u32[]{:S(2)}, u32[]{:S(2)}) collective-permute-start(bf16[256,1536]{1,0:T(8,128)(2,1)} %q_ref.5), channel_id=1, source_target_pairs={{1,3},{2,0},{3,5},{4,2},{5,7},{6,4},{7,9},{8,6},{9,11},{10,8},{11,... | collective-permute-start | bytes 2359304 | tf_op jit(solution)/shard_map/ppermute | solution.py:26
  10.5 64.4 %collective-permute-start.5 = (bf16[272,1536]{1,0:T(8,128)(2,1)}, bf16[272,1536]{1,0:T(8,128)(2,1)}, u32[]{:S(2)}, u32[]{:S(2)}) collective-permute-start(bf16[272,1536]{1,0:T(8,128)(2,1)} %pad_maximum_fusion), channel_id=1, source_target_pairs={{0,2},{2,4},{3,1},{4,6},{5,3},{6,8},{7,5},{8,10},{9,7},{10,12},{11... | collective-permute-start | bytes 2506760 | tf_op jit(solution)/shard_map/ppermute | solution.py:26
  13.0 62.0 %collective-permute-start.3 = (bf16[272,1536]{1,0:T(8,128)(2,1)}, bf16[272,1536]{1,0:T(8,128)(2,1)}, u32[]{:S(2)}, u32[]{:S(2)}) collective-permute-start(bf16[272,1536]{1,0:T(8,128)(2,1)} %pad_maximum_fusion), channel_id=1, source_target_pairs={{1,3},{2,0},{3,5},{4,2},{5,7},{6,4},{7,9},{8,6},{9,11},{10,8},{11,... | collective-permute-start | bytes 2506760 | tf_op jit(solution)/shard_map/ppermute | solution.py:26
  17.3 2.5 %collective-permute-start = (bf16[256,1536]{1,0:T(8,128)(2,1)S(1)}, bf16[256,1536]{1,0:T(8,128)(2,1)}, u32[]{:S(2)}, u32[]{:S(2)}) collective-permute-start(bf16[256,1536]{1,0:T(8,128)(2,1)S(1)} %copy-done.2), channel_id=1, source_target_pairs={{0,1},{1,0},{2,3},{3,2},{4,5},{5,4},{6,7},{7,6},{8,9},{9,8},{10,11... | collective-permute-start | bytes 2359304 | tf_op jit(solution)/shard_map/ppermute | solution.py:26
  19.7 81.4 %collective-permute-start.1 = (bf16[256,1536]{1,0:T(8,128)(2,1)}, bf16[256,1536]{1,0:T(8,128)(2,1)}, u32[]{:S(2)}, u32[]{:S(2)}) collective-permute-start(bf16[256,1536]{1,0:T(8,128)(2,1)} %v_ref.3), channel_id=1, source_target_pairs={{0,1},{1,0},{2,3},{3,2},{4,5},{5,4},{6,7},{7,6},{8,9},{9,8},{10,11... | collective-permute-start | bytes 2359304 | tf_op jit(solution)/shard_map/ppermute | solution.py:26
  21.1 1.1 copy-start.1
  57.0 21.2 %copy-start.8 = (bf16[256,1536]{1,0:T(8,128)(2,1)}, bf16[256,1536]{1,0:T(8,128)(2,1)S(1)}, u32[]{:S(2)}) copy-start(bf16[256,1536]{1,0:T(8,128)(2,1)S(1)} %collective-permute-done.4.q_ref) | copy-start | bytes 2359300
  81.5 12.7 %collective-permute-start.7 = (f32[12,2,256]{2,1,0:T(2,128)}, f32[12,2,256]{2,1,0:T(2,128)S(1)}, u32[]{:S(2)}, u32[]{:S(2)}) collective-permute-start(f32[12,2,256]{2,1,0:T(2,128)} %shard_map.258), channel_id=1, source_target_pairs={{1,3},{2,0},{3,5},{4,2},{5,7},{6,4},{7,9},{8,6},{9,11},{10,8},{11,... | collective-permute-start | bytes 73736 | tf_op jit(solution)/shard_map/ppermute | solution.py:26
  87.3 6.8 %copy-start.9 = (bf16[256,1536]{1,0:T(8,128)(2,1)S(1)}, bf16[256,1536]{1,0:T(8,128)(2,1)}, u32[]{:S(2)}) copy-start(bf16[256,1536]{1,0:T(8,128)(2,1)} %v_ref.3) | copy-start | bytes 2359300
  87.3 11.6 %copy-start.14 = (f32[12,2,256]{2,1,0:T(2,128)S(1)}, f32[12,2,256]{2,1,0:T(2,128)}, u32[]{:S(2)}) copy-start(f32[12,2,256]{2,1,0:T(2,128)} %shard_map.256) | copy-start | bytes 73732
  92.1 6.8 %collective-permute-start.6 = (f32[12,2,256]{2,1,0:T(2,128)}, f32[12,2,256]{2,1,0:T(2,128)S(1)}, u32[]{:S(2)}, u32[]{:S(2)}) collective-permute-start(f32[12,2,256]{2,1,0:T(2,128)} %shard_map.257), channel_id=1, source_target_pairs={{0,2},{2,4},{3,1},{4,6},{5,3},{6,8},{7,5},{8,10},{9,7},{10,12},{11... | collective-permute-start | bytes 73736 | tf_op jit(solution)/shard_map/ppermute | solution.py:26
  99.2 12.9 %copy-start.12 = (f32[12,1,256]{2,1,0:T(1,128)}, f32[12,1,256]{2,1,0:T(1,128)S(1)}, u32[]{:S(2)}) copy-start(f32[12,1,256]{2,1,0:T(1,128)S(1)} %reshape_add_fusion.f_ref) | copy-start | bytes 36868
  99.2 8.0 %collective-permute-start.10 = (f32[12,1,256]{2,1,0:T(1,128)S(1)}, f32[12,1,256]{2,1,0:T(1,128)S(1)}, u32[]{:S(2)}, u32[]{:S(2)}) collective-permute-start(f32[12,1,256]{2,1,0:T(1,128)S(1)} %reshape_add_fusion.f_ref), channel_id=1, source_target_pairs={{0,2},{2,4},{3,1},{4,6},{5,3},{6,8},{7,5},{8,10},{9,7},{10,12},{11... | collective-permute-start | bytes 36872 | tf_op jit(solution)/shard_map/ppermute | solution.py:26
  102.3 9.8 %copy-start = (bf16[512,1536]{1,0:T(8,128)(2,1)}, bf16[512,1536]{1,0:T(8,128)(2,1)S(1)}, u32[]{:S(2)}) copy-start(bf16[512,1536]{1,0:T(8,128)(2,1)S(1)} %constant_dynamic-update-slice_fusion.2.v_ref) | copy-start | bytes 4718596
  102.3 11.7 %collective-permute-start.8 = (f32[12,1,256]{2,1,0:T(1,128)S(1)}, f32[12,1,256]{2,1,0:T(1,128)S(1)}, u32[]{:S(2)}, u32[]{:S(2)}) collective-permute-start(f32[12,1,256]{2,1,0:T(1,128)S(1)} %reshape_add_fusion.f_ref), channel_id=1, source_target_pairs={{1,3},{2,0},{3,5},{4,2},{5,7},{6,4},{7,9},{8,6},{9,11},{10,8},{11,... | collective-permute-start | bytes 36872 | tf_op jit(solution)/shard_map/ppermute | solution.py:26
  107.2 0.6 copy-start.16
  112.1 19.8 %collective-permute-start.11 = (f32[12,1,256]{2,1,0:T(1,128)}, f32[12,1,256]{2,1,0:T(1,128)S(1)}, u32[]{:S(2)}, u32[]{:S(2)}) collective-permute-start(f32[12,1,256]{2,1,0:T(1,128)} %shard_map.261), channel_id=1, source_target_pairs={{1,3},{2,0},{3,5},{4,2},{5,7},{6,4},{7,9},{8,6},{9,11},{10,8},{11,... | collective-permute-start | bytes 36872 | tf_op jit(solution)/shard_map/ppermute | solution.py:26
  114.0 0.6 copy-start.17
  121.2 11.5 %copy-start.13 = (f32[12,1,256]{2,1,0:T(1,128)S(1)}, f32[12,1,256]{2,1,0:T(1,128)}, u32[]{:S(2)}) copy-start(f32[12,1,256]{2,1,0:T(1,128)} %copy-done.12) | copy-start | bytes 36868
  121.2 10.8 %collective-permute-start.9 = (f32[12,1,256]{2,1,0:T(1,128)}, f32[12,1,256]{2,1,0:T(1,128)S(1)}, u32[]{:S(2)}, u32[]{:S(2)}) collective-permute-start(f32[12,1,256]{2,1,0:T(1,128)} %shard_map.260), channel_id=1, source_target_pairs={{0,2},{2,4},{3,1},{4,6},{5,3},{6,8},{7,5},{8,10},{9,7},{10,12},{11... | collective-permute-start | bytes 36872 | tf_op jit(solution)/shard_map/ppermute | solution.py:26
  132.7 6.8 %copy-start.15 = (f32[12,2,256]{2,1,0:T(2,128)}, f32[12,2,256]{2,1,0:T(2,128)S(1)}, u32[]{:S(2)}) copy-start(f32[12,2,256]{2,1,0:T(2,128)S(1)} %pad_maximum_fusion.1.f_ref) | copy-start | bytes 73732
  132.7 15.9 %collective-permute-start.13 = (f32[12,2,256]{2,1,0:T(2,128)S(1)}, f32[12,2,256]{2,1,0:T(2,128)S(1)}, u32[]{:S(2)}, u32[]{:S(2)}) collective-permute-start(f32[12,2,256]{2,1,0:T(2,128)S(1)} %pad_maximum_fusion.1.f_ref), channel_id=1, source_target_pairs={{0,2},{2,4},{3,1},{4,6},{5,3},{6,8},{7,5},{8,10},{9,7},{10,12},{11... | collective-permute-start | bytes 73736 | tf_op jit(solution)/shard_map/ppermute | solution.py:26
  135.6 13.0 %collective-permute-start.12 = (f32[12,2,256]{2,1,0:T(2,128)S(1)}, f32[12,2,256]{2,1,0:T(2,128)S(1)}, u32[]{:S(2)}, u32[]{:S(2)}) collective-permute-start(f32[12,2,256]{2,1,0:T(2,128)S(1)} %pad_maximum_fusion.1.f_ref), channel_id=1, source_target_pairs={{1,3},{2,0},{3,5},{4,2},{5,7},{6,4},{7,9},{8,6},{9,11},{10,8},{11,... | collective-permute-start | bytes 73736 | tf_op jit(solution)/shard_map/ppermute | solution.py:26
  148.6 2.1 %copy-start.24 = (f32[12,2,256]{2,1,0:T(2,128)}, f32[12,2,256]{2,1,0:T(2,128)S(1)}, u32[]{:S(2)}) copy-start(f32[12,2,256]{2,1,0:T(2,128)S(1)} %collective-permute-done.13.f_ref) | copy-start | bytes 73732
  148.7 2.1 %copy-start.25 = (f32[12,2,256]{2,1,0:T(2,128)}, f32[12,2,256]{2,1,0:T(2,128)S(1)}, u32[]{:S(2)}) copy-start(f32[12,2,256]{2,1,0:T(2,128)S(1)} %collective-permute-done.12.f_ref) | copy-start | bytes 73732
  161.8 1.7 copy-start.5
  161.9 3.0 %copy-start.6 = (f32[512,1536]{1,0:T(8,128)S(1)}, f32[512,1536]{1,0:T(8,128)}, u32[]{:S(2)}) copy-start(f32[512,1536]{1,0:T(8,128)} %get-tuple-element.38) | copy-start | bytes 9437188
  163.5 2.4 %copy-start.7 = (f32[512,1536]{1,0:T(8,128)S(1)}, f32[512,1536]{1,0:T(8,128)}, u32[]{:S(2)}) copy-start(f32[512,1536]{1,0:T(8,128)} %get-tuple-element.37) | copy-start | bytes 9437188
  163.5 17.9 %collective-permute-start.17 = (f32[256,1536]{1,0:T(8,128)}, f32[256,1536]{1,0:T(8,128)}, u32[]{:S(2)}, u32[]{:S(2)}) collective-permute-start(f32[256,1536]{1,0:T(8,128)} %convert_add_fusion), channel_id=1, source_target_pairs={{0,1},{1,0},{2,3},{3,2},{4,5},{5,4},{6,7},{7,6},{8,9},{9,8},{10,11... | collective-permute-start | bytes 4718600 | tf_op jit(solution)/shard_map/ppermute | solution.py:26
  166.2 1.7 copy-start.3
  167.8 17.2 %collective-permute-start.16 = (f32[256,1536]{1,0:T(8,128)}, f32[256,1536]{1,0:T(8,128)}, u32[]{:S(2)}, u32[]{:S(2)}) collective-permute-start(f32[256,1536]{1,0:T(8,128)} %convert_add_fusion.1), channel_id=1, source_target_pairs={{0,1},{1,0},{2,3},{3,2},{4,5},{5,4},{6,7},{7,6},{8,9},{9,8},{10,11... | collective-permute-start | bytes 4718600 | tf_op jit(solution)/shard_map/ppermute | solution.py:26
  167.8 35.5 %collective-permute-start.14 = (bf16[256,1536]{1,0:T(8,128)(2,1)}, bf16[256,1536]{1,0:T(8,128)(2,1)}, u32[]{:S(2)}, u32[]{:S(2)}) collective-permute-start(bf16[256,1536]{1,0:T(8,128)(2,1)} %get-tuple-element.34), channel_id=1, source_target_pairs={{0,2},{2,4},{3,1},{4,6},{5,3},{6,8},{7,5},{8,10},{9,7},{10,12},{11... | collective-permute-start | bytes 2359304 | tf_op jit(solution)/shard_map/ppermute | solution.py:26
  176.7 30.0 %collective-permute-start.15 = (bf16[256,1536]{1,0:T(8,128)(2,1)}, bf16[256,1536]{1,0:T(8,128)(2,1)S(1)}, u32[]{:S(2)}, u32[]{:S(2)}) collective-permute-start(bf16[256,1536]{1,0:T(8,128)(2,1)} %get-tuple-element.36), channel_id=1, source_target_pairs={{1,3},{2,0},{3,5},{4,2},{5,7},{6,4},{7,9},{8,6},{9,11},{10,8},{11,... | collective-permute-start | bytes 2359304 | tf_op jit(solution)/shard_map/ppermute | solution.py:26
  181.4 3.6 %copy-start.4 = (bf16[512,1536]{1,0:T(8,128)(2,1)S(1)}, bf16[512,1536]{1,0:T(8,128)(2,1)}, u32[]{:S(2)}) copy-start(bf16[512,1536]{1,0:T(8,128)(2,1)} %copy-done.3) | copy-start | bytes 4718596
  181.4 3.6 %copy-start.11 = (f32[256,1536]{1,0:T(8,128)S(1)}, f32[256,1536]{1,0:T(8,128)}, u32[]{:S(2)}) copy-start(f32[256,1536]{1,0:T(8,128)} %get-tuple-element.39) | copy-start | bytes 4718596
  185.0 21.7 %copy-start.10 = (f32[256,1536]{1,0:T(8,128)S(1)}, f32[256,1536]{1,0:T(8,128)}, u32[]{:S(2)}) copy-start(f32[256,1536]{1,0:T(8,128)} %get-tuple-element.30) | copy-start | bytes 4718596
